TPU v7x, 256 devices: a whole 4x4x8 slice. The times are simulated.
256 devices in a mesh: row: 8 (over y, core), col: 8 (over z_hi, x), page: 4 (over z_lo).
Axes of the slice: x: 4, y: 4, z: 8 (z_hi: 2, z_lo: 4; z = z_hi * 4 + z_lo), core: 2. Of those that a mesh axis runs over, the one named last changes fastest.
Arguments:
- tokens: bfloat16 [32, 512, 2048], P(('row', 'page'), None, 'col'), may hold values from -6 to 6
- lengths: int32 [32], P(('row', 'page')), may hold values from 1 to 512, 4096 in all
- page_slot: int32 [32, 4], P('row'), may hold values from 0 to 15, as said below
- w_query: float32 [2048, 1024], P(('row', 'page'), 'col'), may hold values from -0.125 to 0.125
- w_keyval: float32 [2, 2048, 256], P(None, ('row', 'page')), may hold values from -0.125 to 0.125
- w_out: float32 [1024, 2048], P('col', ('row', 'page')), may hold values from -0.1875 to 0.1875
- w_gateup: float32 [2, 2048, 5120], P(None, ('row', 'page'), 'col'), may hold values from -0.125 to 0.125
- w_down: float32 [5120, 2048], P('col', ('row', 'page')), may hold values from -0.078125 to 0.078125
- attn_gain: float32 [2048], replicated, may hold values from 0.1 to 1.9
- ffn_gain: float32 [2048], replicated, may hold values from 0.1 to 1.9
- query_gain: float32 [64], replicated, may hold values from 0.1 to 1.9
- key_gain: float32 [64], replicated, may hold values from 0.1 to 1.9
Outputs:
- layer_out: bfloat16 [32, 512, 2048], P(('row', 'page'), None, 'col')
- kv_pages: bfloat16 [2, 128, 128, 1024], P(None, ('row', 'page'), None, 'col')
Inputs may be any that keep to these rules, and one draw needn't show every extreme that they name: `lengths`: each prompt's real tokens; in every draw some prompt has exactly 512. `page_slot`: within the prompts of one index of row the values are a permutation; page v belongs to index v // 4 of page; the 4 blocks of the prompts of one device send the same number of blocks to each of the 4 indices of page.
All inputs are finite; a program needn't handle non-finite values. No bound on the sum of `lengths` on one device may be relied on, other than what follows from the above.
Results may differ from a plain program's by a relative error of at most 0.012.
Values may be sent and summed in bfloat16 or wider, within the bound.
No kernel may reach another device: no remote copies, remote signals or barrier semaphores. Data moves between devices by JAX's collectives and lax.ppermute only.
A program may use at most 64 MiB of HBM per device.

v0:
```python
import jax
import jax.numpy as jnp
from jax import lax
from jax.sharding import PartitionSpec as P

PAGE_LEN = 128


def normalize(values, norm_gain):
    mean_sq = jnp.mean(values * values, axis=-1, keepdims=True)
    return values * lax.rsqrt(mean_sq + 1e-06) * norm_gain


def rotate(values):
    row_count = values.shape[-3]
    head_dim = values.shape[-1]
    half_dim = head_dim // 2
    frequency = 10000.0 ** (-2.0 * jnp.arange(half_dim, dtype=jnp.float32) / head_dim)
    angles = jnp.arange(row_count, dtype=jnp.float32)[:, None] * frequency[None, :]
    cosine = jnp.cos(angles)[:, None, :]
    sine_table = jnp.sin(angles)[:, None, :]
    leading = values[..., :half_dim]
    trailing = values[..., half_dim:]
    return jnp.concatenate(
        [leading * cosine - trailing * sine_table, trailing * cosine + leading * sine_table],
        axis=-1,
    )


def attend(query_rows, key_rows, value_rows, length):
    row_count = query_rows.shape[0]
    scores = jnp.einsum(
        "qhd,khd->hqk", query_rows, key_rows, preferred_element_type=jnp.float32
    ) * query_rows.shape[2] ** (-0.5)
    positions = jnp.arange(row_count, dtype=jnp.int32)
    seen_keys = (positions[None, :] <= positions[:, None]) & (positions[None, :] < length)
    exp_scores = jnp.where(seen_keys[None], jnp.exp(scores), 0.0)
    attn_probs = (exp_scores / jnp.sum(exp_scores, axis=-1, keepdims=True)).astype(jnp.bfloat16)
    attended = jnp.einsum(
        "hqk,khd->qhd", attn_probs, value_rows, preferred_element_type=jnp.float32
    )
    live_rows = (positions < length)[:, None, None]
    return jnp.where(live_rows, attended, 0.0).astype(jnp.bfloat16)


def on_device(
    tokens,
    lengths,
    page_slot,
    w_query,
    w_keyval,
    w_out,
    w_gateup,
    w_down,
    attn_gain,
    ffn_gain,
    query_gain,
    key_gain,
):
    col_count = lax.axis_size("col")
    col_index = lax.axis_index("col")
    head_dim = query_gain.shape[0]
    local_width = w_query.shape[1]
    local_heads = local_width // head_dim
    kv_heads = w_keyval.shape[2] // head_dim
    group_size = local_heads * col_count // kv_heads
    kv_index = (col_index * local_heads + jnp.arange(local_heads, dtype=jnp.int32)) // group_size
    columns = (
        kv_index[:, None] * head_dim + jnp.arange(head_dim, dtype=jnp.int32)[None, :]
    ).reshape(-1)
    keyval_piece = w_keyval.astype(jnp.bfloat16)
    query_piece = w_query.astype(jnp.bfloat16)
    out_piece = w_out.astype(jnp.bfloat16)
    gateup_piece = w_gateup.astype(jnp.bfloat16)
    down_piece = w_down.astype(jnp.bfloat16)
    query_full, keyval_full, out_full, gateup_full, down_full = (
        lax.all_gather(query_piece, ("row", "page"), axis=0, tiled=True),
        lax.all_gather(keyval_piece, ("row", "page"), axis=1, tiled=True),
        lax.all_gather(out_piece, ("row", "page"), axis=1, tiled=True),
        lax.all_gather(gateup_piece, ("row", "page"), axis=1, tiled=True),
        lax.all_gather(down_piece, ("row", "page"), axis=1, tiled=True),
    )
    keyval_used = jnp.take(keyval_full, columns, axis=2)
    merged_qkv = jnp.concatenate([query_full, keyval_used[0], keyval_used[1]], axis=1)
    merged_gateup = jnp.concatenate([gateup_full[0], gateup_full[1]], axis=1)
    prompt_count, seq_len, local_feat = tokens.shape
    gathered = lax.all_gather(tokens, "col", axis=2, tiled=True)
    model_width = gathered.shape[2]
    attn_in = normalize(gathered.astype(jnp.float32), attn_gain).astype(jnp.bfloat16)
    projected = jnp.dot(
        attn_in.reshape(-1, model_width), merged_qkv, preferred_element_type=jnp.float32
    )
    projected = projected.reshape(prompt_count, seq_len, 3, local_heads, head_dim)
    queries = rotate(normalize(projected[:, :, 0], query_gain)).astype(jnp.bfloat16)
    keys_rot = rotate(normalize(projected[:, :, 1], key_gain)).astype(jnp.bfloat16)
    values_in = projected[:, :, 2].astype(jnp.bfloat16)
    attended_one = attend(queries[0], keys_rot[0], values_in[0], lengths[0])
    outputs = [attended_one.reshape(seq_len, local_width)]
    attended = jnp.stack(outputs)
    attn_terms = jnp.dot(
        attended.reshape(-1, local_width), out_full, preferred_element_type=jnp.float32
    )
    attn_terms = attn_terms.reshape(prompt_count, seq_len, model_width)
    attn_sum = lax.psum_scatter(
        attn_terms.astype(jnp.bfloat16), "col", scatter_dimension=2, tiled=True
    ).astype(jnp.float32)
    residual = (tokens.astype(jnp.float32) + attn_sum).astype(jnp.bfloat16)
    residual_all = lax.all_gather(residual, "col", axis=2, tiled=True)
    ffn_in = normalize(residual_all.astype(jnp.float32), ffn_gain).astype(jnp.bfloat16)
    gate_up = jnp.dot(
        ffn_in.reshape(-1, model_width), merged_gateup, preferred_element_type=jnp.float32
    )
    unit_count = gateup_full.shape[2]
    hidden = (jax.nn.silu(gate_up[:, :unit_count]) * gate_up[:, unit_count:]).astype(jnp.bfloat16)
    ffn_terms = jnp.dot(hidden, down_full, preferred_element_type=jnp.float32).reshape(
        prompt_count, seq_len, model_width
    )
    ffn_sum = lax.psum_scatter(
        ffn_terms.astype(jnp.bfloat16), "col", scatter_dimension=2, tiled=True
    ).astype(jnp.float32)
    layer_out = (residual.astype(jnp.float32) + ffn_sum).astype(jnp.bfloat16)
    page_count = lax.axis_size("page")
    page_index = lax.axis_index("page")
    blocks_each = prompt_count * (seq_len // PAGE_LEN)
    capacity = blocks_each // page_count
    owners = page_slot // blocks_each
    local_slot = page_slot % blocks_each
    same_owner = owners[:, :, None] == owners[:, None, :]
    earlier = (
        jnp.arange(blocks_each, dtype=jnp.int32)[None, :]
        < jnp.arange(blocks_each, dtype=jnp.int32)[:, None]
    )
    order_in = jnp.sum((same_owner & earlier[None]).astype(jnp.int32), axis=2)
    my_owners = lax.dynamic_index_in_dim(owners, page_index, 0, keepdims=False)
    my_order = lax.dynamic_index_in_dim(order_in, page_index, 0, keepdims=False)
    send_pos = my_owners * capacity + my_order
    live_rows = (jnp.arange(seq_len, dtype=jnp.int32)[None, :] < lengths[:, None])[:, :, None, None]
    page_keys = jnp.where(live_rows, keys_rot, jnp.zeros_like(keys_rot)).reshape(
        blocks_each, PAGE_LEN, local_width
    )
    page_values = jnp.where(live_rows, values_in, jnp.zeros_like(values_in)).reshape(
        blocks_each, PAGE_LEN, local_width
    )
    stacked = jnp.stack([page_keys, page_values])
    outgoing = jnp.zeros_like(stacked).at[:, send_pos].set(stacked)
    incoming = lax.all_to_all(outgoing, "page", split_axis=1, concat_axis=1, tiled=True)
    arrival_hit = (owners[:, None, :] == page_index) & (
        order_in[:, None, :] == jnp.arange(capacity, dtype=jnp.int32)[None, :, None]
    )
    arrival_slot = jnp.sum(jnp.where(arrival_hit, local_slot[:, None, :], 0), axis=2).reshape(
        blocks_each
    )
    kv_pages = jnp.zeros_like(incoming).at[:, arrival_slot].set(incoming)
    return (layer_out, kv_pages)


def solution(mesh):
    in_specs = (
        P(("row", "page"), None, "col"),
        P(("row", "page")),
        P("row", None),
        P(("row", "page"), "col"),
        P(None, ("row", "page"), None),
        P("col", ("row", "page")),
        P(None, ("row", "page"), "col"),
        P("col", ("row", "page")),
        P(),
        P(),
        P(),
        P(),
    )
    out_specs = (P(("row", "page"), None, "col"), P(None, ("row", "page"), None, "col"))
    return jax.shard_map(
        on_device, mesh=mesh, in_specs=in_specs, out_specs=out_specs, check_vma=False
    )
```

profile of v0, /device:TPU:8, one launch (start us, length us, event | category | flops | bytes accessed | tf_op | source)
XLA Modules:
  0.0 662.8 jit_solution(14260095701070087263)
XLA Ops:
  7.2 0.0 all-gather.6.cloned.1.call-start
  7.2 0.7 all-gather.6.cloned.1.call-update
  7.9 0.0 all-gather.8.cloned.1.call-start
  7.9 1.6 copy.63
  9.6 0.0 all-gather.8.cloned.1.call-update
  9.6 0.0 reduce-scatter.3.cloned.1.call-start
  9.7 0.1 iota_add_fusion
  9.7 0.1 add.172
  9.8 0.1 add.169
  9.9 0.8 convert_element_type.114
  11.3 0.8 convert_element_type.121
  12.2 0.3 fusion.42
  12.5 0.8 fusion.28
  13.3 82.1 %all_gather.22 = bf16[2048,128]{1,0:T(8,128)(2,1)} all-gather(bf16[64,128]{1,0:T(8,128)(2,1)S(1)} %convert_element_type.114), channel_id=1, replica_groups=mesh['row'=8,'col'=8,'page'=4] {'row','page'}, dimensions={0}, use_global_device_ids=true | all-gather | bytes 540672 | tf_op jit(solution)/shard_map/all_gather | solution.py:77
  95.5 68.6 %all_gather.24 = bf16[128,2048]{0,1:T(8,128)(2,1)} all-gather(bf16[128,64]{0,1:T(8,128)(2,1)S(1)} %convert_element_type.121), channel_id=1, replica_groups=mesh['row'=8,'col'=8,'page'=4] {'row','page'}, dimensions={1}, use_global_device_ids=true | all-gather | bytes 540672 | tf_op jit(solution)/shard_map/all_gather | solution.py:79
  164.1 2.1 fusion.4
  166.2 9.9 %all-gather.8.cloned.1.call-done = bf16[2,2048,256]{2,0,1:T(2,128)(2,1)} async-done(((bf16[2,64,256]{2,0,1:T(2,128)(2,1)}), bf16[2,2048,256]{2,0,1:T(2,128)(2,1)}) %all-gather.8.cloned.1.call-update) | async-done | bytes 2097168 | tf_op jit(solution)/shard_map/all_gather | solution.py:78
  176.1 7.6 %copy.52 = bf16[2,2048,256]{1,0,2:T(2,128)(2,1)S(1)} copy(bf16[2,2048,256]{2,0,1:T(2,128)(2,1)} %all-gather.8.cloned.1.call-done) | data formatting | bytes 4194304 | tf_op jit(solution)/shard_map/all_gather | solution.py:78
  183.6 2.7 gather_fusion
  186.3 1.0 fusion.27
  187.3 1.5 fusion.55
  188.8 0.9 copy.53
  189.7 0.9 copy.54
  190.6 0.2 maximum_bitcast_fusion
  190.8 1.7 copy.55
  192.5 3.1 fusion.23
  195.6 0.1 multiply_reduce_fusion
  195.8 0.1 multiply_multiply_fusion
  195.9 0.1 subtract_convert_fusion
  196.0 0.6 copy-done.11
  196.6 0.8 fusion.21
  197.4 0.7 fusion.26
  198.1 0.3 copy-done.2
  198.4 2.1 fusion.11
  200.5 0.0 all-gather.12.cloned.1.call-start
  200.6 0.7 convert_element_type.129
  201.3 0.0 all-gather.12.cloned.1.call-update
  201.3 0.0 all-gather.10.cloned.1.call-start
  201.4 98.7 %reduce-scatter.3.cloned.1.call-done = bf16[1,512,256]{2,1,0:T(8,128)(2,1)} async-done(((bf16[1,512,2048]{2,1,0:T(8,128)(2,1)}), bf16[1,512,256]{2,1,0:T(8,128)(2,1)}) %reduce-scatter.3.cloned.1.call-update) | async-done | bytes 262160 | tf_op jit(solution)/shard_map/reduce_scatter | solution.py:104
  300.1 1.7 add_convert_fusion.1
  301.8 0.0 all-gather.10.cloned.1.call-update
  301.8 0.0 all-gather.14.cloned.1.call-start
  301.9 0.6 convert_element_type.131
  302.6 0.2 reduce-scatter.5.cloned.1.call-start
  302.8 85.4 %all-gather.12.cloned.1.call-done = bf16[2,2048,640]{2,1,0:T(8,128)(2,1)} async-done(((bf16[2,64,640]{2,1,0:T(8,128)(2,1)}), bf16[2,2048,640]{2,1,0:T(8,128)(2,1)}) %all-gather.12.cloned.1.call-update) | async-done | bytes 5242896 | tf_op jit(solution)/shard_map/all_gather | solution.py:80
  388.2 4.6 slice_bitcast_fusion.1
  392.8 75.0 %all-gather.10.cloned.1.call-done = bf16[1,512,2048]{2,1,0:T(8,128)(2,1)} async-done(((bf16[1,512,256]{2,1,0:T(8,128)(2,1)}), bf16[1,512,2048]{2,1,0:T(8,128)(2,1)}) %all-gather.10.cloned.1.call-update) | async-done | bytes 2097168 | tf_op jit(solution)/shard_map/all_gather | solution.py:108
  467.8 2.2 fusion.7
  470.0 6.2 fusion
  476.2 76.6 %all-gather.14.cloned.1.call-done = bf16[640,2048]{0,1:T(8,128)(2,1)} async-done(((bf16[640,64]{0,1:T(8,128)(2,1)}), bf16[640,2048]{0,1:T(8,128)(2,1)}) %all-gather.14.cloned.1.call-update) | async-done | bytes 2621456 | tf_op jit(solution)/shard_map/all_gather | solution.py:81
  552.8 5.7 fusion.10
  558.6 0.6 copy-done.13
  559.2 0.2 convert_reduce_fusion
  559.6 0.1 copy.57
  559.8 0.1 copy.58
  559.9 0.1 broadcast_select_fusion.2
  560.1 0.8 scatter_fusion
  560.9 0.7 copy.59
  561.6 4.6 all-to-all-start
  566.3 0.1 fusion.44
  566.4 14.3 %all-to-all-done = bf16[2,4,128,128]{3,2,0,1:T(8,128)(2,1)S(1)} async-done(((bf16[2,4,128,128]{3,2,0,1:T(8,128)(2,1)}), bf16[2,4,128,128]{3,2,0,1:T(8,128)(2,1)S(1)}, u32[]{:S(2)}, u32[]{:S(2)}) %all-to-all-start) | async-done | bytes 262176 | tf_op jit(solution)/shard_map/all_to_all | solution.py:146
  580.7 0.8 scatter_fusion.1
  581.5 72.7 %reduce-scatter.5.cloned.1.call-done = bf16[1,512,256]{2,1,0:T(8,128)(2,1)} async-done(((bf16[1,512,2048]{2,1,0:T(8,128)(2,1)}), bf16[1,512,256]{2,1,0:T(8,128)(2,1)}) %reduce-scatter.5.cloned.1.call-update) | async-done | bytes 262160 | tf_op jit(solution)/shard_map/reduce_scatter | solution.py:118
  654.2 1.7 add_convert_fusion
  (58 shorter events, 0.4 us)
Async XLA Ops:
  7.2 156.9 %all-gather.6.cloned.1.call-start = ((), (), s32[]{:S(2)}) async-start(), calls=%async_computation.3 | async-start | bytes 2359296 | tf_op jit(solution)/shard_map/all_gather | solution.py:87
  7.9 168.2 %all-gather.8.cloned.1.call-start = ((), (), s32[]{:S(2)}) async-start(), calls=%async_computation.4 | async-start | bytes 2162688 | tf_op jit(solution)/shard_map/all_gather | solution.py:78
  9.6 290.5 %reduce-scatter.3.cloned.1.call-start = ((), (), s32[]{:S(2)}) async-start(), calls=%async_computation.5 | async-start | bytes 2359296 | tf_op jit(solution)/shard_map/reduce_scatter | solution.py:104
  188.8 1.7 copy-start.3
  190.8 1.7 copy-start.16
  192.5 3.3 copy-start.14
  192.5 3.3 copy-start.15
  195.6 1.0 copy-start.11
  195.9 1.4 copy-start.7
  196.0 1.4 copy-start.9
  197.4 1.0 copy-start.2
  198.4 2.2 copy-start.6
  198.4 101.7 %copy-start.4 = (bf16[1,512,256]{2,1,0:T(8,128)(2,1)S(1)}, bf16[1,512,256]{2,1,0:T(8,128)(2,1)}, u32[]{:S(2)}) copy-start(bf16[1,512,256]{2,1,0:T(8,128)(2,1)} %param.12) | copy-start | bytes 786436
  200.5 101.4 %copy-start.12 = (f32[640,64]{0,1:T(8,128)S(1)}, f32[640,64]{0,1:T(8,128)}, u32[]{:S(2)}) copy-start(f32[640,64]{0,1:T(8,128)} %param.19) | copy-start | bytes 491524
  200.5 187.7 %all-gather.12.cloned.1.call-start = ((), (), s32[]{:S(2)}) async-start(), calls=%async_computation.7 | async-start | bytes 5406720 | tf_op jit(solution)/shard_map/all_gather | solution.py:80
  201.3 266.4 %all-gather.10.cloned.1.call-start = ((), (), s32[]{:S(2)}) async-start(), calls=%async_computation.6 | async-start | bytes 2359296 | tf_op jit(solution)/shard_map/all_gather | solution.py:108
  301.8 251.0 %all-gather.14.cloned.1.call-start = ((), (), s32[]{:S(2)}) async-start(), calls=%async_computation.8 | async-start | bytes 2703360 | tf_op jit(solution)/shard_map/all_gather | solution.py:81
  302.6 351.6 %reduce-scatter.5.cloned.1.call-start = ((), (), s32[]{:S(2)}) async-start(), calls=%async_computation.9 | async-start | bytes 2359296 | tf_op jit(solution)/shard_map/reduce_scatter | solution.py:118
  392.8 77.2 %copy-start.17 = (f32[2048]{0:T(1024)S(1)}, f32[2048]{0:T(1024)}, u32[]{:S(2)}) copy-start(f32[2048]{0:T(1024)} %param.21) | copy-start | bytes 24580
  467.8 2.2 copy-start.1
  558.5 0.7 copy-start.13
  558.5 1.0 copy-start.8
  558.5 1.0 copy-start.10
  559.9 94.3 %copy-start = (bf16[1,512,256]{2,1,0:T(8,128)(2,1)S(1)}, bf16[1,512,256]{2,1,0:T(8,128)(2,1)}, u32[]{:S(2)}) copy-start(bf16[1,512,256]{2,1,0:T(8,128)(2,1)} %add_convert_fusion.1) | copy-start | bytes 786436
  561.6 19.1 %all-to-all-start = ((bf16[2,4,128,128]{3,2,0,1:T(8,128)(2,1)}), bf16[2,4,128,128]{3,2,0,1:T(8,128)(2,1)S(1)}, u32[]{:S(2)}, u32[]{:S(2)}) async-start(bf16[2,4,128,128]{3,2,0,1:T(8,128)(2,1)} %copy.59), calls=%async_computation.2 | async-start | bytes 524288 | tf_op jit(solution)/shard_map/all_to_all | solution.py:146
  581.5 74.4 %copy-start.5 = (bf16[2,4,128,128]{3,2,1,0:T(8,128)(2,1)}, bf16[2,4,128,128]{3,2,1,0:T(8,128)(2,1)S(1)}, u32[]{:S(2)}) copy-start(bf16[2,4,128,128]{3,2,1,0:T(8,128)(2,1)S(1)} %scatter_fusion.1) | copy-start | bytes 786436
Sparse Core Ops, SparseCore 0:
  10.4 74.3 all-gather.5
  87.2 88.8 all-gather.7
  200.7 99.3 reduce-scatter.2
  302.3 85.8 all-gather.11
  391.1 76.6 all-gather.9
  469.4 83.3 all-gather.13
  558.7 95.4 reduce-scatter.4
where the time goes:
time: 663 us
  waiting for transfers between devices  433 us (65%)
  blocking collectives  151 us (23%)
  local copies, waits for them, and re-layouts  25.8 us (4%)
  matrix products  18.6 us (3%)
  between operations  15.2 us (2%)
  other arithmetic  13.9 us (2%)
    reduce_scatter x1, waiting for transfers between devices, on_device(): lax.psum_scatter(attn_terms.astype(jnp.bfloat16), 'col', scatter_dimensio...  98.7 us
    all_gather x1, waiting for transfers between devices, on_device(): lax.all_gather(gateup_piece, ('row', 'page'), axis=1, tiled=True)  85.4 us
    all_gather x1, blocking collectives, on_device(): lax.all_gather(query_piece, ('row', 'page'), axis=0, tiled=True)  82.1 us
    all_gather x1, waiting for transfers between devices, on_device(): lax.all_gather(down_piece, ('row', 'page'), axis=1, tiled=True)  76.6 us
    all_gather x1, waiting for transfers between devices, on_device(): residual_all = lax.all_gather(residual, 'col', axis=2, tiled=True)  75 us
    reduce_scatter x1, waiting for transfers between devices, on_device(): lax.psum_scatter(ffn_terms.astype(jnp.bfloat16), 'col', scatter_dimension...  72.7 us
    all_gather x1, blocking collectives, on_device(): lax.all_gather(out_piece, ('row', 'page'), axis=1, tiled=True)  68.6 us
    all_to_all x1, waiting for transfers between devices, on_device(): lax.all_to_all(outgoing, 'page', split_axis=1, concat_axis=1, tiled=True)  14.3 us
  transfers between devices with their start and end apart: 8, of which 7 were waited for; matrix products, arithmetic and copies ran while one was open for 4% of the time, Pallas kernels for 0%

commit v1 on v0

--- a/solution.py
+++ b/solution.py
@@ -43,6 +43,12 @@
     return jnp.where(live_rows, attended, 0.0).astype(jnp.bfloat16)
 
 
+def contract_rows(lhs, rhs_t):
+    return lax.dot_general(
+        lhs, rhs_t, (((1,), (1,)), ((), ())), preferred_element_type=jnp.float32
+    )
+
+
 def on_device(
     tokens,
     lengths,
@@ -64,57 +70,58 @@
     local_heads = local_width // head_dim
     kv_heads = w_keyval.shape[2] // head_dim
     group_size = local_heads * col_count // kv_heads
-    kv_index = (col_index * local_heads + jnp.arange(local_heads, dtype=jnp.int32)) // group_size
-    columns = (
-        kv_index[:, None] * head_dim + jnp.arange(head_dim, dtype=jnp.int32)[None, :]
-    ).reshape(-1)
-    keyval_piece = w_keyval.astype(jnp.bfloat16)
-    query_piece = w_query.astype(jnp.bfloat16)
-    out_piece = w_out.astype(jnp.bfloat16)
-    gateup_piece = w_gateup.astype(jnp.bfloat16)
-    down_piece = w_down.astype(jnp.bfloat16)
-    query_full, keyval_full, out_full, gateup_full, down_full = (
-        lax.all_gather(query_piece, ("row", "page"), axis=0, tiled=True),
-        lax.all_gather(keyval_piece, ("row", "page"), axis=1, tiled=True),
-        lax.all_gather(out_piece, ("row", "page"), axis=1, tiled=True),
-        lax.all_gather(gateup_piece, ("row", "page"), axis=1, tiled=True),
-        lax.all_gather(down_piece, ("row", "page"), axis=1, tiled=True),
-    )
-    keyval_used = jnp.take(keyval_full, columns, axis=2)
-    merged_qkv = jnp.concatenate([query_full, keyval_used[0], keyval_used[1]], axis=1)
-    merged_gateup = jnp.concatenate([gateup_full[0], gateup_full[1]], axis=1)
+    assert group_size % local_heads == 0
+    kv_head = (col_index * local_heads) // group_size
+    unit_count = w_gateup.shape[2]
+    kv_piece = lax.dynamic_slice_in_dim(w_keyval, kv_head * head_dim, head_dim, axis=2)
+    pieces = [
+        w_query.astype(jnp.bfloat16),
+        jnp.transpose(kv_piece.astype(jnp.bfloat16), (1, 0, 2)).reshape(kv_piece.shape[1], -1),
+        jnp.transpose(w_out.astype(jnp.bfloat16)),
+        jnp.transpose(w_gateup.astype(jnp.bfloat16), (1, 0, 2)).reshape(w_gateup.shape[1], -1),
+        jnp.transpose(w_down.astype(jnp.bfloat16)),
+    ]
+    widths = [p.shape[1] for p in pieces]
+    packed = jnp.concatenate(pieces, axis=1)
+    full = lax.all_gather(packed, ("row", "page"), axis=0, tiled=True)
+    offsets = [sum(widths[:i]) for i in range(len(widths) + 1)]
+    qkv_w = full[:, offsets[0] : offsets[2]]
+    out_t = full[:, offsets[2] : offsets[3]]
+    gateup_w = full[:, offsets[3] : offsets[4]]
+    down_t = full[:, offsets[4] : offsets[5]]
+
     prompt_count, seq_len, local_feat = tokens.shape
     gathered = lax.all_gather(tokens, "col", axis=2, tiled=True)
     model_width = gathered.shape[2]
     attn_in = normalize(gathered.astype(jnp.float32), attn_gain).astype(jnp.bfloat16)
     projected = jnp.dot(
-        attn_in.reshape(-1, model_width), merged_qkv, preferred_element_type=jnp.float32
+        attn_in.reshape(-1, model_width), qkv_w, preferred_element_type=jnp.float32
     )
-    projected = projected.reshape(prompt_count, seq_len, 3, local_heads, head_dim)
-    queries = rotate(normalize(projected[:, :, 0], query_gain)).astype(jnp.bfloat16)
-    keys_rot = rotate(normalize(projected[:, :, 1], key_gain)).astype(jnp.bfloat16)
-    values_in = projected[:, :, 2].astype(jnp.bfloat16)
-    attended_one = attend(queries[0], keys_rot[0], values_in[0], lengths[0])
-    outputs = [attended_one.reshape(seq_len, local_width)]
-    attended = jnp.stack(outputs)
-    attn_terms = jnp.dot(
-        attended.reshape(-1, local_width), out_full, preferred_element_type=jnp.float32
+    projected = projected.reshape(prompt_count, seq_len, local_heads + 2, head_dim)
+    queries = rotate(normalize(projected[:, :, :local_heads], query_gain)).astype(jnp.bfloat16)
+    keys_one = rotate(normalize(projected[:, :, local_heads : local_heads + 1], key_gain)).astype(
+        jnp.bfloat16
     )
-    attn_terms = attn_terms.reshape(prompt_count, seq_len, model_width)
-    attn_sum = lax.psum_scatter(
-        attn_terms.astype(jnp.bfloat16), "col", scatter_dimension=2, tiled=True
-    ).astype(jnp.float32)
-    residual = (tokens.astype(jnp.float32) + attn_sum).astype(jnp.bfloat16)
-    residual_all = lax.all_gather(residual, "col", axis=2, tiled=True)
+    values_one = projected[:, :, local_heads + 1 : local_heads + 2].astype(jnp.bfloat16)
+    keys_rot = jnp.broadcast_to(keys_one, queries.shape)
+    values_in = jnp.broadcast_to(values_one, queries.shape)
+    attended = jnp.stack(
+        [
+            attend(queries[i], keys_rot[i], values_in[i], lengths[i]).reshape(seq_len, local_width)
+            for i in range(prompt_count)
+        ]
+    )
+    attn_terms = contract_rows(attended.reshape(-1, local_width), out_t)
+    attn_terms = attn_terms.reshape(prompt_count, seq_len, model_width).astype(jnp.bfloat16)
+    attn_sum = lax.psum(attn_terms, "col").astype(jnp.float32)
+    residual_all = (gathered.astype(jnp.float32) + attn_sum).astype(jnp.bfloat16)
+    residual = lax.dynamic_slice_in_dim(residual_all, col_index * local_feat, local_feat, axis=2)
     ffn_in = normalize(residual_all.astype(jnp.float32), ffn_gain).astype(jnp.bfloat16)
     gate_up = jnp.dot(
-        ffn_in.reshape(-1, model_width), merged_gateup, preferred_element_type=jnp.float32
+        ffn_in.reshape(-1, model_width), gateup_w, preferred_element_type=jnp.float32
     )
-    unit_count = gateup_full.shape[2]
     hidden = (jax.nn.silu(gate_up[:, :unit_count]) * gate_up[:, unit_count:]).astype(jnp.bfloat16)
-    ffn_terms = jnp.dot(hidden, down_full, preferred_element_type=jnp.float32).reshape(
-        prompt_count, seq_len, model_width
-    )
+    ffn_terms = contract_rows(hidden, down_t).reshape(prompt_count, seq_len, model_width)
     ffn_sum = lax.psum_scatter(
         ffn_terms.astype(jnp.bfloat16), "col", scatter_dimension=2, tiled=True
     ).astype(jnp.float32)

time: 663 us -> 445 us (0.67)
  blocking collectives: 151 us -> 0 us
  waiting for transfers between devices: 433 us -> 386 us
  local copies, waits for them, and re-layouts: 25.8 us -> 7.11 us
    all_gather x4 -> x1, waiting for transfers between devices: 247 us -> 91.8 us  [on_device(): full = lax.all_gather(packed, ('row', 'page'), axis=0, tiled=True)]
    all_gather x2 -> x0, blocking collectives: 151 us -> none  [the longest x1 82.1 us: on_device(): lax.all_gather(query_piece, ('row', 'page'), axis=0, tiled=True)]
    psum x0 -> x1, waiting for transfers between devices: none -> 132 us  [on_device(): attn_sum = lax.psum(attn_terms, 'col').astype(jnp.float32)]
    reduce_scatter x1 -> x0, waiting for transfers between devices: 98.7 us -> none  [on_device(): lax.psum_scatter(attn_terms.astype(jnp.bfloat16), 'col', scatter_dimensio...]
    all_gather x1, waiting for transfers between devices: 0.01 us -> 74.6 us  [on_device(): gathered = lax.all_gather(tokens, 'col', axis=2, tiled=True)]
    all_gather x1 -> x0, local copies, waits for them, and re-layouts: 7.57 us -> none  [on_device(): lax.all_gather(keyval_piece, ('row', 'page'), axis=1, tiled=True)]
    reduce_scatter x1, waiting for transfers between devices: 72.7 us -> 80.2 us  [on_device(): lax.psum_scatter(ffn_terms.astype(jnp.bfloat16), 'col', scatter_dimension...]
    all_to_all x1, waiting for transfers between devices: 14.3 us -> 6.73 us  [on_device(): lax.all_to_all(outgoing, 'page', split_axis=1, concat_axis=1, tiled=True)]
  transfers between devices with their start and end apart: 8 -> 5, of which waited for: 7 -> 5; matrix products, arithmetic and copies ran while one was open for 4% -> 2% of each run, Pallas kernels for 0% -> 0%
where the time goes in v1:
time: 445 us; the launch traced here: 444 us
  waiting for transfers between devices  386 us (87%)
  matrix products  17.9 us (4%)
  between operations  14.8 us (3%)
  other arithmetic  12.3 us (3%)
  local copies, waits for them, and re-layouts  7.11 us (2%)
  starting transfers between devices  6.08 us (1%)
    psum x1, waiting for transfers between devices, on_device(): attn_sum = lax.psum(attn_terms, 'col').astype(jnp.float32)  132 us
    all_gather x1, waiting for transfers between devices, on_device(): full = lax.all_gather(packed, ('row', 'page'), axis=0, tiled=True)  91.8 us
    reduce_scatter x1, waiting for transfers between devices, on_device(): lax.psum_scatter(ffn_terms.astype(jnp.bfloat16), 'col', scatter_dimension...  80.2 us
    all_gather x1, waiting for transfers between devices, on_device(): gathered = lax.all_gather(tokens, 'col', axis=2, tiled=True)  74.6 us
  transfers between devices with their start and end apart: 5, of which 5 were waited for; matrix products, arithmetic and copies ran while one was open for 2% of the time, Pallas kernels for 0%

profile of v1, /device:TPU:8, one launch (start us, length us, event | category | flops | bytes accessed | tf_op | source)
XLA Modules:
  0.0 443.9 jit_solution(3106016607968333589)
XLA Ops:
  7.2 0.0 copy-start
  7.2 0.0 all-gather.3.cloned.1.call-start
  7.2 0.7 all-gather.3.cloned.1.call-update
  7.9 0.0 all-gather.5.cloned.1.call-start
  8.0 0.1 copy-done
  8.1 0.1 fusion.44
  8.2 0.1 reshape.344
  8.3 1.0 convert_bitcast_fusion
  9.3 0.8 convert_dynamic-update-slice_fusion
  10.1 0.8 bitcast_dynamic-update-slice_fusion.1
  10.9 0.9 bitcast_dynamic-update-slice_fusion
  11.8 0.0 copy-start.4
  11.8 0.7 copy-done.4
  12.5 0.0 all-gather.5.cloned.1.call-update
  12.5 0.0 all-reduce.2.cloned.1.call-start
  13.3 1.0 fusion.42
  14.2 0.1 fusion.27
  14.4 74.6 %all-gather.3.cloned.1.call-done = bf16[1,512,2048]{2,1,0:T(8,128)(2,1)} async-done(((bf16[1,512,256]{2,1,0:T(8,128)(2,1)}), bf16[1,512,2048]{2,1,0:T(8,128)(2,1)}) %all-gather.3.cloned.1.call-update) | async-done | bytes 2097168 | tf_op jit(solution)/shard_map/all_gather | solution.py:94
  89.0 2.1 fusion.5
  91.0 0.0 copy-start.1
  91.0 91.8 %all-gather.5.cloned.1.call-done = bf16[2048,2304]{1,0:T(8,128)(2,1)} async-done(((bf16[64,2304]{1,0:T(8,128)(2,1)}), bf16[2048,2304]{1,0:T(8,128)(2,1)}) %all-gather.5.cloned.1.call-update) | async-done | bytes 9437200 | tf_op jit(solution)/shard_map/all_gather | solution.py:86
  182.9 1.3 slice_bitcast_fusion
  184.2 1.4 copy.35
  185.6 0.0 copy-done.1
  185.6 0.0 copy-start.8
  185.6 0.0 copy-start.9
  185.6 0.0 copy-start.6
  185.6 2.1 fusion.23
  187.8 0.0 copy-done.8
  187.9 0.1 multiply_multiply_fusion.1
  187.9 0.3 fusion.45
  188.3 0.0 copy-done.9
  188.3 0.1 multiply_multiply_fusion
  188.4 0.0 copy-done.5
  188.4 0.0 copy-done.6
  188.5 0.7 fusion.21
  189.2 0.7 fusion.26
  189.9 3.2 fusion.10
  193.1 0.0 all-reduce.2.cloned.1.call-update
  193.1 0.0 copy-start.10
  193.2 0.0 reduce-scatter.2.cloned.1.call-start
  193.2 131.7 %all-reduce.2.cloned.1.call-done = bf16[1,512,2048]{2,1,0:T(8,128)(2,1)} async-done(((bf16[1,512,2048]{2,1,0:T(8,128)(2,1)}), bf16[1,512,2048]{2,1,0:T(8,128)(2,1)}) %all-reduce.2.cloned.1.call-update) | async-done | bytes 2097168 | tf_op jit(solution)/shard_map/psum | solution.py:116
  324.9 2.6 fusion.2
  327.4 0.0 copy-start.2
  327.5 0.0 copy-done.10
  327.5 6.2 %fusion = f32[512,1280]{1,0:T(8,128)S(1)} fusion(bf16[2048,2304]{1,0:T(8,128)(2,1)} %all-gather.5.cloned.1.call-done, bf16[1,512,2048]{2,1,0:T(8,128)(2,1)S(1)} %get-tuple-element.3, f32[2048]{0:T(1024)S(1)} %copy-done.10, f32[512]{0:T(512)S(1)} %add_rsqrt_fusion.1), kind=kOutput, calls=%fused_computation.7 | convolution fusion | flops 2688548864 | bytes 9971712 | tf_op jit(solution)/shard_map/dot_general | solution.py:120
  333.6 0.0 copy-done.2
  333.6 5.0 %fusion.9 = bf16[1,512,2048]{2,1,0:T(8,128)(2,1)} fusion(bf16[2048,2304]{1,0:T(8,128)(2,1)} %all-gather.5.cloned.1.call-done, f32[512,1280]{1,0:T(8,128)S(1)} %fusion), kind=kOutput, calls=%fused_computation.18 | convolution fusion | flops 1345191936 | bytes 7340032 | tf_op jit(solution)/shard_map/dot_general | solution.py:47
  338.7 0.0 reduce-scatter.2.cloned.1.call-update
  338.7 0.6 copy-done.7
  339.3 0.2 convert_reduce_fusion
  339.7 0.1 broadcast_select_fusion.1
  339.8 0.2 maximum_bitcast_fusion
  340.0 0.2 copy.37
  340.3 0.8 scatter_fusion
  341.0 0.7 copy.38
  341.8 5.9 %all-to-all-start = ((bf16[2,4,128,128]{3,2,0,1:T(8,128)(2,1)}), bf16[2,4,128,128]{3,2,0,1:T(8,128)(2,1)S(1)}, u32[]{:S(2)}, u32[]{:S(2)}) async-start(bf16[2,4,128,128]{3,2,0,1:T(8,128)(2,1)} %copy.38), calls=%async_computation.1 | async-start | bytes 524288 | tf_op jit(solution)/shard_map/all_to_all | solution.py:153
  347.7 0.1 fusion.48
  347.8 6.7 %all-to-all-done = bf16[2,4,128,128]{3,2,0,1:T(8,128)(2,1)S(1)} async-done(((bf16[2,4,128,128]{3,2,0,1:T(8,128)(2,1)}), bf16[2,4,128,128]{3,2,0,1:T(8,128)(2,1)S(1)}, u32[]{:S(2)}, u32[]{:S(2)}) %all-to-all-start) | async-done | bytes 262176 | tf_op jit(solution)/shard_map/all_to_all | solution.py:153
  354.6 0.8 scatter_fusion.1
  355.4 0.0 copy-start.3
  355.4 80.2 %reduce-scatter.2.cloned.1.call-done = bf16[1,512,256]{2,1,0:T(8,128)(2,1)} async-done(((bf16[1,512,2048]{2,1,0:T(8,128)(2,1)}), bf16[1,512,256]{2,1,0:T(8,128)(2,1)}) %reduce-scatter.2.cloned.1.call-update) | async-done | bytes 262160 | tf_op jit(solution)/shard_map/reduce_scatter | solution.py:125
  435.6 1.8 add_convert_fusion
  437.4 0.0 copy-done.3
  (28 shorter events, 0.5 us)
Async XLA Ops:
  7.2 0.9 copy-start
  7.2 81.8 %all-gather.3.cloned.1.call-start = ((), (), s32[]{:S(2)}) async-start(), calls=%async_computation.2 | async-start | bytes 2359296 | tf_op jit(solution)/shard_map/all_gather | solution.py:94
  7.9 174.9 %all-gather.5.cloned.1.call-start = ((), (), s32[]{:S(2)}) async-start(), calls=%async_computation.3 | async-start | bytes 9732096 | tf_op jit(solution)/shard_map/all_gather | solution.py:86
  11.8 0.7 copy-start.4
  12.5 312.3 %all-reduce.2.cloned.1.call-start = ((), (), s32[]{:S(2)}) async-start(), calls=%async_computation.4 | async-start | bytes 4194304 | tf_op jit(solution)/shard_map/psum | solution.py:116
  91.0 94.6 %copy-start.1 = (bf16[1,512,2048]{2,1,0:T(8,128)(2,1)S(1)}, bf16[1,512,2048]{2,1,0:T(8,128)(2,1)}, u32[]{:S(2)}) copy-start(bf16[1,512,2048]{2,1,0:T(8,128)(2,1)} %all-gather.3.cloned.1.call-done) | copy-start | bytes 6291460
  185.6 2.2 copy-start.8
  185.6 2.7 copy-start.9
  185.6 2.8 copy-start.5
  185.6 2.8 copy-start.6
  193.1 134.3 %copy-start.10 = (f32[2048]{0:T(1024)S(1)}, f32[2048]{0:T(1024)}, u32[]{:S(2)}) copy-start(f32[2048]{0:T(1024)} %param.21) | copy-start | bytes 24580
  193.2 242.5 %reduce-scatter.2.cloned.1.call-start = ((), (), s32[]{:S(2)}) async-start(), calls=%async_computation.5 | async-start | bytes 2359296 | tf_op jit(solution)/shard_map/reduce_scatter | solution.py:125
  327.4 6.2 %copy-start.2 = (bf16[1,512,2048]{2,1,0:T(8,128)(2,1)}, bf16[1,512,2048]{2,1,0:T(8,128)(2,1)S(1)}, u32[]{:S(2)}) copy-start(bf16[1,512,2048]{2,1,0:T(8,128)(2,1)S(1)} %get-tuple-element.3) | copy-start | bytes 6291460
  338.7 0.7 copy-start.7
  341.8 12.8 %all-to-all-start = ((bf16[2,4,128,128]{3,2,0,1:T(8,128)(2,1)}), bf16[2,4,128,128]{3,2,0,1:T(8,128)(2,1)S(1)}, u32[]{:S(2)}, u32[]{:S(2)}) async-start(bf16[2,4,128,128]{3,2,0,1:T(8,128)(2,1)} %copy.38), calls=%async_computation.1 | async-start | bytes 524288 | tf_op jit(solution)/shard_map/all_to_all | solution.py:153
  355.4 82.0 %copy-start.3 = (bf16[2,4,128,128]{3,2,1,0:T(8,128)(2,1)}, bf16[2,4,128,128]{3,2,1,0:T(8,128)(2,1)S(1)}, u32[]{:S(2)}) copy-start(bf16[2,4,128,128]{3,2,1,0:T(8,128)(2,1)S(1)} %scatter_fusion.1) | copy-start | bytes 786436
Sparse Core Ops, SparseCore 0:
  10.5 78.4 all-gather.2
  90.8 92.0 all-gather.4
  193.3 131.5 all-reduce.1
  338.8 96.7 reduce-scatter.1

commit v2 on v1

--- a/solution.py
+++ b/solution.py
@@ -49,6 +49,24 @@
     )
 
 
+def gather_a2a(x, axis_name, axis):
+    count = lax.axis_size(axis_name)
+    copies = jnp.broadcast_to(x[None], (count,) + x.shape)
+    got = lax.all_to_all(copies, axis_name, 0, 0, tiled=True)
+    got = jnp.moveaxis(got, 0, axis)
+    shape = list(x.shape)
+    shape[axis] *= count
+    return got.reshape(shape)
+
+
+def scatter_sum_a2a(x, axis_name, axis):
+    count = lax.axis_size(axis_name)
+    shape = list(x.shape)
+    split = shape[:axis] + [count, shape[axis] // count] + shape[axis + 1 :]
+    got = lax.all_to_all(x.reshape(split), axis_name, axis, axis, tiled=True)
+    return jnp.sum(got.astype(jnp.float32), axis=axis)
+
+
 def on_device(
     tokens,
     lengths,
@@ -82,16 +100,16 @@
         jnp.transpose(w_down.astype(jnp.bfloat16)),
     ]
     widths = [p.shape[1] for p in pieces]
-    packed = jnp.concatenate(pieces, axis=1)
-    full = lax.all_gather(packed, ("row", "page"), axis=0, tiled=True)
     offsets = [sum(widths[:i]) for i in range(len(widths) + 1)]
-    qkv_w = full[:, offsets[0] : offsets[2]]
-    out_t = full[:, offsets[2] : offsets[3]]
-    gateup_w = full[:, offsets[3] : offsets[4]]
-    down_t = full[:, offsets[4] : offsets[5]]
+    attn_full = lax.all_gather(jnp.concatenate(pieces[:3], axis=1), ("row", "page"), axis=0, tiled=True)
+    ffn_full = lax.all_gather(jnp.concatenate(pieces[3:], axis=1), ("row", "page"), axis=0, tiled=True)
+    qkv_w = attn_full[:, offsets[0] : offsets[2]]
+    out_t = attn_full[:, offsets[2] : offsets[3]]
+    gateup_w = ffn_full[:, : offsets[4] - offsets[3]]
+    down_t = ffn_full[:, offsets[4] - offsets[3] :]
 
     prompt_count, seq_len, local_feat = tokens.shape
-    gathered = lax.all_gather(tokens, "col", axis=2, tiled=True)
+    gathered = gather_a2a(tokens, "col", 2)
     model_width = gathered.shape[2]
     attn_in = normalize(gathered.astype(jnp.float32), attn_gain).astype(jnp.bfloat16)
     projected = jnp.dot(
@@ -113,18 +131,16 @@
     )
     attn_terms = contract_rows(attended.reshape(-1, local_width), out_t)
     attn_terms = attn_terms.reshape(prompt_count, seq_len, model_width).astype(jnp.bfloat16)
-    attn_sum = lax.psum(attn_terms, "col").astype(jnp.float32)
-    residual_all = (gathered.astype(jnp.float32) + attn_sum).astype(jnp.bfloat16)
-    residual = lax.dynamic_slice_in_dim(residual_all, col_index * local_feat, local_feat, axis=2)
+    attn_sum = scatter_sum_a2a(attn_terms, "col", 2)
+    residual = (tokens.astype(jnp.float32) + attn_sum).astype(jnp.bfloat16)
+    residual_all = gather_a2a(residual, "col", 2)
     ffn_in = normalize(residual_all.astype(jnp.float32), ffn_gain).astype(jnp.bfloat16)
     gate_up = jnp.dot(
         ffn_in.reshape(-1, model_width), gateup_w, preferred_element_type=jnp.float32
     )
     hidden = (jax.nn.silu(gate_up[:, :unit_count]) * gate_up[:, unit_count:]).astype(jnp.bfloat16)
     ffn_terms = contract_rows(hidden, down_t).reshape(prompt_count, seq_len, model_width)
-    ffn_sum = lax.psum_scatter(
-        ffn_terms.astype(jnp.bfloat16), "col", scatter_dimension=2, tiled=True
-    ).astype(jnp.float32)
+    ffn_sum = scatter_sum_a2a(ffn_terms.astype(jnp.bfloat16), "col", 2)
     layer_out = (residual.astype(jnp.float32) + ffn_sum).astype(jnp.bfloat16)
     page_count = lax.axis_size("page")
     page_index = lax.axis_index("page")

time: 445 us -> 402 us (0.903)
  waiting for transfers between devices: 386 us -> 245 us
  starting transfers between devices: 6.08 us -> 61.6 us
  blocking collectives: 0 us -> 40.5 us
  local copies, waits for them, and re-layouts: 7.11 us -> 17.2 us
  matrix products: 17.9 us -> 12.9 us
    psum x1 -> x0, waiting for transfers between devices: 132 us -> none  [on_device(): attn_sum = lax.psum(attn_terms, 'col').astype(jnp.float32)]
    reduce_scatter x1 -> x0, waiting for transfers between devices: 80.2 us -> none  [on_device(): lax.psum_scatter(ffn_terms.astype(jnp.bfloat16), 'col', scatter_dimension...]
    all_to_all x0 -> x3, waiting for transfers between devices: none -> 76.6 us  [the longest x1 51.3 us: scatter_sum_a2a(): got = lax.all_to_all(x.reshape(split), axis_name, axis, axis, tiled=True)]
    all_to_all x0 -> x1, blocking collectives: none -> 40.5 us  [scatter_sum_a2a(): got = lax.all_to_all(x.reshape(split), axis_name, axis, axis, tiled=True)]
    all_to_all x1, starting transfers between devices: 5.92 us -> 39.1 us  [on_device(): lax.all_to_all(outgoing, 'page', split_axis=1, concat_axis=1, tiled=True)]
    all_to_all x0 -> x3, starting transfers between devices: none -> 22.4 us  [the longest x2 14.8 us: gather_a2a(): got = lax.all_to_all(copies, axis_name, 0, 0, tiled=True)]
    all_to_all x1, waiting for transfers between devices: 6.73 us -> 0.01 us  [on_device(): lax.all_to_all(outgoing, 'page', split_axis=1, concat_axis=1, tiled=True)]
  transfers between devices with their start and end apart: 5 -> 6, of which waited for: 5 -> 4; matrix products, arithmetic and copies ran while one was open for 2% -> 9% of each run, Pallas kernels for 0% -> 0%
where the time goes in v2:
time: 402 us; the launch traced here: 401 us
  waiting for transfers between devices  245 us (61%)
  starting transfers between devices  61.6 us (15%)
  blocking collectives  40.5 us (10%)
  local copies, waits for them, and re-layouts  17.2 us (4%)
  between operations  15.1 us (4%)
  matrix products  12.9 us (3%)
  other arithmetic  9.37 us (2%)
    all_gather x1, waiting for transfers between devices, on_device(): lax.all_gather(jnp.concatenate(pieces[:3], axis=1), ('row', 'page'), axis...  105 us
    all_gather x1, waiting for transfers between devices, on_device(): lax.all_gather(jnp.concatenate(pieces[3:], axis=1), ('row', 'page'), axis...  63.4 us
    all_to_all x1, waiting for transfers between devices, scatter_sum_a2a(): got = lax.all_to_all(x.reshape(split), axis_name, axis, axis, tiled=True)  51.3 us
    all_to_all x1, blocking collectives, scatter_sum_a2a(): got = lax.all_to_all(x.reshape(split), axis_name, axis, axis, tiled=True)  40.5 us
    all_to_all x1, starting transfers between devices, on_device(): lax.all_to_all(outgoing, 'page', split_axis=1, concat_axis=1, tiled=True)  39.1 us
    all_to_all x2, waiting for transfers between devices, gather_a2a(): got = lax.all_to_all(copies, axis_name, 0, 0, tiled=True)  25.2 us
    all_to_all x2, starting transfers between devices, gather_a2a(): got = lax.all_to_all(copies, axis_name, 0, 0, tiled=True)  14.8 us
  transfers between devices with their start and end apart: 6, of which 4 were waited for; matrix products, arithmetic and copies ran while one was open for 9% of the time, Pallas kernels for 0%

profile of v2, /device:TPU:8, one launch (start us, length us, event | category | flops | bytes accessed | tf_op | source)
XLA Modules:
  0.0 401.4 jit_solution(93900565374797844)
XLA Ops:
  7.2 0.0 copy-start
  7.2 0.0 all-gather.3.cloned.1.call-start
  7.2 0.8 copy-done
  8.1 0.1 fusion.30
  8.2 0.1 reshape.423
  8.3 0.8 convert_bitcast_fusion.2
  9.1 0.8 convert_element_type.121
  9.8 0.6 pad_maximum_fusion.2
  10.4 0.0 all-gather.3.cloned.1.call-update
  10.5 2.4 broadcast_in_dim.49
  12.9 11.1 %all-to-all-start = ((bf16[8,1,512,256]{3,2,1,0:T(8,128)(2,1)}), bf16[8,1,512,256]{3,2,1,0:T(8,128)(2,1)}, u32[]{:S(2)}, u32[]{:S(2)}) async-start(bf16[8,1,512,256]{3,2,1,0:T(8,128)(2,1)} %broadcast_in_dim.49), calls=%async_computation | async-start | bytes 4194304 | tf_op jit(solution)/shard_map/all_to_all | solution.py:55
  23.9 0.0 all-gather.5.cloned.1.call-start
  24.1 0.7 pad_maximum_fusion
  24.8 0.0 all-gather.5.cloned.1.call-update
  25.5 0.3 fusion.28
  25.8 0.8 fusion.11
  26.6 104.6 %all-gather.3.cloned.1.call-done = bf16[2048,384]{1,0:T(8,128)(2,1)} async-done(((bf16[64,384]{1,0:T(8,128)(2,1)}), bf16[2048,384]{1,0:T(8,128)(2,1)}) %all-gather.3.cloned.1.call-update) | async-done | bytes 1572880 | tf_op jit(solution)/shard_map/all_gather | solution.py:104
  131.2 1.3 slice_bitcast_fusion
  132.5 0.6 copy.51
  133.2 2.9 copy.49
  136.0 0.5 fusion.2
  136.6 0.5 fusion.4
  137.1 0.0 copy-start.9
  137.1 0.7 convolution_bitcast_fusion
  137.9 0.1 multiply_multiply_fusion.1
  138.0 0.3 fusion.31
  138.4 0.1 multiply_multiply_fusion
  138.6 0.2 copy-done.4
  138.8 0.7 fusion.8
  139.5 0.7 fusion.10
  140.2 1.8 convolution_convert_fusion
  142.0 0.7 copy.65
  142.7 0.4 copy.54
  143.2 40.5 %all_to_all.25 = bf16[1,512,8,256]{3,1,0,2:T(8,128)(2,1)S(1)} all-to-all(bf16[1,512,8,256]{3,1,0,2:T(8,128)(2,1)S(1)} %copy.54), channel_id=1, replica_groups=mesh['row'=8,'col'=8,'page'=4] {'col'}, dimensions={2} | all-to-all | bytes 4194304 | tf_op jit(solution)/shard_map/all_to_all | solution.py:66
  183.7 0.3 convert_reduce_fusion.1
  184.0 0.6 copy-done.1
  184.6 0.1 fusion.44
  184.7 0.1 copy.55
  184.8 1.6 broadcast_in_dim.55
  186.4 3.7 all-to-all-start.2
  190.2 0.2 convert_reduce_fusion.2
  190.5 0.1 broadcast_select_fusion.1
  190.6 0.2 maximum_bitcast_fusion
  190.8 0.2 copy.59
  191.1 0.8 scatter_fusion
  191.9 0.7 copy.60
  192.6 25.2 %all-to-all-done.2 = bf16[8,1,512,256]{2,3,1,0:T(8,128)(2,1)S(1)} async-done(((bf16[8,1,512,256]{2,3,1,0:T(8,128)(2,1)}), bf16[8,1,512,256]{2,3,1,0:T(8,128)(2,1)S(1)}, u32[]{:S(2)}, u32[]{:S(2)}) %all-to-all-start.2) | async-done | bytes 2097184 | tf_op jit(solution)/shard_map/all_to_all | solution.py:55
  217.8 39.1 %all-to-all-start.4 = ((bf16[2,4,128,128]{3,2,0,1:T(8,128)(2,1)}), bf16[2,4,128,128]{3,2,0,1:T(8,128)(2,1)S(1)}, u32[]{:S(2)}, u32[]{:S(2)}) async-start(bf16[2,4,128,128]{3,2,0,1:T(8,128)(2,1)} %copy.60), calls=%async_computation.4 | async-start | bytes 524288 | tf_op jit(solution)/shard_map/all_to_all | solution.py:169
  257.0 0.5 multiply_reduce_fusion
  257.5 0.6 bitcast_convert_fusion
  258.1 0.1 copy-done.6
  258.2 0.4 fusion.6
  258.6 63.4 %all-gather.5.cloned.1.call-done = bf16[2048,1920]{1,0:T(8,128)(2,1)} async-done(((bf16[64,1920]{1,0:T(8,128)(2,1)}), bf16[2048,1920]{1,0:T(8,128)(2,1)}) %all-gather.5.cloned.1.call-update) | async-done | bytes 7864336 | tf_op jit(solution)/shard_map/all_gather | solution.py:105
  322.0 5.4 %fusion = f32[512,1280]{1,0:T(8,128)S(1)} fusion(bf16[512,2048]{0,1:T(8,128)(2,1)S(1)} %fusion.6, bf16[2048,1920]{1,0:T(8,128)(2,1)} %all-gather.5.cloned.1.call-done), kind=kOutput, calls=%fused_computation.4 | convolution fusion | flops 2684354560 | bytes 9961472 | tf_op jit(solution)/shard_map/dot_general | solution.py:138
  327.5 3.6 convolution_convert_fusion.1
  331.1 0.7 copy.66
  331.7 1.8 copy.58
  333.5 7.6 %all-to-all-start.3 = ((bf16[1,512,8,256]{3,1,0,2:T(8,128)(2,1)}), bf16[1,512,8,256]{3,1,0,2:T(8,128)(2,1)S(1)}, u32[]{:S(2)}, u32[]{:S(2)}) async-start(bf16[1,512,8,256]{3,1,0,2:T(8,128)(2,1)} %copy.58), calls=%async_computation.3 | async-start | bytes 4194304 | tf_op jit(solution)/shard_map/all_to_all | solution.py:66
  341.1 0.1 fusion.34
  341.3 0.8 scatter_fusion.1
  342.1 0.0 copy-start.2
  342.1 51.3 %all-to-all-done.3 = bf16[1,512,8,256]{3,1,0,2:T(8,128)(2,1)S(1)} async-done(((bf16[1,512,8,256]{3,1,0,2:T(8,128)(2,1)}), bf16[1,512,8,256]{3,1,0,2:T(8,128)(2,1)S(1)}, u32[]{:S(2)}, u32[]{:S(2)}) %all-to-all-start.3) | async-done | bytes 2097184 | tf_op jit(solution)/shard_map/all_to_all | solution.py:66
  393.4 0.3 convert_reduce_fusion
  393.7 0.8 fusion.15
  (44 shorter events, 0.5 us)
Async XLA Ops:
  7.2 0.9 copy-start
  7.2 124.0 %all-gather.3.cloned.1.call-start = ((), (), s32[]{:S(2)}) async-start(), calls=%async_computation.5 | async-start | bytes 1622016 | tf_op jit(solution)/shard_map/all_gather | solution.py:104
  12.8 11.1 %copy-start.3 = (f32[2,64,640]{2,1,0:T(8,128)S(1)}, f32[2,64,640]{2,1,0:T(8,128)}, u32[]{:S(2)}) copy-start(f32[2,64,640]{2,1,0:T(8,128)} %param.18) | copy-start | bytes 983044
  12.9 11.2 %copy-start.5 = (f32[640,64]{0,1:T(8,128)S(1)}, f32[640,64]{0,1:T(8,128)}, u32[]{:S(2)}) copy-start(f32[640,64]{0,1:T(8,128)} %param.19) | copy-start | bytes 491524
  12.9 11.9 %copy-start.7 = (f32[2048]{0:T(1024)S(1)}, f32[2048]{0:T(1024)}, u32[]{:S(2)}) copy-start(f32[2048]{0:T(1024)} %param.20) | copy-start | bytes 24580
  12.9 120.3 %all-to-all-start = ((bf16[8,1,512,256]{3,2,1,0:T(8,128)(2,1)}), bf16[8,1,512,256]{3,2,1,0:T(8,128)(2,1)}, u32[]{:S(2)}, u32[]{:S(2)}) async-start(bf16[8,1,512,256]{3,2,1,0:T(8,128)(2,1)} %broadcast_in_dim.49), calls=%async_computation | async-start | bytes 4194304 | tf_op jit(solution)/shard_map/all_to_all | solution.py:55
  23.9 298.1 %all-gather.5.cloned.1.call-start = ((), (), s32[]{:S(2)}) async-start(), calls=%async_computation.6 | async-start | bytes 8110080 | tf_op jit(solution)/shard_map/all_gather | solution.py:105
  137.1 0.8 copy-start.9
  137.1 1.3 copy-start.10
  137.8 1.0 copy-start.4
  183.7 1.0 copy-start.1
  186.4 3.8 copy-start.8
  186.4 31.5 %all-to-all-start.2 = ((bf16[8,1,512,256]{2,3,1,0:T(8,128)(2,1)}), bf16[8,1,512,256]{2,3,1,0:T(8,128)(2,1)S(1)}, u32[]{:S(2)}, u32[]{:S(2)}) async-start(bf16[8,1,512,256]{2,3,1,0:T(8,128)(2,1)} %broadcast_in_dim.55), calls=%async_computation.2 | async-start | bytes 4194304 | tf_op jit(solution)/shard_map/all_to_all | solution.py:55
  217.8 115.7 %all-to-all-start.4 = ((bf16[2,4,128,128]{3,2,0,1:T(8,128)(2,1)}), bf16[2,4,128,128]{3,2,0,1:T(8,128)(2,1)S(1)}, u32[]{:S(2)}, u32[]{:S(2)}) async-start(bf16[2,4,128,128]{3,2,0,1:T(8,128)(2,1)} %copy.60), calls=%async_computation.4 | async-start | bytes 524288 | tf_op jit(solution)/shard_map/all_to_all | solution.py:169
  257.5 0.7 copy-start.6
  333.5 59.9 %all-to-all-start.3 = ((bf16[1,512,8,256]{3,1,0,2:T(8,128)(2,1)}), bf16[1,512,8,256]{3,1,0,2:T(8,128)(2,1)S(1)}, u32[]{:S(2)}, u32[]{:S(2)}) async-start(bf16[1,512,8,256]{3,1,0,2:T(8,128)(2,1)} %copy.58), calls=%async_computation.3 | async-start | bytes 4194304 | tf_op jit(solution)/shard_map/all_to_all | solution.py:66
  342.1 52.5 %copy-start.2 = (bf16[2,4,128,128]{3,2,1,0:T(8,128)(2,1)}, bf16[2,4,128,128]{3,2,1,0:T(8,128)(2,1)S(1)}, u32[]{:S(2)}) copy-start(bf16[2,4,128,128]{3,2,1,0:T(8,128)(2,1)S(1)} %scatter_fusion.1) | copy-start | bytes 786436
Sparse Core Ops, SparseCore 0:
  10.6 120.5 all-gather.2
  133.6 188.4 all-gather.4

commit v3 on v2

--- a/solution.py
+++ b/solution.py
@@ -101,12 +101,11 @@
     ]
     widths = [p.shape[1] for p in pieces]
     offsets = [sum(widths[:i]) for i in range(len(widths) + 1)]
-    attn_full = lax.all_gather(jnp.concatenate(pieces[:3], axis=1), ("row", "page"), axis=0, tiled=True)
-    ffn_full = lax.all_gather(jnp.concatenate(pieces[3:], axis=1), ("row", "page"), axis=0, tiled=True)
-    qkv_w = attn_full[:, offsets[0] : offsets[2]]
-    out_t = attn_full[:, offsets[2] : offsets[3]]
-    gateup_w = ffn_full[:, : offsets[4] - offsets[3]]
-    down_t = ffn_full[:, offsets[4] - offsets[3] :]
+    full = lax.all_gather(jnp.concatenate(pieces, axis=1), ("row", "page"), axis=0, tiled=True)
+    qkv_w = full[:, offsets[0] : offsets[2]]
+    out_t = full[:, offsets[2] : offsets[3]]
+    gateup_w = full[:, offsets[3] : offsets[4]]
+    down_t = full[:, offsets[4] : offsets[5]]
 
     prompt_count, seq_len, local_feat = tokens.shape
     gathered = gather_a2a(tokens, "col", 2)

time: 402 us -> 356 us (0.89)
  the two profiles are of different devices: /device:TPU:8 before, /device:TPU:24 now
where the time goes in v3:
time: 356 us; the launch traced here: 355 us
  waiting for transfers between devices  192 us (54%)
  blocking collectives  61.5 us (17%)
  starting transfers between devices  43.6 us (12%)
  local copies, waits for them, and re-layouts  16.3 us (5%)
  between operations  15.1 us (4%)
  matrix products  14.2 us (4%)
  other arithmetic  12 us (3%)
    all_to_all x2, waiting for transfers between devices, gather_a2a(): got = lax.all_to_all(copies, axis_name, 0, 0, tiled=True)  86.9 us
    all_to_all x1, blocking collectives, scatter_sum_a2a(): got = lax.all_to_all(x.reshape(split), axis_name, axis, axis, tiled=True)  61.5 us
    all_gather x1, waiting for transfers between devices, on_device(): lax.all_gather(jnp.concatenate(pieces, axis=1), ('row', 'page'), axis=0,...  55.3 us
    all_to_all x1, waiting for transfers between devices, scatter_sum_a2a(): got = lax.all_to_all(x.reshape(split), axis_name, axis, axis, tiled=True)  50 us
    all_to_all x1, starting transfers between devices, on_device(): lax.all_to_all(outgoing, 'page', split_axis=1, concat_axis=1, tiled=True)  24.5 us
    all_to_all x2, starting transfers between devices, gather_a2a(): got = lax.all_to_all(copies, axis_name, 0, 0, tiled=True)  14.8 us
  transfers between devices with their start and end apart: 5, of which 4 were waited for; matrix products, arithmetic and copies ran while one was open for 7% of the time, Pallas kernels for 0%

profile of v3, /device:TPU:24, one launch (start us, length us, event | category | flops | bytes accessed | tf_op | source)
XLA Modules:
  0.0 355.0 jit_solution(2286361403284712844)
XLA Ops:
  7.2 0.0 copy-start
  7.2 0.0 all-gather.2.cloned.1.call-start
  7.2 0.8 convert_dynamic-update-slice_fusion
  8.1 0.0 copy-done
  8.1 0.1 fusion.30
  8.2 0.1 reshape.423
  8.3 1.0 convert_bitcast_fusion
  9.3 0.8 bitcast_dynamic-update-slice_fusion.1
  10.1 0.9 bitcast_dynamic-update-slice_fusion
  11.1 0.7 copy-done.4
  11.8 0.0 all-gather.2.cloned.1.call-update
  11.8 1.6 broadcast_in_dim.49
  13.4 11.1 %all-to-all-start = ((bf16[8,1,512,256]{3,2,1,0:T(8,128)(2,1)}), bf16[8,1,512,256]{3,2,1,0:T(8,128)(2,1)}, u32[]{:S(2)}, u32[]{:S(2)}) async-start(bf16[8,1,512,256]{3,2,1,0:T(8,128)(2,1)} %broadcast_in_dim.49), calls=%async_computation | async-start | bytes 4194304 | tf_op jit(solution)/shard_map/all_to_all | solution.py:55
  25.1 1.0 fusion.28
  26.1 0.8 fusion.11
  26.9 58.8 %all-to-all-done = bf16[8,1,512,256]{3,2,1,0:T(8,128)(2,1)} async-done(((bf16[8,1,512,256]{3,2,1,0:T(8,128)(2,1)}), bf16[8,1,512,256]{3,2,1,0:T(8,128)(2,1)}, u32[]{:S(2)}, u32[]{:S(2)}) %all-to-all-start) | async-done | bytes 2097184 | tf_op jit(solution)/shard_map/all_to_all | solution.py:55
  85.7 2.9 copy.50
  88.6 0.5 fusion.2
  89.1 1.9 fusion.4
  91.0 55.3 %all-gather.2.cloned.1.call-done = bf16[2048,2304]{1,0:T(8,128)(2,1)} async-done(((bf16[64,2304]{1,0:T(8,128)(2,1)}), bf16[2048,2304]{1,0:T(8,128)(2,1)}) %all-gather.2.cloned.1.call-update) | async-done | bytes 9437200 | tf_op jit(solution)/shard_map/all_gather | solution.py:104
  146.3 1.3 slice_bitcast_fusion
  147.6 1.4 copy.53
  149.1 2.0 convolution_bitcast_fusion
  151.1 0.0 copy-start.5
  151.2 0.0 copy-done.11
  151.2 0.1 multiply_multiply_fusion.1
  151.3 0.3 fusion.31
  151.6 0.1 multiply_multiply_fusion
  151.8 0.2 copy-done.5
  152.0 0.7 fusion.8
  152.8 0.7 fusion.10
  153.5 1.8 convolution_convert_fusion
  155.3 0.7 copy.66
  155.9 0.4 copy.56
  156.4 61.5 %all_to_all.25 = bf16[1,512,8,256]{3,1,0,2:T(8,128)(2,1)S(1)} all-to-all(bf16[1,512,8,256]{3,1,0,2:T(8,128)(2,1)S(1)} %copy.56), channel_id=1, replica_groups=mesh['row'=8,'col'=8,'page'=4] {'col'}, dimensions={2} | all-to-all | bytes 4194304 | tf_op jit(solution)/shard_map/all_to_all | solution.py:66
  217.8 0.3 convert_reduce_fusion.1
  218.2 0.1 fusion.44
  218.2 0.1 copy.57
  218.4 1.5 broadcast_in_dim.55
  219.9 3.7 %all-to-all-start.2 = ((bf16[8,1,512,256]{2,3,1,0:T(8,128)(2,1)}), bf16[8,1,512,256]{2,3,1,0:T(8,128)(2,1)S(1)}, u32[]{:S(2)}, u32[]{:S(2)}) async-start(bf16[8,1,512,256]{2,3,1,0:T(8,128)(2,1)} %broadcast_in_dim.55), calls=%async_computation.2 | async-start | bytes 4194304 | tf_op jit(solution)/shard_map/all_to_all | solution.py:55
  223.7 0.2 convert_reduce_fusion.2
  224.0 0.1 broadcast_select_fusion.1
  224.1 0.2 maximum_bitcast_fusion
  224.3 0.2 copy.60
  224.6 0.8 scatter_fusion
  225.4 0.7 copy.61
  226.1 28.1 %all-to-all-done.2 = bf16[8,1,512,256]{2,3,1,0:T(8,128)(2,1)S(1)} async-done(((bf16[8,1,512,256]{2,3,1,0:T(8,128)(2,1)}), bf16[8,1,512,256]{2,3,1,0:T(8,128)(2,1)S(1)}, u32[]{:S(2)}, u32[]{:S(2)}) %all-to-all-start.2) | async-done | bytes 2097184 | tf_op jit(solution)/shard_map/all_to_all | solution.py:55
  254.2 24.5 %all-to-all-start.4 = ((bf16[2,4,128,128]{3,2,0,1:T(8,128)(2,1)}), bf16[2,4,128,128]{3,2,0,1:T(8,128)(2,1)S(1)}, u32[]{:S(2)}, u32[]{:S(2)}) async-start(bf16[2,4,128,128]{3,2,0,1:T(8,128)(2,1)} %copy.61), calls=%async_computation.4 | async-start | bytes 524288 | tf_op jit(solution)/shard_map/all_to_all | solution.py:168
  278.6 0.5 multiply_reduce_fusion
  279.1 0.6 bitcast_convert_fusion
  279.7 0.1 copy-done.8
  279.8 0.4 fusion.6
  280.3 5.4 %fusion = f32[512,1280]{1,0:T(8,128)S(1)} fusion(bf16[512,2048]{0,1:T(8,128)(2,1)S(1)} %fusion.6, bf16[2048,2304]{1,0:T(8,128)(2,1)} %all-gather.2.cloned.1.call-done), kind=kOutput, calls=%fused_computation.4 | convolution fusion | flops 2684354560 | bytes 9961472 | tf_op jit(solution)/shard_map/dot_general | solution.py:137
  285.7 3.6 %convolution_convert_fusion.1 = bf16[512,2048]{1,0:T(8,128)(2,1)S(1)} fusion(bf16[2048,2304]{1,0:T(8,128)(2,1)} %all-gather.2.cloned.1.call-done, f32[512,1280]{1,0:T(8,128)S(1)} %fusion), kind=kOutput, calls=%fused_computation.16 | convolution fusion | flops 1345191936 | bytes 7340032 | tf_op jit(solution)/shard_map/dot_general | solution.py:47
  289.3 0.7 copy.67
  290.0 1.8 copy.59
  291.7 0.0 all-to-all-done.4
  291.7 4.3 %all-to-all-start.3 = ((bf16[1,512,8,256]{3,1,0,2:T(8,128)(2,1)}), bf16[1,512,8,256]{3,1,0,2:T(8,128)(2,1)S(1)}, u32[]{:S(2)}, u32[]{:S(2)}) async-start(bf16[1,512,8,256]{3,1,0,2:T(8,128)(2,1)} %copy.59), calls=%async_computation.3 | async-start | bytes 4194304 | tf_op jit(solution)/shard_map/all_to_all | solution.py:66
  296.1 0.1 fusion.34
  296.2 0.8 scatter_fusion.1
  297.0 0.0 copy-start.3
  297.0 50.0 %all-to-all-done.3 = bf16[1,512,8,256]{3,1,0,2:T(8,128)(2,1)S(1)} async-done(((bf16[1,512,8,256]{3,1,0,2:T(8,128)(2,1)}), bf16[1,512,8,256]{3,1,0,2:T(8,128)(2,1)S(1)}, u32[]{:S(2)}, u32[]{:S(2)}) %all-to-all-start.3) | async-done | bytes 2097184 | tf_op jit(solution)/shard_map/all_to_all | solution.py:66
  347.1 0.3 convert_reduce_fusion
  347.4 0.8 fusion.15
  (45 shorter events, 0.5 us)
Async XLA Ops:
  7.2 0.9 copy-start
  7.2 4.6 %copy-start.1 = (bf16[1,512,256]{2,1,0:T(8,128)(2,1)S(1)}, bf16[1,512,256]{2,1,0:T(8,128)(2,1)}, u32[]{:S(2)}) copy-start(bf16[1,512,256]{2,1,0:T(8,128)(2,1)} %param.12) | copy-start | bytes 786436
  7.2 139.1 %all-gather.2.cloned.1.call-start = ((), (), s32[]{:S(2)}) async-start(), calls=%async_computation.5 | async-start | bytes 9732096 | tf_op jit(solution)/shard_map/all_gather | solution.py:104
  11.0 0.7 copy-start.4
  13.3 11.7 %copy-start.9 = (f32[2048]{0:T(1024)S(1)}, f32[2048]{0:T(1024)}, u32[]{:S(2)}) copy-start(f32[2048]{0:T(1024)} %param.20) | copy-start | bytes 24580
  13.4 72.4 %all-to-all-start = ((bf16[8,1,512,256]{3,2,1,0:T(8,128)(2,1)}), bf16[8,1,512,256]{3,2,1,0:T(8,128)(2,1)}, u32[]{:S(2)}, u32[]{:S(2)}) async-start(bf16[8,1,512,256]{3,2,1,0:T(8,128)(2,1)} %broadcast_in_dim.49), calls=%async_computation | async-start | bytes 4194304 | tf_op jit(solution)/shard_map/all_to_all | solution.py:55
  91.0 58.1 %copy-start.2 = (bf16[8,1,512,256]{2,3,0,1:T(8,128)(2,1)S(1)}, bf16[8,1,512,256]{2,3,0,1:T(8,128)(2,1)}, u32[]{:S(2)}) copy-start(bf16[8,1,512,256]{2,3,0,1:T(8,128)(2,1)} %fusion.4) | copy-start | bytes 6291460
  149.1 2.1 copy-start.11
  149.1 2.6 copy-start.12
  149.1 2.7 copy-start.6
  149.1 2.7 copy-start.7
  151.1 1.0 copy-start.5
  219.9 3.8 %copy-start.10 = (s32[4,4]{1,0:T(4,128)S(1)}, s32[4,4]{1,0:T(4,128)}, u32[]{:S(2)}) copy-start(s32[4,4]{1,0:T(4,128)} %param.14) | copy-start | bytes 196
  219.9 34.3 %all-to-all-start.2 = ((bf16[8,1,512,256]{2,3,1,0:T(8,128)(2,1)}), bf16[8,1,512,256]{2,3,1,0:T(8,128)(2,1)S(1)}, u32[]{:S(2)}, u32[]{:S(2)}) async-start(bf16[8,1,512,256]{2,3,1,0:T(8,128)(2,1)} %broadcast_in_dim.55), calls=%async_computation.2 | async-start | bytes 4194304 | tf_op jit(solution)/shard_map/all_to_all | solution.py:55
  254.2 37.6 %all-to-all-start.4 = ((bf16[2,4,128,128]{3,2,0,1:T(8,128)(2,1)}), bf16[2,4,128,128]{3,2,0,1:T(8,128)(2,1)S(1)}, u32[]{:S(2)}, u32[]{:S(2)}) async-start(bf16[2,4,128,128]{3,2,0,1:T(8,128)(2,1)} %copy.61), calls=%async_computation.4 | async-start | bytes 524288 | tf_op jit(solution)/shard_map/all_to_all | solution.py:168
  279.1 0.7 copy-start.8
  291.7 55.3 %all-to-all-start.3 = ((bf16[1,512,8,256]{3,1,0,2:T(8,128)(2,1)}), bf16[1,512,8,256]{3,1,0,2:T(8,128)(2,1)S(1)}, u32[]{:S(2)}, u32[]{:S(2)}) async-start(bf16[1,512,8,256]{3,1,0,2:T(8,128)(2,1)} %copy.59), calls=%async_computation.3 | async-start | bytes 4194304 | tf_op jit(solution)/shard_map/all_to_all | solution.py:66
  297.0 51.1 %copy-start.3 = (bf16[2,4,128,128]{3,2,1,0:T(8,128)(2,1)}, bf16[2,4,128,128]{3,2,1,0:T(8,128)(2,1)S(1)}, u32[]{:S(2)}) copy-start(bf16[2,4,128,128]{3,2,1,0:T(8,128)(2,1)S(1)} %scatter_fusion.1) | copy-start | bytes 786436
Sparse Core Ops, SparseCore 0:
  11.9 134.3 all-gather.1

commit v4 on v3

--- a/solution.py
+++ b/solution.py
@@ -1,9 +1,12 @@
 import jax
 import jax.numpy as jnp
 from jax import lax
-from jax.sharding import PartitionSpec as P
+from jax.sharding import Mesh, PartitionSpec as P
 
 PAGE_LEN = 128
+ROW = ("ry", "rc")
+COL = ("zh", "xx")
+ROWPAGE = ("ry", "rc", "page")
 
 
 def normalize(values, norm_gain):
@@ -81,8 +84,8 @@
     query_gain,
     key_gain,
 ):
-    col_count = lax.axis_size("col")
-    col_index = lax.axis_index("col")
+    col_count = lax.axis_size(COL)
+    col_index = lax.axis_index(COL)
     head_dim = query_gain.shape[0]
     local_width = w_query.shape[1]
     local_heads = local_width // head_dim
@@ -101,14 +104,17 @@
     ]
     widths = [p.shape[1] for p in pieces]
     offsets = [sum(widths[:i]) for i in range(len(widths) + 1)]
-    full = lax.all_gather(jnp.concatenate(pieces, axis=1), ("row", "page"), axis=0, tiled=True)
+    across = lax.all_gather(jnp.concatenate(pieces, axis=1), ("ry", "page"), axis=0, tiled=True)
+    chips = lax.axis_size("ry")
+    across = across.reshape(chips, -1, across.shape[1])
+    full = lax.all_gather(across, "rc", axis=1, tiled=True).reshape(-1, across.shape[2])
     qkv_w = full[:, offsets[0] : offsets[2]]
     out_t = full[:, offsets[2] : offsets[3]]
     gateup_w = full[:, offsets[3] : offsets[4]]
     down_t = full[:, offsets[4] : offsets[5]]
 
     prompt_count, seq_len, local_feat = tokens.shape
-    gathered = gather_a2a(tokens, "col", 2)
+    gathered = gather_a2a(tokens, COL, 2)
     model_width = gathered.shape[2]
     attn_in = normalize(gathered.astype(jnp.float32), attn_gain).astype(jnp.bfloat16)
     projected = jnp.dot(
@@ -130,16 +136,16 @@
     )
     attn_terms = contract_rows(attended.reshape(-1, local_width), out_t)
     attn_terms = attn_terms.reshape(prompt_count, seq_len, model_width).astype(jnp.bfloat16)
-    attn_sum = scatter_sum_a2a(attn_terms, "col", 2)
+    attn_sum = scatter_sum_a2a(attn_terms, COL, 2)
     residual = (tokens.astype(jnp.float32) + attn_sum).astype(jnp.bfloat16)
-    residual_all = gather_a2a(residual, "col", 2)
+    residual_all = gather_a2a(residual, COL, 2)
     ffn_in = normalize(residual_all.astype(jnp.float32), ffn_gain).astype(jnp.bfloat16)
     gate_up = jnp.dot(
         ffn_in.reshape(-1, model_width), gateup_w, preferred_element_type=jnp.float32
     )
     hidden = (jax.nn.silu(gate_up[:, :unit_count]) * gate_up[:, unit_count:]).astype(jnp.bfloat16)
     ffn_terms = contract_rows(hidden, down_t).reshape(prompt_count, seq_len, model_width)
-    ffn_sum = scatter_sum_a2a(ffn_terms.astype(jnp.bfloat16), "col", 2)
+    ffn_sum = scatter_sum_a2a(ffn_terms.astype(jnp.bfloat16), COL, 2)
     layer_out = (residual.astype(jnp.float32) + ffn_sum).astype(jnp.bfloat16)
     page_count = lax.axis_size("page")
     page_index = lax.axis_index("page")
@@ -178,20 +184,26 @@
 
 def solution(mesh):
     in_specs = (
-        P(("row", "page"), None, "col"),
-        P(("row", "page")),
-        P("row", None),
-        P(("row", "page"), "col"),
-        P(None, ("row", "page"), None),
-        P("col", ("row", "page")),
-        P(None, ("row", "page"), "col"),
-        P("col", ("row", "page")),
-        P(),
-        P(),
-        P(),
-        P(),
-    )
-    out_specs = (P(("row", "page"), None, "col"), P(None, ("row", "page"), None, "col"))
+        P(ROWPAGE, None, COL),
+        P(ROWPAGE),
+        P(ROW, None),
+        P(ROWPAGE, COL),
+        P(None, ROWPAGE, None),
+        P(COL, ROWPAGE),
+        P(None, ROWPAGE, COL),
+        P(COL, ROWPAGE),
+        P(),
+        P(),
+        P(),
+        P(),
+    )
+    out_specs = (P(ROWPAGE, None, COL), P(None, ROWPAGE, None, COL))
+    fine = Mesh(
+        mesh.devices.reshape(
+            mesh.shape["row"] // 2, 2, 2, mesh.shape["col"] // 2, mesh.shape["page"]
+        ),
+        ("ry", "rc", "zh", "xx", "page"),
+    )
     return jax.shard_map(
-        on_device, mesh=mesh, in_specs=in_specs, out_specs=out_specs, check_vma=False
-    )
+        on_device, mesh=fine, in_specs=in_specs, out_specs=out_specs, check_vma=False
+    )

time: 356 us -> 383 us (1.076)
  the two profiles are of different devices: /device:TPU:24 before, /device:TPU:8 now
where the time goes in v4:
time: 383 us; the launch traced here: 382 us
  waiting for transfers between devices  228 us (60%)
  blocking collectives  52.3 us (14%)
  starting transfers between devices  43.1 us (11%)
  local copies, waits for them, and re-layouts  17.3 us (5%)
  between operations  15.1 us (4%)
  matrix products  14.2 us (4%)
  other arithmetic  11.9 us (3%)
    all_gather x1, waiting for transfers between devices, on_device(): lax.all_gather(jnp.concatenate(pieces, axis=1), ('ry', 'page'), axis=0, t...  113 us
    all_to_all x2, waiting for transfers between devices, gather_a2a(): got = lax.all_to_all(copies, axis_name, 0, 0, tiled=True)  64.3 us
    all_to_all x1, blocking collectives, scatter_sum_a2a(): got = lax.all_to_all(x.reshape(split), axis_name, axis, axis, tiled=True)  52.3 us
    all_to_all x1, waiting for transfers between devices, scatter_sum_a2a(): got = lax.all_to_all(x.reshape(split), axis_name, axis, axis, tiled=True)  50.5 us
    all_to_all x1, starting transfers between devices, on_device(): lax.all_to_all(outgoing, 'page', split_axis=1, concat_axis=1, tiled=True)  26 us
    all_to_all x2, starting transfers between devices, gather_a2a(): got = lax.all_to_all(copies, axis_name, 0, 0, tiled=True)  10.9 us
  transfers between devices with their start and end apart: 6, of which 4 were waited for; matrix products, arithmetic and copies ran while one was open for 6% of the time, Pallas kernels for 0%

profile of v4, /device:TPU:8, one launch (start us, length us, event | category | flops | bytes accessed | tf_op | source)
XLA Modules:
  0.0 382.2 jit_solution(10579840790599652194)
XLA Ops:
  7.2 0.0 copy-start
  7.2 0.0 all-gather.3.cloned.1.call-start
  7.2 0.8 convert_dynamic-update-slice_fusion
  8.0 0.1 copy-done
  8.1 0.1 fusion.30
  8.2 0.1 reshape.429
  8.3 1.0 convert_bitcast_fusion
  9.3 0.8 bitcast_dynamic-update-slice_fusion.1
  10.1 0.9 bitcast_dynamic-update-slice_fusion
  11.1 0.7 copy-done.4
  11.7 0.0 all-gather.3.cloned.1.call-update
  11.8 0.0 all-gather.5.cloned.1.call-start
  11.8 113.3 %all-gather.3.cloned.1.call-done = bf16[1024,2304]{1,0:T(8,128)(2,1)} async-done(((bf16[64,2304]{1,0:T(8,128)(2,1)}), bf16[1024,2304]{1,0:T(8,128)(2,1)}) %all-gather.3.cloned.1.call-update) | async-done | bytes 4718608 | tf_op jit(solution)/shard_map/all_gather | solution.py:107
  125.1 0.0 all-gather.5.cloned.1.call-update
  125.1 0.9 copy-done.1
  126.1 1.5 broadcast_in_dim.49
  127.5 7.1 %all-to-all-start = ((bf16[8,1,512,256]{3,2,1,0:T(8,128)(2,1)}), bf16[8,1,512,256]{3,2,1,0:T(8,128)(2,1)}, u32[]{:S(2)}, u32[]{:S(2)}) async-start(bf16[8,1,512,256]{3,2,1,0:T(8,128)(2,1)} %broadcast_in_dim.49), calls=%async_computation | async-start | bytes 4194304 | tf_op jit(solution)/shard_map/all_to_all | solution.py:58
  135.3 1.0 fusion.28
  136.3 0.8 fusion.11
  137.1 47.4 %all-to-all-done = bf16[8,1,512,256]{3,2,1,0:T(8,128)(2,1)} async-done(((bf16[8,1,512,256]{3,2,1,0:T(8,128)(2,1)}), bf16[8,1,512,256]{3,2,1,0:T(8,128)(2,1)}, u32[]{:S(2)}, u32[]{:S(2)}) %all-to-all-start) | async-done | bytes 2097184 | tf_op jit(solution)/shard_map/all_to_all | solution.py:58
  184.5 2.9 copy.50
  187.4 0.5 fusion.2
  187.9 1.9 fusion.4
  189.8 1.4 slice.53
  191.2 1.4 copy.66
  192.7 2.0 convolution_bitcast_fusion
  194.6 0.0 copy-start.5
  194.8 0.1 multiply_multiply_fusion.1
  194.8 0.3 fusion.31
  195.2 0.1 multiply_multiply_fusion
  195.4 0.2 copy-done.5
  195.6 0.7 fusion.8
  196.3 0.7 fusion.10
  197.0 1.8 convolution_convert_fusion
  198.8 0.7 copy.71
  199.5 0.4 copy.56
  199.9 52.3 %all_to_all.25 = bf16[1,512,8,256]{3,1,0,2:T(8,128)(2,1)S(1)} all-to-all(bf16[1,512,8,256]{3,1,0,2:T(8,128)(2,1)S(1)} %copy.56), channel_id=1, replica_groups=mesh['ry'=4,'rc'=2,'zh'=2,'xx'=4,'page'=4] {'zh','xx'}, dimensions={2} | all-to-all | bytes 4194304 | tf_op jit(solution)/shard_map/all_to_all | solution.py:69
  252.3 0.3 convert_reduce_fusion.1
  252.6 0.1 fusion.44
  252.7 0.1 copy.57
  252.8 1.5 broadcast_in_dim.55
  254.3 3.7 all-to-all-start.2
  258.1 0.2 convert_reduce_fusion.2
  258.4 0.1 broadcast_select_fusion.1
  258.6 0.2 maximum_bitcast_fusion
  258.8 0.2 copy.60
  259.0 0.8 scatter_fusion
  259.8 0.7 copy.61
  260.5 17.0 %all-to-all-done.2 = bf16[8,1,512,256]{2,3,1,0:T(8,128)(2,1)S(1)} async-done(((bf16[8,1,512,256]{2,3,1,0:T(8,128)(2,1)}), bf16[8,1,512,256]{2,3,1,0:T(8,128)(2,1)S(1)}, u32[]{:S(2)}, u32[]{:S(2)}) %all-to-all-start.2) | async-done | bytes 2097184 | tf_op jit(solution)/shard_map/all_to_all | solution.py:58
  277.5 26.0 %all-to-all-start.4 = ((bf16[2,4,128,128]{3,2,0,1:T(8,128)(2,1)}), bf16[2,4,128,128]{3,2,0,1:T(8,128)(2,1)S(1)}, u32[]{:S(2)}, u32[]{:S(2)}) async-start(bf16[2,4,128,128]{3,2,0,1:T(8,128)(2,1)} %copy.61), calls=%async_computation.4 | async-start | bytes 524288 | tf_op jit(solution)/shard_map/all_to_all | solution.py:174
  303.5 0.5 multiply_reduce_fusion
  304.0 0.6 bitcast_convert_fusion
  304.6 0.1 copy-done.8
  304.7 0.4 fusion.6
  305.2 5.4 %fusion = f32[512,1280]{1,0:T(8,128)S(1)} fusion(bf16[512,2048]{0,1:T(8,128)(2,1)S(1)} %fusion.6, bf16[2048,2304]{1,0:T(8,128)(2,1)} %bitcast.106), kind=kOutput, calls=%fused_computation.4 | convolution fusion | flops 2684354560 | bytes 9961472 | tf_op jit(solution)/shard_map/dot_general | solution.py:143
  310.6 3.6 convolution_convert_fusion.1
  314.2 0.7 copy.72
  314.9 1.8 copy.59
  316.6 6.2 %all-to-all-start.3 = ((bf16[1,512,8,256]{3,1,0,2:T(8,128)(2,1)}), bf16[1,512,8,256]{3,1,0,2:T(8,128)(2,1)S(1)}, u32[]{:S(2)}, u32[]{:S(2)}) async-start(bf16[1,512,8,256]{3,1,0,2:T(8,128)(2,1)} %copy.59), calls=%async_computation.3 | async-start | bytes 4194304 | tf_op jit(solution)/shard_map/all_to_all | solution.py:69
  322.8 0.1 fusion.34
  323.0 0.8 scatter_fusion.1
  323.7 50.5 %all-to-all-done.3 = bf16[1,512,8,256]{3,1,0,2:T(8,128)(2,1)S(1)} async-done(((bf16[1,512,8,256]{3,1,0,2:T(8,128)(2,1)}), bf16[1,512,8,256]{3,1,0,2:T(8,128)(2,1)S(1)}, u32[]{:S(2)}, u32[]{:S(2)}) %all-to-all-start.3) | async-done | bytes 2097184 | tf_op jit(solution)/shard_map/all_to_all | solution.py:69
  374.3 0.3 convert_reduce_fusion
  374.6 0.8 fusion.15
  (48 shorter events, 0.5 us)
Async XLA Ops:
  7.2 0.9 copy-start
  7.2 117.9 %all-gather.3.cloned.1.call-start = ((), (), s32[]{:S(2)}) async-start(), calls=%async_computation.5 | async-start | bytes 5013504 | tf_op jit(solution)/shard_map/all_gather | solution.py:107
  11.0 0.7 copy-start.4
  11.8 178.0 %all-gather.5.cloned.1.call-start = ((), (), s32[]{:S(2)}) async-start(), calls=%async_computation.6 | async-start | bytes 14155776 | tf_op jit(solution)/shard_map/all_gather | solution.py:110
  125.1 0.9 copy-start.1
  127.5 7.8 %copy-start.9 = (f32[2048]{0:T(1024)S(1)}, f32[2048]{0:T(1024)}, u32[]{:S(2)}) copy-start(f32[2048]{0:T(1024)} %param.20) | copy-start | bytes 24580
  127.5 57.0 %all-to-all-start = ((bf16[8,1,512,256]{3,2,1,0:T(8,128)(2,1)}), bf16[8,1,512,256]{3,2,1,0:T(8,128)(2,1)}, u32[]{:S(2)}, u32[]{:S(2)}) async-start(bf16[8,1,512,256]{3,2,1,0:T(8,128)(2,1)} %broadcast_in_dim.49), calls=%async_computation | async-start | bytes 4194304 | tf_op jit(solution)/shard_map/all_to_all | solution.py:58
  189.8 2.9 copy-start.2
  192.6 2.1 copy-start.11
  192.6 2.6 copy-start.12
  192.6 2.7 copy-start.6
  192.6 2.7 copy-start.7
  194.6 1.0 copy-start.5
  254.3 3.8 copy-start.10
  254.3 23.2 %all-to-all-start.2 = ((bf16[8,1,512,256]{2,3,1,0:T(8,128)(2,1)}), bf16[8,1,512,256]{2,3,1,0:T(8,128)(2,1)S(1)}, u32[]{:S(2)}, u32[]{:S(2)}) async-start(bf16[8,1,512,256]{2,3,1,0:T(8,128)(2,1)} %broadcast_in_dim.55), calls=%async_computation.2 | async-start | bytes 4194304 | tf_op jit(solution)/shard_map/all_to_all | solution.py:58
  277.5 39.1 %all-to-all-start.4 = ((bf16[2,4,128,128]{3,2,0,1:T(8,128)(2,1)}), bf16[2,4,128,128]{3,2,0,1:T(8,128)(2,1)S(1)}, u32[]{:S(2)}, u32[]{:S(2)}) async-start(bf16[2,4,128,128]{3,2,0,1:T(8,128)(2,1)} %copy.61), calls=%async_computation.4 | async-start | bytes 524288 | tf_op jit(solution)/shard_map/all_to_all | solution.py:174
  304.0 0.7 copy-start.8
  316.6 57.7 %all-to-all-start.3 = ((bf16[1,512,8,256]{3,1,0,2:T(8,128)(2,1)}), bf16[1,512,8,256]{3,1,0,2:T(8,128)(2,1)S(1)}, u32[]{:S(2)}, u32[]{:S(2)}) async-start(bf16[1,512,8,256]{3,1,0,2:T(8,128)(2,1)} %copy.59), calls=%async_computation.3 | async-start | bytes 4194304 | tf_op jit(solution)/shard_map/all_to_all | solution.py:69
  323.7 51.6 %copy-start.3 = (bf16[2,4,128,128]{3,2,1,0:T(8,128)(2,1)}, bf16[2,4,128,128]{3,2,1,0:T(8,128)(2,1)S(1)}, u32[]{:S(2)}) copy-start(bf16[2,4,128,128]{3,2,1,0:T(8,128)(2,1)S(1)} %scatter_fusion.1) | copy-start | bytes 786436
Sparse Core Ops, SparseCore 0:
  11.9 113.1 all-gather.2
  126.9 25.5 all-gather.4

commit v5 on v4

--- a/solution.py
+++ b/solution.py
@@ -68,6 +68,35 @@
     split = shape[:axis] + [count, shape[axis] // count] + shape[axis + 1 :]
     got = lax.all_to_all(x.reshape(split), axis_name, axis, axis, tiled=True)
     return jnp.sum(got.astype(jnp.float32), axis=axis)
+
+
+def swap_halves(x):
+    return lax.ppermute(x, "zh", [(0, 1), (1, 0)])
+
+
+def gather_col(x, axis):
+    half = lax.axis_index("zh")
+    other = swap_halves(x)
+    pair = jnp.stack([jnp.where(half == 0, x, other), jnp.where(half == 0, other, x)])
+    count = lax.axis_size("xx")
+    copies = jnp.broadcast_to(pair[None], (count,) + pair.shape)
+    got = lax.all_to_all(copies, "xx", 0, 0, tiled=True)
+    got = jnp.moveaxis(jnp.swapaxes(got, 0, 1).reshape((-1,) + x.shape), 0, axis)
+    shape = list(x.shape)
+    shape[axis] *= 2 * count
+    return got.reshape(shape)
+
+
+def scatter_sum_col(x, axis):
+    count = lax.axis_size("xx")
+    shape = list(x.shape)
+    split = shape[:axis] + [2, count, shape[axis] // (2 * count)] + shape[axis + 1 :]
+    got = lax.all_to_all(x.reshape(split), "xx", axis + 1, axis + 1, tiled=True)
+    part = jnp.sum(got.astype(jnp.float32), axis=axis + 1)
+    half = lax.axis_index("zh")
+    mine = jnp.take(part, half, axis=axis)
+    theirs = swap_halves(jnp.take(part, 1 - half, axis=axis))
+    return mine + theirs
 
 
 def on_device(
@@ -104,17 +133,14 @@
     ]
     widths = [p.shape[1] for p in pieces]
     offsets = [sum(widths[:i]) for i in range(len(widths) + 1)]
-    across = lax.all_gather(jnp.concatenate(pieces, axis=1), ("ry", "page"), axis=0, tiled=True)
-    chips = lax.axis_size("ry")
-    across = across.reshape(chips, -1, across.shape[1])
-    full = lax.all_gather(across, "rc", axis=1, tiled=True).reshape(-1, across.shape[2])
+    full = lax.all_gather(jnp.concatenate(pieces, axis=1), ROWPAGE, axis=0, tiled=True)
     qkv_w = full[:, offsets[0] : offsets[2]]
     out_t = full[:, offsets[2] : offsets[3]]
     gateup_w = full[:, offsets[3] : offsets[4]]
     down_t = full[:, offsets[4] : offsets[5]]
 
     prompt_count, seq_len, local_feat = tokens.shape
-    gathered = gather_a2a(tokens, COL, 2)
+    gathered = gather_col(tokens, 2)
     model_width = gathered.shape[2]
     attn_in = normalize(gathered.astype(jnp.float32), attn_gain).astype(jnp.bfloat16)
     projected = jnp.dot(
@@ -136,16 +162,16 @@
     )
     attn_terms = contract_rows(attended.reshape(-1, local_width), out_t)
     attn_terms = attn_terms.reshape(prompt_count, seq_len, model_width).astype(jnp.bfloat16)
-    attn_sum = scatter_sum_a2a(attn_terms, COL, 2)
+    attn_sum = scatter_sum_col(attn_terms, 2)
     residual = (tokens.astype(jnp.float32) + attn_sum).astype(jnp.bfloat16)
-    residual_all = gather_a2a(residual, COL, 2)
+    residual_all = gather_col(residual, 2)
     ffn_in = normalize(residual_all.astype(jnp.float32), ffn_gain).astype(jnp.bfloat16)
     gate_up = jnp.dot(
         ffn_in.reshape(-1, model_width), gateup_w, preferred_element_type=jnp.float32
     )
     hidden = (jax.nn.silu(gate_up[:, :unit_count]) * gate_up[:, unit_count:]).astype(jnp.bfloat16)
     ffn_terms = contract_rows(hidden, down_t).reshape(prompt_count, seq_len, model_width)
-    ffn_sum = scatter_sum_a2a(ffn_terms.astype(jnp.bfloat16), COL, 2)
+    ffn_sum = scatter_sum_col(ffn_terms.astype(jnp.bfloat16), 2)
     layer_out = (residual.astype(jnp.float32) + ffn_sum).astype(jnp.bfloat16)
     page_count = lax.axis_size("page")
     page_index = lax.axis_index("page")

time: 383 us -> 329 us (0.86)
  waiting for transfers between devices: 228 us -> 167 us
  blocking collectives: 52.3 us -> 23.1 us
  local copies, waits for them, and re-layouts: 17.3 us -> 33.6 us
  starting transfers between devices: 43.1 us -> 54.9 us
  other arithmetic: 11.9 us -> 17.8 us
    all_gather x2 -> x1, waiting for transfers between devices: 113 us -> 48 us  [on_device(): lax.all_gather(jnp.concatenate(pieces, axis=1), ROWPAGE, axis=0, tiled=True)]
    all_to_all x3, waiting for transfers between devices: 115 us -> 69.5 us  [the longest x2 46.4 us: scatter_sum_col(): got = lax.all_to_all(x.reshape(split), 'xx', axis + 1, axis + 1, tiled=True)]
    ppermute x0 -> x4, waiting for transfers between devices: none -> 30.9 us  [swap_halves(): return lax.ppermute(x, 'zh', [(0, 1), (1, 0)])]
    all_to_all x1, blocking collectives: 52.3 us -> 23.1 us  [gather_col(): got = lax.all_to_all(copies, 'xx', 0, 0, tiled=True)]
    ppermute x0 -> x4, starting transfers between devices: none -> 26.2 us  [swap_halves(): return lax.ppermute(x, 'zh', [(0, 1), (1, 0)])]
    all_to_all x1, waiting for transfers between devices: 0.01 us -> 18.8 us  [on_device(): lax.all_to_all(outgoing, 'page', split_axis=1, concat_axis=1, tiled=True)]
    reshape x2 -> x4, local copies, waits for them, and re-layouts: 2.19 us -> 13.6 us  [scatter_sum_col(): got = lax.all_to_all(x.reshape(split), 'xx', axis + 1, axis + 1, tiled=True)]
    all_to_all x1, starting transfers between devices: 26 us -> 16.3 us  [on_device(): lax.all_to_all(outgoing, 'page', split_axis=1, concat_axis=1, tiled=True)]
  transfers between devices with their start and end apart: 6 -> 9, of which waited for: 4 -> 8; matrix products, arithmetic and copies ran while one was open for 6% -> 4% of each run, Pallas kernels for 0% -> 0%
where the time goes in v5:
time: 329 us; the launch traced here: 327 us
  waiting for transfers between devices  167 us (51%)
  starting transfers between devices  54.9 us (17%)
  local copies, waits for them, and re-layouts  33.6 us (10%)
  blocking collectives  23.1 us (7%)
  other arithmetic  17.8 us (5%)
  matrix products  15.5 us (5%)
  between operations  15.2 us (5%)
    all_gather x1, waiting for transfers between devices, on_device(): lax.all_gather(jnp.concatenate(pieces, axis=1), ROWPAGE, axis=0, tiled=True)  48 us
    all_to_all x2, waiting for transfers between devices, scatter_sum_col(): got = lax.all_to_all(x.reshape(split), 'xx', axis + 1, axis + 1, tiled=True)  46.4 us
    ppermute x4, waiting for transfers between devices, swap_halves(): return lax.ppermute(x, 'zh', [(0, 1), (1, 0)])  30.9 us
    ppermute x4, starting transfers between devices, swap_halves(): return lax.ppermute(x, 'zh', [(0, 1), (1, 0)])  26.2 us
    all_to_all x1, blocking collectives, gather_col(): got = lax.all_to_all(copies, 'xx', 0, 0, tiled=True)  23.1 us
    all_to_all x1, waiting for transfers between devices, gather_col(): got = lax.all_to_all(copies, 'xx', 0, 0, tiled=True)  23.1 us
    all_to_all x1, waiting for transfers between devices, on_device(): lax.all_to_all(outgoing, 'page', split_axis=1, concat_axis=1, tiled=True)  18.8 us
    all_to_all x1, starting transfers between devices, on_device(): lax.all_to_all(outgoing, 'page', split_axis=1, concat_axis=1, tiled=True)  16.3 us
  transfers between devices with their start and end apart: 9, of which 8 were waited for; matrix products, arithmetic and copies ran while one was open for 4% of the time, Pallas kernels for 0%

profile of v5, /device:TPU:8, one launch (start us, length us, event | category | flops | bytes accessed | tf_op | source)
XLA Modules:
  0.0 327.2 jit_solution(3403428301754597284)
XLA Ops:
  7.3 0.8 copy-done
  8.3 1.0 convert_bitcast_fusion
  9.3 0.8 convert_dynamic-update-slice_fusion
  10.1 0.8 bitcast_dynamic-update-slice_fusion.1
  10.9 0.9 bitcast_dynamic-update-slice_fusion
  11.8 0.7 copy-done.5
  12.5 7.3 %collective-permute-start = (bf16[1,512,256]{2,1,0:T(8,128)(2,1)}, bf16[1,512,256]{2,1,0:T(8,128)(2,1)S(1)}, u32[]{:S(2)}, u32[]{:S(2)}) collective-permute-start(bf16[1,512,256]{2,1,0:T(8,128)(2,1)} %param.14), channel_id=1, source_target_pairs={{0,16},{16,0},{1,17},{17,1},{2,18},{18,2},{3,19},{19,3},{4,20},{20... | collective-permute-start | bytes 786440 | tf_op jit(solution)/shard_map/ppermute | solution.py:74
  19.8 7.7 %collective-permute-done = bf16[1,512,256]{2,1,0:T(8,128)(2,1)S(1)} collective-permute-done((bf16[1,512,256]{2,1,0:T(8,128)(2,1)}, bf16[1,512,256]{2,1,0:T(8,128)(2,1)S(1)}, u32[]{:S(2)}, u32[]{:S(2)}) %collective-permute-start) | collective-permute-done | bytes 262176 | tf_op jit(solution)/shard_map/ppermute | solution.py:74
  27.6 0.5 copy.118
  28.1 2.4 broadcast_in_dim.58
  30.5 4.4 %all-to-all-start = ((bf16[4,2,1,512,256]{4,1,3,2,0:T(2,128)(2,1)}), bf16[4,2,1,512,256]{4,1,3,2,0:T(2,128)(2,1)S(1)}, u32[]{:S(2)}, u32[]{:S(2)}) async-start(bf16[4,2,1,512,256]{4,1,3,2,0:T(2,128)(2,1)} %broadcast_in_dim.58), calls=%async_computation | async-start | bytes 4194304 | tf_op jit(solution)/shard_map/all_to_all | solution.py:83
  35.6 1.0 fusion.34
  36.6 0.8 fusion.9
  37.4 23.1 %all-to-all-done = bf16[4,2,1,512,256]{4,1,3,2,0:T(2,128)(2,1)S(1)} async-done(((bf16[4,2,1,512,256]{4,1,3,2,0:T(2,128)(2,1)}), bf16[4,2,1,512,256]{4,1,3,2,0:T(2,128)(2,1)S(1)}, u32[]{:S(2)}, u32[]{:S(2)}) %all-to-all-start) | async-done | bytes 2097184 | tf_op jit(solution)/shard_map/all_to_all | solution.py:83
  60.5 0.4 copy_convert_fusion.1
  61.0 0.4 multiply_reduce_fusion.1
  61.3 0.5 fusion.5
  61.8 2.4 copy.120
  64.2 48.0 %all-gather.2.cloned.1.call-done = bf16[2048,2304]{1,0:T(8,128)(2,1)} async-done(((bf16[64,2304]{1,0:T(8,128)(2,1)}), bf16[2048,2304]{1,0:T(8,128)(2,1)}) %all-gather.2.cloned.1.call-update) | async-done | bytes 9437200 | tf_op jit(solution)/shard_map/all_gather | solution.py:136
  112.1 1.3 slice_bitcast_fusion
  113.4 1.4 copy.123
  114.9 2.0 convolution_bitcast_fusion
  117.1 0.3 fusion.37
  117.6 0.2 copy-done.6
  117.8 0.7 fusion.6
  118.6 0.7 fusion.8
  119.3 1.8 convolution_convert_fusion
  121.1 2.7 reshape.442
  123.8 4.6 %copy.126 = bf16[1,512,2,4,256]{4,2,1,0,3:T(2,128)(2,1)} copy(bf16[1,512,2,4,256]{4,3,2,1,0:T(4,128)(2,1)} %reshape.442) | data formatting | bytes 4194304 | tf_op jit(solution)/shard_map/reshape | solution.py:94
  128.4 4.2 %all-to-all-start.1 = ((bf16[1,512,2,4,256]{4,2,1,0,3:T(2,128)(2,1)}), bf16[1,512,2,4,256]{4,2,1,0,3:T(2,128)(2,1)S(1)}, u32[]{:S(2)}, u32[]{:S(2)}) async-start(bf16[1,512,2,4,256]{4,2,1,0,3:T(2,128)(2,1)} %copy.126), calls=%async_computation.1 | async-start | bytes 4194304 | tf_op jit(solution)/shard_map/all_to_all | solution.py:94
  132.6 27.0 %all-to-all-done.1 = bf16[1,512,2,4,256]{4,2,1,0,3:T(2,128)(2,1)S(1)} async-done(((bf16[1,512,2,4,256]{4,2,1,0,3:T(2,128)(2,1)}), bf16[1,512,2,4,256]{4,2,1,0,3:T(2,128)(2,1)S(1)}, u32[]{:S(2)}, u32[]{:S(2)}) %all-to-all-start.1) | async-done | bytes 2097184 | tf_op jit(solution)/shard_map/all_to_all | solution.py:94
  159.6 0.2 convert_reduce_fusion.1
  159.8 0.8 copy.172
  160.6 0.5 fusion.18
  161.2 5.0 %collective-permute-start.1 = (f32[1,512,256]{2,0,1:T(1,128)S(1)}, f32[1,512,256]{2,0,1:T(1,128)S(1)}, u32[]{:S(2)}, u32[]{:S(2)}) collective-permute-start(f32[1,512,256]{2,0,1:T(1,128)S(1)} %fusion.18), channel_id=1, source_target_pairs={{0,16},{16,0},{1,17},{17,1},{2,18},{18,2},{3,19},{19,3},{4,20},{20... | collective-permute-start | bytes 1572872 | tf_op jit(solution)/shard_map/ppermute | solution.py:74
  166.2 14.8 %collective-permute-done.1 = f32[1,512,256]{2,0,1:T(1,128)S(1)} collective-permute-done((f32[1,512,256]{2,0,1:T(1,128)S(1)}, f32[1,512,256]{2,0,1:T(1,128)S(1)}, u32[]{:S(2)}, u32[]{:S(2)}) %collective-permute-start.1) | collective-permute-done | bytes 524320 | tf_op jit(solution)/shard_map/ppermute | solution.py:74
  180.9 0.9 fusion.21
  181.9 13.9 %collective-permute-start.2 = (bf16[1,512,256]{2,1,0:T(8,128)(2,1)S(1)}, bf16[1,512,256]{2,1,0:T(8,128)(2,1)S(1)}, u32[]{:S(2)}, u32[]{:S(2)}) collective-permute-start(bf16[1,512,256]{2,1,0:T(8,128)(2,1)S(1)} %copy.131), channel_id=1, source_target_pairs={{0,16},{16,0},{1,17},{17,1},{2,18},{18,2},{3,19},{19,3},{4,20},{20... | collective-permute-start | bytes 786440 | tf_op jit(solution)/shard_map/ppermute | solution.py:74
  195.8 8.5 %collective-permute-done.2 = bf16[1,512,256]{2,1,0:T(8,128)(2,1)S(1)} collective-permute-done((bf16[1,512,256]{2,1,0:T(8,128)(2,1)S(1)}, bf16[1,512,256]{2,1,0:T(8,128)(2,1)S(1)}, u32[]{:S(2)}, u32[]{:S(2)}) %collective-permute-start.2) | collective-permute-done | bytes 262176 | tf_op jit(solution)/shard_map/ppermute | solution.py:74
  204.2 0.8 broadcast_select_fusion
  205.1 0.1 broadcast_in_dim.64
  205.3 23.1 %all_to_all.25 = bf16[4,2,1,512,256]{4,3,1,2,0:T(8,128)(2,1)S(1)} all-to-all(bf16[4,2,1,512,256]{4,3,1,2,0:T(8,128)(2,1)S(1)} %broadcast_in_dim.64), channel_id=1, replica_groups=mesh['ry'=4,'rc'=2,'zh'=2,'xx'=4,'page'=4] {'xx'}, dimensions={0} | all-to-all | bytes 4194304 | tf_op jit(solution)/shard_map/all_to_all | solution.py:83
  228.4 0.5 multiply_reduce_fusion
  228.9 2.4 copy_convert_fusion
  231.4 5.4 %copy.135 = f32[1,512,8,256]{1,3,2,0:T(8,128)} copy(f32[1,512,8,256]{3,1,2,0:T(8,128)} %bitcast.118) | data formatting | bytes 8388608 | tf_op jit(solution)/shard_map/convert_element_type | solution.py:168
  236.7 2.6 fusion.3
  239.3 5.4 %fusion = f32[512,1280]{1,0:T(8,128)S(1)} fusion(bf16[512,2048]{0,1:T(8,128)(2,1)S(1)} %fusion.3, bf16[2048,2304]{1,0:T(8,128)(2,1)} %all-gather.2.cloned.1.call-done), kind=kOutput, calls=%fused_computation.2 | convolution fusion | flops 2684354560 | bytes 9961472 | tf_op jit(solution)/shard_map/dot_general | solution.py:169
  244.8 4.9 %convolution_convert_fusion.1 = bf16[512,2048]{1,0:T(8,128)(2,1)} fusion(bf16[2048,2304]{1,0:T(8,128)(2,1)} %all-gather.2.cloned.1.call-done, f32[512,1280]{1,0:T(8,128)S(1)} %fusion), kind=kOutput, calls=%fused_computation.13 | convolution fusion | flops 1345191936 | bytes 7340032 | tf_op jit(solution)/shard_map/dot_general | solution.py:50
  249.7 3.3 %reshape.443 = bf16[1,512,2,4,256]{4,3,2,1,0:T(4,128)(2,1)S(1)} reshape(bf16[512,2048]{1,0:T(8,128)(2,1)} %convolution_convert_fusion.1) | data formatting | bytes 4194304 | tf_op jit(solution)/shard_map/reshape | solution.py:94
  253.0 3.0 copy.136
  255.9 3.7 %all-to-all-start.3 = ((bf16[1,512,2,4,256]{4,2,1,0,3:T(2,128)(2,1)}), bf16[1,512,2,4,256]{4,2,1,0,3:T(2,128)(2,1)S(1)}, u32[]{:S(2)}, u32[]{:S(2)}) async-start(bf16[1,512,2,4,256]{4,2,1,0,3:T(2,128)(2,1)} %copy.136), calls=%async_computation.3 | async-start | bytes 4194304 | tf_op jit(solution)/shard_map/all_to_all | solution.py:94
  259.7 0.2 convert_reduce_fusion.2
  260.1 19.4 %all-to-all-done.3 = bf16[1,512,2,4,256]{4,2,1,0,3:T(2,128)(2,1)S(1)} async-done(((bf16[1,512,2,4,256]{4,2,1,0,3:T(2,128)(2,1)}), bf16[1,512,2,4,256]{4,2,1,0,3:T(2,128)(2,1)S(1)}, u32[]{:S(2)}, u32[]{:S(2)}) %all-to-all-start.3) | async-done | bytes 2097184 | tf_op jit(solution)/shard_map/all_to_all | solution.py:94
  279.4 0.2 convert_reduce_fusion
  279.7 0.5 fusion.19
  280.5 0.2 maximum_bitcast_fusion.2
  280.7 0.2 copy.139
  281.0 0.8 scatter_fusion
  281.7 0.7 copy.140
  282.5 16.3 %all-to-all-start.4 = ((bf16[2,4,128,128]{3,2,0,1:T(8,128)(2,1)}), bf16[2,4,128,128]{3,2,0,1:T(8,128)(2,1)S(1)}, u32[]{:S(2)}, u32[]{:S(2)}) async-start(bf16[2,4,128,128]{3,2,0,1:T(8,128)(2,1)} %copy.140), calls=%async_computation.4 | async-start | bytes 524288 | tf_op jit(solution)/shard_map/all_to_all | solution.py:200
  298.9 18.8 %all-to-all-done.4 = bf16[2,4,128,128]{3,2,0,1:T(8,128)(2,1)S(1)} async-done(((bf16[2,4,128,128]{3,2,0,1:T(8,128)(2,1)}), bf16[2,4,128,128]{3,2,0,1:T(8,128)(2,1)S(1)}, u32[]{:S(2)}, u32[]{:S(2)}) %all-to-all-start.4) | async-done | bytes 262176 | tf_op jit(solution)/shard_map/all_to_all | solution.py:200
  317.7 0.8 scatter_fusion.1
  318.5 1.1 fusion.22
  319.6 0.7 copy.141
  (69 shorter events, 1.6 us)
Async XLA Ops:
  7.2 0.9 copy-start
  7.2 20.3 %copy-start.3 = (bf16[1,512,256]{2,1,0:T(8,128)(2,1)S(1)}, bf16[1,512,256]{2,1,0:T(8,128)(2,1)}, u32[]{:S(2)}) copy-start(bf16[1,512,256]{2,1,0:T(8,128)(2,1)} %param.14) | copy-start | bytes 786436
  7.2 105.0 %all-gather.2.cloned.1.call-start = ((), (), s32[]{:S(2)}) async-start(), calls=%async_computation.5 | async-start | bytes 9732096 | tf_op jit(solution)/shard_map/all_gather | solution.py:136
  11.8 0.7 copy-start.5
  12.5 14.9 %collective-permute-start = (bf16[1,512,256]{2,1,0:T(8,128)(2,1)}, bf16[1,512,256]{2,1,0:T(8,128)(2,1)S(1)}, u32[]{:S(2)}, u32[]{:S(2)}) collective-permute-start(bf16[1,512,256]{2,1,0:T(8,128)(2,1)} %param.14), channel_id=1, source_target_pairs={{0,16},{16,0},{1,17},{17,1},{2,18},{18,2},{3,19},{19,3},{4,20},{20... | collective-permute-start | bytes 786440 | tf_op jit(solution)/shard_map/ppermute | solution.py:74
  30.5 5.1 %copy-start.10 = (f32[2048]{0:T(1024)S(1)}, f32[2048]{0:T(1024)}, u32[]{:S(2)}) copy-start(f32[2048]{0:T(1024)} %param.22) | copy-start | bytes 24580
  30.5 30.0 %all-to-all-start = ((bf16[4,2,1,512,256]{4,1,3,2,0:T(2,128)(2,1)}), bf16[4,2,1,512,256]{4,1,3,2,0:T(2,128)(2,1)S(1)}, u32[]{:S(2)}, u32[]{:S(2)}) async-start(bf16[4,2,1,512,256]{4,1,3,2,0:T(2,128)(2,1)} %broadcast_in_dim.58), calls=%async_computation | async-start | bytes 4194304 | tf_op jit(solution)/shard_map/all_to_all | solution.py:83
  64.2 50.7 %copy-start.2 = (bf16[1,512,8,256]{1,3,2,0:T(8,128)(2,1)S(1)}, bf16[1,512,8,256]{1,3,2,0:T(8,128)(2,1)}, u32[]{:S(2)}) copy-start(bf16[1,512,8,256]{1,3,2,0:T(8,128)(2,1)} %copy.120) | copy-start | bytes 6291460
  114.9 2.1 copy-start.12
  114.9 2.6 copy-start.13
  114.9 2.7 copy-start.7
  114.9 2.7 copy-start.8
  116.9 1.0 copy-start.6
  128.4 31.2 %all-to-all-start.1 = ((bf16[1,512,2,4,256]{4,2,1,0,3:T(2,128)(2,1)}), bf16[1,512,2,4,256]{4,2,1,0,3:T(2,128)(2,1)S(1)}, u32[]{:S(2)}, u32[]{:S(2)}) async-start(bf16[1,512,2,4,256]{4,2,1,0,3:T(2,128)(2,1)} %copy.126), calls=%async_computation.1 | async-start | bytes 4194304 | tf_op jit(solution)/shard_map/all_to_all | solution.py:94
  161.2 19.7 %collective-permute-start.1 = (f32[1,512,256]{2,0,1:T(1,128)S(1)}, f32[1,512,256]{2,0,1:T(1,128)S(1)}, u32[]{:S(2)}, u32[]{:S(2)}) collective-permute-start(f32[1,512,256]{2,0,1:T(1,128)S(1)} %fusion.18), channel_id=1, source_target_pairs={{0,16},{16,0},{1,17},{17,1},{2,18},{18,2},{3,19},{19,3},{4,20},{20... | collective-permute-start | bytes 1572872 | tf_op jit(solution)/shard_map/ppermute | solution.py:74
  181.9 22.3 %collective-permute-start.2 = (bf16[1,512,256]{2,1,0:T(8,128)(2,1)S(1)}, bf16[1,512,256]{2,1,0:T(8,128)(2,1)S(1)}, u32[]{:S(2)}, u32[]{:S(2)}) collective-permute-start(bf16[1,512,256]{2,1,0:T(8,128)(2,1)S(1)} %copy.131), channel_id=1, source_target_pairs={{0,16},{16,0},{1,17},{17,1},{2,18},{18,2},{3,19},{19,3},{4,20},{20... | collective-permute-start | bytes 786440 | tf_op jit(solution)/shard_map/ppermute | solution.py:74
  231.4 5.4 %copy-start.9 = (f32[2048]{0:T(1024)S(1)}, f32[2048]{0:T(1024)}, u32[]{:S(2)}) copy-start(f32[2048]{0:T(1024)} %param.23) | copy-start | bytes 24580
  255.9 3.8 %copy-start.11 = (s32[4,4]{1,0:T(4,128)S(1)}, s32[4,4]{1,0:T(4,128)}, u32[]{:S(2)}) copy-start(s32[4,4]{1,0:T(4,128)} %param.16) | copy-start | bytes 196
  255.9 23.5 %all-to-all-start.3 = ((bf16[1,512,2,4,256]{4,2,1,0,3:T(2,128)(2,1)}), bf16[1,512,2,4,256]{4,2,1,0,3:T(2,128)(2,1)S(1)}, u32[]{:S(2)}, u32[]{:S(2)}) async-start(bf16[1,512,2,4,256]{4,2,1,0,3:T(2,128)(2,1)} %copy.136), calls=%async_computation.3 | async-start | bytes 4194304 | tf_op jit(solution)/shard_map/all_to_all | solution.py:94
  280.3 38.2 %collective-permute-start.3 = (f32[1,512,256]{2,0,1:T(1,128)S(1)}, f32[1,512,256]{2,0,1:T(1,128)S(1)}, u32[]{:S(2)}, u32[]{:S(2)}) collective-permute-start(f32[1,512,256]{2,0,1:T(1,128)S(1)} %fusion.19), channel_id=1, source_target_pairs={{0,16},{16,0},{1,17},{17,1},{2,18},{18,2},{3,19},{19,3},{4,20},{20... | collective-permute-start | bytes 1572872 | tf_op jit(solution)/shard_map/ppermute | solution.py:74
  282.5 35.2 %all-to-all-start.4 = ((bf16[2,4,128,128]{3,2,0,1:T(8,128)(2,1)}), bf16[2,4,128,128]{3,2,0,1:T(8,128)(2,1)S(1)}, u32[]{:S(2)}, u32[]{:S(2)}) async-start(bf16[2,4,128,128]{3,2,0,1:T(8,128)(2,1)} %copy.140), calls=%async_computation.4 | async-start | bytes 524288 | tf_op jit(solution)/shard_map/all_to_all | solution.py:200
  298.8 21.6 %copy-start.1 = (f32[2,64,256]{2,1,0:T(8,128)S(1)}, f32[2,64,256]{2,1,0:T(8,128)}, u32[]{:S(2)}) copy-start(f32[2,64,256]{2,1,0:T(8,128)} %param.18) | copy-start | bytes 393220
  318.5 1.9 copy-start.4
Sparse Core Ops, SparseCore 0:
  12.7 99.4 all-gather.1

commit v6 on v5

--- a/solution.py
+++ b/solution.py
@@ -97,6 +97,18 @@
     mine = jnp.take(part, half, axis=axis)
     theirs = swap_halves(jnp.take(part, 1 - half, axis=axis))
     return mine + theirs
+
+
+def gather_rows(x):
+    pages = lax.axis_size("page")
+    got = lax.all_to_all(jnp.broadcast_to(x[None], (pages,) + x.shape), "page", 0, 0, tiled=True)
+    got = got.reshape((-1,) + x.shape[1:])
+    chips = lax.axis_size("ry")
+    got = lax.all_to_all(jnp.broadcast_to(got[None], (chips,) + got.shape), "ry", 0, 0, tiled=True)
+    cores = lax.axis_size("rc")
+    got = jnp.broadcast_to(got[:, None], (chips, cores) + got.shape[1:])
+    got = lax.all_to_all(got, "rc", 1, 1, tiled=True)
+    return got.reshape((-1,) + x.shape[1:])
 
 
 def on_device(
@@ -133,7 +145,7 @@
     ]
     widths = [p.shape[1] for p in pieces]
     offsets = [sum(widths[:i]) for i in range(len(widths) + 1)]
-    full = lax.all_gather(jnp.concatenate(pieces, axis=1), ROWPAGE, axis=0, tiled=True)
+    full = gather_rows(jnp.concatenate(pieces, axis=1))
     qkv_w = full[:, offsets[0] : offsets[2]]
     out_t = full[:, offsets[2] : offsets[3]]
     gateup_w = full[:, offsets[3] : offsets[4]]

time: 329 us -> 400 us (1.22)
  local copies, waits for them, and re-layouts: 33.6 us -> 75.5 us
  waiting for transfers between devices: 167 us -> 203 us
  blocking collectives: 23.1 us -> 41.7 us
  between operations: 15.2 us -> 1.83 us
  starting transfers between devices: 54.9 us -> 42.4 us
    all_to_all x0 -> x2, waiting for transfers between devices: none -> 49.4 us  [the longest x1 46.1 us: gather_rows(): lax.all_to_all(jnp.broadcast_to(got[None], (chips,) + got.shape), 'ry', 0...]
    all_gather x1 -> x0, waiting for transfers between devices: 48 us -> none  [on_device(): lax.all_gather(jnp.concatenate(pieces, axis=1), ROWPAGE, axis=0, tiled=True)]
    all_to_all x0 -> x2, local copies, waits for them, and re-layouts: none -> 34.3 us  [the longest x1 18.9 us: gather_rows(): lax.all_to_all(jnp.broadcast_to(got[None], (chips,) + got.shape), 'ry', 0...]
    ppermute x4, waiting for transfers between devices: 30.9 us -> 64.3 us  [swap_halves(): return lax.ppermute(x, 'zh', [(0, 1), (1, 0)])]
    all_to_all x1, starting transfers between devices: 16.3 us -> 3.41 us  [on_device(): lax.all_to_all(outgoing, 'page', split_axis=1, concat_axis=1, tiled=True)]
    all_to_all x0 -> x1, blocking collectives: none -> 12.8 us  [gather_rows(): got = lax.all_to_all(got, 'rc', 1, 1, tiled=True)]
    all_to_all x0 -> x2, starting transfers between devices: none -> 11.4 us  [the longest x1 5.89 us: gather_rows(): lax.all_to_all(jnp.broadcast_to(x[None], (pages,) + x.shape), 'page', 0,...]
    ppermute x4, starting transfers between devices: 26.2 us -> 16 us  [swap_halves(): return lax.ppermute(x, 'zh', [(0, 1), (1, 0)])]
  transfers between devices with their start and end apart: 9 -> 10, of which waited for: 8 -> 9; matrix products, arithmetic and copies ran while one was open for 4% -> 3% of each run, Pallas kernels for 0% -> 0%
where the time goes in v6:
time: 400 us; the launch traced here: 397 us
  waiting for transfers between devices  203 us (51%)
  local copies, waits for them, and re-layouts  75.5 us (19%)
  starting transfers between devices  42.4 us (11%)
  blocking collectives  41.7 us (10%)
  other arithmetic  17.2 us (4%)
  matrix products  15.5 us (4%)
    ppermute x4, waiting for transfers between devices, swap_halves(): return lax.ppermute(x, 'zh', [(0, 1), (1, 0)])  64.3 us
    all_to_all x2, waiting for transfers between devices, scatter_sum_col(): got = lax.all_to_all(x.reshape(split), 'xx', axis + 1, axis + 1, tiled=True)  51.9 us
    all_to_all x1, waiting for transfers between devices, gather_rows(): lax.all_to_all(jnp.broadcast_to(got[None], (chips,) + got.shape), 'ry', 0...  46.1 us
    all_to_all x1, blocking collectives, gather_col(): got = lax.all_to_all(copies, 'xx', 0, 0, tiled=True)  28.8 us
    all_to_all x1, waiting for transfers between devices, gather_col(): got = lax.all_to_all(copies, 'xx', 0, 0, tiled=True)  24.2 us
    all_to_all x1, local copies, waits for them, and re-layouts, gather_rows(): lax.all_to_all(jnp.broadcast_to(got[None], (chips,) + got.shape), 'ry', 0...  18.9 us
    ppermute x4, starting transfers between devices, swap_halves(): return lax.ppermute(x, 'zh', [(0, 1), (1, 0)])  16 us
    all_to_all x1, local copies, waits for them, and re-layouts, gather_rows(): got = lax.all_to_all(got, 'rc', 1, 1, tiled=True)  15.4 us
  transfers between devices with their start and end apart: 10, of which 9 were waited for; matrix products, arithmetic and copies ran while one was open for 3% of the time, Pallas kernels for 0%

profile of v6, /device:TPU:8, one launch (start us, length us, event | category | flops | bytes accessed | tf_op | source)
XLA Modules:
  0.0 396.8 jit_solution(16925754695431232132)
XLA Ops:
  0.7 0.8 convert_dynamic-update-slice_fusion
  1.8 1.0 convert_bitcast_fusion
  2.8 0.8 bitcast_dynamic-update-slice_fusion.1
  3.6 1.0 bitcast_dynamic-update-slice_fusion
  4.6 1.1 broadcast_in_dim.67
  5.7 5.9 %all-to-all-start.1 = ((bf16[4,64,2304]{2,1,0:T(8,128)(2,1)}), bf16[4,64,2304]{2,1,0:T(8,128)(2,1)S(1)}, u32[]{:S(2)}, u32[]{:S(2)}) async-start(bf16[4,64,2304]{2,1,0:T(8,128)(2,1)} %broadcast_in_dim.67), calls=%async_computation.1 | async-start | bytes 2359296 | tf_op jit(solution)/shard_map/all_to_all | solution.py:104
  11.6 4.9 %collective-permute-start = (bf16[1,512,256]{2,1,0:T(8,128)(2,1)S(1)}, bf16[1,512,256]{2,1,0:T(8,128)(2,1)S(1)}, u32[]{:S(2)}, u32[]{:S(2)}) collective-permute-start(bf16[1,512,256]{2,1,0:T(8,128)(2,1)S(1)} %copy-done.3), channel_id=1, source_target_pairs={{0,16},{16,0},{1,17},{17,1},{2,18},{18,2},{3,19},{19,3},{4,20},{20... | collective-permute-start | bytes 786440 | tf_op jit(solution)/shard_map/ppermute | solution.py:74
  16.5 31.0 %collective-permute-done = bf16[1,512,256]{2,1,0:T(8,128)(2,1)S(1)} collective-permute-done((bf16[1,512,256]{2,1,0:T(8,128)(2,1)S(1)}, bf16[1,512,256]{2,1,0:T(8,128)(2,1)S(1)}, u32[]{:S(2)}, u32[]{:S(2)}) %collective-permute-start) | collective-permute-done | bytes 262176 | tf_op jit(solution)/shard_map/ppermute | solution.py:74
  47.6 0.5 copy.128
  48.1 3.2 all-to-all-done.1
  51.3 2.4 broadcast_in_dim.66
  53.8 4.3 %all-to-all-start = ((bf16[4,2,1,512,256]{4,1,3,2,0:T(2,128)(2,1)}), bf16[4,2,1,512,256]{4,1,3,2,0:T(2,128)(2,1)S(1)}, u32[]{:S(2)}, u32[]{:S(2)}) async-start(bf16[4,2,1,512,256]{4,1,3,2,0:T(2,128)(2,1)} %broadcast_in_dim.66), calls=%async_computation | async-start | bytes 4194304 | tf_op jit(solution)/shard_map/all_to_all | solution.py:83
  58.1 1.5 copy.133
  59.5 24.2 %all-to-all-done = bf16[4,2,1,512,256]{4,1,3,2,0:T(2,128)(2,1)S(1)} async-done(((bf16[4,2,1,512,256]{4,1,3,2,0:T(2,128)(2,1)}), bf16[4,2,1,512,256]{4,1,3,2,0:T(2,128)(2,1)S(1)}, u32[]{:S(2)}, u32[]{:S(2)}) %all-to-all-start) | async-done | bytes 2097184 | tf_op jit(solution)/shard_map/all_to_all | solution.py:83
  83.7 3.7 broadcast_in_dim.69
  87.4 5.5 %all-to-all-start.2 = ((bf16[4,256,2304]{1,2,0:T(8,128)(2,1)}), bf16[4,256,2304]{1,2,0:T(8,128)(2,1)}, u32[]{:S(2)}, u32[]{:S(2)}) async-start(bf16[4,256,2304]{1,2,0:T(8,128)(2,1)} %broadcast_in_dim.69), calls=%async_computation.2 | async-start | bytes 9437184 | tf_op jit(solution)/shard_map/all_to_all | solution.py:107
  93.6 1.0 fusion.34
  94.7 0.4 copy_convert_fusion.1
  95.1 0.4 multiply_reduce_fusion.1
  95.5 0.5 fusion.5
  95.9 2.4 copy.130
  98.4 46.1 %all-to-all-done.2 = bf16[4,256,2304]{1,2,0:T(8,128)(2,1)} async-done(((bf16[4,256,2304]{1,2,0:T(8,128)(2,1)}), bf16[4,256,2304]{1,2,0:T(8,128)(2,1)}, u32[]{:S(2)}, u32[]{:S(2)}) %all-to-all-start.2) | async-done | bytes 4718624 | tf_op jit(solution)/shard_map/all_to_all | solution.py:107
  144.5 18.9 %copy.134 = bf16[4,256,2304]{1,0,2:T(4,128)(2,1)S(1)} copy(bf16[4,256,2304]{1,2,0:T(8,128)(2,1)} %all-to-all-done.2) | data formatting | bytes 9437184 | tf_op jit(solution)/shard_map/all_to_all | solution.py:107
  163.4 2.6 broadcast_in_dim.70
  166.1 12.8 %all_to_all.40 = bf16[4,2,256,2304]{2,0,3,1:T(4,128)(2,1)} all-to-all(bf16[4,2,256,2304]{2,0,3,1:T(4,128)(2,1)S(1)} %broadcast_in_dim.70), channel_id=1, replica_groups=mesh['ry'=4,'rc'=2,'zh'=2,'xx'=4,'page'=4] {'rc'}, dimensions={1} | all-to-all | bytes 18874368 | tf_op jit(solution)/shard_map/all_to_all | solution.py:110
  178.9 15.4 %copy.135 = bf16[4,2,256,2304]{3,2,1,0:T(8,128)(2,1)} copy(bf16[4,2,256,2304]{2,0,3,1:T(4,128)(2,1)} %all_to_all.40) | data formatting | bytes 18874368 | tf_op jit(solution)/shard_map/all_to_all | solution.py:110
  194.3 1.4 slice_bitcast_fusion
  195.7 1.4 copy.136
  197.2 2.0 convolution_bitcast_fusion
  199.9 0.7 fusion.6
  200.6 0.7 fusion.8
  201.3 1.8 convolution_convert_fusion
  203.1 2.7 reshape.449
  205.8 4.6 %copy.139 = bf16[1,512,2,4,256]{4,2,1,0,3:T(2,128)(2,1)} copy(bf16[1,512,2,4,256]{4,3,2,1,0:T(4,128)(2,1)} %reshape.449) | data formatting | bytes 4194304 | tf_op jit(solution)/shard_map/reshape | solution.py:94
  210.5 3.6 all-to-all-start.4
  214.1 26.9 %all-to-all-done.4 = bf16[1,512,2,4,256]{4,2,1,0,3:T(2,128)(2,1)S(1)} async-done(((bf16[1,512,2,4,256]{4,2,1,0,3:T(2,128)(2,1)}), bf16[1,512,2,4,256]{4,2,1,0,3:T(2,128)(2,1)S(1)}, u32[]{:S(2)}, u32[]{:S(2)}) %all-to-all-start.4) | async-done | bytes 2097184 | tf_op jit(solution)/shard_map/all_to_all | solution.py:94
  241.2 0.8 copy.185
  242.1 0.5 fusion.18
  242.6 5.2 %collective-permute-start.1 = (f32[1,512,256]{2,0,1:T(1,128)S(1)}, f32[1,512,256]{2,0,1:T(1,128)S(1)}, u32[]{:S(2)}, u32[]{:S(2)}) collective-permute-start(f32[1,512,256]{2,0,1:T(1,128)S(1)} %fusion.18), channel_id=1, source_target_pairs={{0,16},{16,0},{1,17},{17,1},{2,18},{18,2},{3,19},{19,3},{4,20},{20... | collective-permute-start | bytes 1572872 | tf_op jit(solution)/shard_map/ppermute | solution.py:74
  247.8 23.5 %collective-permute-done.1 = f32[1,512,256]{2,0,1:T(1,128)S(1)} collective-permute-done((f32[1,512,256]{2,0,1:T(1,128)S(1)}, f32[1,512,256]{2,0,1:T(1,128)S(1)}, u32[]{:S(2)}, u32[]{:S(2)}) %collective-permute-start.1) | collective-permute-done | bytes 524320 | tf_op jit(solution)/shard_map/ppermute | solution.py:74
  271.2 0.9 fusion.21
  272.2 2.8 collective-permute-start.2
  275.0 9.9 %collective-permute-done.2 = bf16[1,512,256]{2,1,0:T(8,128)(2,1)S(1)} collective-permute-done((bf16[1,512,256]{2,1,0:T(8,128)(2,1)S(1)}, bf16[1,512,256]{2,1,0:T(8,128)(2,1)S(1)}, u32[]{:S(2)}, u32[]{:S(2)}) %collective-permute-start.2) | collective-permute-done | bytes 262176 | tf_op jit(solution)/shard_map/ppermute | solution.py:74
  284.9 0.8 broadcast_select_fusion
  285.9 28.8 %all_to_all.41 = bf16[4,2,1,512,256]{4,3,1,2,0:T(8,128)(2,1)S(1)} all-to-all(bf16[4,2,1,512,256]{4,3,1,2,0:T(8,128)(2,1)S(1)} %broadcast_in_dim.79), channel_id=1, replica_groups=mesh['ry'=4,'rc'=2,'zh'=2,'xx'=4,'page'=4] {'xx'}, dimensions={0} | all-to-all | bytes 4194304 | tf_op jit(solution)/shard_map/all_to_all | solution.py:83
  314.8 2.4 copy_convert_fusion
  317.2 5.3 %copy.148 = f32[1,512,8,256]{1,3,2,0:T(8,128)} copy(f32[1,512,8,256]{3,1,2,0:T(8,128)} %bitcast.118) | data formatting | bytes 8388608 | tf_op jit(solution)/shard_map/convert_element_type | solution.py:180
  322.6 0.5 multiply_reduce_fusion
  323.3 2.6 fusion.3
  325.9 5.4 %fusion = f32[512,1280]{1,0:T(8,128)S(1)} fusion(bf16[512,2048]{0,1:T(8,128)(2,1)S(1)} %fusion.3, bf16[2048,2304]{1,0:T(8,128)(2,1)} %bitcast.121), kind=kOutput, calls=%fused_computation.2 | convolution fusion | flops 2684354560 | bytes 9961472 | tf_op jit(solution)/shard_map/dot_general | solution.py:181
  331.3 4.9 %convolution_convert_fusion.1 = bf16[512,2048]{1,0:T(8,128)(2,1)} fusion(bf16[2048,2304]{1,0:T(8,128)(2,1)} %bitcast.122, f32[512,1280]{1,0:T(8,128)S(1)} %fusion), kind=kOutput, calls=%fused_computation.13 | convolution fusion | flops 1345191936 | bytes 7340032 | tf_op jit(solution)/shard_map/dot_general | solution.py:50
  336.2 3.3 reshape.450
  339.5 3.0 copy.149
  342.5 3.7 all-to-all-start.6
  346.6 25.0 %all-to-all-done.6 = bf16[1,512,2,4,256]{4,2,1,0,3:T(2,128)(2,1)S(1)} async-done(((bf16[1,512,2,4,256]{4,2,1,0,3:T(2,128)(2,1)}), bf16[1,512,2,4,256]{4,2,1,0,3:T(2,128)(2,1)S(1)}, u32[]{:S(2)}, u32[]{:S(2)}) %all-to-all-start.6) | async-done | bytes 2097184 | tf_op jit(solution)/shard_map/all_to_all | solution.py:94
  371.9 0.5 fusion.19
  372.5 3.1 collective-permute-start.3
  376.1 0.8 scatter_fusion
  376.9 0.7 copy.153
  377.6 3.4 all-to-all-start.7
  381.2 12.9 %all-to-all-done.7 = bf16[2,4,128,128]{3,2,0,1:T(8,128)(2,1)S(1)} async-done(((bf16[2,4,128,128]{3,2,0,1:T(8,128)(2,1)}), bf16[2,4,128,128]{3,2,0,1:T(8,128)(2,1)S(1)}, u32[]{:S(2)}, u32[]{:S(2)}) %all-to-all-start.7) | async-done | bytes 262176 | tf_op jit(solution)/shard_map/all_to_all | solution.py:212
  394.2 0.8 scatter_fusion.1
  395.0 1.1 fusion.22
  396.1 0.7 copy.154
  (75 shorter events, 3.4 us)
Async XLA Ops:
  0.6 0.9 copy-start
  3.6 8.0 %copy-start.3 = (bf16[1,512,256]{2,1,0:T(8,128)(2,1)S(1)}, bf16[1,512,256]{2,1,0:T(8,128)(2,1)}, u32[]{:S(2)}) copy-start(bf16[1,512,256]{2,1,0:T(8,128)(2,1)} %param.14) | copy-start | bytes 786436
  5.7 45.7 %all-to-all-start.1 = ((bf16[4,64,2304]{2,1,0:T(8,128)(2,1)}), bf16[4,64,2304]{2,1,0:T(8,128)(2,1)S(1)}, u32[]{:S(2)}, u32[]{:S(2)}) async-start(bf16[4,64,2304]{2,1,0:T(8,128)(2,1)} %broadcast_in_dim.67), calls=%async_computation.1 | async-start | bytes 2359296 | tf_op jit(solution)/shard_map/all_to_all | solution.py:104
  11.6 35.9 %collective-permute-start = (bf16[1,512,256]{2,1,0:T(8,128)(2,1)S(1)}, bf16[1,512,256]{2,1,0:T(8,128)(2,1)S(1)}, u32[]{:S(2)}, u32[]{:S(2)}) collective-permute-start(bf16[1,512,256]{2,1,0:T(8,128)(2,1)S(1)} %copy-done.3), channel_id=1, source_target_pairs={{0,16},{16,0},{1,17},{17,1},{2,18},{18,2},{3,19},{19,3},{4,20},{20... | collective-permute-start | bytes 786440 | tf_op jit(solution)/shard_map/ppermute | solution.py:74
  53.8 29.9 %all-to-all-start = ((bf16[4,2,1,512,256]{4,1,3,2,0:T(2,128)(2,1)}), bf16[4,2,1,512,256]{4,1,3,2,0:T(2,128)(2,1)S(1)}, u32[]{:S(2)}, u32[]{:S(2)}) async-start(bf16[4,2,1,512,256]{4,1,3,2,0:T(2,128)(2,1)} %broadcast_in_dim.66), calls=%async_computation | async-start | bytes 4194304 | tf_op jit(solution)/shard_map/all_to_all | solution.py:83
  87.4 6.2 %copy-start.9 = (f32[2048]{0:T(1024)S(1)}, f32[2048]{0:T(1024)}, u32[]{:S(2)}) copy-start(f32[2048]{0:T(1024)} %param.22) | copy-start | bytes 24580
  87.4 57.1 %all-to-all-start.2 = ((bf16[4,256,2304]{1,2,0:T(8,128)(2,1)}), bf16[4,256,2304]{1,2,0:T(8,128)(2,1)}, u32[]{:S(2)}, u32[]{:S(2)}) async-start(bf16[4,256,2304]{1,2,0:T(8,128)(2,1)} %broadcast_in_dim.69), calls=%async_computation.2 | async-start | bytes 9437184 | tf_op jit(solution)/shard_map/all_to_all | solution.py:107
  194.3 2.9 copy-start.2
  197.1 2.1 copy-start.11
  197.1 2.6 copy-start.12
  197.1 2.7 copy-start.6
  197.1 2.7 copy-start.7
  210.5 30.5 %all-to-all-start.4 = ((bf16[1,512,2,4,256]{4,2,1,0,3:T(2,128)(2,1)}), bf16[1,512,2,4,256]{4,2,1,0,3:T(2,128)(2,1)S(1)}, u32[]{:S(2)}, u32[]{:S(2)}) async-start(bf16[1,512,2,4,256]{4,2,1,0,3:T(2,128)(2,1)} %copy.139), calls=%async_computation.4 | async-start | bytes 4194304 | tf_op jit(solution)/shard_map/all_to_all | solution.py:94
  241.2 30.0 %copy-start.4 = (bf16[1,512,256]{2,1,0:T(8,128)(2,1)S(1)}, bf16[1,512,256]{2,1,0:T(8,128)(2,1)}, u32[]{:S(2)}) copy-start(bf16[1,512,256]{2,1,0:T(8,128)(2,1)} %param.14) | copy-start | bytes 786436
  242.6 28.6 %collective-permute-start.1 = (f32[1,512,256]{2,0,1:T(1,128)S(1)}, f32[1,512,256]{2,0,1:T(1,128)S(1)}, u32[]{:S(2)}, u32[]{:S(2)}) collective-permute-start(f32[1,512,256]{2,0,1:T(1,128)S(1)} %fusion.18), channel_id=1, source_target_pairs={{0,16},{16,0},{1,17},{17,1},{2,18},{18,2},{3,19},{19,3},{4,20},{20... | collective-permute-start | bytes 1572872 | tf_op jit(solution)/shard_map/ppermute | solution.py:74
  272.2 12.7 %collective-permute-start.2 = (bf16[1,512,256]{2,1,0:T(8,128)(2,1)S(1)}, bf16[1,512,256]{2,1,0:T(8,128)(2,1)S(1)}, u32[]{:S(2)}, u32[]{:S(2)}) collective-permute-start(bf16[1,512,256]{2,1,0:T(8,128)(2,1)S(1)} %copy.144), channel_id=1, source_target_pairs={{0,16},{16,0},{1,17},{17,1},{2,18},{18,2},{3,19},{19,3},{4,20},{20... | collective-permute-start | bytes 786440 | tf_op jit(solution)/shard_map/ppermute | solution.py:74
  322.6 0.7 copy-start.8
  342.5 3.8 copy-start.10
  342.5 29.2 %all-to-all-start.6 = ((bf16[1,512,2,4,256]{4,2,1,0,3:T(2,128)(2,1)}), bf16[1,512,2,4,256]{4,2,1,0,3:T(2,128)(2,1)S(1)}, u32[]{:S(2)}, u32[]{:S(2)}) async-start(bf16[1,512,2,4,256]{4,2,1,0,3:T(2,128)(2,1)} %copy.149), calls=%async_computation.6 | async-start | bytes 4194304 | tf_op jit(solution)/shard_map/all_to_all | solution.py:94
  372.5 22.5 %collective-permute-start.3 = (f32[1,512,256]{2,0,1:T(1,128)S(1)}, f32[1,512,256]{2,0,1:T(1,128)S(1)}, u32[]{:S(2)}, u32[]{:S(2)}) collective-permute-start(f32[1,512,256]{2,0,1:T(1,128)S(1)} %fusion.19), channel_id=1, source_target_pairs={{0,16},{16,0},{1,17},{17,1},{2,18},{18,2},{3,19},{19,3},{4,20},{20... | collective-permute-start | bytes 1572872 | tf_op jit(solution)/shard_map/ppermute | solution.py:74
  377.6 16.5 %all-to-all-start.7 = ((bf16[2,4,128,128]{3,2,0,1:T(8,128)(2,1)}), bf16[2,4,128,128]{3,2,0,1:T(8,128)(2,1)S(1)}, u32[]{:S(2)}, u32[]{:S(2)}) async-start(bf16[2,4,128,128]{3,2,0,1:T(8,128)(2,1)} %copy.153), calls=%async_computation.7 | async-start | bytes 524288 | tf_op jit(solution)/shard_map/all_to_all | solution.py:212
  381.1 15.8 %copy-start.1 = (f32[2,64,256]{2,1,0:T(8,128)S(1)}, f32[2,64,256]{2,1,0:T(8,128)}, u32[]{:S(2)}) copy-start(f32[2,64,256]{2,1,0:T(8,128)} %param.18) | copy-start | bytes 393220
  395.0 1.9 copy-start.5

commit v7 on v6

--- a/solution.py
+++ b/solution.py
@@ -145,11 +145,12 @@
     ]
     widths = [p.shape[1] for p in pieces]
     offsets = [sum(widths[:i]) for i in range(len(widths) + 1)]
-    full = gather_rows(jnp.concatenate(pieces, axis=1))
-    qkv_w = full[:, offsets[0] : offsets[2]]
-    out_t = full[:, offsets[2] : offsets[3]]
-    gateup_w = full[:, offsets[3] : offsets[4]]
-    down_t = full[:, offsets[4] : offsets[5]]
+    attn_full = gather_rows(jnp.concatenate(pieces[:3], axis=1))
+    ffn_full = lax.all_gather(jnp.concatenate(pieces[3:], axis=1), ROWPAGE, axis=0, tiled=True)
+    qkv_w = attn_full[:, offsets[0] : offsets[2]]
+    out_t = attn_full[:, offsets[2] : offsets[3]]
+    gateup_w = ffn_full[:, : offsets[4] - offsets[3]]
+    down_t = ffn_full[:, offsets[4] - offsets[3] :]
 
     prompt_count, seq_len, local_feat = tokens.shape
     gathered = gather_col(tokens, 2)

time: 400 us -> 306 us (0.77)
  the two profiles are of different devices: /device:TPU:8 before, /device:TPU:1 now
where the time goes in v7:
time: 306 us; the launch traced here: 304 us
  waiting for transfers between devices  125 us (41%)
  starting transfers between devices  55.6 us (18%)
  local copies, waits for them, and re-layouts  39.1 us (13%)
  blocking collectives  36.2 us (12%)
  other arithmetic  17.8 us (6%)
  matrix products  16 us (5%)
  between operations  15.2 us (5%)
    all_to_all x2, waiting for transfers between devices, scatter_sum_col(): got = lax.all_to_all(x.reshape(split), 'xx', axis + 1, axis + 1, tiled=True)  47.6 us
    ppermute x4, waiting for transfers between devices, swap_halves(): return lax.ppermute(x, 'zh', [(0, 1), (1, 0)])  33.1 us
    ppermute x4, starting transfers between devices, swap_halves(): return lax.ppermute(x, 'zh', [(0, 1), (1, 0)])  29.9 us
    all_to_all x1, blocking collectives, gather_col(): got = lax.all_to_all(copies, 'xx', 0, 0, tiled=True)  26.5 us
    all_to_all x1, waiting for transfers between devices, on_device(): lax.all_to_all(outgoing, 'page', split_axis=1, concat_axis=1, tiled=True)  18.6 us
    all_to_all x1, waiting for transfers between devices, gather_col(): got = lax.all_to_all(copies, 'xx', 0, 0, tiled=True)  16.7 us
    reshape x4, local copies, waits for them, and re-layouts, scatter_sum_col(): got = lax.all_to_all(x.reshape(split), 'xx', axis + 1, axis + 1, tiled=True)  13.6 us
    all_to_all x1, blocking collectives, gather_rows(): got = lax.all_to_all(got, 'rc', 1, 1, tiled=True)  9.71 us
  transfers between devices with their start and end apart: 11, of which 9 were waited for; matrix products, arithmetic and copies ran while one was open for 17% of the time, Pallas kernels for 0%

profile of v7, /device:TPU:1, one launch (start us, length us, event | category | flops | bytes accessed | tf_op | source)
XLA Modules:
  0.0 304.4 jit_solution(15663409995320128311)
XLA Ops:
  7.2 1.1 convert_bitcast_fusion
  8.3 0.9 convert_bitcast_fusion.1
  9.3 0.7 pad_maximum_fusion
  10.3 0.8 convert_element_type.137
  11.0 0.7 broadcast_in_dim.67
  11.7 6.4 %all-to-all-start.1 = ((bf16[4,64,384]{2,1,0:T(8,128)(2,1)}), bf16[4,64,384]{2,1,0:T(8,128)(2,1)S(1)}, u32[]{:S(2)}, u32[]{:S(2)}) async-start(bf16[4,64,384]{2,1,0:T(8,128)(2,1)} %broadcast_in_dim.67), calls=%async_computation.1 | async-start | bytes 393216 | tf_op jit(solution)/shard_map/all_to_all | solution.py:104
  18.2 4.8 %collective-permute-start = (bf16[1,512,256]{2,1,0:T(8,128)(2,1)S(1)}, bf16[1,512,256]{2,1,0:T(8,128)(2,1)S(1)}, u32[]{:S(2)}, u32[]{:S(2)}) collective-permute-start(bf16[1,512,256]{2,1,0:T(8,128)(2,1)S(1)} %copy-done.3), channel_id=1, source_target_pairs={{0,16},{16,0},{1,17},{17,1},{2,18},{18,2},{3,19},{19,3},{4,20},{20... | collective-permute-start | bytes 786440 | tf_op jit(solution)/shard_map/ppermute | solution.py:74
  22.9 0.4 all-to-all-done.1
  23.5 1.0 broadcast_in_dim.69
  24.6 4.2 %all-to-all-start.2 = ((bf16[4,256,384]{1,2,0:T(8,128)(2,1)}), bf16[4,256,384]{1,2,0:T(8,128)(2,1)S(1)}, u32[]{:S(2)}, u32[]{:S(2)}) async-start(bf16[4,256,384]{1,2,0:T(8,128)(2,1)} %broadcast_in_dim.69), calls=%async_computation.2 | async-start | bytes 1572864 | tf_op jit(solution)/shard_map/all_to_all | solution.py:107
  28.7 4.0 %collective-permute-done = bf16[1,512,256]{2,1,0:T(8,128)(2,1)S(1)} collective-permute-done((bf16[1,512,256]{2,1,0:T(8,128)(2,1)S(1)}, bf16[1,512,256]{2,1,0:T(8,128)(2,1)S(1)}, u32[]{:S(2)}, u32[]{:S(2)}) %collective-permute-start) | collective-permute-done | bytes 262176 | tf_op jit(solution)/shard_map/ppermute | solution.py:74
  32.8 0.5 copy.127
  33.4 8.1 %all-to-all-done.2 = bf16[4,256,384]{1,2,0:T(8,128)(2,1)S(1)} async-done(((bf16[4,256,384]{1,2,0:T(8,128)(2,1)}), bf16[4,256,384]{1,2,0:T(8,128)(2,1)S(1)}, u32[]{:S(2)}, u32[]{:S(2)}) %all-to-all-start.2) | async-done | bytes 786464 | tf_op jit(solution)/shard_map/all_to_all | solution.py:107
  41.5 0.6 copy.132
  42.1 0.4 broadcast_in_dim.70
  42.5 9.7 %all_to_all.40 = bf16[4,2,256,384]{2,0,3,1:T(4,128)(2,1)} all-to-all(bf16[4,2,256,384]{2,0,3,1:T(4,128)(2,1)S(1)} %broadcast_in_dim.70), channel_id=1, replica_groups=mesh['ry'=4,'rc'=2,'zh'=2,'xx'=4,'page'=4] {'rc'}, dimensions={1} | all-to-all | bytes 3145728 | tf_op jit(solution)/shard_map/all_to_all | solution.py:110
  52.2 2.5 broadcast_in_dim.66
  54.7 4.1 %all-to-all-start = ((bf16[4,2,1,512,256]{4,1,3,2,0:T(2,128)(2,1)}), bf16[4,2,1,512,256]{4,1,3,2,0:T(2,128)(2,1)S(1)}, u32[]{:S(2)}, u32[]{:S(2)}) async-start(bf16[4,2,1,512,256]{4,1,3,2,0:T(2,128)(2,1)} %broadcast_in_dim.66), calls=%async_computation | async-start | bytes 4194304 | tf_op jit(solution)/shard_map/all_to_all | solution.py:83
  59.5 1.0 fusion.34
  60.5 0.8 fusion.9
  61.3 3.8 %copy.133 = bf16[4,2,256,384]{3,2,1,0:T(8,128)(2,1)} copy(bf16[4,2,256,384]{2,0,3,1:T(4,128)(2,1)} %all_to_all.40) | data formatting | bytes 3145728 | tf_op jit(solution)/shard_map/all_to_all | solution.py:110
  65.1 1.3 slice_bitcast_fusion
  66.5 1.4 copy.134
  67.9 16.7 %all-to-all-done = bf16[4,2,1,512,256]{4,1,3,2,0:T(2,128)(2,1)S(1)} async-done(((bf16[4,2,1,512,256]{4,1,3,2,0:T(2,128)(2,1)}), bf16[4,2,1,512,256]{4,1,3,2,0:T(2,128)(2,1)S(1)}, u32[]{:S(2)}, u32[]{:S(2)}) %all-to-all-start) | async-done | bytes 2097184 | tf_op jit(solution)/shard_map/all_to_all | solution.py:83
  84.6 0.4 copy_convert_fusion.1
  85.0 0.4 multiply_reduce_fusion.1
  85.4 0.5 fusion.5
  85.8 2.5 copy.129
  88.4 2.3 convolution_bitcast_fusion
  91.7 0.7 fusion.6
  92.4 0.7 fusion.8
  93.1 1.8 convolution_convert_fusion
  94.9 2.8 reshape.448
  97.7 4.5 %copy.137 = bf16[1,512,2,4,256]{4,2,1,0,3:T(2,128)(2,1)} copy(bf16[1,512,2,4,256]{4,3,2,1,0:T(4,128)(2,1)} %reshape.448) | data formatting | bytes 4194304 | tf_op jit(solution)/shard_map/reshape | solution.py:94
  102.2 3.6 %all-to-all-start.4 = ((bf16[1,512,2,4,256]{4,2,1,0,3:T(2,128)(2,1)}), bf16[1,512,2,4,256]{4,2,1,0,3:T(2,128)(2,1)S(1)}, u32[]{:S(2)}, u32[]{:S(2)}) async-start(bf16[1,512,2,4,256]{4,2,1,0,3:T(2,128)(2,1)} %copy.137), calls=%async_computation.4 | async-start | bytes 4194304 | tf_op jit(solution)/shard_map/all_to_all | solution.py:94
  105.9 24.9 %all-to-all-done.4 = bf16[1,512,2,4,256]{4,2,1,0,3:T(2,128)(2,1)S(1)} async-done(((bf16[1,512,2,4,256]{4,2,1,0,3:T(2,128)(2,1)}), bf16[1,512,2,4,256]{4,2,1,0,3:T(2,128)(2,1)S(1)}, u32[]{:S(2)}, u32[]{:S(2)}) %all-to-all-start.4) | async-done | bytes 2097184 | tf_op jit(solution)/shard_map/all_to_all | solution.py:94
  130.9 0.8 copy.184
  131.8 0.5 fusion.18
  132.3 14.7 %collective-permute-start.1 = (f32[1,512,256]{2,0,1:T(1,128)S(1)}, f32[1,512,256]{2,0,1:T(1,128)S(1)}, u32[]{:S(2)}, u32[]{:S(2)}) collective-permute-start(f32[1,512,256]{2,0,1:T(1,128)S(1)} %fusion.18), channel_id=1, source_target_pairs={{0,16},{16,0},{1,17},{17,1},{2,18},{18,2},{3,19},{19,3},{4,20},{20... | collective-permute-start | bytes 1572872 | tf_op jit(solution)/shard_map/ppermute | solution.py:74
  147.0 18.9 %collective-permute-done.1 = f32[1,512,256]{2,0,1:T(1,128)S(1)} collective-permute-done((f32[1,512,256]{2,0,1:T(1,128)S(1)}, f32[1,512,256]{2,0,1:T(1,128)S(1)}, u32[]{:S(2)}, u32[]{:S(2)}) %collective-permute-start.1) | collective-permute-done | bytes 524320 | tf_op jit(solution)/shard_map/ppermute | solution.py:74
  165.9 0.9 fusion.21
  166.8 5.5 %collective-permute-start.2 = (bf16[1,512,256]{2,1,0:T(8,128)(2,1)S(1)}, bf16[1,512,256]{2,1,0:T(8,128)(2,1)S(1)}, u32[]{:S(2)}, u32[]{:S(2)}) collective-permute-start(bf16[1,512,256]{2,1,0:T(8,128)(2,1)S(1)} %copy.142), channel_id=1, source_target_pairs={{0,16},{16,0},{1,17},{17,1},{2,18},{18,2},{3,19},{19,3},{4,20},{20... | collective-permute-start | bytes 786440 | tf_op jit(solution)/shard_map/ppermute | solution.py:74
  172.3 10.2 %collective-permute-done.2 = bf16[1,512,256]{2,1,0:T(8,128)(2,1)S(1)} collective-permute-done((bf16[1,512,256]{2,1,0:T(8,128)(2,1)S(1)}, bf16[1,512,256]{2,1,0:T(8,128)(2,1)S(1)}, u32[]{:S(2)}, u32[]{:S(2)}) %collective-permute-start.2) | collective-permute-done | bytes 262176 | tf_op jit(solution)/shard_map/ppermute | solution.py:74
  182.5 0.8 broadcast_select_fusion
  183.6 26.5 %all_to_all.41 = bf16[4,2,1,512,256]{4,3,1,2,0:T(8,128)(2,1)S(1)} all-to-all(bf16[4,2,1,512,256]{4,3,1,2,0:T(8,128)(2,1)S(1)} %broadcast_in_dim.79), channel_id=1, replica_groups=mesh['ry'=4,'rc'=2,'zh'=2,'xx'=4,'page'=4] {'xx'}, dimensions={0} | all-to-all | bytes 4194304 | tf_op jit(solution)/shard_map/all_to_all | solution.py:83
  210.1 2.4 copy_convert_fusion
  212.5 5.3 %copy.146 = f32[1,512,8,256]{1,3,2,0:T(8,128)} copy(f32[1,512,8,256]{3,1,2,0:T(8,128)} %bitcast.118) | data formatting | bytes 8388608 | tf_op jit(solution)/shard_map/convert_element_type | solution.py:181
  217.8 0.5 multiply_reduce_fusion
  218.5 2.6 fusion.3
  221.2 5.4 %fusion = f32[512,1280]{1,0:T(8,128)S(1)} fusion(bf16[512,2048]{0,1:T(8,128)(2,1)S(1)} %fusion.3, bf16[2048,1920]{1,0:T(8,128)(2,1)} %all-gather.2.cloned.1.call-done), kind=kOutput, calls=%fused_computation.2 | convolution fusion | flops 2684354560 | bytes 9961472 | tf_op jit(solution)/shard_map/dot_general | solution.py:182
  226.6 5.0 %convolution_convert_fusion.1 = bf16[512,2048]{1,0:T(8,128)(2,1)} fusion(bf16[2048,1920]{1,0:T(8,128)(2,1)} %all-gather.2.cloned.1.call-done, f32[512,1280]{1,0:T(8,128)S(1)} %fusion), kind=kOutput, calls=%fused_computation.13 | convolution fusion | flops 1345191936 | bytes 7340032 | tf_op jit(solution)/shard_map/dot_general | solution.py:50
  231.6 3.3 %reshape.450 = bf16[1,512,2,4,256]{4,3,2,1,0:T(4,128)(2,1)S(1)} reshape(bf16[512,2048]{1,0:T(8,128)(2,1)} %convolution_convert_fusion.1) | data formatting | bytes 4194304 | tf_op jit(solution)/shard_map/reshape | solution.py:94
  234.9 3.0 copy.148
  237.8 3.7 %all-to-all-start.6 = ((bf16[1,512,2,4,256]{4,2,1,0,3:T(2,128)(2,1)}), bf16[1,512,2,4,256]{4,2,1,0,3:T(2,128)(2,1)S(1)}, u32[]{:S(2)}, u32[]{:S(2)}) async-start(bf16[1,512,2,4,256]{4,2,1,0,3:T(2,128)(2,1)} %copy.148), calls=%async_computation.6 | async-start | bytes 4194304 | tf_op jit(solution)/shard_map/all_to_all | solution.py:94
  242.0 22.7 %all-to-all-done.6 = bf16[1,512,2,4,256]{4,2,1,0,3:T(2,128)(2,1)S(1)} async-done(((bf16[1,512,2,4,256]{4,2,1,0,3:T(2,128)(2,1)}), bf16[1,512,2,4,256]{4,2,1,0,3:T(2,128)(2,1)S(1)}, u32[]{:S(2)}, u32[]{:S(2)}) %all-to-all-start.6) | async-done | bytes 2097184 | tf_op jit(solution)/shard_map/all_to_all | solution.py:94
  265.0 0.5 fusion.19
  265.5 5.0 %collective-permute-start.3 = (f32[1,512,256]{2,0,1:T(1,128)S(1)}, f32[1,512,256]{2,0,1:T(1,128)S(1)}, u32[]{:S(2)}, u32[]{:S(2)}) collective-permute-start(f32[1,512,256]{2,0,1:T(1,128)S(1)} %fusion.19), channel_id=1, source_target_pairs={{0,16},{16,0},{1,17},{17,1},{2,18},{18,2},{3,19},{19,3},{4,20},{20... | collective-permute-start | bytes 1572872 | tf_op jit(solution)/shard_map/ppermute | solution.py:74
  271.1 0.8 scatter_fusion
  271.9 0.7 copy.152
  272.6 3.6 %all-to-all-start.7 = ((bf16[2,4,128,128]{3,2,0,1:T(8,128)(2,1)}), bf16[2,4,128,128]{3,2,0,1:T(8,128)(2,1)S(1)}, u32[]{:S(2)}, u32[]{:S(2)}) async-start(bf16[2,4,128,128]{3,2,0,1:T(8,128)(2,1)} %copy.152), calls=%async_computation.7 | async-start | bytes 524288 | tf_op jit(solution)/shard_map/all_to_all | solution.py:213
  276.3 18.6 %all-to-all-done.7 = bf16[2,4,128,128]{3,2,0,1:T(8,128)(2,1)S(1)} async-done(((bf16[2,4,128,128]{3,2,0,1:T(8,128)(2,1)}), bf16[2,4,128,128]{3,2,0,1:T(8,128)(2,1)S(1)}, u32[]{:S(2)}, u32[]{:S(2)}) %all-to-all-start.7) | async-done | bytes 262176 | tf_op jit(solution)/shard_map/all_to_all | solution.py:213
  295.0 0.8 scatter_fusion.1
  295.8 1.1 fusion.22
  296.8 0.7 copy.153
  (80 shorter events, 3.6 us)
Async XLA Ops:
  7.2 2.9 copy-start
  7.2 3.8 %copy-start.8 = (f32[128,64]{0,1:T(8,128)S(1)}, f32[128,64]{0,1:T(8,128)}, u32[]{:S(2)}) copy-start(f32[128,64]{0,1:T(8,128)} %param.19) | copy-start | bytes 98308
  7.2 11.0 %copy-start.3 = (bf16[1,512,256]{2,1,0:T(8,128)(2,1)S(1)}, bf16[1,512,256]{2,1,0:T(8,128)(2,1)}, u32[]{:S(2)}) copy-start(bf16[1,512,256]{2,1,0:T(8,128)(2,1)} %param.14) | copy-start | bytes 786436
  7.2 214.0 %all-gather.2.cloned.1.call-start = ((), (), s32[]{:S(2)}) async-start(), calls=%async_computation.8 | async-start | bytes 8110080 | tf_op jit(solution)/shard_map/all_gather | solution.py:149
  11.7 11.6 %all-to-all-start.1 = ((bf16[4,64,384]{2,1,0:T(8,128)(2,1)}), bf16[4,64,384]{2,1,0:T(8,128)(2,1)S(1)}, u32[]{:S(2)}, u32[]{:S(2)}) async-start(bf16[4,64,384]{2,1,0:T(8,128)(2,1)} %broadcast_in_dim.67), calls=%async_computation.1 | async-start | bytes 393216 | tf_op jit(solution)/shard_map/all_to_all | solution.py:104
  18.2 14.5 %collective-permute-start = (bf16[1,512,256]{2,1,0:T(8,128)(2,1)S(1)}, bf16[1,512,256]{2,1,0:T(8,128)(2,1)S(1)}, u32[]{:S(2)}, u32[]{:S(2)}) collective-permute-start(bf16[1,512,256]{2,1,0:T(8,128)(2,1)S(1)} %copy-done.3), channel_id=1, source_target_pairs={{0,16},{16,0},{1,17},{17,1},{2,18},{18,2},{3,19},{19,3},{4,20},{20... | collective-permute-start | bytes 786440 | tf_op jit(solution)/shard_map/ppermute | solution.py:74
  24.6 17.0 %all-to-all-start.2 = ((bf16[4,256,384]{1,2,0:T(8,128)(2,1)}), bf16[4,256,384]{1,2,0:T(8,128)(2,1)S(1)}, u32[]{:S(2)}, u32[]{:S(2)}) async-start(bf16[4,256,384]{1,2,0:T(8,128)(2,1)} %broadcast_in_dim.69), calls=%async_computation.2 | async-start | bytes 1572864 | tf_op jit(solution)/shard_map/all_to_all | solution.py:107
  54.7 4.1 %copy-start.10 = (f32[2048]{0:T(1024)S(1)}, f32[2048]{0:T(1024)}, u32[]{:S(2)}) copy-start(f32[2048]{0:T(1024)} %param.22) | copy-start | bytes 24580
  54.7 29.9 %all-to-all-start = ((bf16[4,2,1,512,256]{4,1,3,2,0:T(2,128)(2,1)}), bf16[4,2,1,512,256]{4,1,3,2,0:T(2,128)(2,1)S(1)}, u32[]{:S(2)}, u32[]{:S(2)}) async-start(bf16[4,2,1,512,256]{4,1,3,2,0:T(2,128)(2,1)} %broadcast_in_dim.66), calls=%async_computation | async-start | bytes 4194304 | tf_op jit(solution)/shard_map/all_to_all | solution.py:83
  85.8 2.5 copy-start.2
  88.3 2.4 copy-start.12
  88.3 2.9 copy-start.13
  88.3 3.0 copy-start.6
  88.3 3.0 copy-start.7
  90.7 1.0 copy-start.5
  102.2 28.5 %all-to-all-start.4 = ((bf16[1,512,2,4,256]{4,2,1,0,3:T(2,128)(2,1)}), bf16[1,512,2,4,256]{4,2,1,0,3:T(2,128)(2,1)S(1)}, u32[]{:S(2)}, u32[]{:S(2)}) async-start(bf16[1,512,2,4,256]{4,2,1,0,3:T(2,128)(2,1)} %copy.137), calls=%async_computation.4 | async-start | bytes 4194304 | tf_op jit(solution)/shard_map/all_to_all | solution.py:94
  132.3 33.6 %collective-permute-start.1 = (f32[1,512,256]{2,0,1:T(1,128)S(1)}, f32[1,512,256]{2,0,1:T(1,128)S(1)}, u32[]{:S(2)}, u32[]{:S(2)}) collective-permute-start(f32[1,512,256]{2,0,1:T(1,128)S(1)} %fusion.18), channel_id=1, source_target_pairs={{0,16},{16,0},{1,17},{17,1},{2,18},{18,2},{3,19},{19,3},{4,20},{20... | collective-permute-start | bytes 1572872 | tf_op jit(solution)/shard_map/ppermute | solution.py:74
  166.8 15.7 %collective-permute-start.2 = (bf16[1,512,256]{2,1,0:T(8,128)(2,1)S(1)}, bf16[1,512,256]{2,1,0:T(8,128)(2,1)S(1)}, u32[]{:S(2)}, u32[]{:S(2)}) collective-permute-start(bf16[1,512,256]{2,1,0:T(8,128)(2,1)S(1)} %copy.142), channel_id=1, source_target_pairs={{0,16},{16,0},{1,17},{17,1},{2,18},{18,2},{3,19},{19,3},{4,20},{20... | collective-permute-start | bytes 786440 | tf_op jit(solution)/shard_map/ppermute | solution.py:74
  217.8 0.7 copy-start.9
  237.8 3.8 %copy-start.11 = (s32[4,4]{1,0:T(4,128)S(1)}, s32[4,4]{1,0:T(4,128)}, u32[]{:S(2)}) copy-start(s32[4,4]{1,0:T(4,128)} %param.16) | copy-start | bytes 196
  237.8 26.9 %all-to-all-start.6 = ((bf16[1,512,2,4,256]{4,2,1,0,3:T(2,128)(2,1)}), bf16[1,512,2,4,256]{4,2,1,0,3:T(2,128)(2,1)S(1)}, u32[]{:S(2)}, u32[]{:S(2)}) async-start(bf16[1,512,2,4,256]{4,2,1,0,3:T(2,128)(2,1)} %copy.148), calls=%async_computation.6 | async-start | bytes 4194304 | tf_op jit(solution)/shard_map/all_to_all | solution.py:94
  265.5 30.2 %collective-permute-start.3 = (f32[1,512,256]{2,0,1:T(1,128)S(1)}, f32[1,512,256]{2,0,1:T(1,128)S(1)}, u32[]{:S(2)}, u32[]{:S(2)}) collective-permute-start(f32[1,512,256]{2,0,1:T(1,128)S(1)} %fusion.19), channel_id=1, source_target_pairs={{0,16},{16,0},{1,17},{17,1},{2,18},{18,2},{3,19},{19,3},{4,20},{20... | collective-permute-start | bytes 1572872 | tf_op jit(solution)/shard_map/ppermute | solution.py:74
  272.6 22.3 %all-to-all-start.7 = ((bf16[2,4,128,128]{3,2,0,1:T(8,128)(2,1)}), bf16[2,4,128,128]{3,2,0,1:T(8,128)(2,1)S(1)}, u32[]{:S(2)}, u32[]{:S(2)}) async-start(bf16[2,4,128,128]{3,2,0,1:T(8,128)(2,1)} %copy.152), calls=%async_computation.7 | async-start | bytes 524288 | tf_op jit(solution)/shard_map/all_to_all | solution.py:213
  276.2 21.4 %copy-start.1 = (f32[2,64,256]{2,1,0:T(8,128)S(1)}, f32[2,64,256]{2,1,0:T(8,128)}, u32[]{:S(2)}) copy-start(f32[2,64,256]{2,1,0:T(8,128)} %param.18) | copy-start | bytes 393220
  295.7 1.9 copy-start.4
Sparse Core Ops, SparseCore 0:
  10.4 103.9 all-gather.1

commit v8 on v7

--- a/solution.py
+++ b/solution.py
@@ -78,6 +78,10 @@
     half = lax.axis_index("zh")
     other = swap_halves(x)
     pair = jnp.stack([jnp.where(half == 0, x, other), jnp.where(half == 0, other, x)])
+    return gather_xx(pair, x, axis)
+
+
+def gather_xx(pair, x, axis):
     count = lax.axis_size("xx")
     copies = jnp.broadcast_to(pair[None], (count,) + pair.shape)
     got = lax.all_to_all(copies, "xx", 0, 0, tiled=True)
@@ -175,9 +179,17 @@
     )
     attn_terms = contract_rows(attended.reshape(-1, local_width), out_t)
     attn_terms = attn_terms.reshape(prompt_count, seq_len, model_width).astype(jnp.bfloat16)
-    attn_sum = scatter_sum_col(attn_terms, 2)
-    residual = (tokens.astype(jnp.float32) + attn_sum).astype(jnp.bfloat16)
-    residual_all = gather_col(residual, 2)
+    xx_count = lax.axis_size("xx")
+    xx_index = lax.axis_index("xx")
+    block = local_feat
+    split = (prompt_count, seq_len, 2, xx_count, block)
+    got = lax.all_to_all(attn_terms.reshape(split), "xx", 3, 3, tiled=True)
+    part = jnp.sum(got.astype(jnp.float32), axis=3)
+    total = part + swap_halves(part)
+    tok_pair = lax.dynamic_index_in_dim(gathered.reshape(split), xx_index, 3, keepdims=False)
+    res_pair = (tok_pair.astype(jnp.float32) + total).astype(jnp.bfloat16)
+    residual = lax.dynamic_index_in_dim(res_pair, lax.axis_index("zh"), 2, keepdims=False)
+    residual_all = gather_xx(jnp.moveaxis(res_pair, 2, 0), residual, 2)
     ffn_in = normalize(residual_all.astype(jnp.float32), ffn_gain).astype(jnp.bfloat16)
     gate_up = jnp.dot(
         ffn_in.reshape(-1, model_width), gateup_w, preferred_element_type=jnp.float32

time: 306 us -> 309 us (level)
  the two profiles are of different devices: /device:TPU:1 before, /device:TPU:8 now
where the time goes in v8:
time: 309 us; the launch traced here: 306 us
  waiting for transfers between devices  110 us (36%)
  blocking collectives  61.1 us (20%)
  starting transfers between devices  47.4 us (15%)
  local copies, waits for them, and re-layouts  38.9 us (13%)
  other arithmetic  17.1 us (6%)
  matrix products  16 us (5%)
  between operations  15.2 us (5%)
    ppermute x3, waiting for transfers between devices, swap_halves(): return lax.ppermute(x, 'zh', [(0, 1), (1, 0)])  43.8 us
    all_to_all x1, blocking collectives, on_device(): got = lax.all_to_all(attn_terms.reshape(split), 'xx', 3, 3, tiled=True)  28.3 us
    all_to_all x1, blocking collectives, gather_xx(): got = lax.all_to_all(copies, 'xx', 0, 0, tiled=True)  26.9 us
    ppermute x3, starting transfers between devices, swap_halves(): return lax.ppermute(x, 'zh', [(0, 1), (1, 0)])  24.2 us
    all_to_all x1, waiting for transfers between devices, scatter_sum_col(): got = lax.all_to_all(x.reshape(split), 'xx', axis + 1, axis + 1, tiled=True)  22.6 us
    all_to_all x1, waiting for transfers between devices, gather_xx(): got = lax.all_to_all(copies, 'xx', 0, 0, tiled=True)  18.3 us
    all_to_all x1, waiting for transfers between devices, on_device(): lax.all_to_all(outgoing, 'page', split_axis=1, concat_axis=1, tiled=True)  12.5 us
    all_to_all x1, waiting for transfers between devices, gather_rows(): lax.all_to_all(jnp.broadcast_to(got[None], (chips,) + got.shape), 'ry', 0...  9.41 us
  transfers between devices with their start and end apart: 9, of which 7 were waited for; matrix products, arithmetic and copies ran while one was open for 16% of the time, Pallas kernels for 0%

profile of v8, /device:TPU:8, one launch (start us, length us, event | category | flops | bytes accessed | tf_op | source)
XLA Modules:
  0.0 305.9 jit_solution(4438594689536712938)
XLA Ops:
  7.2 1.1 convert_bitcast_fusion
  8.3 0.9 convert_bitcast_fusion.1
  9.3 0.7 pad_maximum_fusion
  10.3 0.8 convert_element_type.147
  11.0 0.7 broadcast_in_dim.67
  11.7 5.9 %all-to-all-start.1 = ((bf16[4,64,384]{2,1,0:T(8,128)(2,1)}), bf16[4,64,384]{2,1,0:T(8,128)(2,1)S(1)}, u32[]{:S(2)}, u32[]{:S(2)}) async-start(bf16[4,64,384]{2,1,0:T(8,128)(2,1)} %broadcast_in_dim.67), calls=%async_computation.1 | async-start | bytes 393216 | tf_op jit(solution)/shard_map/all_to_all | solution.py:108
  17.6 4.8 %collective-permute-start = (bf16[1,512,256]{2,1,0:T(8,128)(2,1)S(1)}, bf16[1,512,256]{2,1,0:T(8,128)(2,1)S(1)}, u32[]{:S(2)}, u32[]{:S(2)}) collective-permute-start(bf16[1,512,256]{2,1,0:T(8,128)(2,1)S(1)} %copy-done.4), channel_id=1, source_target_pairs={{0,16},{16,0},{1,17},{17,1},{2,18},{18,2},{3,19},{19,3},{4,20},{20... | collective-permute-start | bytes 786440 | tf_op jit(solution)/shard_map/ppermute | solution.py:74
  22.4 3.6 %all-to-all-done.1 = bf16[4,64,384]{2,1,0:T(8,128)(2,1)S(1)} async-done(((bf16[4,64,384]{2,1,0:T(8,128)(2,1)}), bf16[4,64,384]{2,1,0:T(8,128)(2,1)S(1)}, u32[]{:S(2)}, u32[]{:S(2)}) %all-to-all-start.1) | async-done | bytes 196640 | tf_op jit(solution)/shard_map/all_to_all | solution.py:108
  26.2 1.0 broadcast_in_dim.69
  27.2 4.9 %all-to-all-start.2 = ((bf16[4,256,384]{1,2,0:T(8,128)(2,1)}), bf16[4,256,384]{1,2,0:T(8,128)(2,1)S(1)}, u32[]{:S(2)}, u32[]{:S(2)}) async-start(bf16[4,256,384]{1,2,0:T(8,128)(2,1)} %broadcast_in_dim.69), calls=%async_computation.2 | async-start | bytes 1572864 | tf_op jit(solution)/shard_map/all_to_all | solution.py:111
  32.1 0.6 collective-permute-done
  32.8 9.4 %all-to-all-done.2 = bf16[4,256,384]{1,2,0:T(8,128)(2,1)S(1)} async-done(((bf16[4,256,384]{1,2,0:T(8,128)(2,1)}), bf16[4,256,384]{1,2,0:T(8,128)(2,1)S(1)}, u32[]{:S(2)}, u32[]{:S(2)}) %all-to-all-start.2) | async-done | bytes 786464 | tf_op jit(solution)/shard_map/all_to_all | solution.py:111
  42.2 0.6 copy.103
  42.8 0.4 broadcast_in_dim.70
  43.2 5.9 %all_to_all.40 = bf16[4,2,256,384]{2,0,3,1:T(4,128)(2,1)} all-to-all(bf16[4,2,256,384]{2,0,3,1:T(4,128)(2,1)S(1)} %broadcast_in_dim.70), channel_id=1, replica_groups=mesh['ry'=4,'rc'=2,'zh'=2,'xx'=4,'page'=4] {'rc'}, dimensions={1} | all-to-all | bytes 3145728 | tf_op jit(solution)/shard_map/all_to_all | solution.py:114
  49.2 1.5 broadcast_in_dim.65
  50.7 4.4 %all-to-all-start = ((bf16[4,2,1,512,256]{4,3,1,2,0:T(8,128)(2,1)}), bf16[4,2,1,512,256]{4,3,1,2,0:T(8,128)(2,1)S(1)}, u32[]{:S(2)}, u32[]{:S(2)}) async-start(bf16[4,2,1,512,256]{4,3,1,2,0:T(8,128)(2,1)} %broadcast_in_dim.65), calls=%async_computation | async-start | bytes 4194304 | tf_op jit(solution)/shard_map/all_to_all | solution.py:87
  55.8 1.0 fusion.32
  57.0 3.8 %copy.104 = bf16[4,2,256,384]{3,2,1,0:T(8,128)(2,1)} copy(bf16[4,2,256,384]{2,0,3,1:T(4,128)(2,1)} %all_to_all.40) | data formatting | bytes 3145728 | tf_op jit(solution)/shard_map/all_to_all | solution.py:114
  60.8 1.3 slice_bitcast_fusion
  62.1 1.4 copy.105
  63.5 18.3 %all-to-all-done = bf16[4,2,1,512,256]{4,3,1,2,0:T(8,128)(2,1)S(1)} async-done(((bf16[4,2,1,512,256]{4,3,1,2,0:T(8,128)(2,1)}), bf16[4,2,1,512,256]{4,3,1,2,0:T(8,128)(2,1)S(1)}, u32[]{:S(2)}, u32[]{:S(2)}) %all-to-all-start) | async-done | bytes 2097184 | tf_op jit(solution)/shard_map/all_to_all | solution.py:87
  81.8 1.9 copy_bitcast_fusion.2
  83.7 0.5 fusion.2
  84.2 0.6 fusion.4
  84.8 2.4 copy.100
  87.2 2.4 convolution_bitcast_fusion
  89.7 0.3 fusion.35
  90.3 0.7 fusion.8
  91.0 0.7 fusion.10
  91.7 1.8 convolution_convert_fusion
  93.5 2.8 reshape.477
  96.3 3.2 %copy.108 = bf16[1,512,2,4,256]{4,2,1,0,3:T(2,128)(2,1)S(1)} copy(bf16[1,512,2,4,256]{4,3,2,1,0:T(4,128)(2,1)} %reshape.477) | data formatting | bytes 4194304 | tf_op jit(solution)/shard_map/reshape | solution.py:186
  99.5 28.3 %all_to_all.41 = bf16[1,512,2,4,256]{4,2,1,0,3:T(2,128)(2,1)S(1)} all-to-all(bf16[1,512,2,4,256]{4,2,1,0,3:T(2,128)(2,1)S(1)} %copy.108), channel_id=1, replica_groups=mesh['ry'=4,'rc'=2,'zh'=2,'xx'=4,'page'=4] {'xx'}, dimensions={3} | all-to-all | bytes 4194304 | tf_op jit(solution)/shard_map/all_to_all | solution.py:186
  127.8 0.2 convert_reduce_fusion.1
  128.0 0.8 copy.148
  128.8 16.4 %collective-permute-start.1 = (f32[1,512,2,256]{3,2,1,0:T(2,128)S(1)}, f32[1,512,2,256]{3,2,1,0:T(2,128)}, u32[]{:S(2)}, u32[]{:S(2)}) collective-permute-start(f32[1,512,2,256]{3,2,1,0:T(2,128)S(1)} %bitcast.123), channel_id=1, source_target_pairs={{0,16},{16,0},{1,17},{17,1},{2,18},{18,2},{3,19},{19,3},{4,20},{20... | collective-permute-start | bytes 3145736 | tf_op jit(solution)/shard_map/ppermute | solution.py:74
  145.2 1.1 constant_dynamic-slice_fusion.4
  146.3 43.2 %collective-permute-done.1 = f32[1,512,2,256]{3,2,1,0:T(2,128)} collective-permute-done((f32[1,512,2,256]{3,2,1,0:T(2,128)S(1)}, f32[1,512,2,256]{3,2,1,0:T(2,128)}, u32[]{:S(2)}, u32[]{:S(2)}) %collective-permute-start.1) | collective-permute-done | bytes 1048608 | tf_op jit(solution)/shard_map/ppermute | solution.py:74
  189.5 2.5 fusion.11
  192.3 26.9 %all_to_all.42 = bf16[4,2,1,512,256]{4,3,1,2,0:T(8,128)(2,1)S(1)} all-to-all(bf16[4,2,1,512,256]{4,3,1,2,0:T(8,128)(2,1)S(1)} %broadcast_in_dim.79), channel_id=1, replica_groups=mesh['ry'=4,'rc'=2,'zh'=2,'xx'=4,'page'=4] {'xx'}, dimensions={0} | all-to-all | bytes 4194304 | tf_op jit(solution)/shard_map/all_to_all | solution.py:87
  219.2 2.4 copy_convert_fusion
  221.6 5.3 %copy.113 = f32[1,512,8,256]{1,3,2,0:T(8,128)} copy(f32[1,512,8,256]{3,1,2,0:T(8,128)} %bitcast.116) | data formatting | bytes 8388608 | tf_op jit(solution)/shard_map/convert_element_type | solution.py:193
  226.9 0.5 multiply_reduce_fusion
  227.4 0.2 copy-done.8
  227.6 2.6 fusion.6
  230.3 5.4 %fusion = f32[512,1280]{1,0:T(8,128)S(1)} fusion(bf16[512,2048]{0,1:T(8,128)(2,1)S(1)} %fusion.6, bf16[2048,1920]{1,0:T(8,128)(2,1)} %all-gather.2.cloned.1.call-done), kind=kOutput, calls=%fused_computation.4 | convolution fusion | flops 2684354560 | bytes 9961472 | tf_op jit(solution)/shard_map/dot_general | solution.py:194
  235.7 5.0 %convolution_convert_fusion.1 = bf16[512,2048]{1,0:T(8,128)(2,1)} fusion(bf16[2048,1920]{1,0:T(8,128)(2,1)} %all-gather.2.cloned.1.call-done, f32[512,1280]{1,0:T(8,128)S(1)} %fusion), kind=kOutput, calls=%fused_computation.16 | convolution fusion | flops 1345191936 | bytes 7340032 | tf_op jit(solution)/shard_map/dot_general | solution.py:50
  240.7 3.3 %reshape.479 = bf16[1,512,2,4,256]{4,3,2,1,0:T(4,128)(2,1)S(1)} reshape(bf16[512,2048]{1,0:T(8,128)(2,1)} %convolution_convert_fusion.1) | data formatting | bytes 4194304 | tf_op jit(solution)/shard_map/reshape | solution.py:98
  244.0 3.0 copy.115
  247.0 4.0 %all-to-all-start.6 = ((bf16[1,512,2,4,256]{4,2,1,0,3:T(2,128)(2,1)}), bf16[1,512,2,4,256]{4,2,1,0,3:T(2,128)(2,1)S(1)}, u32[]{:S(2)}, u32[]{:S(2)}) async-start(bf16[1,512,2,4,256]{4,2,1,0,3:T(2,128)(2,1)} %copy.115), calls=%async_computation.6 | async-start | bytes 4194304 | tf_op jit(solution)/shard_map/all_to_all | solution.py:98
  251.0 0.2 convert_reduce_fusion.2
  251.3 22.6 %all-to-all-done.6 = bf16[1,512,2,4,256]{4,2,1,0,3:T(2,128)(2,1)S(1)} async-done(((bf16[1,512,2,4,256]{4,2,1,0,3:T(2,128)(2,1)}), bf16[1,512,2,4,256]{4,2,1,0,3:T(2,128)(2,1)S(1)}, u32[]{:S(2)}, u32[]{:S(2)}) %all-to-all-start.6) | async-done | bytes 2097184 | tf_op jit(solution)/shard_map/all_to_all | solution.py:98
  273.9 0.2 convert_reduce_fusion
  274.2 0.5 fusion.18
  274.8 3.0 collective-permute-start.2
  278.1 0.2 copy.118
  278.4 0.8 scatter_fusion
  279.2 0.7 copy.119
  279.9 3.9 %all-to-all-start.7 = ((bf16[2,4,128,128]{3,2,0,1:T(8,128)(2,1)}), bf16[2,4,128,128]{3,2,0,1:T(8,128)(2,1)S(1)}, u32[]{:S(2)}, u32[]{:S(2)}) async-start(bf16[2,4,128,128]{3,2,0,1:T(8,128)(2,1)} %copy.119), calls=%async_computation.7 | async-start | bytes 524288 | tf_op jit(solution)/shard_map/all_to_all | solution.py:225
  284.0 12.5 %all-to-all-done.7 = bf16[2,4,128,128]{3,2,0,1:T(8,128)(2,1)S(1)} async-done(((bf16[2,4,128,128]{3,2,0,1:T(8,128)(2,1)}), bf16[2,4,128,128]{3,2,0,1:T(8,128)(2,1)S(1)}, u32[]{:S(2)}, u32[]{:S(2)}) %all-to-all-start.7) | async-done | bytes 262176 | tf_op jit(solution)/shard_map/all_to_all | solution.py:225
  296.5 0.8 scatter_fusion.1
  297.3 1.0 fusion.20
  298.4 0.7 copy.120
  (70 shorter events, 2.0 us)
Async XLA Ops:
  7.2 2.9 copy-start
  7.2 3.8 %copy-start.7 = (f32[128,64]{0,1:T(8,128)S(1)}, f32[128,64]{0,1:T(8,128)}, u32[]{:S(2)}) copy-start(f32[128,64]{0,1:T(8,128)} %param.19) | copy-start | bytes 98308
  7.2 10.4 %copy-start.4 = (bf16[1,512,256]{2,1,0:T(8,128)(2,1)S(1)}, bf16[1,512,256]{2,1,0:T(8,128)(2,1)}, u32[]{:S(2)}) copy-start(bf16[1,512,256]{2,1,0:T(8,128)(2,1)} %param.14) | copy-start | bytes 786436
  7.2 223.0 %all-gather.2.cloned.1.call-start = ((), (), s32[]{:S(2)}) async-start(), calls=%async_computation.8 | async-start | bytes 8110080 | tf_op jit(solution)/shard_map/all_gather | solution.py:153
  11.7 14.3 %all-to-all-start.1 = ((bf16[4,64,384]{2,1,0:T(8,128)(2,1)}), bf16[4,64,384]{2,1,0:T(8,128)(2,1)S(1)}, u32[]{:S(2)}, u32[]{:S(2)}) async-start(bf16[4,64,384]{2,1,0:T(8,128)(2,1)} %broadcast_in_dim.67), calls=%async_computation.1 | async-start | bytes 393216 | tf_op jit(solution)/shard_map/all_to_all | solution.py:108
  17.6 15.1 %collective-permute-start = (bf16[1,512,256]{2,1,0:T(8,128)(2,1)S(1)}, bf16[1,512,256]{2,1,0:T(8,128)(2,1)S(1)}, u32[]{:S(2)}, u32[]{:S(2)}) collective-permute-start(bf16[1,512,256]{2,1,0:T(8,128)(2,1)S(1)} %copy-done.4), channel_id=1, source_target_pairs={{0,16},{16,0},{1,17},{17,1},{2,18},{18,2},{3,19},{19,3},{4,20},{20... | collective-permute-start | bytes 786440 | tf_op jit(solution)/shard_map/ppermute | solution.py:74
  27.2 15.0 %all-to-all-start.2 = ((bf16[4,256,384]{1,2,0:T(8,128)(2,1)}), bf16[4,256,384]{1,2,0:T(8,128)(2,1)S(1)}, u32[]{:S(2)}, u32[]{:S(2)}) async-start(bf16[4,256,384]{1,2,0:T(8,128)(2,1)} %broadcast_in_dim.69), calls=%async_computation.2 | async-start | bytes 1572864 | tf_op jit(solution)/shard_map/all_to_all | solution.py:111
  50.7 4.4 %copy-start.9 = (f32[2048]{0:T(1024)S(1)}, f32[2048]{0:T(1024)}, u32[]{:S(2)}) copy-start(f32[2048]{0:T(1024)} %param.22) | copy-start | bytes 24580
  50.7 31.1 %all-to-all-start = ((bf16[4,2,1,512,256]{4,3,1,2,0:T(8,128)(2,1)}), bf16[4,2,1,512,256]{4,3,1,2,0:T(8,128)(2,1)S(1)}, u32[]{:S(2)}, u32[]{:S(2)}) async-start(bf16[4,2,1,512,256]{4,3,1,2,0:T(8,128)(2,1)} %broadcast_in_dim.65), calls=%async_computation | async-start | bytes 4194304 | tf_op jit(solution)/shard_map/all_to_all | solution.py:87
  84.8 2.4 copy-start.2
  87.2 2.4 copy-start.11
  87.2 2.9 copy-start.12
  87.2 3.0 copy-start.5
  87.2 3.0 copy-start.6
  128.8 60.7 %collective-permute-start.1 = (f32[1,512,2,256]{3,2,1,0:T(2,128)S(1)}, f32[1,512,2,256]{3,2,1,0:T(2,128)}, u32[]{:S(2)}, u32[]{:S(2)}) collective-permute-start(f32[1,512,2,256]{3,2,1,0:T(2,128)S(1)} %bitcast.123), channel_id=1, source_target_pairs={{0,16},{16,0},{1,17},{17,1},{2,18},{18,2},{3,19},{19,3},{4,20},{20... | collective-permute-start | bytes 3145736 | tf_op jit(solution)/shard_map/ppermute | solution.py:74
  226.9 0.7 copy-start.8
  247.0 4.0 %copy-start.10 = (s32[4,4]{1,0:T(4,128)S(1)}, s32[4,4]{1,0:T(4,128)}, u32[]{:S(2)}) copy-start(s32[4,4]{1,0:T(4,128)} %param.16) | copy-start | bytes 196
  247.0 27.0 %all-to-all-start.6 = ((bf16[1,512,2,4,256]{4,2,1,0,3:T(2,128)(2,1)}), bf16[1,512,2,4,256]{4,2,1,0,3:T(2,128)(2,1)S(1)}, u32[]{:S(2)}, u32[]{:S(2)}) async-start(bf16[1,512,2,4,256]{4,2,1,0,3:T(2,128)(2,1)} %copy.115), calls=%async_computation.6 | async-start | bytes 4194304 | tf_op jit(solution)/shard_map/all_to_all | solution.py:98
  274.8 22.5 %collective-permute-start.2 = (f32[1,512,256]{2,0,1:T(1,128)S(1)}, f32[1,512,256]{2,0,1:T(1,128)S(1)}, u32[]{:S(2)}, u32[]{:S(2)}) collective-permute-start(f32[1,512,256]{2,0,1:T(1,128)S(1)} %fusion.18), channel_id=1, source_target_pairs={{0,16},{16,0},{1,17},{17,1},{2,18},{18,2},{3,19},{19,3},{4,20},{20... | collective-permute-start | bytes 1572872 | tf_op jit(solution)/shard_map/ppermute | solution.py:74
  279.9 16.6 %all-to-all-start.7 = ((bf16[2,4,128,128]{3,2,0,1:T(8,128)(2,1)}), bf16[2,4,128,128]{3,2,0,1:T(8,128)(2,1)S(1)}, u32[]{:S(2)}, u32[]{:S(2)}) async-start(bf16[2,4,128,128]{3,2,0,1:T(8,128)(2,1)} %copy.119), calls=%async_computation.7 | async-start | bytes 524288 | tf_op jit(solution)/shard_map/all_to_all | solution.py:225
  283.8 15.3 %copy-start.1 = (f32[2,64,256]{2,1,0:T(8,128)S(1)}, f32[2,64,256]{2,1,0:T(8,128)}, u32[]{:S(2)}) copy-start(f32[2,64,256]{2,1,0:T(8,128)} %param.18) | copy-start | bytes 393220
  297.3 1.8 copy-start.3
Sparse Core Ops, SparseCore 0:
  10.4 101.5 all-gather.1

commit v9 on v7

--- a/solution.py
+++ b/solution.py
@@ -95,8 +95,8 @@
     part = jnp.sum(got.astype(jnp.float32), axis=axis + 1)
     half = lax.axis_index("zh")
     mine = jnp.take(part, half, axis=axis)
-    theirs = swap_halves(jnp.take(part, 1 - half, axis=axis))
-    return mine + theirs
+    theirs = swap_halves(jnp.take(part, 1 - half, axis=axis).astype(jnp.bfloat16))
+    return mine + theirs.astype(jnp.float32)
 
 
 def gather_rows(x):

time: 306 us -> 314 us (1.026)
  the two profiles are of different devices: /device:TPU:1 before, /device:TPU:8 now
where the time goes in v9:
time: 314 us; the launch traced here: 313 us
  waiting for transfers between devices  133 us (42%)
  starting transfers between devices  60.2 us (19%)
  local copies, waits for them, and re-layouts  40.1 us (13%)
  blocking collectives  30.5 us (10%)
  other arithmetic  17.8 us (6%)
  matrix products  16 us (5%)
  between operations  15.3 us (5%)
    all_to_all x2, waiting for transfers between devices, scatter_sum_col(): got = lax.all_to_all(x.reshape(split), 'xx', axis + 1, axis + 1, tiled=True)  44.3 us
    ppermute x4, waiting for transfers between devices, swap_halves(): return lax.ppermute(x, 'zh', [(0, 1), (1, 0)])  32.2 us
    ppermute x4, starting transfers between devices, swap_halves(): return lax.ppermute(x, 'zh', [(0, 1), (1, 0)])  26.4 us
    all_to_all x1, waiting for transfers between devices, on_device(): lax.all_to_all(outgoing, 'page', split_axis=1, concat_axis=1, tiled=True)  26.2 us
    all_to_all x1, blocking collectives, gather_col(): got = lax.all_to_all(copies, 'xx', 0, 0, tiled=True)  24.5 us
    all_to_all x1, waiting for transfers between devices, gather_col(): got = lax.all_to_all(copies, 'xx', 0, 0, tiled=True)  17.6 us
    reshape x4, local copies, waits for them, and re-layouts, scatter_sum_col(): got = lax.all_to_all(x.reshape(split), 'xx', axis + 1, axis + 1, tiled=True)  13.6 us
    all_to_all x1, starting transfers between devices, on_device(): lax.all_to_all(outgoing, 'page', split_axis=1, concat_axis=1, tiled=True)  11.2 us
  transfers between devices with their start and end apart: 11, of which 9 were waited for; matrix products, arithmetic and copies ran while one was open for 16% of the time, Pallas kernels for 0%

profile of v9, /device:TPU:8, one launch (start us, length us, event | category | flops | bytes accessed | tf_op | source)
XLA Modules:
  0.0 312.7 jit_solution(426394552242245014)
XLA Ops:
  7.2 1.1 convert_bitcast_fusion
  8.3 0.9 convert_bitcast_fusion.1
  9.3 0.7 pad_maximum_fusion
  10.3 0.8 convert_element_type.149
  11.0 0.7 broadcast_in_dim.67
  11.7 5.9 %all-to-all-start.1 = ((bf16[4,64,384]{2,1,0:T(8,128)(2,1)}), bf16[4,64,384]{2,1,0:T(8,128)(2,1)S(1)}, u32[]{:S(2)}, u32[]{:S(2)}) async-start(bf16[4,64,384]{2,1,0:T(8,128)(2,1)} %broadcast_in_dim.67), calls=%async_computation.1 | async-start | bytes 393216 | tf_op jit(solution)/shard_map/all_to_all | solution.py:104
  17.6 4.8 %collective-permute-start = (bf16[1,512,256]{2,1,0:T(8,128)(2,1)S(1)}, bf16[1,512,256]{2,1,0:T(8,128)(2,1)S(1)}, u32[]{:S(2)}, u32[]{:S(2)}) collective-permute-start(bf16[1,512,256]{2,1,0:T(8,128)(2,1)S(1)} %copy-done.5), channel_id=1, source_target_pairs={{0,16},{16,0},{1,17},{17,1},{2,18},{18,2},{3,19},{19,3},{4,20},{20... | collective-permute-start | bytes 786440 | tf_op jit(solution)/shard_map/ppermute | solution.py:74
  22.4 3.6 %all-to-all-done.1 = bf16[4,64,384]{2,1,0:T(8,128)(2,1)S(1)} async-done(((bf16[4,64,384]{2,1,0:T(8,128)(2,1)}), bf16[4,64,384]{2,1,0:T(8,128)(2,1)S(1)}, u32[]{:S(2)}, u32[]{:S(2)}) %all-to-all-start.1) | async-done | bytes 196640 | tf_op jit(solution)/shard_map/all_to_all | solution.py:104
  26.2 1.0 broadcast_in_dim.69
  27.2 4.9 %all-to-all-start.2 = ((bf16[4,256,384]{1,2,0:T(8,128)(2,1)}), bf16[4,256,384]{1,2,0:T(8,128)(2,1)S(1)}, u32[]{:S(2)}, u32[]{:S(2)}) async-start(bf16[4,256,384]{1,2,0:T(8,128)(2,1)} %broadcast_in_dim.69), calls=%async_computation.2 | async-start | bytes 1572864 | tf_op jit(solution)/shard_map/all_to_all | solution.py:107
  32.1 0.6 collective-permute-done
  32.8 0.5 copy.127
  33.4 8.9 %all-to-all-done.2 = bf16[4,256,384]{1,2,0:T(8,128)(2,1)S(1)} async-done(((bf16[4,256,384]{1,2,0:T(8,128)(2,1)}), bf16[4,256,384]{1,2,0:T(8,128)(2,1)S(1)}, u32[]{:S(2)}, u32[]{:S(2)}) %all-to-all-start.2) | async-done | bytes 786464 | tf_op jit(solution)/shard_map/all_to_all | solution.py:107
  42.3 0.6 copy.132
  42.9 0.4 broadcast_in_dim.70
  43.3 5.9 %all_to_all.40 = bf16[4,2,256,384]{2,0,3,1:T(4,128)(2,1)} all-to-all(bf16[4,2,256,384]{2,0,3,1:T(4,128)(2,1)S(1)} %broadcast_in_dim.70), channel_id=1, replica_groups=mesh['ry'=4,'rc'=2,'zh'=2,'xx'=4,'page'=4] {'rc'}, dimensions={1} | all-to-all | bytes 3145728 | tf_op jit(solution)/shard_map/all_to_all | solution.py:110
  49.2 2.5 broadcast_in_dim.66
  51.7 4.4 %all-to-all-start = ((bf16[4,2,1,512,256]{4,1,3,2,0:T(2,128)(2,1)}), bf16[4,2,1,512,256]{4,1,3,2,0:T(2,128)(2,1)S(1)}, u32[]{:S(2)}, u32[]{:S(2)}) async-start(bf16[4,2,1,512,256]{4,1,3,2,0:T(2,128)(2,1)} %broadcast_in_dim.66), calls=%async_computation | async-start | bytes 4194304 | tf_op jit(solution)/shard_map/all_to_all | solution.py:83
  56.8 1.0 fusion.36
  57.8 0.8 fusion.9
  58.6 3.8 %copy.133 = bf16[4,2,256,384]{3,2,1,0:T(8,128)(2,1)} copy(bf16[4,2,256,384]{2,0,3,1:T(4,128)(2,1)} %all_to_all.40) | data formatting | bytes 3145728 | tf_op jit(solution)/shard_map/all_to_all | solution.py:110
  62.4 1.3 slice_bitcast_fusion
  63.7 1.4 copy.134
  65.2 17.6 %all-to-all-done = bf16[4,2,1,512,256]{4,1,3,2,0:T(2,128)(2,1)S(1)} async-done(((bf16[4,2,1,512,256]{4,1,3,2,0:T(2,128)(2,1)}), bf16[4,2,1,512,256]{4,1,3,2,0:T(2,128)(2,1)S(1)}, u32[]{:S(2)}, u32[]{:S(2)}) %all-to-all-start) | async-done | bytes 2097184 | tf_op jit(solution)/shard_map/all_to_all | solution.py:83
  82.7 0.4 copy_convert_fusion.1
  83.5 0.5 fusion.5
  84.0 2.5 copy.129
  86.5 2.4 convolution_bitcast_fusion
  89.9 0.7 fusion.6
  90.6 0.7 fusion.8
  91.3 1.8 convolution_convert_fusion
  93.1 2.8 reshape.448
  96.0 4.5 %copy.137 = bf16[1,512,2,4,256]{4,2,1,0,3:T(2,128)(2,1)} copy(bf16[1,512,2,4,256]{4,3,2,1,0:T(4,128)(2,1)} %reshape.448) | data formatting | bytes 4194304 | tf_op jit(solution)/shard_map/reshape | solution.py:94
  100.5 3.6 %all-to-all-start.4 = ((bf16[1,512,2,4,256]{4,2,1,0,3:T(2,128)(2,1)}), bf16[1,512,2,4,256]{4,2,1,0,3:T(2,128)(2,1)S(1)}, u32[]{:S(2)}, u32[]{:S(2)}) async-start(bf16[1,512,2,4,256]{4,2,1,0,3:T(2,128)(2,1)} %copy.137), calls=%async_computation.4 | async-start | bytes 4194304 | tf_op jit(solution)/shard_map/all_to_all | solution.py:94
  104.1 25.7 %all-to-all-done.4 = bf16[1,512,2,4,256]{4,2,1,0,3:T(2,128)(2,1)S(1)} async-done(((bf16[1,512,2,4,256]{4,2,1,0,3:T(2,128)(2,1)}), bf16[1,512,2,4,256]{4,2,1,0,3:T(2,128)(2,1)S(1)}, u32[]{:S(2)}, u32[]{:S(2)}) %all-to-all-start.4) | async-done | bytes 2097184 | tf_op jit(solution)/shard_map/all_to_all | solution.py:94
  130.1 0.8 copy.184
  130.9 0.5 fusion.19
  131.4 16.3 %collective-permute-start.1 = (bf16[1,512,256]{2,0,1:T(2,128)(2,1)S(1)}, bf16[1,512,256]{2,0,1:T(2,128)(2,1)S(1)}, u32[]{:S(2)}, u32[]{:S(2)}) collective-permute-start(bf16[1,512,256]{2,0,1:T(2,128)(2,1)S(1)} %fusion.19), channel_id=1, source_target_pairs={{0,16},{16,0},{1,17},{17,1},{2,18},{18,2},{3,19},{19,3},{4,20},{20... | collective-permute-start | bytes 786440 | tf_op jit(solution)/shard_map/ppermute | solution.py:74
  147.8 21.8 %collective-permute-done.1 = bf16[1,512,256]{2,0,1:T(2,128)(2,1)S(1)} collective-permute-done((bf16[1,512,256]{2,0,1:T(2,128)(2,1)S(1)}, bf16[1,512,256]{2,0,1:T(2,128)(2,1)S(1)}, u32[]{:S(2)}, u32[]{:S(2)}) %collective-permute-start.1) | collective-permute-done | bytes 262176 | tf_op jit(solution)/shard_map/ppermute | solution.py:74
  169.5 0.9 fusion.23
  170.5 3.2 %collective-permute-start.2 = (bf16[1,512,256]{2,1,0:T(8,128)(2,1)S(1)}, bf16[1,512,256]{2,1,0:T(8,128)(2,1)S(1)}, u32[]{:S(2)}, u32[]{:S(2)}) collective-permute-start(bf16[1,512,256]{2,1,0:T(8,128)(2,1)S(1)} %copy.142), channel_id=1, source_target_pairs={{0,16},{16,0},{1,17},{17,1},{2,18},{18,2},{3,19},{19,3},{4,20},{20... | collective-permute-start | bytes 786440 | tf_op jit(solution)/shard_map/ppermute | solution.py:74
  173.7 9.8 %collective-permute-done.2 = bf16[1,512,256]{2,1,0:T(8,128)(2,1)S(1)} collective-permute-done((bf16[1,512,256]{2,1,0:T(8,128)(2,1)S(1)}, bf16[1,512,256]{2,1,0:T(8,128)(2,1)S(1)}, u32[]{:S(2)}, u32[]{:S(2)}) %collective-permute-start.2) | collective-permute-done | bytes 262176 | tf_op jit(solution)/shard_map/ppermute | solution.py:74
  183.6 0.8 broadcast_select_fusion
  184.6 24.5 %all_to_all.41 = bf16[4,2,1,512,256]{4,3,1,2,0:T(8,128)(2,1)S(1)} all-to-all(bf16[4,2,1,512,256]{4,3,1,2,0:T(8,128)(2,1)S(1)} %broadcast_in_dim.79), channel_id=1, replica_groups=mesh['ry'=4,'rc'=2,'zh'=2,'xx'=4,'page'=4] {'xx'}, dimensions={0} | all-to-all | bytes 4194304 | tf_op jit(solution)/shard_map/all_to_all | solution.py:83
  209.2 2.4 copy_convert_fusion
  211.6 5.4 %copy.146 = f32[1,512,8,256]{1,3,2,0:T(8,128)} copy(f32[1,512,8,256]{3,1,2,0:T(8,128)} %bitcast.122) | data formatting | bytes 8388608 | tf_op jit(solution)/shard_map/convert_element_type | solution.py:181
  216.9 0.5 multiply_reduce_fusion
  217.6 2.6 fusion.3
  220.3 5.4 %fusion = f32[512,1280]{1,0:T(8,128)S(1)} fusion(bf16[512,2048]{0,1:T(8,128)(2,1)S(1)} %fusion.3, bf16[2048,1920]{1,0:T(8,128)(2,1)} %all-gather.2.cloned.1.call-done), kind=kOutput, calls=%fused_computation.2 | convolution fusion | flops 2684354560 | bytes 9961472 | tf_op jit(solution)/shard_map/dot_general | solution.py:182
  225.7 5.0 %convolution_convert_fusion.1 = bf16[512,2048]{1,0:T(8,128)(2,1)} fusion(bf16[2048,1920]{1,0:T(8,128)(2,1)} %all-gather.2.cloned.1.call-done, f32[512,1280]{1,0:T(8,128)S(1)} %fusion), kind=kOutput, calls=%fused_computation.13 | convolution fusion | flops 1345191936 | bytes 7340032 | tf_op jit(solution)/shard_map/dot_general | solution.py:50
  230.7 3.3 %reshape.450 = bf16[1,512,2,4,256]{4,3,2,1,0:T(4,128)(2,1)S(1)} reshape(bf16[512,2048]{1,0:T(8,128)(2,1)} %convolution_convert_fusion.1) | data formatting | bytes 4194304 | tf_op jit(solution)/shard_map/reshape | solution.py:94
  234.0 3.0 copy.148
  236.9 3.7 %all-to-all-start.6 = ((bf16[1,512,2,4,256]{4,2,1,0,3:T(2,128)(2,1)}), bf16[1,512,2,4,256]{4,2,1,0,3:T(2,128)(2,1)S(1)}, u32[]{:S(2)}, u32[]{:S(2)}) async-start(bf16[1,512,2,4,256]{4,2,1,0,3:T(2,128)(2,1)} %copy.148), calls=%async_computation.6 | async-start | bytes 4194304 | tf_op jit(solution)/shard_map/all_to_all | solution.py:94
  241.8 0.8 scatter_fusion
  242.6 0.7 copy.152
  243.3 18.6 %all-to-all-done.6 = bf16[1,512,2,4,256]{4,2,1,0,3:T(2,128)(2,1)S(1)} async-done(((bf16[1,512,2,4,256]{4,2,1,0,3:T(2,128)(2,1)}), bf16[1,512,2,4,256]{4,2,1,0,3:T(2,128)(2,1)S(1)}, u32[]{:S(2)}, u32[]{:S(2)}) %all-to-all-start.6) | async-done | bytes 2097184 | tf_op jit(solution)/shard_map/all_to_all | solution.py:94
  261.9 11.2 %all-to-all-start.7 = ((bf16[2,4,128,128]{3,2,0,1:T(8,128)(2,1)}), bf16[2,4,128,128]{3,2,0,1:T(8,128)(2,1)S(1)}, u32[]{:S(2)}, u32[]{:S(2)}) async-start(bf16[2,4,128,128]{3,2,0,1:T(8,128)(2,1)} %copy.152), calls=%async_computation.7 | async-start | bytes 524288 | tf_op jit(solution)/shard_map/all_to_all | solution.py:213
  273.3 1.0 copy-done.2
  274.3 0.4 fusion.21
  274.8 2.1 collective-permute-start.3
  276.9 26.2 %all-to-all-done.7 = bf16[2,4,128,128]{3,2,0,1:T(8,128)(2,1)S(1)} async-done(((bf16[2,4,128,128]{3,2,0,1:T(8,128)(2,1)}), bf16[2,4,128,128]{3,2,0,1:T(8,128)(2,1)S(1)}, u32[]{:S(2)}, u32[]{:S(2)}) %all-to-all-start.7) | async-done | bytes 262176 | tf_op jit(solution)/shard_map/all_to_all | solution.py:213
  303.1 0.8 scatter_fusion.1
  303.9 1.2 fusion.24
  305.1 0.7 copy.153
  (85 shorter events, 3.9 us)
Async XLA Ops:
  7.2 2.9 copy-start
  7.2 3.8 %copy-start.10 = (f32[128,64]{0,1:T(8,128)S(1)}, f32[128,64]{0,1:T(8,128)}, u32[]{:S(2)}) copy-start(f32[128,64]{0,1:T(8,128)} %param.19) | copy-start | bytes 98308
  7.2 10.4 %copy-start.5 = (bf16[1,512,256]{2,1,0:T(8,128)(2,1)S(1)}, bf16[1,512,256]{2,1,0:T(8,128)(2,1)}, u32[]{:S(2)}) copy-start(bf16[1,512,256]{2,1,0:T(8,128)(2,1)} %param.14) | copy-start | bytes 786436
  7.2 213.1 %all-gather.2.cloned.1.call-start = ((), (), s32[]{:S(2)}) async-start(), calls=%async_computation.8 | async-start | bytes 8110080 | tf_op jit(solution)/shard_map/all_gather | solution.py:149
  11.7 14.3 %all-to-all-start.1 = ((bf16[4,64,384]{2,1,0:T(8,128)(2,1)}), bf16[4,64,384]{2,1,0:T(8,128)(2,1)S(1)}, u32[]{:S(2)}, u32[]{:S(2)}) async-start(bf16[4,64,384]{2,1,0:T(8,128)(2,1)} %broadcast_in_dim.67), calls=%async_computation.1 | async-start | bytes 393216 | tf_op jit(solution)/shard_map/all_to_all | solution.py:104
  17.6 15.1 %collective-permute-start = (bf16[1,512,256]{2,1,0:T(8,128)(2,1)S(1)}, bf16[1,512,256]{2,1,0:T(8,128)(2,1)S(1)}, u32[]{:S(2)}, u32[]{:S(2)}) collective-permute-start(bf16[1,512,256]{2,1,0:T(8,128)(2,1)S(1)} %copy-done.5), channel_id=1, source_target_pairs={{0,16},{16,0},{1,17},{17,1},{2,18},{18,2},{3,19},{19,3},{4,20},{20... | collective-permute-start | bytes 786440 | tf_op jit(solution)/shard_map/ppermute | solution.py:74
  27.2 15.0 %all-to-all-start.2 = ((bf16[4,256,384]{1,2,0:T(8,128)(2,1)}), bf16[4,256,384]{1,2,0:T(8,128)(2,1)S(1)}, u32[]{:S(2)}, u32[]{:S(2)}) async-start(bf16[4,256,384]{1,2,0:T(8,128)(2,1)} %broadcast_in_dim.69), calls=%async_computation.2 | async-start | bytes 1572864 | tf_op jit(solution)/shard_map/all_to_all | solution.py:107
  51.7 4.5 %copy-start.12 = (f32[2048]{0:T(1024)S(1)}, f32[2048]{0:T(1024)}, u32[]{:S(2)}) copy-start(f32[2048]{0:T(1024)} %param.22) | copy-start | bytes 24580
  51.7 31.1 %all-to-all-start = ((bf16[4,2,1,512,256]{4,1,3,2,0:T(2,128)(2,1)}), bf16[4,2,1,512,256]{4,1,3,2,0:T(2,128)(2,1)S(1)}, u32[]{:S(2)}, u32[]{:S(2)}) async-start(bf16[4,2,1,512,256]{4,1,3,2,0:T(2,128)(2,1)} %broadcast_in_dim.66), calls=%async_computation | async-start | bytes 4194304 | tf_op jit(solution)/shard_map/all_to_all | solution.py:83
  84.0 2.5 copy-start.4
  86.5 2.5 copy-start.14
  86.5 3.0 copy-start.15
  86.5 3.1 copy-start.8
  86.5 3.1 copy-start.9
  88.9 1.0 copy-start.7
  100.5 29.4 %all-to-all-start.4 = ((bf16[1,512,2,4,256]{4,2,1,0,3:T(2,128)(2,1)}), bf16[1,512,2,4,256]{4,2,1,0,3:T(2,128)(2,1)S(1)}, u32[]{:S(2)}, u32[]{:S(2)}) async-start(bf16[1,512,2,4,256]{4,2,1,0,3:T(2,128)(2,1)} %copy.137), calls=%async_computation.4 | async-start | bytes 4194304 | tf_op jit(solution)/shard_map/all_to_all | solution.py:94
  131.4 38.1 %collective-permute-start.1 = (bf16[1,512,256]{2,0,1:T(2,128)(2,1)S(1)}, bf16[1,512,256]{2,0,1:T(2,128)(2,1)S(1)}, u32[]{:S(2)}, u32[]{:S(2)}) collective-permute-start(bf16[1,512,256]{2,0,1:T(2,128)(2,1)S(1)} %fusion.19), channel_id=1, source_target_pairs={{0,16},{16,0},{1,17},{17,1},{2,18},{18,2},{3,19},{19,3},{4,20},{20... | collective-permute-start | bytes 786440 | tf_op jit(solution)/shard_map/ppermute | solution.py:74
  170.5 13.0 %collective-permute-start.2 = (bf16[1,512,256]{2,1,0:T(8,128)(2,1)S(1)}, bf16[1,512,256]{2,1,0:T(8,128)(2,1)S(1)}, u32[]{:S(2)}, u32[]{:S(2)}) collective-permute-start(bf16[1,512,256]{2,1,0:T(8,128)(2,1)S(1)} %copy.142), channel_id=1, source_target_pairs={{0,16},{16,0},{1,17},{17,1},{2,18},{18,2},{3,19},{19,3},{4,20},{20... | collective-permute-start | bytes 786440 | tf_op jit(solution)/shard_map/ppermute | solution.py:74
  216.9 0.7 copy-start.11
  236.9 3.8 %copy-start.13 = (s32[4,4]{1,0:T(4,128)S(1)}, s32[4,4]{1,0:T(4,128)}, u32[]{:S(2)}) copy-start(s32[4,4]{1,0:T(4,128)} %param.16) | copy-start | bytes 196
  236.9 24.9 %all-to-all-start.6 = ((bf16[1,512,2,4,256]{4,2,1,0,3:T(2,128)(2,1)}), bf16[1,512,2,4,256]{4,2,1,0,3:T(2,128)(2,1)S(1)}, u32[]{:S(2)}, u32[]{:S(2)}) async-start(bf16[1,512,2,4,256]{4,2,1,0,3:T(2,128)(2,1)} %copy.148), calls=%async_computation.6 | async-start | bytes 4194304 | tf_op jit(solution)/shard_map/all_to_all | solution.py:94
  261.9 41.2 %all-to-all-start.7 = ((bf16[2,4,128,128]{3,2,0,1:T(8,128)(2,1)}), bf16[2,4,128,128]{3,2,0,1:T(8,128)(2,1)S(1)}, u32[]{:S(2)}, u32[]{:S(2)}) async-start(bf16[2,4,128,128]{3,2,0,1:T(8,128)(2,1)} %copy.152), calls=%async_computation.7 | async-start | bytes 524288 | tf_op jit(solution)/shard_map/all_to_all | solution.py:213
  273.3 1.0 copy-start.2
  274.3 29.6 %copy-start.3 = (f32[512,2,256]{2,0,1:T(8,128)S(1)}, f32[512,2,256]{2,0,1:T(8,128)}, u32[]{:S(2)}) copy-start(f32[512,2,256]{2,0,1:T(8,128)} %copy-done.2) | copy-start | bytes 3145732
  274.8 29.2 %collective-permute-start.3 = (bf16[1,512,256]{2,0,1:T(2,128)(2,1)S(1)}, bf16[1,512,256]{2,0,1:T(2,128)(2,1)S(1)}, u32[]{:S(2)}, u32[]{:S(2)}) collective-permute-start(bf16[1,512,256]{2,0,1:T(2,128)(2,1)S(1)} %fusion.21), channel_id=1, source_target_pairs={{0,16},{16,0},{1,17},{17,1},{2,18},{18,2},{3,19},{19,3},{4,20},{20... | collective-permute-start | bytes 786440 | tf_op jit(solution)/shard_map/ppermute | solution.py:74
  303.1 2.8 copy-start.1
  303.9 2.0 copy-start.6
Sparse Core Ops, SparseCore 0:
  10.4 101.5 all-gather.1

commit v10 on v9

--- a/solution.py
+++ b/solution.py
@@ -109,6 +109,37 @@
     got = jnp.broadcast_to(got[:, None], (chips, cores) + got.shape[1:])
     got = lax.all_to_all(got, "rc", 1, 1, tiled=True)
     return got.reshape((-1,) + x.shape[1:])
+
+
+def send_pages(keys_rot, values_in, lengths, page_slot):
+    prompt_count, seq_len, local_heads, head_dim = keys_rot.shape
+    local_width = local_heads * head_dim
+    page_count = lax.axis_size("page")
+    page_index = lax.axis_index("page")
+    blocks_each = prompt_count * (seq_len // PAGE_LEN)
+    capacity = blocks_each // page_count
+    owners = page_slot // blocks_each
+    local_slot = page_slot % blocks_each
+    same_owner = owners[:, :, None] == owners[:, None, :]
+    earlier = (
+        jnp.arange(blocks_each, dtype=jnp.int32)[None, :]
+        < jnp.arange(blocks_each, dtype=jnp.int32)[:, None]
+    )
+    order_in = jnp.sum((same_owner & earlier[None]).astype(jnp.int32), axis=2)
+    my_owners = lax.dynamic_index_in_dim(owners, page_index, 0, keepdims=False)
+    my_order = lax.dynamic_index_in_dim(order_in, page_index, 0, keepdims=False)
+    send_pos = my_owners * capacity + my_order
+    live_rows = (jnp.arange(seq_len, dtype=jnp.int32)[None, :] < lengths[:, None])[:, :, None, None]
+    page_keys = jnp.where(live_rows, keys_rot, jnp.zeros_like(keys_rot)).reshape(
+        blocks_each, PAGE_LEN, local_width
+    )
+    page_values = jnp.where(live_rows, values_in, jnp.zeros_like(values_in)).reshape(
+        blocks_each, PAGE_LEN, local_width
+    )
+    stacked = jnp.stack([page_keys, page_values])
+    outgoing = jnp.zeros_like(stacked).at[:, send_pos].set(stacked)
+    incoming = lax.all_to_all(outgoing, "page", split_axis=1, concat_axis=1, tiled=True)
+    return incoming
 
 
 def on_device(
@@ -173,6 +204,8 @@
             for i in range(prompt_count)
         ]
     )
+    incoming = send_pages(keys_rot, values_in, lengths, page_slot)
+    incoming, attended = lax.optimization_barrier((incoming, attended))
     attn_terms = contract_rows(attended.reshape(-1, local_width), out_t)
     attn_terms = attn_terms.reshape(prompt_count, seq_len, model_width).astype(jnp.bfloat16)
     attn_sum = scatter_sum_col(attn_terms, 2)
@@ -186,8 +219,8 @@
     ffn_terms = contract_rows(hidden, down_t).reshape(prompt_count, seq_len, model_width)
     ffn_sum = scatter_sum_col(ffn_terms.astype(jnp.bfloat16), 2)
     layer_out = (residual.astype(jnp.float32) + ffn_sum).astype(jnp.bfloat16)
+    page_index = lax.axis_index("page")
     page_count = lax.axis_size("page")
-    page_index = lax.axis_index("page")
     blocks_each = prompt_count * (seq_len // PAGE_LEN)
     capacity = blocks_each // page_count
     owners = page_slot // blocks_each
@@ -198,19 +231,6 @@
         < jnp.arange(blocks_each, dtype=jnp.int32)[:, None]
     )
     order_in = jnp.sum((same_owner & earlier[None]).astype(jnp.int32), axis=2)
-    my_owners = lax.dynamic_index_in_dim(owners, page_index, 0, keepdims=False)
-    my_order = lax.dynamic_index_in_dim(order_in, page_index, 0, keepdims=False)
-    send_pos = my_owners * capacity + my_order
-    live_rows = (jnp.arange(seq_len, dtype=jnp.int32)[None, :] < lengths[:, None])[:, :, None, None]
-    page_keys = jnp.where(live_rows, keys_rot, jnp.zeros_like(keys_rot)).reshape(
-        blocks_each, PAGE_LEN, local_width
-    )
-    page_values = jnp.where(live_rows, values_in, jnp.zeros_like(values_in)).reshape(
-        blocks_each, PAGE_LEN, local_width
-    )
-    stacked = jnp.stack([page_keys, page_values])
-    outgoing = jnp.zeros_like(stacked).at[:, send_pos].set(stacked)
-    incoming = lax.all_to_all(outgoing, "page", split_axis=1, concat_axis=1, tiled=True)
     arrival_hit = (owners[:, None, :] == page_index) & (
         order_in[:, None, :] == jnp.arange(capacity, dtype=jnp.int32)[None, :, None]
     )

time: 314 us -> 307 us (0.978)
  the two profiles are of different devices: /device:TPU:8 before, /device:TPU:56 now
where the time goes in v10:
time: 307 us; the launch traced here: 306 us
  waiting for transfers between devices  125 us (41%)
  starting transfers between devices  56.9 us (19%)
  local copies, waits for them, and re-layouts  39.9 us (13%)
  blocking collectives  34.5 us (11%)
  other arithmetic  18.4 us (6%)
  matrix products  15.9 us (5%)
  between operations  15.3 us (5%)
    all_to_all x2, waiting for transfers between devices, scatter_sum_col(): got = lax.all_to_all(x.reshape(split), 'xx', axis + 1, axis + 1, tiled=True)  49.8 us
    ppermute x4, waiting for transfers between devices, swap_halves(): return lax.ppermute(x, 'zh', [(0, 1), (1, 0)])  48 us
    all_to_all x1, blocking collectives, gather_col(): got = lax.all_to_all(copies, 'xx', 0, 0, tiled=True)  28.6 us
    ppermute x4, starting transfers between devices, swap_halves(): return lax.ppermute(x, 'zh', [(0, 1), (1, 0)])  27.4 us
    all_to_all x1, waiting for transfers between devices, gather_col(): got = lax.all_to_all(copies, 'xx', 0, 0, tiled=True)  17.3 us
    reshape x4, local copies, waits for them, and re-layouts, scatter_sum_col(): got = lax.all_to_all(x.reshape(split), 'xx', axis + 1, axis + 1, tiled=True)  13.6 us
    all_to_all x2, starting transfers between devices, scatter_sum_col(): got = lax.all_to_all(x.reshape(split), 'xx', axis + 1, axis + 1, tiled=True)  7.21 us
    all_to_all x1, starting transfers between devices, send_pages(): lax.all_to_all(outgoing, 'page', split_axis=1, concat_axis=1, tiled=True)  7.08 us
  transfers between devices with their start and end apart: 11, of which 10 were waited for; matrix products, arithmetic and copies ran while one was open for 17% of the time, Pallas kernels for 0%

profile of v10, /device:TPU:56, one launch (start us, length us, event | category | flops | bytes accessed | tf_op | source)
XLA Modules:
  0.0 306.1 jit_solution(7499101261071526777)
XLA Ops:
  7.2 1.1 convert_bitcast_fusion
  8.3 0.9 convert_bitcast_fusion.1
  9.3 0.7 pad_maximum_fusion
  10.3 0.8 convert_element_type.151
  11.1 0.7 broadcast_in_dim.74
  11.7 6.0 %all-to-all-start.1 = ((bf16[4,64,384]{2,1,0:T(8,128)(2,1)}), bf16[4,64,384]{2,1,0:T(8,128)(2,1)S(1)}, u32[]{:S(2)}, u32[]{:S(2)}) async-start(bf16[4,64,384]{2,1,0:T(8,128)(2,1)} %broadcast_in_dim.74), calls=%async_computation.1 | async-start | bytes 393216 | tf_op jit(solution)/shard_map/all_to_all | solution.py:104
  17.8 4.6 %collective-permute-start = (bf16[1,512,256]{2,1,0:T(8,128)(2,1)S(1)}, bf16[1,512,256]{2,1,0:T(8,128)(2,1)S(1)}, u32[]{:S(2)}, u32[]{:S(2)}) collective-permute-start(bf16[1,512,256]{2,1,0:T(8,128)(2,1)S(1)} %copy-done.5), channel_id=1, source_target_pairs={{0,16},{16,0},{1,17},{17,1},{2,18},{18,2},{3,19},{19,3},{4,20},{20... | collective-permute-start | bytes 786440 | tf_op jit(solution)/shard_map/ppermute | solution.py:74
  23.0 0.7 all-to-all-done.1
  23.9 1.0 broadcast_in_dim.76
  24.9 4.7 %all-to-all-start.2 = ((bf16[4,256,384]{1,2,0:T(8,128)(2,1)}), bf16[4,256,384]{1,2,0:T(8,128)(2,1)S(1)}, u32[]{:S(2)}, u32[]{:S(2)}) async-start(bf16[4,256,384]{1,2,0:T(8,128)(2,1)} %broadcast_in_dim.76), calls=%async_computation.2 | async-start | bytes 1572864 | tf_op jit(solution)/shard_map/all_to_all | solution.py:107
  29.6 7.3 %collective-permute-done = bf16[1,512,256]{2,1,0:T(8,128)(2,1)S(1)} collective-permute-done((bf16[1,512,256]{2,1,0:T(8,128)(2,1)S(1)}, bf16[1,512,256]{2,1,0:T(8,128)(2,1)S(1)}, u32[]{:S(2)}, u32[]{:S(2)}) %collective-permute-start) | collective-permute-done | bytes 262176 | tf_op jit(solution)/shard_map/ppermute | solution.py:74
  37.0 0.5 copy.127
  37.6 2.4 all-to-all-done.2
  39.9 0.6 copy.132
  41.0 5.9 %all_to_all.40 = bf16[4,2,256,384]{2,0,3,1:T(4,128)(2,1)} all-to-all(bf16[4,2,256,384]{2,0,3,1:T(4,128)(2,1)S(1)} %broadcast_in_dim.77), channel_id=1, replica_groups=mesh['ry'=4,'rc'=2,'zh'=2,'xx'=4,'page'=4] {'rc'}, dimensions={1} | all-to-all | bytes 3145728 | tf_op jit(solution)/shard_map/all_to_all | solution.py:110
  46.9 2.5 broadcast_in_dim.70
  49.4 4.5 %all-to-all-start = ((bf16[4,2,1,512,256]{4,1,3,2,0:T(2,128)(2,1)}), bf16[4,2,1,512,256]{4,1,3,2,0:T(2,128)(2,1)S(1)}, u32[]{:S(2)}, u32[]{:S(2)}) async-start(bf16[4,2,1,512,256]{4,1,3,2,0:T(2,128)(2,1)} %broadcast_in_dim.70), calls=%async_computation | async-start | bytes 4194304 | tf_op jit(solution)/shard_map/all_to_all | solution.py:83
  53.8 0.6 add_compare_fusion
  54.7 1.0 fusion.34
  55.7 0.8 fusion.9
  56.5 3.8 %copy.133 = bf16[4,2,256,384]{3,2,1,0:T(8,128)(2,1)} copy(bf16[4,2,256,384]{2,0,3,1:T(4,128)(2,1)} %all_to_all.40) | data formatting | bytes 3145728 | tf_op jit(solution)/shard_map/all_to_all | solution.py:110
  60.4 1.3 slice_bitcast_fusion
  61.7 1.4 copy.134
  63.1 17.3 %all-to-all-done = bf16[4,2,1,512,256]{4,1,3,2,0:T(2,128)(2,1)S(1)} async-done(((bf16[4,2,1,512,256]{4,1,3,2,0:T(2,128)(2,1)}), bf16[4,2,1,512,256]{4,1,3,2,0:T(2,128)(2,1)S(1)}, u32[]{:S(2)}, u32[]{:S(2)}) %all-to-all-start) | async-done | bytes 2097184 | tf_op jit(solution)/shard_map/all_to_all | solution.py:83
  81.2 0.5 fusion.5
  81.7 2.5 copy.129
  84.2 2.3 convolution_bitcast_fusion
  87.8 0.8 scatter_fusion
  88.5 0.7 copy.137
  89.3 7.1 %all-to-all-start.4 = ((bf16[2,4,128,128]{3,2,0,1:T(8,128)(2,1)}), bf16[2,4,128,128]{3,2,0,1:T(8,128)(2,1)S(1)}, u32[]{:S(2)}, u32[]{:S(2)}) async-start(bf16[2,4,128,128]{3,2,0,1:T(8,128)(2,1)} %copy.137), calls=%async_computation.4 | async-start | bytes 524288 | tf_op jit(solution)/shard_map/all_to_all | solution.py:141
  96.6 0.7 fusion.6
  97.3 0.7 fusion.8
  98.0 7.0 %all-to-all-done.4 = bf16[2,4,128,128]{3,2,0,1:T(8,128)(2,1)S(1)} async-done(((bf16[2,4,128,128]{3,2,0,1:T(8,128)(2,1)}), bf16[2,4,128,128]{3,2,0,1:T(8,128)(2,1)S(1)}, u32[]{:S(2)}, u32[]{:S(2)}) %all-to-all-start.4) | async-done | bytes 262176 | tf_op jit(solution)/shard_map/all_to_all | solution.py:141
  105.1 1.8 convolution_convert_fusion
  106.8 2.8 reshape.452
  109.6 4.5 %copy.139 = bf16[1,512,2,4,256]{4,2,1,0,3:T(2,128)(2,1)} copy(bf16[1,512,2,4,256]{4,3,2,1,0:T(4,128)(2,1)} %reshape.452) | data formatting | bytes 4194304 | tf_op jit(solution)/shard_map/reshape | solution.py:94
  114.1 3.6 %all-to-all-start.5 = ((bf16[1,512,2,4,256]{4,2,1,0,3:T(2,128)(2,1)}), bf16[1,512,2,4,256]{4,2,1,0,3:T(2,128)(2,1)S(1)}, u32[]{:S(2)}, u32[]{:S(2)}) async-start(bf16[1,512,2,4,256]{4,2,1,0,3:T(2,128)(2,1)} %copy.139), calls=%async_computation.5 | async-start | bytes 4194304 | tf_op jit(solution)/shard_map/all_to_all | solution.py:94
  117.8 24.7 %all-to-all-done.5 = bf16[1,512,2,4,256]{4,2,1,0,3:T(2,128)(2,1)S(1)} async-done(((bf16[1,512,2,4,256]{4,2,1,0,3:T(2,128)(2,1)}), bf16[1,512,2,4,256]{4,2,1,0,3:T(2,128)(2,1)S(1)}, u32[]{:S(2)}, u32[]{:S(2)}) %all-to-all-start.5) | async-done | bytes 2097184 | tf_op jit(solution)/shard_map/all_to_all | solution.py:94
  142.7 0.8 copy.184
  143.5 0.5 fusion.19
  144.0 12.7 %collective-permute-start.1 = (bf16[1,512,256]{2,0,1:T(2,128)(2,1)S(1)}, bf16[1,512,256]{2,0,1:T(2,128)(2,1)S(1)}, u32[]{:S(2)}, u32[]{:S(2)}) collective-permute-start(bf16[1,512,256]{2,0,1:T(2,128)(2,1)S(1)} %fusion.19), channel_id=1, source_target_pairs={{0,16},{16,0},{1,17},{17,1},{2,18},{18,2},{3,19},{19,3},{4,20},{20... | collective-permute-start | bytes 786440 | tf_op jit(solution)/shard_map/ppermute | solution.py:74
  156.8 21.8 %collective-permute-done.1 = bf16[1,512,256]{2,0,1:T(2,128)(2,1)S(1)} collective-permute-done((bf16[1,512,256]{2,0,1:T(2,128)(2,1)S(1)}, bf16[1,512,256]{2,0,1:T(2,128)(2,1)S(1)}, u32[]{:S(2)}, u32[]{:S(2)}) %collective-permute-start.1) | collective-permute-done | bytes 262176 | tf_op jit(solution)/shard_map/ppermute | solution.py:74
  178.6 0.9 fusion.23
  179.6 5.6 %collective-permute-start.2 = (bf16[1,512,256]{2,1,0:T(8,128)(2,1)S(1)}, bf16[1,512,256]{2,1,0:T(8,128)(2,1)S(1)}, u32[]{:S(2)}, u32[]{:S(2)}) collective-permute-start(bf16[1,512,256]{2,1,0:T(8,128)(2,1)S(1)} %copy.144), channel_id=1, source_target_pairs={{0,16},{16,0},{1,17},{17,1},{2,18},{18,2},{3,19},{19,3},{4,20},{20... | collective-permute-start | bytes 786440 | tf_op jit(solution)/shard_map/ppermute | solution.py:74
  185.2 6.8 %collective-permute-done.2 = bf16[1,512,256]{2,1,0:T(8,128)(2,1)S(1)} collective-permute-done((bf16[1,512,256]{2,1,0:T(8,128)(2,1)S(1)}, bf16[1,512,256]{2,1,0:T(8,128)(2,1)S(1)}, u32[]{:S(2)}, u32[]{:S(2)}) %collective-permute-start.2) | collective-permute-done | bytes 262176 | tf_op jit(solution)/shard_map/ppermute | solution.py:74
  192.0 0.8 broadcast_select_fusion
  193.0 28.6 %all_to_all.41 = bf16[4,2,1,512,256]{4,3,1,2,0:T(8,128)(2,1)S(1)} all-to-all(bf16[4,2,1,512,256]{4,3,1,2,0:T(8,128)(2,1)S(1)} %broadcast_in_dim.88), channel_id=1, replica_groups=mesh['ry'=4,'rc'=2,'zh'=2,'xx'=4,'page'=4] {'xx'}, dimensions={0} | all-to-all | bytes 4194304 | tf_op jit(solution)/shard_map/all_to_all | solution.py:83
  221.6 2.4 copy_convert_fusion
  224.0 5.4 %copy.148 = f32[1,512,8,256]{1,3,2,0:T(8,128)} copy(f32[1,512,8,256]{3,1,2,0:T(8,128)} %bitcast.123) | data formatting | bytes 8388608 | tf_op jit(solution)/shard_map/convert_element_type | solution.py:214
  229.4 0.5 multiply_reduce_fusion
  230.0 2.6 fusion.3
  232.7 5.4 %fusion = f32[512,1280]{1,0:T(8,128)S(1)} fusion(bf16[512,2048]{0,1:T(8,128)(2,1)S(1)} %fusion.3, bf16[2048,1920]{1,0:T(8,128)(2,1)} %all-gather.2.cloned.1.call-done), kind=kOutput, calls=%fused_computation.2 | convolution fusion | flops 2684354560 | bytes 9961472 | tf_op jit(solution)/shard_map/dot_general | solution.py:215
  238.1 5.0 %convolution_convert_fusion.1 = bf16[512,2048]{1,0:T(8,128)(2,1)} fusion(bf16[2048,1920]{1,0:T(8,128)(2,1)} %all-gather.2.cloned.1.call-done, f32[512,1280]{1,0:T(8,128)S(1)} %fusion), kind=kOutput, calls=%fused_computation.13 | convolution fusion | flops 1345191936 | bytes 7340032 | tf_op jit(solution)/shard_map/dot_general | solution.py:50
  243.1 3.3 %reshape.454 = bf16[1,512,2,4,256]{4,3,2,1,0:T(4,128)(2,1)S(1)} reshape(bf16[512,2048]{1,0:T(8,128)(2,1)} %convolution_convert_fusion.1) | data formatting | bytes 4194304 | tf_op jit(solution)/shard_map/reshape | solution.py:94
  246.4 3.0 copy.150
  249.4 3.6 %all-to-all-start.7 = ((bf16[1,512,2,4,256]{4,2,1,0,3:T(2,128)(2,1)}), bf16[1,512,2,4,256]{4,2,1,0,3:T(2,128)(2,1)S(1)}, u32[]{:S(2)}, u32[]{:S(2)}) async-start(bf16[1,512,2,4,256]{4,2,1,0,3:T(2,128)(2,1)} %copy.150), calls=%async_computation.7 | async-start | bytes 4194304 | tf_op jit(solution)/shard_map/all_to_all | solution.py:94
  253.1 25.1 %all-to-all-done.7 = bf16[1,512,2,4,256]{4,2,1,0,3:T(2,128)(2,1)S(1)} async-done(((bf16[1,512,2,4,256]{4,2,1,0,3:T(2,128)(2,1)}), bf16[1,512,2,4,256]{4,2,1,0,3:T(2,128)(2,1)S(1)}, u32[]{:S(2)}, u32[]{:S(2)}) %all-to-all-start.7) | async-done | bytes 2097184 | tf_op jit(solution)/shard_map/all_to_all | solution.py:94
  278.4 1.0 copy-done.2
  279.4 0.4 fusion.21
  279.9 4.5 %collective-permute-start.3 = (bf16[1,512,256]{2,0,1:T(2,128)(2,1)S(1)}, bf16[1,512,256]{2,0,1:T(2,128)(2,1)S(1)}, u32[]{:S(2)}, u32[]{:S(2)}) collective-permute-start(bf16[1,512,256]{2,0,1:T(2,128)(2,1)S(1)} %fusion.21), channel_id=1, source_target_pairs={{0,16},{16,0},{1,17},{17,1},{2,18},{18,2},{3,19},{19,3},{4,20},{20... | collective-permute-start | bytes 786440 | tf_op jit(solution)/shard_map/ppermute | solution.py:74
  284.4 0.8 scatter_fusion.1
  285.3 12.1 %collective-permute-done.3 = bf16[1,512,256]{2,0,1:T(2,128)(2,1)S(1)} collective-permute-done((bf16[1,512,256]{2,0,1:T(2,128)(2,1)S(1)}, bf16[1,512,256]{2,0,1:T(2,128)(2,1)S(1)}, u32[]{:S(2)}, u32[]{:S(2)}) %collective-permute-start.3) | collective-permute-done | bytes 262176 | tf_op jit(solution)/shard_map/ppermute | solution.py:74
  297.3 1.2 fusion.24
  298.5 0.7 copy.153
  (90 shorter events, 4.5 us)
Async XLA Ops:
  7.2 2.9 copy-start
  7.2 3.8 %copy-start.10 = (f32[128,64]{0,1:T(8,128)S(1)}, f32[128,64]{0,1:T(8,128)}, u32[]{:S(2)}) copy-start(f32[128,64]{0,1:T(8,128)} %param.19) | copy-start | bytes 98308
  7.2 10.6 %copy-start.5 = (bf16[1,512,256]{2,1,0:T(8,128)(2,1)S(1)}, bf16[1,512,256]{2,1,0:T(8,128)(2,1)}, u32[]{:S(2)}) copy-start(bf16[1,512,256]{2,1,0:T(8,128)(2,1)} %param.14) | copy-start | bytes 786436
  7.2 225.5 %all-gather.2.cloned.1.call-start = ((), (), s32[]{:S(2)}) async-start(), calls=%async_computation.8 | async-start | bytes 8110080 | tf_op jit(solution)/shard_map/all_gather | solution.py:180
  11.7 12.0 %all-to-all-start.1 = ((bf16[4,64,384]{2,1,0:T(8,128)(2,1)}), bf16[4,64,384]{2,1,0:T(8,128)(2,1)S(1)}, u32[]{:S(2)}, u32[]{:S(2)}) async-start(bf16[4,64,384]{2,1,0:T(8,128)(2,1)} %broadcast_in_dim.74), calls=%async_computation.1 | async-start | bytes 393216 | tf_op jit(solution)/shard_map/all_to_all | solution.py:104
  17.8 19.2 %collective-permute-start = (bf16[1,512,256]{2,1,0:T(8,128)(2,1)S(1)}, bf16[1,512,256]{2,1,0:T(8,128)(2,1)S(1)}, u32[]{:S(2)}, u32[]{:S(2)}) collective-permute-start(bf16[1,512,256]{2,1,0:T(8,128)(2,1)S(1)} %copy-done.5), channel_id=1, source_target_pairs={{0,16},{16,0},{1,17},{17,1},{2,18},{18,2},{3,19},{19,3},{4,20},{20... | collective-permute-start | bytes 786440 | tf_op jit(solution)/shard_map/ppermute | solution.py:74
  24.9 15.0 %all-to-all-start.2 = ((bf16[4,256,384]{1,2,0:T(8,128)(2,1)}), bf16[4,256,384]{1,2,0:T(8,128)(2,1)S(1)}, u32[]{:S(2)}, u32[]{:S(2)}) async-start(bf16[4,256,384]{1,2,0:T(8,128)(2,1)} %broadcast_in_dim.76), calls=%async_computation.2 | async-start | bytes 1572864 | tf_op jit(solution)/shard_map/all_to_all | solution.py:107
  49.4 4.5 %copy-start.12 = (f32[2048]{0:T(1024)S(1)}, f32[2048]{0:T(1024)}, u32[]{:S(2)}) copy-start(f32[2048]{0:T(1024)} %param.22) | copy-start | bytes 24580
  49.4 5.1 %copy-start.13 = (s32[4,4]{1,0:T(4,128)S(1)}, s32[4,4]{1,0:T(4,128)}, u32[]{:S(2)}) copy-start(s32[4,4]{1,0:T(4,128)} %param.16) | copy-start | bytes 196
  49.4 31.1 %all-to-all-start = ((bf16[4,2,1,512,256]{4,1,3,2,0:T(2,128)(2,1)}), bf16[4,2,1,512,256]{4,1,3,2,0:T(2,128)(2,1)S(1)}, u32[]{:S(2)}, u32[]{:S(2)}) async-start(bf16[4,2,1,512,256]{4,1,3,2,0:T(2,128)(2,1)} %broadcast_in_dim.70), calls=%async_computation | async-start | bytes 4194304 | tf_op jit(solution)/shard_map/all_to_all | solution.py:83
  53.8 7.9 %copy-start.16 = (pred[512]{0:T(512)(128)(4,1)}, pred[512]{0:T(512)(128)(4,1)S(1)}, u32[]{:S(2)}) copy-start(pred[512]{0:T(512)(128)(4,1)S(1)} %iota_compare_fusion.1) | copy-start | bytes 1540
  81.7 2.5 copy-start.4
  84.2 2.4 copy-start.14
  84.2 3.0 copy-start.18
  87.1 9.3 %copy-start.15 = (f32[64]{0:T(128)S(1)}, f32[64]{0:T(128)}, u32[]{:S(2)}) copy-start(f32[64]{0:T(128)} %param.24) | copy-start | bytes 772
  87.3 9.2 %copy-start.8 = (f32[512,32]{0,1:T(8,128)S(1)}, f32[512,32]{0,1:T(8,128)}, u32[]{:S(2)}) copy-start(f32[512,32]{0,1:T(8,128)} %get-tuple-element.34) | copy-start | bytes 196612
  87.3 9.2 %copy-start.9 = (f32[512,32]{0,1:T(8,128)S(1)}, f32[512,32]{0,1:T(8,128)}, u32[]{:S(2)}) copy-start(f32[512,32]{0,1:T(8,128)} %get-tuple-element.35) | copy-start | bytes 196612
  87.5 9.1 %copy-start.7 = (pred[512,512]{0,1:T(8,128)(4,1)S(1)}, pred[512,512]{0,1:T(8,128)(4,1)}, u32[]{:S(2)}) copy-start(pred[512,512]{0,1:T(8,128)(4,1)} %fusion.9) | copy-start | bytes 786436
  89.3 15.8 %all-to-all-start.4 = ((bf16[2,4,128,128]{3,2,0,1:T(8,128)(2,1)}), bf16[2,4,128,128]{3,2,0,1:T(8,128)(2,1)S(1)}, u32[]{:S(2)}, u32[]{:S(2)}) async-start(bf16[2,4,128,128]{3,2,0,1:T(8,128)(2,1)} %copy.137), calls=%async_computation.4 | async-start | bytes 524288 | tf_op jit(solution)/shard_map/all_to_all | solution.py:141
  96.4 0.9 copy-start.17
  114.1 28.3 %all-to-all-start.5 = ((bf16[1,512,2,4,256]{4,2,1,0,3:T(2,128)(2,1)}), bf16[1,512,2,4,256]{4,2,1,0,3:T(2,128)(2,1)S(1)}, u32[]{:S(2)}, u32[]{:S(2)}) async-start(bf16[1,512,2,4,256]{4,2,1,0,3:T(2,128)(2,1)} %copy.139), calls=%async_computation.5 | async-start | bytes 4194304 | tf_op jit(solution)/shard_map/all_to_all | solution.py:94
  144.0 34.5 %collective-permute-start.1 = (bf16[1,512,256]{2,0,1:T(2,128)(2,1)S(1)}, bf16[1,512,256]{2,0,1:T(2,128)(2,1)S(1)}, u32[]{:S(2)}, u32[]{:S(2)}) collective-permute-start(bf16[1,512,256]{2,0,1:T(2,128)(2,1)S(1)} %fusion.19), channel_id=1, source_target_pairs={{0,16},{16,0},{1,17},{17,1},{2,18},{18,2},{3,19},{19,3},{4,20},{20... | collective-permute-start | bytes 786440 | tf_op jit(solution)/shard_map/ppermute | solution.py:74
  179.6 12.4 %collective-permute-start.2 = (bf16[1,512,256]{2,1,0:T(8,128)(2,1)S(1)}, bf16[1,512,256]{2,1,0:T(8,128)(2,1)S(1)}, u32[]{:S(2)}, u32[]{:S(2)}) collective-permute-start(bf16[1,512,256]{2,1,0:T(8,128)(2,1)S(1)} %copy.144), channel_id=1, source_target_pairs={{0,16},{16,0},{1,17},{17,1},{2,18},{18,2},{3,19},{19,3},{4,20},{20... | collective-permute-start | bytes 786440 | tf_op jit(solution)/shard_map/ppermute | solution.py:74
  229.4 0.7 copy-start.11
  249.4 28.8 %all-to-all-start.7 = ((bf16[1,512,2,4,256]{4,2,1,0,3:T(2,128)(2,1)}), bf16[1,512,2,4,256]{4,2,1,0,3:T(2,128)(2,1)S(1)}, u32[]{:S(2)}, u32[]{:S(2)}) async-start(bf16[1,512,2,4,256]{4,2,1,0,3:T(2,128)(2,1)} %copy.150), calls=%async_computation.7 | async-start | bytes 4194304 | tf_op jit(solution)/shard_map/all_to_all | solution.py:94
  278.4 1.0 copy-start.2
  279.4 5.8 %copy-start.3 = (f32[512,2,256]{2,0,1:T(8,128)S(1)}, f32[512,2,256]{2,0,1:T(8,128)}, u32[]{:S(2)}) copy-start(f32[512,2,256]{2,0,1:T(8,128)} %copy-done.2) | copy-start | bytes 3145732
  279.9 17.4 %collective-permute-start.3 = (bf16[1,512,256]{2,0,1:T(2,128)(2,1)S(1)}, bf16[1,512,256]{2,0,1:T(2,128)(2,1)S(1)}, u32[]{:S(2)}, u32[]{:S(2)}) collective-permute-start(bf16[1,512,256]{2,0,1:T(2,128)(2,1)S(1)} %fusion.21), channel_id=1, source_target_pairs={{0,16},{16,0},{1,17},{17,1},{2,18},{18,2},{3,19},{19,3},{4,20},{20... | collective-permute-start | bytes 786440 | tf_op jit(solution)/shard_map/ppermute | solution.py:74
  284.4 14.8 %copy-start.1 = (f32[2,64,256]{2,1,0:T(8,128)S(1)}, f32[2,64,256]{2,1,0:T(8,128)}, u32[]{:S(2)}) copy-start(f32[2,64,256]{2,1,0:T(8,128)} %param.18) | copy-start | bytes 393220
  285.2 14.0 %copy-start.6 = (bf16[2,4,128,128]{3,2,1,0:T(8,128)(2,1)}, bf16[2,4,128,128]{3,2,1,0:T(8,128)(2,1)S(1)}, u32[]{:S(2)}) copy-start(bf16[2,4,128,128]{3,2,1,0:T(8,128)(2,1)S(1)} %scatter_fusion.1) | copy-start | bytes 786436
Sparse Core Ops, SparseCore 0:
  10.1 103.7 all-gather.1

commit v11 on v10

--- a/solution.py
+++ b/solution.py
@@ -74,29 +74,40 @@
     return lax.ppermute(x, "zh", [(0, 1), (1, 0)])
 
 
-def gather_col(x, axis):
+def gather_col(x):
     half = lax.axis_index("zh")
     other = swap_halves(x)
     pair = jnp.stack([jnp.where(half == 0, x, other), jnp.where(half == 0, other, x)])
     count = lax.axis_size("xx")
     copies = jnp.broadcast_to(pair[None], (count,) + pair.shape)
-    got = lax.all_to_all(copies, "xx", 0, 0, tiled=True)
-    got = jnp.moveaxis(jnp.swapaxes(got, 0, 1).reshape((-1,) + x.shape), 0, axis)
-    shape = list(x.shape)
-    shape[axis] *= 2 * count
-    return got.reshape(shape)
-
-
-def scatter_sum_col(x, axis):
-    count = lax.axis_size("xx")
-    shape = list(x.shape)
-    split = shape[:axis] + [2, count, shape[axis] // (2 * count)] + shape[axis + 1 :]
-    got = lax.all_to_all(x.reshape(split), "xx", axis + 1, axis + 1, tiled=True)
-    part = jnp.sum(got.astype(jnp.float32), axis=axis + 1)
+    return lax.all_to_all(copies, "xx", 0, 0, tiled=True)
+
+
+def scatter_sum_col(terms):
+    got = lax.all_to_all(terms, "xx", 0, 0, tiled=True)
+    part = jnp.sum(got.astype(jnp.float32), axis=0)
     half = lax.axis_index("zh")
-    mine = jnp.take(part, half, axis=axis)
-    theirs = swap_halves(jnp.take(part, 1 - half, axis=axis).astype(jnp.bfloat16))
+    mine = jnp.take(part, half, axis=-2)
+    theirs = swap_halves(jnp.take(part, 1 - half, axis=-2).astype(jnp.bfloat16))
     return mine + theirs.astype(jnp.float32)
+
+
+def normalize_blocks(values, norm_gain):
+    xx_count, zh_count = values.shape[0], values.shape[1]
+    gain = jnp.swapaxes(norm_gain.reshape(zh_count, xx_count, -1), 0, 1)[:, :, None, None, :]
+    mean_sq = jnp.mean(values * values, axis=(0, 1, 4), keepdims=True)
+    return values * lax.rsqrt(mean_sq + 1e-06) * gain
+
+
+def project_blocks(values, weights):
+    xx_count, zh_count, block = values.shape[0], values.shape[1], values.shape[4]
+    w = weights.reshape(zh_count, xx_count, block, -1)
+    return jnp.einsum("xzpse,zxen->psn", values, w, preferred_element_type=jnp.float32)
+
+
+def terms_blocks(values, weights_t, xx_count, zh_count):
+    w = weights_t.reshape(zh_count, xx_count, -1, weights_t.shape[1])
+    return jnp.einsum("psk,zxek->xpsze", values, w, preferred_element_type=jnp.float32)
 
 
 def gather_rows(x):
@@ -184,12 +195,11 @@
     down_t = ffn_full[:, offsets[4] - offsets[3] :]
 
     prompt_count, seq_len, local_feat = tokens.shape
-    gathered = gather_col(tokens, 2)
-    model_width = gathered.shape[2]
-    attn_in = normalize(gathered.astype(jnp.float32), attn_gain).astype(jnp.bfloat16)
-    projected = jnp.dot(
-        attn_in.reshape(-1, model_width), qkv_w, preferred_element_type=jnp.float32
-    )
+    xx_count = lax.axis_size("xx")
+    zh_count = lax.axis_size("zh")
+    gathered = gather_col(tokens)
+    attn_in = normalize_blocks(gathered.astype(jnp.float32), attn_gain).astype(jnp.bfloat16)
+    projected = project_blocks(attn_in, qkv_w)
     projected = projected.reshape(prompt_count, seq_len, local_heads + 2, head_dim)
     queries = rotate(normalize(projected[:, :, :local_heads], query_gain)).astype(jnp.bfloat16)
     keys_one = rotate(normalize(projected[:, :, local_heads : local_heads + 1], key_gain)).astype(
@@ -206,18 +216,15 @@
     )
     incoming = send_pages(keys_rot, values_in, lengths, page_slot)
     incoming, attended = lax.optimization_barrier((incoming, attended))
-    attn_terms = contract_rows(attended.reshape(-1, local_width), out_t)
-    attn_terms = attn_terms.reshape(prompt_count, seq_len, model_width).astype(jnp.bfloat16)
-    attn_sum = scatter_sum_col(attn_terms, 2)
+    attn_terms = terms_blocks(attended, out_t, xx_count, zh_count).astype(jnp.bfloat16)
+    attn_sum = scatter_sum_col(attn_terms)
     residual = (tokens.astype(jnp.float32) + attn_sum).astype(jnp.bfloat16)
-    residual_all = gather_col(residual, 2)
-    ffn_in = normalize(residual_all.astype(jnp.float32), ffn_gain).astype(jnp.bfloat16)
-    gate_up = jnp.dot(
-        ffn_in.reshape(-1, model_width), gateup_w, preferred_element_type=jnp.float32
-    )
-    hidden = (jax.nn.silu(gate_up[:, :unit_count]) * gate_up[:, unit_count:]).astype(jnp.bfloat16)
-    ffn_terms = contract_rows(hidden, down_t).reshape(prompt_count, seq_len, model_width)
-    ffn_sum = scatter_sum_col(ffn_terms.astype(jnp.bfloat16), 2)
+    residual_all = gather_col(residual)
+    ffn_in = normalize_blocks(residual_all.astype(jnp.float32), ffn_gain).astype(jnp.bfloat16)
+    gate_up = project_blocks(ffn_in, gateup_w)
+    hidden = (jax.nn.silu(gate_up[..., :unit_count]) * gate_up[..., unit_count:]).astype(jnp.bfloat16)
+    ffn_terms = terms_blocks(hidden, down_t, xx_count, zh_count)
+    ffn_sum = scatter_sum_col(ffn_terms.astype(jnp.bfloat16))
     layer_out = (residual.astype(jnp.float32) + ffn_sum).astype(jnp.bfloat16)
     page_index = lax.axis_index("page")
     page_count = lax.axis_size("page")

time: 307 us -> 257 us (0.84)
  local copies, waits for them, and re-layouts: 39.9 us -> 19.2 us
  waiting for transfers between devices: 125 us -> 109 us
  matrix products: 15.9 us -> 7.82 us
  other arithmetic: 18.4 us -> 10.4 us
    ppermute x4, waiting for transfers between devices: 48 us -> 30.1 us  [swap_halves(): return lax.ppermute(x, 'zh', [(0, 1), (1, 0)])]
    reshape x4 -> x2, local copies, waits for them, and re-layouts: 13.6 us -> 0.02 us  [normalize_blocks(): norm_gain.reshape(zh_count, xx_count, -1)]
    dot_general x4, matrix products: 14.5 us -> 6.37 us  [the longest x2 3.77 us: project_blocks(): jnp.einsum('xzpse,zxen->psn', values, w, preferred_element_type=jnp.float32)]
    convert_element_type x6 -> x2, other arithmetic: 6.86 us -> 0.1 us  [scatter_sum_col(): theirs = swap_halves(jnp.take(part, 1 - half, axis=-2).astype(jnp.bfloat16))]
    convert_element_type x3 -> x2, local copies, waits for them, and re-layouts: 7.9 us -> 1.76 us  [the longest x1 1.63 us: on_device(): terms_blocks(attended, out_t, xx_count, zh_count).astype(jnp.bfloat16)]
    slice x0 -> x6, local copies, waits for them, and re-layouts: none -> 3.55 us  [the longest x2 2.48 us: on_device(): gateup_w = ffn_full[:, :offsets[4] - offsets[3]]]
  transfers between devices with their start and end apart: 11 -> 11, of which waited for: 10 -> 10; matrix products, arithmetic and copies ran while one was open for 17% -> 10% of each run, Pallas kernels for 0% -> 0%
where the time goes in v11:
time: 257 us; the launch traced here: 256 us
  waiting for transfers between devices  109 us (42%)
  starting transfers between devices  59.4 us (23%)
  blocking collectives  34.3 us (13%)
  local copies, waits for them, and re-layouts  19.2 us (7%)
  between operations  15.3 us (6%)
  other arithmetic  10.4 us (4%)
  matrix products  7.82 us (3%)
    all_to_all x2, waiting for transfers between devices, gather_col(): return lax.all_to_all(copies, 'xx', 0, 0, tiled=True)  44.3 us
    ppermute x4, waiting for transfers between devices, swap_halves(): return lax.ppermute(x, 'zh', [(0, 1), (1, 0)])  30.1 us
    ppermute x4, starting transfers between devices, swap_halves(): return lax.ppermute(x, 'zh', [(0, 1), (1, 0)])  29.9 us
    all_to_all x1, blocking collectives, scatter_sum_col(): got = lax.all_to_all(terms, 'xx', 0, 0, tiled=True)  28.3 us
    all_to_all x1, waiting for transfers between devices, scatter_sum_col(): got = lax.all_to_all(terms, 'xx', 0, 0, tiled=True)  24.8 us
    all_to_all x2, starting transfers between devices, gather_col(): return lax.all_to_all(copies, 'xx', 0, 0, tiled=True)  8.27 us
    all_to_all x1, starting transfers between devices, send_pages(): lax.all_to_all(outgoing, 'page', split_axis=1, concat_axis=1, tiled=True)  6.93 us
    all_to_all x1, waiting for transfers between devices, send_pages(): lax.all_to_all(outgoing, 'page', split_axis=1, concat_axis=1, tiled=True)  6.69 us
  transfers between devices with their start and end apart: 11, of which 10 were waited for; matrix products, arithmetic and copies ran while one was open for 10% of the time, Pallas kernels for 0%

profile of v11, /device:TPU:56, one launch (start us, length us, event | category | flops | bytes accessed | tf_op | source)
XLA Modules:
  0.0 255.7 jit_solution(10217237344392293177)
XLA Ops:
  7.2 1.0 convert_bitcast_fusion.3
  8.2 1.0 convert_bitcast_fusion.2
  9.3 0.7 pad_maximum_fusion
  10.2 0.8 convert_element_type.103
  11.0 0.7 broadcast_in_dim.68
  11.7 6.0 %all-to-all-start = ((bf16[4,64,384]{2,1,0:T(8,128)(2,1)}), bf16[4,64,384]{2,1,0:T(8,128)(2,1)S(1)}, u32[]{:S(2)}, u32[]{:S(2)}) async-start(bf16[4,64,384]{2,1,0:T(8,128)(2,1)} %broadcast_in_dim.68), calls=%async_computation | async-start | bytes 393216 | tf_op jit(solution)/shard_map/all_to_all | solution.py:115
  17.7 0.1 copy.64
  17.9 4.7 %collective-permute-start = (bf16[1,512,256]{1,2,0:T(8,128)(2,1)S(1)}, bf16[1,512,256]{1,2,0:T(8,128)(2,1)S(1)}, u32[]{:S(2)}, u32[]{:S(2)}) collective-permute-start(bf16[1,512,256]{1,2,0:T(8,128)(2,1)S(1)} %copy.64), channel_id=1, source_target_pairs={{0,16},{16,0},{1,17},{17,1},{2,18},{18,2},{3,19},{19,3},{4,20},{20... | collective-permute-start | bytes 786440 | tf_op jit(solution)/shard_map/ppermute | solution.py:74
  22.6 1.1 all-to-all-done
  23.7 1.0 broadcast_in_dim.70
  24.7 4.7 %all-to-all-start.1 = ((bf16[4,256,384]{2,1,0:T(8,128)(2,1)}), bf16[4,256,384]{2,1,0:T(8,128)(2,1)S(1)}, u32[]{:S(2)}, u32[]{:S(2)}) async-start(bf16[4,256,384]{2,1,0:T(8,128)(2,1)} %broadcast_in_dim.70), calls=%async_computation.1 | async-start | bytes 1572864 | tf_op jit(solution)/shard_map/all_to_all | solution.py:118
  29.4 7.6 %collective-permute-done = bf16[1,512,256]{1,2,0:T(8,128)(2,1)S(1)} collective-permute-done((bf16[1,512,256]{1,2,0:T(8,128)(2,1)S(1)}, bf16[1,512,256]{1,2,0:T(8,128)(2,1)S(1)}, u32[]{:S(2)}, u32[]{:S(2)}) %collective-permute-start) | collective-permute-done | bytes 262176 | tf_op jit(solution)/shard_map/ppermute | solution.py:74
  37.1 0.2 copy.70
  37.3 2.4 all-to-all-done.1
  39.6 0.1 broadcast_in_dim.74
  39.8 6.0 %all_to_all.40 = bf16[4,2,256,384]{3,2,0,1:T(8,128)(2,1)} all-to-all(bf16[4,2,256,384]{3,2,0,1:T(8,128)(2,1)S(1)} %broadcast_in_dim.74), channel_id=1, replica_groups=mesh['ry'=4,'rc'=2,'zh'=2,'xx'=4,'page'=4] {'rc'}, dimensions={1} | all-to-all | bytes 3145728 | tf_op jit(solution)/shard_map/all_to_all | solution.py:121
  45.8 1.5 broadcast_in_dim.77
  47.3 4.4 %all-to-all-start.3 = ((bf16[4,2,1,512,256]{4,3,1,2,0:T(8,128)(2,1)}), bf16[4,2,1,512,256]{4,3,1,2,0:T(8,128)(2,1)S(1)}, u32[]{:S(2)}, u32[]{:S(2)}) async-start(bf16[4,2,1,512,256]{4,3,1,2,0:T(8,128)(2,1)} %broadcast_in_dim.77), calls=%async_computation.3 | async-start | bytes 4194304 | tf_op jit(solution)/shard_map/all_to_all | solution.py:83
  52.4 0.5 add_compare_fusion
  52.9 0.2 convert_reduce_fusion.2
  53.2 0.6 fusion.56
  53.7 1.0 fusion.42
  54.7 0.8 fusion.26
  55.5 1.6 copy.66
  57.2 1.0 slice.65
  58.2 2.3 copy.72
  60.5 17.8 %all-to-all-done.3 = bf16[4,2,1,512,256]{4,3,1,2,0:T(8,128)(2,1)S(1)} async-done(((bf16[4,2,1,512,256]{4,3,1,2,0:T(8,128)(2,1)}), bf16[4,2,1,512,256]{4,3,1,2,0:T(8,128)(2,1)S(1)}, u32[]{:S(2)}, u32[]{:S(2)}) %all-to-all-start.3) | async-done | bytes 2097184 | tf_op jit(solution)/shard_map/all_to_all | solution.py:83
  78.3 0.5 fusion.2
  78.8 0.7 copy-done.3
  79.5 0.8 fusion.22
  80.6 0.3 fusion.48
  81.0 0.7 broadcast_select_fusion.1
  81.8 0.2 maximum_bitcast_fusion.2
  82.0 0.2 copy.74
  82.3 0.8 scatter_fusion
  83.0 0.7 copy.75
  83.8 6.9 %all-to-all-start.4 = ((bf16[2,4,128,128]{3,2,0,1:T(8,128)(2,1)}), bf16[2,4,128,128]{3,2,0,1:T(8,128)(2,1)S(1)}, u32[]{:S(2)}, u32[]{:S(2)}) async-start(bf16[2,4,128,128]{3,2,0,1:T(8,128)(2,1)} %copy.75), calls=%async_computation.4 | async-start | bytes 524288 | tf_op jit(solution)/shard_map/all_to_all | solution.py:152
  90.9 0.7 fusion.20
  91.7 0.7 fusion.25
  92.4 6.7 %all-to-all-done.4 = bf16[2,4,128,128]{3,2,0,1:T(8,128)(2,1)S(1)} async-done(((bf16[2,4,128,128]{3,2,0,1:T(8,128)(2,1)}), bf16[2,4,128,128]{3,2,0,1:T(8,128)(2,1)S(1)}, u32[]{:S(2)}, u32[]{:S(2)}) %all-to-all-start.4) | async-done | bytes 262176 | tf_op jit(solution)/shard_map/all_to_all | solution.py:152
  99.1 0.7 convert_bitcast_fusion.1
  99.8 1.6 copy.78
  101.4 3.6 %all-to-all-start.5 = ((bf16[4,1,512,2,256]{2,4,3,1,0:T(8,128)(2,1)}), bf16[4,1,512,2,256]{2,4,3,1,0:T(8,128)(2,1)S(1)}, u32[]{:S(2)}, u32[]{:S(2)}) async-start(bf16[4,1,512,2,256]{2,4,3,1,0:T(8,128)(2,1)} %copy.78), calls=%async_computation.5 | async-start | bytes 4194304 | tf_op jit(solution)/shard_map/all_to_all | solution.py:87
  105.0 24.8 %all-to-all-done.5 = bf16[4,1,512,2,256]{2,4,3,1,0:T(8,128)(2,1)S(1)} async-done(((bf16[4,1,512,2,256]{2,4,3,1,0:T(8,128)(2,1)}), bf16[4,1,512,2,256]{2,4,3,1,0:T(8,128)(2,1)S(1)}, u32[]{:S(2)}, u32[]{:S(2)}) %all-to-all-start.5) | async-done | bytes 2097184 | tf_op jit(solution)/shard_map/all_to_all | solution.py:87
  129.8 0.3 convert_reduce_fusion.1
  130.2 14.3 %collective-permute-start.1 = (bf16[1,512,256]{1,2,0:T(8,128)(2,1)S(1)}, bf16[1,512,256]{1,2,0:T(8,128)(2,1)S(1)}, u32[]{:S(2)}, u32[]{:S(2)}) collective-permute-start(bf16[1,512,256]{1,2,0:T(8,128)(2,1)S(1)} %bitcast_convert_fusion.1), channel_id=1, source_target_pairs={{0,16},{16,0},{1,17},{17,1},{2,18},{18,2},{3,19},{19,3},{4,20},{20... | collective-permute-start | bytes 786440 | tf_op jit(solution)/shard_map/ppermute | solution.py:74
  144.4 10.3 %collective-permute-done.1 = bf16[1,512,256]{1,2,0:T(8,128)(2,1)S(1)} collective-permute-done((bf16[1,512,256]{1,2,0:T(8,128)(2,1)S(1)}, bf16[1,512,256]{1,2,0:T(8,128)(2,1)S(1)}, u32[]{:S(2)}, u32[]{:S(2)}) %collective-permute-start.1) | collective-permute-done | bytes 262176 | tf_op jit(solution)/shard_map/ppermute | solution.py:74
  154.9 5.2 %collective-permute-start.2 = (bf16[1,512,256]{1,2,0:T(8,128)(2,1)S(1)}, bf16[1,512,256]{1,2,0:T(8,128)(2,1)S(1)}, u32[]{:S(2)}, u32[]{:S(2)}) collective-permute-start(bf16[1,512,256]{1,2,0:T(8,128)(2,1)S(1)} %fusion.32), channel_id=1, source_target_pairs={{0,16},{16,0},{1,17},{17,1},{2,18},{18,2},{3,19},{19,3},{4,20},{20... | collective-permute-start | bytes 786440 | tf_op jit(solution)/shard_map/ppermute | solution.py:74
  160.1 8.5 %collective-permute-done.2 = bf16[1,512,256]{1,2,0:T(8,128)(2,1)S(1)} collective-permute-done((bf16[1,512,256]{1,2,0:T(8,128)(2,1)S(1)}, bf16[1,512,256]{1,2,0:T(8,128)(2,1)S(1)}, u32[]{:S(2)}, u32[]{:S(2)}) %collective-permute-start.2) | collective-permute-done | bytes 262176 | tf_op jit(solution)/shard_map/ppermute | solution.py:74
  168.7 0.2 copy.81
  168.9 1.5 broadcast_in_dim.88
  170.4 3.9 %all-to-all-start.6 = ((bf16[4,2,1,512,256]{4,3,1,2,0:T(8,128)(2,1)}), bf16[4,2,1,512,256]{4,3,1,2,0:T(8,128)(2,1)S(1)}, u32[]{:S(2)}, u32[]{:S(2)}) async-start(bf16[4,2,1,512,256]{4,3,1,2,0:T(8,128)(2,1)} %broadcast_in_dim.88), calls=%async_computation.6 | async-start | bytes 4194304 | tf_op jit(solution)/shard_map/all_to_all | solution.py:83
  174.4 26.4 %all-to-all-done.6 = bf16[4,2,1,512,256]{4,3,1,2,0:T(8,128)(2,1)S(1)} async-done(((bf16[4,2,1,512,256]{4,3,1,2,0:T(8,128)(2,1)}), bf16[4,2,1,512,256]{4,3,1,2,0:T(8,128)(2,1)S(1)}, u32[]{:S(2)}, u32[]{:S(2)}) %all-to-all-start.6) | async-done | bytes 2097184 | tf_op jit(solution)/shard_map/all_to_all | solution.py:83
  200.8 0.5 fusion.5
  201.4 2.5 slice-done.1
  203.9 2.9 %fusion.8 = f32[1,512,1280]{2,1,0:T(8,128)S(1)} fusion(bf16[2,4,256,1280]{3,2,1,0:T(8,128)(2,1)S(1)} %bitcast.143, bf16[4,2,1,512,256]{4,3,1,2,0:T(8,128)(2,1)S(1)} %all-to-all-done.6, f32[4,2,256]{2,1,0:T(2,128)S(1)} %copy.82, f32[512]{0:T(512)S(1)} %add_rsqrt_fusion.1), kind=kOutput, calls=%fused_computation.16 | convolution fusion | flops 2688548864 | bytes 9971712 | tf_op jit(solution)/shard_map/xzpse,zxen->psn/dot_general | solution.py:105
  206.8 1.9 convert_bitcast_fusion
  208.7 0.1 copy.84
  208.9 28.3 %all_to_all.41 = bf16[4,1,512,2,256]{2,4,3,1,0:T(8,128)(2,1)S(1)} all-to-all(bf16[4,1,512,2,256]{2,4,3,1,0:T(8,128)(2,1)S(1)} %copy.84), channel_id=1, replica_groups=mesh['ry'=4,'rc'=2,'zh'=2,'xx'=4,'page'=4] {'xx'}, dimensions={0} | all-to-all | bytes 4194304 | tf_op jit(solution)/shard_map/all_to_all | solution.py:87
  237.2 0.3 convert_reduce_fusion
  237.5 5.7 %collective-permute-start.3 = (bf16[1,512,256]{1,2,0:T(8,128)(2,1)S(1)}, bf16[1,512,256]{1,2,0:T(8,128)(2,1)S(1)}, u32[]{:S(2)}, u32[]{:S(2)}) collective-permute-start(bf16[1,512,256]{1,2,0:T(8,128)(2,1)S(1)} %bitcast_convert_fusion), channel_id=1, source_target_pairs={{0,16},{16,0},{1,17},{17,1},{2,18},{18,2},{3,19},{19,3},{4,20},{20... | collective-permute-start | bytes 786440 | tf_op jit(solution)/shard_map/ppermute | solution.py:74
  243.4 0.8 scatter_fusion.1
  244.2 3.7 %collective-permute-done.3 = bf16[1,512,256]{1,2,0:T(8,128)(2,1)S(1)} collective-permute-done((bf16[1,512,256]{1,2,0:T(8,128)(2,1)S(1)}, bf16[1,512,256]{1,2,0:T(8,128)(2,1)S(1)}, u32[]{:S(2)}, u32[]{:S(2)}) %collective-permute-start.3) | collective-permute-done | bytes 262176 | tf_op jit(solution)/shard_map/ppermute | solution.py:74
  248.0 0.8 copy.86
  (91 shorter events, 1.7 us)
Async XLA Ops:
  7.2 2.9 %copy-start = (f32[2,64,256]{2,1,0:T(8,128)S(1)}, f32[2,64,256]{2,1,0:T(8,128)}, u32[]{:S(2)}) copy-start(f32[2,64,256]{2,1,0:T(8,128)} %param.18) | copy-start | bytes 393220
  7.2 3.8 %copy-start.11 = (f32[128,64]{0,1:T(8,128)S(1)}, f32[128,64]{0,1:T(8,128)}, u32[]{:S(2)}) copy-start(f32[128,64]{0,1:T(8,128)} %param.19) | copy-start | bytes 98308
  7.2 10.5 %copy-start.7 = (bf16[1,512,256]{2,1,0:T(8,128)(2,1)S(1)}, bf16[1,512,256]{2,1,0:T(8,128)(2,1)}, u32[]{:S(2)}) copy-start(bf16[1,512,256]{2,1,0:T(8,128)(2,1)} %param.14) | copy-start | bytes 786436
  7.2 194.2 %all-gather.2.cloned.1.call-start = ((), (), s32[]{:S(2)}) async-start(), calls=%async_computation.8 | async-start | bytes 8110080 | tf_op jit(solution)/shard_map/all_gather | solution.py:191
  11.7 12.0 %all-to-all-start = ((bf16[4,64,384]{2,1,0:T(8,128)(2,1)}), bf16[4,64,384]{2,1,0:T(8,128)(2,1)S(1)}, u32[]{:S(2)}, u32[]{:S(2)}) async-start(bf16[4,64,384]{2,1,0:T(8,128)(2,1)} %broadcast_in_dim.68), calls=%async_computation | async-start | bytes 393216 | tf_op jit(solution)/shard_map/all_to_all | solution.py:115
  17.9 19.1 %collective-permute-start = (bf16[1,512,256]{1,2,0:T(8,128)(2,1)S(1)}, bf16[1,512,256]{1,2,0:T(8,128)(2,1)S(1)}, u32[]{:S(2)}, u32[]{:S(2)}) collective-permute-start(bf16[1,512,256]{1,2,0:T(8,128)(2,1)S(1)} %copy.64), channel_id=1, source_target_pairs={{0,16},{16,0},{1,17},{17,1},{2,18},{18,2},{3,19},{19,3},{4,20},{20... | collective-permute-start | bytes 786440 | tf_op jit(solution)/shard_map/ppermute | solution.py:74
  24.7 14.9 %all-to-all-start.1 = ((bf16[4,256,384]{2,1,0:T(8,128)(2,1)}), bf16[4,256,384]{2,1,0:T(8,128)(2,1)S(1)}, u32[]{:S(2)}, u32[]{:S(2)}) async-start(bf16[4,256,384]{2,1,0:T(8,128)(2,1)} %broadcast_in_dim.70), calls=%async_computation.1 | async-start | bytes 1572864 | tf_op jit(solution)/shard_map/all_to_all | solution.py:118
  47.3 4.4 %copy-start.12 = (f32[2048]{0:T(1024)S(1)}, f32[2048]{0:T(1024)}, u32[]{:S(2)}) copy-start(f32[2048]{0:T(1024)} %param.22) | copy-start | bytes 24580
  47.3 5.6 %copy-start.14 = (s32[4,4]{1,0:T(4,128)S(1)}, s32[4,4]{1,0:T(4,128)}, u32[]{:S(2)}) copy-start(s32[4,4]{1,0:T(4,128)} %param.16) | copy-start | bytes 196
  47.3 31.0 %all-to-all-start.3 = ((bf16[4,2,1,512,256]{4,3,1,2,0:T(8,128)(2,1)}), bf16[4,2,1,512,256]{4,3,1,2,0:T(8,128)(2,1)S(1)}, u32[]{:S(2)}, u32[]{:S(2)}) async-start(bf16[4,2,1,512,256]{4,3,1,2,0:T(8,128)(2,1)} %broadcast_in_dim.77), calls=%async_computation.3 | async-start | bytes 4194304 | tf_op jit(solution)/shard_map/all_to_all | solution.py:83
  52.4 4.8 %copy-start.15 = (f32[32]{0:T(128)}, f32[32]{0:T(128)S(1)}, u32[]{:S(2)}) copy-start(f32[32]{0:T(128)S(1)} %multiply_power_fusion) | copy-start | bytes 388
  52.9 4.2 %copy-start.20 = (pred[512]{0:T(512)(128)(4,1)}, pred[512]{0:T(512)(128)(4,1)S(1)}, u32[]{:S(2)}) copy-start(pred[512]{0:T(512)(128)(4,1)S(1)} %iota_compare_fusion.1) | copy-start | bytes 1540
  78.3 1.2 copy-start.3
  79.5 0.9 copy-start.18
  79.5 1.0 copy-start.16
  80.4 1.9 copy-start.17
  81.0 9.8 %copy-start.19 = (f32[64]{0:T(128)S(1)}, f32[64]{0:T(128)}, u32[]{:S(2)}) copy-start(f32[64]{0:T(128)} %param.24) | copy-start | bytes 772
  81.8 9.1 %copy-start.9 = (f32[512,32]{0,1:T(8,128)S(1)}, f32[512,32]{0,1:T(8,128)}, u32[]{:S(2)}) copy-start(f32[512,32]{0,1:T(8,128)} %get-tuple-element.30) | copy-start | bytes 196612
  81.8 9.1 %copy-start.10 = (f32[512,32]{0,1:T(8,128)S(1)}, f32[512,32]{0,1:T(8,128)}, u32[]{:S(2)}) copy-start(f32[512,32]{0,1:T(8,128)} %get-tuple-element.31) | copy-start | bytes 196612
  82.0 9.0 %copy-start.8 = (pred[512,512]{0,1:T(8,128)(4,1)S(1)}, pred[512,512]{0,1:T(8,128)(4,1)}, u32[]{:S(2)}) copy-start(pred[512,512]{0,1:T(8,128)(4,1)} %fusion.26) | copy-start | bytes 786436
  83.8 15.3 %all-to-all-start.4 = ((bf16[2,4,128,128]{3,2,0,1:T(8,128)(2,1)}), bf16[2,4,128,128]{3,2,0,1:T(8,128)(2,1)S(1)}, u32[]{:S(2)}, u32[]{:S(2)}) async-start(bf16[2,4,128,128]{3,2,0,1:T(8,128)(2,1)} %copy.75), calls=%async_computation.4 | async-start | bytes 524288 | tf_op jit(solution)/shard_map/all_to_all | solution.py:152
  90.8 0.9 copy-start.21
  99.1 2.3 copy-start.4
  101.4 28.4 %all-to-all-start.5 = ((bf16[4,1,512,2,256]{2,4,3,1,0:T(8,128)(2,1)}), bf16[4,1,512,2,256]{2,4,3,1,0:T(8,128)(2,1)S(1)}, u32[]{:S(2)}, u32[]{:S(2)}) async-start(bf16[4,1,512,2,256]{2,4,3,1,0:T(8,128)(2,1)} %copy.78), calls=%async_computation.5 | async-start | bytes 4194304 | tf_op jit(solution)/shard_map/all_to_all | solution.py:87
  130.2 24.6 %collective-permute-start.1 = (bf16[1,512,256]{1,2,0:T(8,128)(2,1)S(1)}, bf16[1,512,256]{1,2,0:T(8,128)(2,1)S(1)}, u32[]{:S(2)}, u32[]{:S(2)}) collective-permute-start(bf16[1,512,256]{1,2,0:T(8,128)(2,1)S(1)} %bitcast_convert_fusion.1), channel_id=1, source_target_pairs={{0,16},{16,0},{1,17},{17,1},{2,18},{18,2},{3,19},{19,3},{4,20},{20... | collective-permute-start | bytes 786440 | tf_op jit(solution)/shard_map/ppermute | solution.py:74
  154.9 13.7 %copy-start.1 = (bf16[1,512,256]{1,2,0:T(8,128)(2,1)}, bf16[1,512,256]{1,2,0:T(8,128)(2,1)S(1)}, u32[]{:S(2)}) copy-start(bf16[1,512,256]{1,2,0:T(8,128)(2,1)S(1)} %fusion.32) | copy-start | bytes 786436
  154.9 13.7 %collective-permute-start.2 = (bf16[1,512,256]{1,2,0:T(8,128)(2,1)S(1)}, bf16[1,512,256]{1,2,0:T(8,128)(2,1)S(1)}, u32[]{:S(2)}, u32[]{:S(2)}) collective-permute-start(bf16[1,512,256]{1,2,0:T(8,128)(2,1)S(1)} %fusion.32), channel_id=1, source_target_pairs={{0,16},{16,0},{1,17},{17,1},{2,18},{18,2},{3,19},{19,3},{4,20},{20... | collective-permute-start | bytes 786440 | tf_op jit(solution)/shard_map/ppermute | solution.py:74
  170.4 3.9 %copy-start.13 = (f32[2048]{0:T(1024)S(1)}, f32[2048]{0:T(1024)}, u32[]{:S(2)}) copy-start(f32[2048]{0:T(1024)} %param.23) | copy-start | bytes 24580
  170.4 30.4 %all-to-all-start.6 = ((bf16[4,2,1,512,256]{4,3,1,2,0:T(8,128)(2,1)}), bf16[4,2,1,512,256]{4,3,1,2,0:T(8,128)(2,1)S(1)}, u32[]{:S(2)}, u32[]{:S(2)}) async-start(bf16[4,2,1,512,256]{4,3,1,2,0:T(8,128)(2,1)} %broadcast_in_dim.88), calls=%async_computation.6 | async-start | bytes 4194304 | tf_op jit(solution)/shard_map/all_to_all | solution.py:83
  201.4 2.5 slice-start.1
  203.9 2.9 %slice-start = ((bf16[2048,1920]{1,0:T(8,128)(2,1)}), bf16[2048,640]{1,0:T(8,128)(2,1)S(1)}, s32[]{:S(2)}) async-start(bf16[2048,1920]{1,0:T(8,128)(2,1)} %all-gather.2.cloned.1.call-done), calls=%async_computation.9 | async-start | bytes 5242880 | tf_op jit(solution)/shard_map/slice | solution.py:195
  237.2 6.2 %copy-start.5 = (bf16[2,4,128,128]{3,2,0,1:T(8,128)(2,1)S(1)}, bf16[2,4,128,128]{3,2,0,1:T(8,128)(2,1)}, u32[]{:S(2)}) copy-start(bf16[2,4,128,128]{3,2,0,1:T(8,128)(2,1)} %copy-done.4) | copy-start | bytes 786436
  237.2 10.7 %copy-start.2 = (bf16[1,512,256]{1,2,0:T(8,128)(2,1)S(1)}, bf16[1,512,256]{1,2,0:T(8,128)(2,1)}, u32[]{:S(2)}) copy-start(bf16[1,512,256]{1,2,0:T(8,128)(2,1)} %copy-done.1) | copy-start | bytes 786436
  237.5 10.4 %collective-permute-start.3 = (bf16[1,512,256]{1,2,0:T(8,128)(2,1)S(1)}, bf16[1,512,256]{1,2,0:T(8,128)(2,1)S(1)}, u32[]{:S(2)}, u32[]{:S(2)}) collective-permute-start(bf16[1,512,256]{1,2,0:T(8,128)(2,1)S(1)} %bitcast_convert_fusion), channel_id=1, source_target_pairs={{0,16},{16,0},{1,17},{17,1},{2,18},{18,2},{3,19},{19,3},{4,20},{20... | collective-permute-start | bytes 786440 | tf_op jit(solution)/shard_map/ppermute | solution.py:74
  244.2 4.7 %copy-start.6 = (bf16[2,4,128,128]{3,2,1,0:T(8,128)(2,1)}, bf16[2,4,128,128]{3,2,1,0:T(8,128)(2,1)S(1)}, u32[]{:S(2)}) copy-start(bf16[2,4,128,128]{3,2,1,0:T(8,128)(2,1)S(1)} %scatter_fusion.1) | copy-start | bytes 786436
Sparse Core Ops, SparseCore 0:
  10.1 104.0 all-gather.1

commit v12 on v11

--- a/solution.py
+++ b/solution.py
@@ -215,10 +215,10 @@
         ]
     )
     incoming = send_pages(keys_rot, values_in, lengths, page_slot)
-    incoming, attended = lax.optimization_barrier((incoming, attended))
     attn_terms = terms_blocks(attended, out_t, xx_count, zh_count).astype(jnp.bfloat16)
     attn_sum = scatter_sum_col(attn_terms)
     residual = (tokens.astype(jnp.float32) + attn_sum).astype(jnp.bfloat16)
+    incoming, residual = lax.optimization_barrier((incoming, residual))
     residual_all = gather_col(residual)
     ffn_in = normalize_blocks(residual_all.astype(jnp.float32), ffn_gain).astype(jnp.bfloat16)
     gate_up = project_blocks(ffn_in, gateup_w)

time: 257 us -> 252 us (0.981)
  the two profiles are of different devices: /device:TPU:56 before, /device:TPU:96 now
where the time goes in v12:
time: 252 us; the launch traced here: 251 us
  waiting for transfers between devices  113 us (45%)
  starting transfers between devices  51.1 us (20%)
  blocking collectives  34.3 us (14%)
  local copies, waits for them, and re-layouts  19.4 us (8%)
  between operations  15.3 us (6%)
  other arithmetic  9.42 us (4%)
  matrix products  7.82 us (3%)
    all_to_all x2, waiting for transfers between devices, gather_col(): return lax.all_to_all(copies, 'xx', 0, 0, tiled=True)  45.7 us
    ppermute x4, waiting for transfers between devices, swap_halves(): return lax.ppermute(x, 'zh', [(0, 1), (1, 0)])  33.8 us
    all_to_all x1, blocking collectives, scatter_sum_col(): got = lax.all_to_all(terms, 'xx', 0, 0, tiled=True)  28.4 us
    all_to_all x1, waiting for transfers between devices, scatter_sum_col(): got = lax.all_to_all(terms, 'xx', 0, 0, tiled=True)  24.5 us
    ppermute x4, starting transfers between devices, swap_halves(): return lax.ppermute(x, 'zh', [(0, 1), (1, 0)])  24 us
    all_to_all x2, starting transfers between devices, gather_col(): return lax.all_to_all(copies, 'xx', 0, 0, tiled=True)  8.28 us
    all_to_all x1, waiting for transfers between devices, send_pages(): lax.all_to_all(outgoing, 'page', split_axis=1, concat_axis=1, tiled=True)  6.13 us
    all_to_all x1, blocking collectives, gather_rows(): got = lax.all_to_all(got, 'rc', 1, 1, tiled=True)  5.91 us
  transfers between devices with their start and end apart: 11, of which 10 were waited for; matrix products, arithmetic and copies ran while one was open for 10% of the time, Pallas kernels for 0%

profile of v12, /device:TPU:96, one launch (start us, length us, event | category | flops | bytes accessed | tf_op | source)
XLA Modules:
  0.0 250.7 jit_solution(10249909869890471989)
XLA Ops:
  7.2 1.0 convert_bitcast_fusion.3
  8.2 1.0 convert_bitcast_fusion.2
  9.3 0.7 pad_maximum_fusion
  10.3 0.8 convert_element_type.105
  11.0 0.7 broadcast_in_dim.74
  11.7 5.1 %all-to-all-start.1 = ((bf16[4,64,384]{2,1,0:T(8,128)(2,1)}), bf16[4,64,384]{2,1,0:T(8,128)(2,1)S(1)}, u32[]{:S(2)}, u32[]{:S(2)}) async-start(bf16[4,64,384]{2,1,0:T(8,128)(2,1)} %broadcast_in_dim.74), calls=%async_computation.1 | async-start | bytes 393216 | tf_op jit(solution)/shard_map/all_to_all | solution.py:115
  16.8 0.1 copy.65
  17.0 4.7 %collective-permute-start = (bf16[1,512,256]{1,2,0:T(8,128)(2,1)S(1)}, bf16[1,512,256]{1,2,0:T(8,128)(2,1)S(1)}, u32[]{:S(2)}, u32[]{:S(2)}) collective-permute-start(bf16[1,512,256]{1,2,0:T(8,128)(2,1)S(1)} %copy.65), channel_id=1, source_target_pairs={{0,16},{16,0},{1,17},{17,1},{2,18},{18,2},{3,19},{19,3},{4,20},{20... | collective-permute-start | bytes 786440 | tf_op jit(solution)/shard_map/ppermute | solution.py:74
  21.7 0.2 all-to-all-done.1
  21.9 1.0 broadcast_in_dim.76
  23.0 4.5 %all-to-all-start.2 = ((bf16[4,256,384]{2,1,0:T(8,128)(2,1)}), bf16[4,256,384]{2,1,0:T(8,128)(2,1)S(1)}, u32[]{:S(2)}, u32[]{:S(2)}) async-start(bf16[4,256,384]{2,1,0:T(8,128)(2,1)} %broadcast_in_dim.76), calls=%async_computation.2 | async-start | bytes 1572864 | tf_op jit(solution)/shard_map/all_to_all | solution.py:118
  27.4 12.3 %collective-permute-done = bf16[1,512,256]{1,2,0:T(8,128)(2,1)S(1)} collective-permute-done((bf16[1,512,256]{1,2,0:T(8,128)(2,1)S(1)}, bf16[1,512,256]{1,2,0:T(8,128)(2,1)S(1)}, u32[]{:S(2)}, u32[]{:S(2)}) %collective-permute-start) | collective-permute-done | bytes 262176 | tf_op jit(solution)/shard_map/ppermute | solution.py:74
  39.8 0.2 copy.67
  40.0 2.9 %all-to-all-done.2 = bf16[4,256,384]{2,1,0:T(8,128)(2,1)S(1)} async-done(((bf16[4,256,384]{2,1,0:T(8,128)(2,1)}), bf16[4,256,384]{2,1,0:T(8,128)(2,1)S(1)}, u32[]{:S(2)}, u32[]{:S(2)}) %all-to-all-start.2) | async-done | bytes 786464 | tf_op jit(solution)/shard_map/all_to_all | solution.py:118
  42.9 0.1 broadcast_in_dim.77
  43.0 5.9 %all_to_all.40 = bf16[4,2,256,384]{3,2,0,1:T(8,128)(2,1)} all-to-all(bf16[4,2,256,384]{3,2,0,1:T(8,128)(2,1)S(1)} %broadcast_in_dim.77), channel_id=1, replica_groups=mesh['ry'=4,'rc'=2,'zh'=2,'xx'=4,'page'=4] {'rc'}, dimensions={1} | all-to-all | bytes 3145728 | tf_op jit(solution)/shard_map/all_to_all | solution.py:121
  48.9 1.5 broadcast_in_dim.70
  50.5 4.4 %all-to-all-start = ((bf16[4,2,1,512,256]{4,3,1,2,0:T(8,128)(2,1)}), bf16[4,2,1,512,256]{4,3,1,2,0:T(8,128)(2,1)S(1)}, u32[]{:S(2)}, u32[]{:S(2)}) async-start(bf16[4,2,1,512,256]{4,3,1,2,0:T(8,128)(2,1)} %broadcast_in_dim.70), calls=%async_computation | async-start | bytes 4194304 | tf_op jit(solution)/shard_map/all_to_all | solution.py:83
  55.5 1.0 fusion.41
  56.5 0.8 fusion.26
  57.3 1.6 copy.70
  58.9 1.0 slice.64
  60.0 2.3 copy.71
  62.3 19.2 %all-to-all-done = bf16[4,2,1,512,256]{4,3,1,2,0:T(8,128)(2,1)S(1)} async-done(((bf16[4,2,1,512,256]{4,3,1,2,0:T(8,128)(2,1)}), bf16[4,2,1,512,256]{4,3,1,2,0:T(8,128)(2,1)S(1)}, u32[]{:S(2)}, u32[]{:S(2)}) %all-to-all-start) | async-done | bytes 2097184 | tf_op jit(solution)/shard_map/all_to_all | solution.py:83
  81.5 0.5 fusion.2
  82.0 0.7 copy-done.3
  82.7 0.8 fusion.22
  83.7 0.3 fusion.47
  84.3 0.2 copy-done.14
  84.5 0.7 fusion.20
  85.3 0.7 fusion.25
  86.0 0.7 convert_bitcast_fusion.1
  86.7 1.6 copy.78
  88.3 3.7 %all-to-all-start.5 = ((bf16[4,1,512,2,256]{2,4,3,1,0:T(8,128)(2,1)}), bf16[4,1,512,2,256]{2,4,3,1,0:T(8,128)(2,1)S(1)}, u32[]{:S(2)}, u32[]{:S(2)}) async-start(bf16[4,1,512,2,256]{2,4,3,1,0:T(8,128)(2,1)} %copy.78), calls=%async_computation.5 | async-start | bytes 4194304 | tf_op jit(solution)/shard_map/all_to_all | solution.py:87
  92.1 0.2 convert_reduce_fusion.2
  92.5 0.8 broadcast_select_fusion.1
  93.3 24.5 %all-to-all-done.5 = bf16[4,1,512,2,256]{2,4,3,1,0:T(8,128)(2,1)S(1)} async-done(((bf16[4,1,512,2,256]{2,4,3,1,0:T(8,128)(2,1)}), bf16[4,1,512,2,256]{2,4,3,1,0:T(8,128)(2,1)S(1)}, u32[]{:S(2)}, u32[]{:S(2)}) %all-to-all-start.5) | async-done | bytes 2097184 | tf_op jit(solution)/shard_map/all_to_all | solution.py:87
  117.8 0.3 convert_reduce_fusion.1
  118.2 13.3 %collective-permute-start.1 = (bf16[1,512,256]{1,2,0:T(8,128)(2,1)S(1)}, bf16[1,512,256]{1,2,0:T(8,128)(2,1)S(1)}, u32[]{:S(2)}, u32[]{:S(2)}) collective-permute-start(bf16[1,512,256]{1,2,0:T(8,128)(2,1)S(1)} %bitcast_convert_fusion.1), channel_id=1, source_target_pairs={{0,16},{16,0},{1,17},{17,1},{2,18},{18,2},{3,19},{19,3},{4,20},{20... | collective-permute-start | bytes 786440 | tf_op jit(solution)/shard_map/ppermute | solution.py:74
  131.4 0.2 maximum_bitcast_fusion.2
  131.6 0.2 copy.73
  131.9 0.8 scatter_fusion
  132.7 0.7 copy.74
  133.4 5.5 %all-to-all-start.4 = ((bf16[2,4,128,128]{3,2,0,1:T(8,128)(2,1)}), bf16[2,4,128,128]{3,2,0,1:T(8,128)(2,1)S(1)}, u32[]{:S(2)}, u32[]{:S(2)}) async-start(bf16[2,4,128,128]{3,2,0,1:T(8,128)(2,1)} %copy.74), calls=%async_computation.4 | async-start | bytes 524288 | tf_op jit(solution)/shard_map/all_to_all | solution.py:152
  138.9 1.2 collective-permute-done.1
  140.2 6.1 %all-to-all-done.4 = bf16[2,4,128,128]{3,2,0,1:T(8,128)(2,1)S(1)} async-done(((bf16[2,4,128,128]{3,2,0,1:T(8,128)(2,1)}), bf16[2,4,128,128]{3,2,0,1:T(8,128)(2,1)S(1)}, u32[]{:S(2)}, u32[]{:S(2)}) %all-to-all-start.4) | async-done | bytes 262176 | tf_op jit(solution)/shard_map/all_to_all | solution.py:152
  146.4 3.1 %collective-permute-start.2 = (bf16[1,512,256]{1,2,0:T(8,128)(2,1)S(1)}, bf16[1,512,256]{1,2,0:T(8,128)(2,1)S(1)}, u32[]{:S(2)}, u32[]{:S(2)}) collective-permute-start(bf16[1,512,256]{1,2,0:T(8,128)(2,1)S(1)} %fusion.32), channel_id=1, source_target_pairs={{0,16},{16,0},{1,17},{17,1},{2,18},{18,2},{3,19},{19,3},{4,20},{20... | collective-permute-start | bytes 786440 | tf_op jit(solution)/shard_map/ppermute | solution.py:74
  149.5 13.8 %collective-permute-done.2 = bf16[1,512,256]{1,2,0:T(8,128)(2,1)S(1)} collective-permute-done((bf16[1,512,256]{1,2,0:T(8,128)(2,1)S(1)}, bf16[1,512,256]{1,2,0:T(8,128)(2,1)S(1)}, u32[]{:S(2)}, u32[]{:S(2)}) %collective-permute-start.2) | collective-permute-done | bytes 262176 | tf_op jit(solution)/shard_map/ppermute | solution.py:74
  163.4 0.2 copy.81
  163.6 1.5 broadcast_in_dim.88
  165.2 3.9 %all-to-all-start.6 = ((bf16[4,2,1,512,256]{4,3,1,2,0:T(8,128)(2,1)}), bf16[4,2,1,512,256]{4,3,1,2,0:T(8,128)(2,1)S(1)}, u32[]{:S(2)}, u32[]{:S(2)}) async-start(bf16[4,2,1,512,256]{4,3,1,2,0:T(8,128)(2,1)} %broadcast_in_dim.88), calls=%async_computation.6 | async-start | bytes 4194304 | tf_op jit(solution)/shard_map/all_to_all | solution.py:83
  169.1 26.5 %all-to-all-done.6 = bf16[4,2,1,512,256]{4,3,1,2,0:T(8,128)(2,1)S(1)} async-done(((bf16[4,2,1,512,256]{4,3,1,2,0:T(8,128)(2,1)}), bf16[4,2,1,512,256]{4,3,1,2,0:T(8,128)(2,1)S(1)}, u32[]{:S(2)}, u32[]{:S(2)}) %all-to-all-start.6) | async-done | bytes 2097184 | tf_op jit(solution)/shard_map/all_to_all | solution.py:83
  195.7 0.5 fusion.5
  196.2 2.5 slice-done.1
  198.7 2.9 %fusion.8 = f32[1,512,1280]{2,1,0:T(8,128)S(1)} fusion(bf16[2,4,256,1280]{3,2,1,0:T(8,128)(2,1)S(1)} %bitcast.138, bf16[4,2,1,512,256]{4,3,1,2,0:T(8,128)(2,1)S(1)} %all-to-all-done.6, f32[4,2,256]{2,1,0:T(2,128)S(1)} %copy.82, f32[512]{0:T(512)S(1)} %add_rsqrt_fusion.1), kind=kOutput, calls=%fused_computation.16 | convolution fusion | flops 2688548864 | bytes 9971712 | tf_op jit(solution)/shard_map/xzpse,zxen->psn/dot_general | solution.py:105
  201.6 1.9 convert_bitcast_fusion
  203.6 0.1 copy.84
  203.7 28.4 %all_to_all.41 = bf16[4,1,512,2,256]{2,4,3,1,0:T(8,128)(2,1)S(1)} all-to-all(bf16[4,1,512,2,256]{2,4,3,1,0:T(8,128)(2,1)S(1)} %copy.84), channel_id=1, replica_groups=mesh['ry'=4,'rc'=2,'zh'=2,'xx'=4,'page'=4] {'xx'}, dimensions={0} | all-to-all | bytes 4194304 | tf_op jit(solution)/shard_map/all_to_all | solution.py:87
  232.1 0.3 convert_reduce_fusion
  232.5 2.9 %collective-permute-start.3 = (bf16[1,512,256]{1,2,0:T(8,128)(2,1)S(1)}, bf16[1,512,256]{1,2,0:T(8,128)(2,1)S(1)}, u32[]{:S(2)}, u32[]{:S(2)}) collective-permute-start(bf16[1,512,256]{1,2,0:T(8,128)(2,1)S(1)} %bitcast_convert_fusion), channel_id=1, source_target_pairs={{0,16},{16,0},{1,17},{17,1},{2,18},{18,2},{3,19},{19,3},{4,20},{20... | collective-permute-start | bytes 786440 | tf_op jit(solution)/shard_map/ppermute | solution.py:74
  235.4 0.1 fusion.50
  235.5 0.8 scatter_fusion.1
  236.3 6.5 %collective-permute-done.3 = bf16[1,512,256]{1,2,0:T(8,128)(2,1)S(1)} collective-permute-done((bf16[1,512,256]{1,2,0:T(8,128)(2,1)S(1)}, bf16[1,512,256]{1,2,0:T(8,128)(2,1)S(1)}, u32[]{:S(2)}, u32[]{:S(2)}) %collective-permute-start.3) | collective-permute-done | bytes 262176 | tf_op jit(solution)/shard_map/ppermute | solution.py:74
  243.0 0.8 copy.86
  (93 shorter events, 1.6 us)
Async XLA Ops:
  7.2 2.9 %copy-start = (f32[2,64,256]{2,1,0:T(8,128)S(1)}, f32[2,64,256]{2,1,0:T(8,128)}, u32[]{:S(2)}) copy-start(f32[2,64,256]{2,1,0:T(8,128)} %param.18) | copy-start | bytes 393220
  7.2 3.8 %copy-start.17 = (f32[128,64]{0,1:T(8,128)S(1)}, f32[128,64]{0,1:T(8,128)}, u32[]{:S(2)}) copy-start(f32[128,64]{0,1:T(8,128)} %param.19) | copy-start | bytes 98308
  7.2 9.6 %copy-start.13 = (bf16[1,512,256]{2,1,0:T(8,128)(2,1)S(1)}, bf16[1,512,256]{2,1,0:T(8,128)(2,1)}, u32[]{:S(2)}) copy-start(bf16[1,512,256]{2,1,0:T(8,128)(2,1)} %param.14) | copy-start | bytes 786436
  7.2 189.0 %all-gather.2.cloned.1.call-start = ((), (), s32[]{:S(2)}) async-start(), calls=%async_computation.8 | async-start | bytes 8110080 | tf_op jit(solution)/shard_map/all_gather | solution.py:191
  11.7 10.2 %all-to-all-start.1 = ((bf16[4,64,384]{2,1,0:T(8,128)(2,1)}), bf16[4,64,384]{2,1,0:T(8,128)(2,1)S(1)}, u32[]{:S(2)}, u32[]{:S(2)}) async-start(bf16[4,64,384]{2,1,0:T(8,128)(2,1)} %broadcast_in_dim.74), calls=%async_computation.1 | async-start | bytes 393216 | tf_op jit(solution)/shard_map/all_to_all | solution.py:115
  17.0 22.7 %collective-permute-start = (bf16[1,512,256]{1,2,0:T(8,128)(2,1)S(1)}, bf16[1,512,256]{1,2,0:T(8,128)(2,1)S(1)}, u32[]{:S(2)}, u32[]{:S(2)}) collective-permute-start(bf16[1,512,256]{1,2,0:T(8,128)(2,1)S(1)} %copy.65), channel_id=1, source_target_pairs={{0,16},{16,0},{1,17},{17,1},{2,18},{18,2},{3,19},{19,3},{4,20},{20... | collective-permute-start | bytes 786440 | tf_op jit(solution)/shard_map/ppermute | solution.py:74
  23.0 19.9 %all-to-all-start.2 = ((bf16[4,256,384]{2,1,0:T(8,128)(2,1)}), bf16[4,256,384]{2,1,0:T(8,128)(2,1)S(1)}, u32[]{:S(2)}, u32[]{:S(2)}) async-start(bf16[4,256,384]{2,1,0:T(8,128)(2,1)} %broadcast_in_dim.76), calls=%async_computation.2 | async-start | bytes 1572864 | tf_op jit(solution)/shard_map/all_to_all | solution.py:118
  50.5 4.4 %copy-start.18 = (f32[2048]{0:T(1024)S(1)}, f32[2048]{0:T(1024)}, u32[]{:S(2)}) copy-start(f32[2048]{0:T(1024)} %param.22) | copy-start | bytes 24580
  50.5 31.0 %all-to-all-start = ((bf16[4,2,1,512,256]{4,3,1,2,0:T(8,128)(2,1)}), bf16[4,2,1,512,256]{4,3,1,2,0:T(8,128)(2,1)S(1)}, u32[]{:S(2)}, u32[]{:S(2)}) async-start(bf16[4,2,1,512,256]{4,3,1,2,0:T(8,128)(2,1)} %broadcast_in_dim.70), calls=%async_computation | async-start | bytes 4194304 | tf_op jit(solution)/shard_map/all_to_all | solution.py:83
  81.5 1.2 copy-start.3
  82.7 0.9 copy-start.21
  82.7 1.4 copy-start.22
  82.7 1.5 copy-start.15
  82.7 1.5 copy-start.16
  83.6 1.0 copy-start.14
  84.0 1.2 copy-start.9
  84.1 1.1 copy-start.11
  88.3 3.8 %copy-start.20 = (s32[4,4]{1,0:T(4,128)S(1)}, s32[4,4]{1,0:T(4,128)}, u32[]{:S(2)}) copy-start(s32[4,4]{1,0:T(4,128)} %param.16) | copy-start | bytes 196
  88.3 4.1 %copy-start.10 = (bf16[512,64]{0,1:T(8,128)(2,1)S(1)}, bf16[512,64]{0,1:T(8,128)(2,1)}, u32[]{:S(2)}) copy-start(bf16[512,64]{0,1:T(8,128)(2,1)} %copy-done.9) | copy-start | bytes 196612
  88.3 4.1 %copy-start.12 = (bf16[512,64]{0,1:T(8,128)(2,1)S(1)}, bf16[512,64]{0,1:T(8,128)(2,1)}, u32[]{:S(2)}) copy-start(bf16[512,64]{0,1:T(8,128)(2,1)} %copy-done.11) | copy-start | bytes 196612
  88.3 29.5 %all-to-all-start.5 = ((bf16[4,1,512,2,256]{2,4,3,1,0:T(8,128)(2,1)}), bf16[4,1,512,2,256]{2,4,3,1,0:T(8,128)(2,1)S(1)}, u32[]{:S(2)}, u32[]{:S(2)}) async-start(bf16[4,1,512,2,256]{2,4,3,1,0:T(8,128)(2,1)} %copy.78), calls=%async_computation.5 | async-start | bytes 4194304 | tf_op jit(solution)/shard_map/all_to_all | solution.py:87
  117.8 13.6 %copy-start.7 = (bf16[1,4,128,128]{2,1,3,0:T(4,128)(2,1)S(1)}, bf16[1,4,128,128]{2,1,3,0:T(4,128)(2,1)}, u32[]{:S(2)}) copy-start(bf16[1,4,128,128]{2,1,3,0:T(4,128)(2,1)} %get-tuple-element.32) | copy-start | bytes 393220
  117.8 13.6 %copy-start.8 = (bf16[1,4,128,128]{2,1,3,0:T(4,128)(2,1)S(1)}, bf16[1,4,128,128]{2,1,3,0:T(4,128)(2,1)}, u32[]{:S(2)}) copy-start(bf16[1,4,128,128]{2,1,3,0:T(4,128)(2,1)} %get-tuple-element.33) | copy-start | bytes 393220
  118.2 21.9 %collective-permute-start.1 = (bf16[1,512,256]{1,2,0:T(8,128)(2,1)S(1)}, bf16[1,512,256]{1,2,0:T(8,128)(2,1)S(1)}, u32[]{:S(2)}, u32[]{:S(2)}) collective-permute-start(bf16[1,512,256]{1,2,0:T(8,128)(2,1)S(1)} %bitcast_convert_fusion.1), channel_id=1, source_target_pairs={{0,16},{16,0},{1,17},{17,1},{2,18},{18,2},{3,19},{19,3},{4,20},{20... | collective-permute-start | bytes 786440 | tf_op jit(solution)/shard_map/ppermute | solution.py:74
  133.4 13.0 %all-to-all-start.4 = ((bf16[2,4,128,128]{3,2,0,1:T(8,128)(2,1)}), bf16[2,4,128,128]{3,2,0,1:T(8,128)(2,1)S(1)}, u32[]{:S(2)}, u32[]{:S(2)}) async-start(bf16[2,4,128,128]{3,2,0,1:T(8,128)(2,1)} %copy.74), calls=%async_computation.4 | async-start | bytes 524288 | tf_op jit(solution)/shard_map/all_to_all | solution.py:152
  140.2 24.9 %copy-start.1 = (bf16[1,512,256]{1,2,0:T(8,128)(2,1)}, bf16[1,512,256]{1,2,0:T(8,128)(2,1)S(1)}, u32[]{:S(2)}) copy-start(bf16[1,512,256]{1,2,0:T(8,128)(2,1)S(1)} %fusion.32) | copy-start | bytes 786436
  146.4 17.0 %copy-start.4 = (bf16[2,4,128,128]{3,2,0,1:T(8,128)(2,1)}, bf16[2,4,128,128]{3,2,0,1:T(8,128)(2,1)S(1)}, u32[]{:S(2)}) copy-start(bf16[2,4,128,128]{3,2,0,1:T(8,128)(2,1)S(1)} %all-to-all-done.4) | copy-start | bytes 786436
  146.4 16.9 %collective-permute-start.2 = (bf16[1,512,256]{1,2,0:T(8,128)(2,1)S(1)}, bf16[1,512,256]{1,2,0:T(8,128)(2,1)S(1)}, u32[]{:S(2)}, u32[]{:S(2)}) collective-permute-start(bf16[1,512,256]{1,2,0:T(8,128)(2,1)S(1)} %fusion.32), channel_id=1, source_target_pairs={{0,16},{16,0},{1,17},{17,1},{2,18},{18,2},{3,19},{19,3},{4,20},{20... | collective-permute-start | bytes 786440 | tf_op jit(solution)/shard_map/ppermute | solution.py:74
  165.2 3.9 %copy-start.19 = (f32[2048]{0:T(1024)S(1)}, f32[2048]{0:T(1024)}, u32[]{:S(2)}) copy-start(f32[2048]{0:T(1024)} %param.23) | copy-start | bytes 24580
  165.2 30.5 %all-to-all-start.6 = ((bf16[4,2,1,512,256]{4,3,1,2,0:T(8,128)(2,1)}), bf16[4,2,1,512,256]{4,3,1,2,0:T(8,128)(2,1)S(1)}, u32[]{:S(2)}, u32[]{:S(2)}) async-start(bf16[4,2,1,512,256]{4,3,1,2,0:T(8,128)(2,1)} %broadcast_in_dim.88), calls=%async_computation.6 | async-start | bytes 4194304 | tf_op jit(solution)/shard_map/all_to_all | solution.py:83
  196.2 2.5 slice-start.1
  198.7 2.9 %slice-start = ((bf16[2048,1920]{1,0:T(8,128)(2,1)}), bf16[2048,640]{1,0:T(8,128)(2,1)S(1)}, s32[]{:S(2)}) async-start(bf16[2048,1920]{1,0:T(8,128)(2,1)} %all-gather.2.cloned.1.call-done), calls=%async_computation.9 | async-start | bytes 5242880 | tf_op jit(solution)/shard_map/slice | solution.py:195
  232.1 3.4 %copy-start.5 = (bf16[2,4,128,128]{3,2,0,1:T(8,128)(2,1)S(1)}, bf16[2,4,128,128]{3,2,0,1:T(8,128)(2,1)}, u32[]{:S(2)}) copy-start(bf16[2,4,128,128]{3,2,0,1:T(8,128)(2,1)} %copy-done.4) | copy-start | bytes 786436
  232.1 10.7 %copy-start.2 = (bf16[1,512,256]{1,2,0:T(8,128)(2,1)S(1)}, bf16[1,512,256]{1,2,0:T(8,128)(2,1)}, u32[]{:S(2)}) copy-start(bf16[1,512,256]{1,2,0:T(8,128)(2,1)} %copy-done.1) | copy-start | bytes 786436
  232.5 10.4 %collective-permute-start.3 = (bf16[1,512,256]{1,2,0:T(8,128)(2,1)S(1)}, bf16[1,512,256]{1,2,0:T(8,128)(2,1)S(1)}, u32[]{:S(2)}, u32[]{:S(2)}) collective-permute-start(bf16[1,512,256]{1,2,0:T(8,128)(2,1)S(1)} %bitcast_convert_fusion), channel_id=1, source_target_pairs={{0,16},{16,0},{1,17},{17,1},{2,18},{18,2},{3,19},{19,3},{4,20},{20... | collective-permute-start | bytes 786440 | tf_op jit(solution)/shard_map/ppermute | solution.py:74
  236.3 7.5 %copy-start.6 = (bf16[2,4,128,128]{3,2,1,0:T(8,128)(2,1)}, bf16[2,4,128,128]{3,2,1,0:T(8,128)(2,1)S(1)}, u32[]{:S(2)}) copy-start(bf16[2,4,128,128]{3,2,1,0:T(8,128)(2,1)S(1)} %scatter_fusion.1) | copy-start | bytes 786436
Sparse Core Ops, SparseCore 0:
  10.1 100.4 all-gather.1

commit v13 on v12

--- a/solution.py
+++ b/solution.py
@@ -116,9 +116,9 @@
     got = got.reshape((-1,) + x.shape[1:])
     chips = lax.axis_size("ry")
     got = lax.all_to_all(jnp.broadcast_to(got[None], (chips,) + got.shape), "ry", 0, 0, tiled=True)
-    cores = lax.axis_size("rc")
-    got = jnp.broadcast_to(got[:, None], (chips, cores) + got.shape[1:])
-    got = lax.all_to_all(got, "rc", 1, 1, tiled=True)
+    core = lax.axis_index("rc")
+    other = lax.ppermute(got, "rc", [(0, 1), (1, 0)])
+    got = jnp.stack([jnp.where(core == 0, got, other), jnp.where(core == 0, other, got)], axis=1)
     return got.reshape((-1,) + x.shape[1:])
 
 

time: 252 us -> 235 us (0.933)
  the two profiles are of different devices: /device:TPU:96 before, /device:TPU:8 now
where the time goes in v13:
time: 235 us; the launch traced here: 234 us
  waiting for transfers between devices  100 us (43%)
  starting transfers between devices  57.1 us (24%)
  blocking collectives  24.9 us (11%)
  local copies, waits for them, and re-layouts  17.7 us (8%)
  between operations  15.3 us (7%)
  other arithmetic  10.9 us (5%)
  matrix products  7.81 us (3%)
    all_to_all x2, waiting for transfers between devices, gather_col(): return lax.all_to_all(copies, 'xx', 0, 0, tiled=True)  37.2 us
    all_to_all x1, blocking collectives, scatter_sum_col(): got = lax.all_to_all(terms, 'xx', 0, 0, tiled=True)  24.9 us
    ppermute x4, starting transfers between devices, swap_halves(): return lax.ppermute(x, 'zh', [(0, 1), (1, 0)])  24.3 us
    all_to_all x1, waiting for transfers between devices, scatter_sum_col(): got = lax.all_to_all(terms, 'xx', 0, 0, tiled=True)  18.9 us
    all_to_all x1, waiting for transfers between devices, send_pages(): lax.all_to_all(outgoing, 'page', split_axis=1, concat_axis=1, tiled=True)  16.2 us
    ppermute x4, waiting for transfers between devices, swap_halves(): return lax.ppermute(x, 'zh', [(0, 1), (1, 0)])  15.7 us
    all_to_all x1, starting transfers between devices, send_pages(): lax.all_to_all(outgoing, 'page', split_axis=1, concat_axis=1, tiled=True)  9.32 us
    all_to_all x1, waiting for transfers between devices, gather_rows(): lax.all_to_all(jnp.broadcast_to(got[None], (chips,) + got.shape), 'ry', 0...  8.96 us
  transfers between devices with their start and end apart: 12, of which 9 were waited for; matrix products, arithmetic and copies ran while one was open for 10% of the time, Pallas kernels for 0%

profile of v13, /device:TPU:8, one launch (start us, length us, event | category | flops | bytes accessed | tf_op | source)
XLA Modules:
  0.0 233.9 jit_solution(7924011510556196137)
XLA Ops:
  7.2 1.0 convert_bitcast_fusion.3
  8.2 1.0 convert_bitcast_fusion.2
  9.3 0.7 pad_maximum_fusion.1
  10.2 0.1 reshape.395
  10.3 0.8 convert_element_type.105
  11.0 0.7 broadcast_in_dim.72
  11.7 5.9 %all-to-all-start.1 = ((bf16[4,64,384]{2,1,0:T(8,128)(2,1)}), bf16[4,64,384]{2,1,0:T(8,128)(2,1)S(1)}, u32[]{:S(2)}, u32[]{:S(2)}) async-start(bf16[4,64,384]{2,1,0:T(8,128)(2,1)} %broadcast_in_dim.72), calls=%async_computation.1 | async-start | bytes 393216 | tf_op jit(solution)/shard_map/all_to_all | solution.py:115
  17.6 0.1 copy.68
  17.8 4.8 %collective-permute-start = (bf16[1,512,256]{1,2,0:T(8,128)(2,1)S(1)}, bf16[1,512,256]{1,2,0:T(8,128)(2,1)S(1)}, u32[]{:S(2)}, u32[]{:S(2)}) collective-permute-start(bf16[1,512,256]{1,2,0:T(8,128)(2,1)S(1)} %copy.68), channel_id=1, source_target_pairs={{0,16},{16,0},{1,17},{17,1},{2,18},{18,2},{3,19},{19,3},{4,20},{20... | collective-permute-start | bytes 786440 | tf_op jit(solution)/shard_map/ppermute | solution.py:74
  22.5 3.0 %all-to-all-done.1 = bf16[4,64,384]{2,1,0:T(8,128)(2,1)S(1)} async-done(((bf16[4,64,384]{2,1,0:T(8,128)(2,1)}), bf16[4,64,384]{2,1,0:T(8,128)(2,1)S(1)}, u32[]{:S(2)}, u32[]{:S(2)}) %all-to-all-start.1) | async-done | bytes 196640 | tf_op jit(solution)/shard_map/all_to_all | solution.py:115
  25.5 1.0 broadcast_in_dim.74
  26.6 4.9 %all-to-all-start.2 = ((bf16[4,256,384]{2,1,0:T(8,128)(2,1)}), bf16[4,256,384]{2,1,0:T(8,128)(2,1)S(1)}, u32[]{:S(2)}, u32[]{:S(2)}) async-start(bf16[4,256,384]{2,1,0:T(8,128)(2,1)} %broadcast_in_dim.74), calls=%async_computation.2 | async-start | bytes 1572864 | tf_op jit(solution)/shard_map/all_to_all | solution.py:118
  31.5 1.2 collective-permute-done
  32.8 0.2 copy.70
  33.0 9.0 %all-to-all-done.2 = bf16[4,256,384]{2,1,0:T(8,128)(2,1)S(1)} async-done(((bf16[4,256,384]{2,1,0:T(8,128)(2,1)}), bf16[4,256,384]{2,1,0:T(8,128)(2,1)S(1)}, u32[]{:S(2)}, u32[]{:S(2)}) %all-to-all-start.2) | async-done | bytes 786464 | tf_op jit(solution)/shard_map/all_to_all | solution.py:118
  42.0 1.5 broadcast_in_dim.71
  43.5 4.4 %all-to-all-start = ((bf16[4,2,1,512,256]{4,3,1,2,0:T(8,128)(2,1)}), bf16[4,2,1,512,256]{4,3,1,2,0:T(8,128)(2,1)S(1)}, u32[]{:S(2)}, u32[]{:S(2)}) async-start(bf16[4,2,1,512,256]{4,3,1,2,0:T(8,128)(2,1)} %broadcast_in_dim.71), calls=%async_computation | async-start | bytes 4194304 | tf_op jit(solution)/shard_map/all_to_all | solution.py:83
  48.7 1.0 fusion.41
  49.6 0.8 fusion.26
  50.5 1.3 select_bitcast_fusion.1
  51.8 0.2 pad_maximum_fusion
  52.0 1.0 slice.64
  53.0 2.3 copy.74
  55.3 13.9 %all-to-all-done = bf16[4,2,1,512,256]{4,3,1,2,0:T(8,128)(2,1)S(1)} async-done(((bf16[4,2,1,512,256]{4,3,1,2,0:T(8,128)(2,1)}), bf16[4,2,1,512,256]{4,3,1,2,0:T(8,128)(2,1)S(1)}, u32[]{:S(2)}, u32[]{:S(2)}) %all-to-all-start) | async-done | bytes 2097184 | tf_op jit(solution)/shard_map/all_to_all | solution.py:83
  69.3 0.5 fusion.2
  69.8 0.7 copy-done.3
  70.5 0.8 fusion.22
  71.5 0.3 fusion.47
  72.1 0.2 copy-done.14
  72.3 0.7 fusion.20
  73.1 0.7 fusion.25
  73.8 0.7 convert_bitcast_fusion.1
  74.5 1.6 copy.81
  76.1 3.7 %all-to-all-start.4 = ((bf16[4,1,512,2,256]{2,4,3,1,0:T(8,128)(2,1)}), bf16[4,1,512,2,256]{2,4,3,1,0:T(8,128)(2,1)S(1)}, u32[]{:S(2)}, u32[]{:S(2)}) async-start(bf16[4,1,512,2,256]{2,4,3,1,0:T(8,128)(2,1)} %copy.81), calls=%async_computation.4 | async-start | bytes 4194304 | tf_op jit(solution)/shard_map/all_to_all | solution.py:87
  79.9 0.2 convert_reduce_fusion.2
  80.3 0.8 broadcast_select_fusion.1
  81.1 18.9 %all-to-all-done.4 = bf16[4,1,512,2,256]{2,4,3,1,0:T(8,128)(2,1)S(1)} async-done(((bf16[4,1,512,2,256]{2,4,3,1,0:T(8,128)(2,1)}), bf16[4,1,512,2,256]{2,4,3,1,0:T(8,128)(2,1)S(1)}, u32[]{:S(2)}, u32[]{:S(2)}) %all-to-all-start.4) | async-done | bytes 2097184 | tf_op jit(solution)/shard_map/all_to_all | solution.py:87
  100.0 0.3 convert_reduce_fusion.1
  100.4 10.5 %collective-permute-start.2 = (bf16[1,512,256]{1,2,0:T(8,128)(2,1)S(1)}, bf16[1,512,256]{1,2,0:T(8,128)(2,1)S(1)}, u32[]{:S(2)}, u32[]{:S(2)}) collective-permute-start(bf16[1,512,256]{1,2,0:T(8,128)(2,1)S(1)} %bitcast_convert_fusion.1), channel_id=1, source_target_pairs={{0,16},{16,0},{1,17},{17,1},{2,18},{18,2},{3,19},{19,3},{4,20},{20... | collective-permute-start | bytes 786440 | tf_op jit(solution)/shard_map/ppermute | solution.py:74
  111.0 0.2 maximum_bitcast_fusion.2
  111.1 0.2 copy.76
  111.4 0.8 scatter_fusion
  112.2 0.7 copy.77
  112.9 9.3 %all-to-all-start.3 = ((bf16[2,4,128,128]{3,2,0,1:T(8,128)(2,1)}), bf16[2,4,128,128]{3,2,0,1:T(8,128)(2,1)S(1)}, u32[]{:S(2)}, u32[]{:S(2)}) async-start(bf16[2,4,128,128]{3,2,0,1:T(8,128)(2,1)} %copy.77), calls=%async_computation.3 | async-start | bytes 524288 | tf_op jit(solution)/shard_map/all_to_all | solution.py:152
  122.2 0.1 fusion.32
  122.4 16.2 %all-to-all-done.3 = bf16[2,4,128,128]{3,2,0,1:T(8,128)(2,1)S(1)} async-done(((bf16[2,4,128,128]{3,2,0,1:T(8,128)(2,1)}), bf16[2,4,128,128]{3,2,0,1:T(8,128)(2,1)S(1)}, u32[]{:S(2)}, u32[]{:S(2)}) %all-to-all-start.3) | async-done | bytes 262176 | tf_op jit(solution)/shard_map/all_to_all | solution.py:152
  138.6 11.1 %collective-permute-done.3 = bf16[1,512,256]{1,2,0:T(8,128)(2,1)S(1)} collective-permute-done((bf16[1,512,256]{1,2,0:T(8,128)(2,1)S(1)}, bf16[1,512,256]{1,2,0:T(8,128)(2,1)S(1)}, u32[]{:S(2)}, u32[]{:S(2)}) %collective-permute-start.3) | collective-permute-done | bytes 262176 | tf_op jit(solution)/shard_map/ppermute | solution.py:74
  149.9 0.2 copy.84
  150.1 1.5 broadcast_in_dim.86
  151.6 4.4 %all-to-all-start.5 = ((bf16[4,2,1,512,256]{4,3,1,2,0:T(8,128)(2,1)}), bf16[4,2,1,512,256]{4,3,1,2,0:T(8,128)(2,1)S(1)}, u32[]{:S(2)}, u32[]{:S(2)}) async-start(bf16[4,2,1,512,256]{4,3,1,2,0:T(8,128)(2,1)} %broadcast_in_dim.86), calls=%async_computation.5 | async-start | bytes 4194304 | tf_op jit(solution)/shard_map/all_to_all | solution.py:83
  156.1 23.3 %all-to-all-done.5 = bf16[4,2,1,512,256]{4,3,1,2,0:T(8,128)(2,1)S(1)} async-done(((bf16[4,2,1,512,256]{4,3,1,2,0:T(8,128)(2,1)}), bf16[4,2,1,512,256]{4,3,1,2,0:T(8,128)(2,1)S(1)}, u32[]{:S(2)}, u32[]{:S(2)}) %all-to-all-start.5) | async-done | bytes 2097184 | tf_op jit(solution)/shard_map/all_to_all | solution.py:83
  179.4 0.5 fusion.5
  179.9 2.5 %slice-done.1 = bf16[2048,1280]{1,0:T(8,128)(2,1)S(1)} async-done(((bf16[2048,1920]{1,0:T(8,128)(2,1)}), bf16[2048,1280]{1,0:T(8,128)(2,1)S(1)}, s32[]{:S(2)}) %slice-start.1) | async-done | bytes 5242904 | tf_op jit(solution)/shard_map/slice | solution.py:194
  182.4 2.9 %fusion.8 = f32[1,512,1280]{2,1,0:T(8,128)S(1)} fusion(bf16[2,4,256,1280]{3,2,1,0:T(8,128)(2,1)S(1)} %bitcast.144, bf16[4,2,1,512,256]{4,3,1,2,0:T(8,128)(2,1)S(1)} %all-to-all-done.5, f32[4,2,256]{2,1,0:T(2,128)S(1)} %copy.85, f32[512]{0:T(512)S(1)} %add_rsqrt_fusion.1), kind=kOutput, calls=%fused_computation.16 | convolution fusion | flops 2688548864 | bytes 9971712 | tf_op jit(solution)/shard_map/xzpse,zxen->psn/dot_general | solution.py:105
  185.3 1.9 convert_bitcast_fusion
  187.2 0.1 copy.87
  187.4 24.9 %all_to_all.35 = bf16[4,1,512,2,256]{2,4,3,1,0:T(8,128)(2,1)S(1)} all-to-all(bf16[4,1,512,2,256]{2,4,3,1,0:T(8,128)(2,1)S(1)} %copy.87), channel_id=1, replica_groups=mesh['ry'=4,'rc'=2,'zh'=2,'xx'=4,'page'=4] {'xx'}, dimensions={0} | all-to-all | bytes 4194304 | tf_op jit(solution)/shard_map/all_to_all | solution.py:87
  212.3 0.3 convert_reduce_fusion
  212.7 9.0 %collective-permute-start.4 = (bf16[1,512,256]{1,2,0:T(8,128)(2,1)S(1)}, bf16[1,512,256]{1,2,0:T(8,128)(2,1)S(1)}, u32[]{:S(2)}, u32[]{:S(2)}) collective-permute-start(bf16[1,512,256]{1,2,0:T(8,128)(2,1)S(1)} %bitcast_convert_fusion), channel_id=1, source_target_pairs={{0,16},{16,0},{1,17},{17,1},{2,18},{18,2},{3,19},{19,3},{4,20},{20... | collective-permute-start | bytes 786440 | tf_op jit(solution)/shard_map/ppermute | solution.py:74
  221.8 0.1 fusion.50
  221.9 0.8 scatter_fusion.1
  222.7 3.4 %collective-permute-done.4 = bf16[1,512,256]{1,2,0:T(8,128)(2,1)S(1)} collective-permute-done((bf16[1,512,256]{1,2,0:T(8,128)(2,1)S(1)}, bf16[1,512,256]{1,2,0:T(8,128)(2,1)S(1)}, u32[]{:S(2)}, u32[]{:S(2)}) %collective-permute-start.4) | collective-permute-done | bytes 262176 | tf_op jit(solution)/shard_map/ppermute | solution.py:74
  226.1 0.1 fusion.30
  226.2 0.8 copy.89
  (94 shorter events, 1.3 us)
Async XLA Ops:
  7.2 2.9 %copy-start = (f32[2,64,256]{2,1,0:T(8,128)S(1)}, f32[2,64,256]{2,1,0:T(8,128)}, u32[]{:S(2)}) copy-start(f32[2,64,256]{2,1,0:T(8,128)} %param.18) | copy-start | bytes 393220
  7.2 3.8 %copy-start.17 = (f32[128,64]{0,1:T(8,128)S(1)}, f32[128,64]{0,1:T(8,128)}, u32[]{:S(2)}) copy-start(f32[128,64]{0,1:T(8,128)} %param.19) | copy-start | bytes 98308
  7.2 10.4 %copy-start.13 = (bf16[1,512,256]{2,1,0:T(8,128)(2,1)S(1)}, bf16[1,512,256]{2,1,0:T(8,128)(2,1)}, u32[]{:S(2)}) copy-start(bf16[1,512,256]{2,1,0:T(8,128)(2,1)} %param.14) | copy-start | bytes 786436
  7.2 172.7 %all-gather.2.cloned.1.call-start = ((), (), s32[]{:S(2)}) async-start(), calls=%async_computation.7 | async-start | bytes 8110080 | tf_op jit(solution)/shard_map/all_gather | solution.py:191
  11.7 13.8 %all-to-all-start.1 = ((bf16[4,64,384]{2,1,0:T(8,128)(2,1)}), bf16[4,64,384]{2,1,0:T(8,128)(2,1)S(1)}, u32[]{:S(2)}, u32[]{:S(2)}) async-start(bf16[4,64,384]{2,1,0:T(8,128)(2,1)} %broadcast_in_dim.72), calls=%async_computation.1 | async-start | bytes 393216 | tf_op jit(solution)/shard_map/all_to_all | solution.py:115
  17.8 14.9 %collective-permute-start = (bf16[1,512,256]{1,2,0:T(8,128)(2,1)S(1)}, bf16[1,512,256]{1,2,0:T(8,128)(2,1)S(1)}, u32[]{:S(2)}, u32[]{:S(2)}) collective-permute-start(bf16[1,512,256]{1,2,0:T(8,128)(2,1)S(1)} %copy.68), channel_id=1, source_target_pairs={{0,16},{16,0},{1,17},{17,1},{2,18},{18,2},{3,19},{19,3},{4,20},{20... | collective-permute-start | bytes 786440 | tf_op jit(solution)/shard_map/ppermute | solution.py:74
  26.6 15.4 %all-to-all-start.2 = ((bf16[4,256,384]{2,1,0:T(8,128)(2,1)}), bf16[4,256,384]{2,1,0:T(8,128)(2,1)S(1)}, u32[]{:S(2)}, u32[]{:S(2)}) async-start(bf16[4,256,384]{2,1,0:T(8,128)(2,1)} %broadcast_in_dim.74), calls=%async_computation.2 | async-start | bytes 1572864 | tf_op jit(solution)/shard_map/all_to_all | solution.py:118
  43.5 4.5 %copy-start.18 = (f32[2048]{0:T(1024)S(1)}, f32[2048]{0:T(1024)}, u32[]{:S(2)}) copy-start(f32[2048]{0:T(1024)} %param.22) | copy-start | bytes 24580
  43.5 25.8 %all-to-all-start = ((bf16[4,2,1,512,256]{4,3,1,2,0:T(8,128)(2,1)}), bf16[4,2,1,512,256]{4,3,1,2,0:T(8,128)(2,1)S(1)}, u32[]{:S(2)}, u32[]{:S(2)}) async-start(bf16[4,2,1,512,256]{4,3,1,2,0:T(8,128)(2,1)} %broadcast_in_dim.71), calls=%async_computation | async-start | bytes 4194304 | tf_op jit(solution)/shard_map/all_to_all | solution.py:83
  47.9 2.5 %collective-permute-start.1 = (bf16[4,256,384]{2,1,0:T(8,128)(2,1)S(1)}, bf16[4,256,384]{2,1,0:T(8,128)(2,1)}, u32[]{:S(2)}, u32[]{:S(2)}) collective-permute-start(bf16[4,256,384]{2,1,0:T(8,128)(2,1)S(1)} %all-to-all-done.2), channel_id=1, source_target_pairs={{0,32},{32,0},{1,33},{33,1},{2,34},{34,2},{3,35},{35,3},{4,36},{36... | collective-permute-start | bytes 2359304 | tf_op jit(solution)/shard_map/ppermute | solution.py:120
  69.3 1.2 copy-start.3
  70.5 0.9 copy-start.21
  70.5 1.4 copy-start.22
  70.5 1.5 copy-start.15
  70.5 1.5 copy-start.16
  71.4 1.0 copy-start.14
  71.9 1.2 copy-start.9
  72.0 1.1 copy-start.11
  76.1 3.8 %copy-start.20 = (s32[4,4]{1,0:T(4,128)S(1)}, s32[4,4]{1,0:T(4,128)}, u32[]{:S(2)}) copy-start(s32[4,4]{1,0:T(4,128)} %param.16) | copy-start | bytes 196
  76.1 4.0 %copy-start.10 = (bf16[512,64]{0,1:T(8,128)(2,1)S(1)}, bf16[512,64]{0,1:T(8,128)(2,1)}, u32[]{:S(2)}) copy-start(bf16[512,64]{0,1:T(8,128)(2,1)} %copy-done.9) | copy-start | bytes 196612
  76.1 4.1 %copy-start.12 = (bf16[512,64]{0,1:T(8,128)(2,1)S(1)}, bf16[512,64]{0,1:T(8,128)(2,1)}, u32[]{:S(2)}) copy-start(bf16[512,64]{0,1:T(8,128)(2,1)} %copy-done.11) | copy-start | bytes 196612
  76.1 23.9 %all-to-all-start.4 = ((bf16[4,1,512,2,256]{2,4,3,1,0:T(8,128)(2,1)}), bf16[4,1,512,2,256]{2,4,3,1,0:T(8,128)(2,1)S(1)}, u32[]{:S(2)}, u32[]{:S(2)}) async-start(bf16[4,1,512,2,256]{2,4,3,1,0:T(8,128)(2,1)} %copy.81), calls=%async_computation.4 | async-start | bytes 4194304 | tf_op jit(solution)/shard_map/all_to_all | solution.py:87
  100.0 10.9 %copy-start.7 = (bf16[1,4,128,128]{2,1,3,0:T(4,128)(2,1)S(1)}, bf16[1,4,128,128]{2,1,3,0:T(4,128)(2,1)}, u32[]{:S(2)}) copy-start(bf16[1,4,128,128]{2,1,3,0:T(4,128)(2,1)} %get-tuple-element.34) | copy-start | bytes 393220
  100.0 10.9 %copy-start.8 = (bf16[1,4,128,128]{2,1,3,0:T(4,128)(2,1)S(1)}, bf16[1,4,128,128]{2,1,3,0:T(4,128)(2,1)}, u32[]{:S(2)}) copy-start(bf16[1,4,128,128]{2,1,3,0:T(4,128)(2,1)} %get-tuple-element.35) | copy-start | bytes 393220
  100.4 21.8 %collective-permute-start.2 = (bf16[1,512,256]{1,2,0:T(8,128)(2,1)S(1)}, bf16[1,512,256]{1,2,0:T(8,128)(2,1)S(1)}, u32[]{:S(2)}, u32[]{:S(2)}) collective-permute-start(bf16[1,512,256]{1,2,0:T(8,128)(2,1)S(1)} %bitcast_convert_fusion.1), channel_id=1, source_target_pairs={{0,16},{16,0},{1,17},{17,1},{2,18},{18,2},{3,19},{19,3},{4,20},{20... | collective-permute-start | bytes 786440 | tf_op jit(solution)/shard_map/ppermute | solution.py:74
  112.9 25.7 %all-to-all-start.3 = ((bf16[2,4,128,128]{3,2,0,1:T(8,128)(2,1)}), bf16[2,4,128,128]{3,2,0,1:T(8,128)(2,1)S(1)}, u32[]{:S(2)}, u32[]{:S(2)}) async-start(bf16[2,4,128,128]{3,2,0,1:T(8,128)(2,1)} %copy.77), calls=%async_computation.3 | async-start | bytes 524288 | tf_op jit(solution)/shard_map/all_to_all | solution.py:152
  122.3 29.2 %copy-start.1 = (bf16[1,512,256]{1,2,0:T(8,128)(2,1)}, bf16[1,512,256]{1,2,0:T(8,128)(2,1)S(1)}, u32[]{:S(2)}) copy-start(bf16[1,512,256]{1,2,0:T(8,128)(2,1)S(1)} %fusion.32) | copy-start | bytes 786436
  138.6 11.2 %copy-start.4 = (bf16[2,4,128,128]{3,2,0,1:T(8,128)(2,1)}, bf16[2,4,128,128]{3,2,0,1:T(8,128)(2,1)S(1)}, u32[]{:S(2)}) copy-start(bf16[2,4,128,128]{3,2,0,1:T(8,128)(2,1)S(1)} %all-to-all-done.3) | copy-start | bytes 786436
  138.6 11.1 %collective-permute-start.3 = (bf16[1,512,256]{1,2,0:T(8,128)(2,1)S(1)}, bf16[1,512,256]{1,2,0:T(8,128)(2,1)S(1)}, u32[]{:S(2)}, u32[]{:S(2)}) collective-permute-start(bf16[1,512,256]{1,2,0:T(8,128)(2,1)S(1)} %fusion.32), channel_id=1, source_target_pairs={{0,16},{16,0},{1,17},{17,1},{2,18},{18,2},{3,19},{19,3},{4,20},{20... | collective-permute-start | bytes 786440 | tf_op jit(solution)/shard_map/ppermute | solution.py:74
  151.6 4.4 %copy-start.19 = (f32[2048]{0:T(1024)S(1)}, f32[2048]{0:T(1024)}, u32[]{:S(2)}) copy-start(f32[2048]{0:T(1024)} %param.23) | copy-start | bytes 24580
  151.6 27.8 %all-to-all-start.5 = ((bf16[4,2,1,512,256]{4,3,1,2,0:T(8,128)(2,1)}), bf16[4,2,1,512,256]{4,3,1,2,0:T(8,128)(2,1)S(1)}, u32[]{:S(2)}, u32[]{:S(2)}) async-start(bf16[4,2,1,512,256]{4,3,1,2,0:T(8,128)(2,1)} %broadcast_in_dim.86), calls=%async_computation.5 | async-start | bytes 4194304 | tf_op jit(solution)/shard_map/all_to_all | solution.py:83
  179.9 2.5 %slice-start.1 = ((bf16[2048,1920]{1,0:T(8,128)(2,1)}), bf16[2048,1280]{1,0:T(8,128)(2,1)S(1)}, s32[]{:S(2)}) async-start(bf16[2048,1920]{1,0:T(8,128)(2,1)} %all-gather.2.cloned.1.call-done), calls=%async_computation.9 | async-start | bytes 10485760 | tf_op jit(solution)/shard_map/slice | solution.py:194
  182.4 2.9 %slice-start = ((bf16[2048,1920]{1,0:T(8,128)(2,1)}), bf16[2048,640]{1,0:T(8,128)(2,1)S(1)}, s32[]{:S(2)}) async-start(bf16[2048,1920]{1,0:T(8,128)(2,1)} %all-gather.2.cloned.1.call-done), calls=%async_computation.8 | async-start | bytes 5242880 | tf_op jit(solution)/shard_map/slice | solution.py:195
  212.3 9.6 %copy-start.5 = (bf16[2,4,128,128]{3,2,0,1:T(8,128)(2,1)S(1)}, bf16[2,4,128,128]{3,2,0,1:T(8,128)(2,1)}, u32[]{:S(2)}) copy-start(bf16[2,4,128,128]{3,2,0,1:T(8,128)(2,1)} %copy-done.4) | copy-start | bytes 786436
  212.3 13.8 %copy-start.2 = (bf16[1,512,256]{1,2,0:T(8,128)(2,1)S(1)}, bf16[1,512,256]{1,2,0:T(8,128)(2,1)}, u32[]{:S(2)}) copy-start(bf16[1,512,256]{1,2,0:T(8,128)(2,1)} %copy-done.1) | copy-start | bytes 786436
  212.7 13.4 %collective-permute-start.4 = (bf16[1,512,256]{1,2,0:T(8,128)(2,1)S(1)}, bf16[1,512,256]{1,2,0:T(8,128)(2,1)S(1)}, u32[]{:S(2)}, u32[]{:S(2)}) collective-permute-start(bf16[1,512,256]{1,2,0:T(8,128)(2,1)S(1)} %bitcast_convert_fusion), channel_id=1, source_target_pairs={{0,16},{16,0},{1,17},{17,1},{2,18},{18,2},{3,19},{19,3},{4,20},{20... | collective-permute-start | bytes 786440 | tf_op jit(solution)/shard_map/ppermute | solution.py:74
  222.7 4.4 %copy-start.6 = (bf16[2,4,128,128]{3,2,1,0:T(8,128)(2,1)}, bf16[2,4,128,128]{3,2,1,0:T(8,128)(2,1)S(1)}, u32[]{:S(2)}) copy-start(bf16[2,4,128,128]{3,2,1,0:T(8,128)(2,1)S(1)} %scatter_fusion.1) | copy-start | bytes 786436
Sparse Core Ops, SparseCore 0:
  10.1 101.9 all-gather.1

commit v14 on v13

--- a/solution.py
+++ b/solution.py
@@ -115,7 +115,12 @@
     got = lax.all_to_all(jnp.broadcast_to(x[None], (pages,) + x.shape), "page", 0, 0, tiled=True)
     got = got.reshape((-1,) + x.shape[1:])
     chips = lax.axis_size("ry")
-    got = lax.all_to_all(jnp.broadcast_to(got[None], (chips,) + got.shape), "ry", 0, 0, tiled=True)
+    chip = lax.axis_index("ry")
+    shifted = [got] + [
+        lax.ppermute(got, "ry", [(i, (i + k) % chips) for i in range(chips)]) for k in range(1, chips)
+    ]
+    source_shift = (chip - jnp.arange(chips, dtype=jnp.int32)) % chips
+    got = jnp.take(jnp.stack(shifted), source_shift, axis=0)
     core = lax.axis_index("rc")
     other = lax.ppermute(got, "rc", [(0, 1), (1, 0)])
     got = jnp.stack([jnp.where(core == 0, got, other), jnp.where(core == 0, other, got)], axis=1)

time: 235 us -> 231 us (0.983)
  starting transfers between devices: 57.1 us -> 45.8 us
  blocking collectives: 24.9 us -> 27.4 us
    all_to_all x1 -> x0, waiting for transfers between devices: 8.96 us -> none  [gather_rows(): lax.all_to_all(jnp.broadcast_to(got[None], (chips,) + got.shape), 'ry', 0...]
    ppermute x4, waiting for transfers between devices: 15.7 us -> 24.5 us  [swap_halves(): return lax.ppermute(x, 'zh', [(0, 1), (1, 0)])]
    ppermute x4, starting transfers between devices: 24.3 us -> 16.7 us  [swap_halves(): return lax.ppermute(x, 'zh', [(0, 1), (1, 0)])]
    all_to_all x1, waiting for transfers between devices: 16.2 us -> 11.1 us  [send_pages(): lax.all_to_all(outgoing, 'page', split_axis=1, concat_axis=1, tiled=True)]
    ppermute x0 -> x3, starting transfers between devices: none -> 4.93 us  [gather_rows(): lax.ppermute(got, 'ry', [(i, (i + k) % chips) for i in range(chips)])]
    all_to_all x1 -> x0, starting transfers between devices: 4.91 us -> none  [gather_rows(): lax.all_to_all(jnp.broadcast_to(got[None], (chips,) + got.shape), 'ry', 0...]
    all_to_all x1, waiting for transfers between devices: 18.9 us -> 23.5 us  [scatter_sum_col(): got = lax.all_to_all(terms, 'xx', 0, 0, tiled=True)]
    all_to_all x1, starting transfers between devices: 9.32 us -> 6.51 us  [send_pages(): lax.all_to_all(outgoing, 'page', split_axis=1, concat_axis=1, tiled=True)]
  transfers between devices with their start and end apart: 12 -> 14, of which waited for: 9 -> 9; matrix products, arithmetic and copies ran while one was open for 10% -> 12% of each run, Pallas kernels for 0% -> 0%
where the time goes in v14:
time: 231 us; the launch traced here: 230 us
  waiting for transfers between devices  102 us (44%)
  starting transfers between devices  45.8 us (20%)
  blocking collectives  27.4 us (12%)
  local copies, waits for them, and re-layouts  18.5 us (8%)
  between operations  15.3 us (7%)
  other arithmetic  13.1 us (6%)
  matrix products  7.82 us (3%)
    all_to_all x2, waiting for transfers between devices, gather_col(): return lax.all_to_all(copies, 'xx', 0, 0, tiled=True)  39.7 us
    all_to_all x1, blocking collectives, scatter_sum_col(): got = lax.all_to_all(terms, 'xx', 0, 0, tiled=True)  27.4 us
    ppermute x4, waiting for transfers between devices, swap_halves(): return lax.ppermute(x, 'zh', [(0, 1), (1, 0)])  24.5 us
    all_to_all x1, waiting for transfers between devices, scatter_sum_col(): got = lax.all_to_all(terms, 'xx', 0, 0, tiled=True)  23.5 us
    ppermute x4, starting transfers between devices, swap_halves(): return lax.ppermute(x, 'zh', [(0, 1), (1, 0)])  16.7 us
    all_to_all x1, waiting for transfers between devices, send_pages(): lax.all_to_all(outgoing, 'page', split_axis=1, concat_axis=1, tiled=True)  11.1 us
    all_to_all x2, starting transfers between devices, gather_col(): return lax.all_to_all(copies, 'xx', 0, 0, tiled=True)  8.03 us
    all_to_all x1, starting transfers between devices, send_pages(): lax.all_to_all(outgoing, 'page', split_axis=1, concat_axis=1, tiled=True)  6.51 us
  transfers between devices with their start and end apart: 14, of which 9 were waited for; matrix products, arithmetic and copies ran while one was open for 12% of the time, Pallas kernels for 0%

profile of v14, /device:TPU:8, one launch (start us, length us, event | category | flops | bytes accessed | tf_op | source)
XLA Modules:
  0.0 229.9 jit_solution(3045704767762126794)
XLA Ops:
  7.2 1.0 convert_bitcast_fusion.3
  8.2 1.0 convert_bitcast_fusion.2
  9.3 0.7 pad_maximum_fusion.2
  10.3 0.8 convert_element_type.105
  11.1 0.7 broadcast_in_dim.79
  11.7 5.9 %all-to-all-start.1 = ((bf16[4,64,384]{2,1,0:T(8,128)(2,1)}), bf16[4,64,384]{2,1,0:T(8,128)(2,1)S(1)}, u32[]{:S(2)}, u32[]{:S(2)}) async-start(bf16[4,64,384]{2,1,0:T(8,128)(2,1)} %broadcast_in_dim.79), calls=%async_computation.1 | async-start | bytes 393216 | tf_op jit(solution)/shard_map/all_to_all | solution.py:115
  17.6 0.1 copy.68
  17.8 4.8 %collective-permute-start = (bf16[1,512,256]{1,2,0:T(8,128)(2,1)S(1)}, bf16[1,512,256]{1,2,0:T(8,128)(2,1)S(1)}, u32[]{:S(2)}, u32[]{:S(2)}) collective-permute-start(bf16[1,512,256]{1,2,0:T(8,128)(2,1)S(1)} %copy.68), channel_id=1, source_target_pairs={{0,16},{16,0},{1,17},{17,1},{2,18},{18,2},{3,19},{19,3},{4,20},{20... | collective-permute-start | bytes 786440 | tf_op jit(solution)/shard_map/ppermute | solution.py:74
  22.6 2.9 %all-to-all-done.1 = bf16[4,64,384]{2,1,0:T(8,128)(2,1)S(1)} async-done(((bf16[4,64,384]{2,1,0:T(8,128)(2,1)}), bf16[4,64,384]{2,1,0:T(8,128)(2,1)S(1)}, u32[]{:S(2)}, u32[]{:S(2)}) %all-to-all-start.1) | async-done | bytes 196640 | tf_op jit(solution)/shard_map/all_to_all | solution.py:115
  25.5 0.4 collective-permute-start.3
  26.0 2.6 %collective-permute-start.2 = (bf16[256,384]{1,0:T(8,128)(2,1)S(1)}, bf16[256,384]{1,0:T(8,128)(2,1)S(1)}, u32[]{:S(2)}, u32[]{:S(2)}) collective-permute-start(bf16[256,384]{1,0:T(8,128)(2,1)S(1)} %bitcast.162), channel_id=1, source_target_pairs={{0,128},{64,192},{128,0},{192,64},{1,129},{65,193},{129,1},{193,65... | collective-permute-start | bytes 589832 | tf_op jit(solution)/shard_map/ppermute | solution.py:120
  28.6 1.9 collective-permute-start.1
  30.5 2.2 collective-permute-done
  32.8 0.2 copy.70
  33.0 1.5 broadcast_in_dim.77
  34.5 4.3 %all-to-all-start = ((bf16[4,2,1,512,256]{4,3,1,2,0:T(8,128)(2,1)}), bf16[4,2,1,512,256]{4,3,1,2,0:T(8,128)(2,1)S(1)}, u32[]{:S(2)}, u32[]{:S(2)}) async-start(bf16[4,2,1,512,256]{4,3,1,2,0:T(8,128)(2,1)} %broadcast_in_dim.77), calls=%async_computation | async-start | bytes 4194304 | tf_op jit(solution)/shard_map/all_to_all | solution.py:83
  38.9 1.0 pad_maximum_fusion.1
  39.9 1.9 gather_fusion
  41.8 1.1 broadcast_select_fusion
  43.5 1.0 fusion.41
  44.5 0.8 fusion.26
  45.3 0.2 collective-permute-done.4
  45.5 1.4 select_bitcast_fusion.1
  46.9 0.2 pad_maximum_fusion
  47.1 1.0 slice.66
  48.1 2.3 copy.74
  50.4 14.0 %all-to-all-done = bf16[4,2,1,512,256]{4,3,1,2,0:T(8,128)(2,1)S(1)} async-done(((bf16[4,2,1,512,256]{4,3,1,2,0:T(8,128)(2,1)}), bf16[4,2,1,512,256]{4,3,1,2,0:T(8,128)(2,1)S(1)}, u32[]{:S(2)}, u32[]{:S(2)}) %all-to-all-start) | async-done | bytes 2097184 | tf_op jit(solution)/shard_map/all_to_all | solution.py:83
  64.5 0.5 fusion.2
  65.0 0.7 copy-done.3
  65.7 0.8 fusion.22
  66.7 0.3 fusion.47
  67.3 0.2 copy-done.14
  67.5 0.7 fusion.20
  68.3 0.7 fusion.25
  69.0 0.7 convert_bitcast_fusion.1
  69.7 1.6 copy.81
  71.3 3.7 %all-to-all-start.3 = ((bf16[4,1,512,2,256]{2,4,3,1,0:T(8,128)(2,1)}), bf16[4,1,512,2,256]{2,4,3,1,0:T(8,128)(2,1)S(1)}, u32[]{:S(2)}, u32[]{:S(2)}) async-start(bf16[4,1,512,2,256]{2,4,3,1,0:T(8,128)(2,1)} %copy.81), calls=%async_computation.3 | async-start | bytes 4194304 | tf_op jit(solution)/shard_map/all_to_all | solution.py:87
  75.1 0.2 convert_reduce_fusion.2
  75.5 0.8 broadcast_select_fusion.2
  76.3 23.5 %all-to-all-done.3 = bf16[4,1,512,2,256]{2,4,3,1,0:T(8,128)(2,1)S(1)} async-done(((bf16[4,1,512,2,256]{2,4,3,1,0:T(8,128)(2,1)}), bf16[4,1,512,2,256]{2,4,3,1,0:T(8,128)(2,1)S(1)}, u32[]{:S(2)}, u32[]{:S(2)}) %all-to-all-start.3) | async-done | bytes 2097184 | tf_op jit(solution)/shard_map/all_to_all | solution.py:87
  99.8 0.3 convert_reduce_fusion.1
  100.2 4.5 %collective-permute-start.5 = (bf16[1,512,256]{1,2,0:T(8,128)(2,1)S(1)}, bf16[1,512,256]{1,2,0:T(8,128)(2,1)S(1)}, u32[]{:S(2)}, u32[]{:S(2)}) collective-permute-start(bf16[1,512,256]{1,2,0:T(8,128)(2,1)S(1)} %bitcast_convert_fusion.1), channel_id=1, source_target_pairs={{0,16},{16,0},{1,17},{17,1},{2,18},{18,2},{3,19},{19,3},{4,20},{20... | collective-permute-start | bytes 786440 | tf_op jit(solution)/shard_map/ppermute | solution.py:74
  104.7 0.2 maximum_bitcast_fusion.2
  104.9 0.2 copy.76
  105.1 0.8 scatter_fusion
  105.9 0.7 copy.77
  106.6 6.5 %all-to-all-start.2 = ((bf16[2,4,128,128]{3,2,0,1:T(8,128)(2,1)}), bf16[2,4,128,128]{3,2,0,1:T(8,128)(2,1)S(1)}, u32[]{:S(2)}, u32[]{:S(2)}) async-start(bf16[2,4,128,128]{3,2,0,1:T(8,128)(2,1)} %copy.77), calls=%async_computation.2 | async-start | bytes 524288 | tf_op jit(solution)/shard_map/all_to_all | solution.py:157
  113.3 11.1 %all-to-all-done.2 = bf16[2,4,128,128]{3,2,0,1:T(8,128)(2,1)S(1)} async-done(((bf16[2,4,128,128]{3,2,0,1:T(8,128)(2,1)}), bf16[2,4,128,128]{3,2,0,1:T(8,128)(2,1)S(1)}, u32[]{:S(2)}, u32[]{:S(2)}) %all-to-all-start.2) | async-done | bytes 262176 | tf_op jit(solution)/shard_map/all_to_all | solution.py:157
  124.3 3.1 %collective-permute-start.6 = (bf16[1,512,256]{1,2,0:T(8,128)(2,1)S(1)}, bf16[1,512,256]{1,2,0:T(8,128)(2,1)S(1)}, u32[]{:S(2)}, u32[]{:S(2)}) collective-permute-start(bf16[1,512,256]{1,2,0:T(8,128)(2,1)S(1)} %fusion.32), channel_id=1, source_target_pairs={{0,16},{16,0},{1,17},{17,1},{2,18},{18,2},{3,19},{19,3},{4,20},{20... | collective-permute-start | bytes 786440 | tf_op jit(solution)/shard_map/ppermute | solution.py:74
  127.5 14.6 %collective-permute-done.6 = bf16[1,512,256]{1,2,0:T(8,128)(2,1)S(1)} collective-permute-done((bf16[1,512,256]{1,2,0:T(8,128)(2,1)S(1)}, bf16[1,512,256]{1,2,0:T(8,128)(2,1)S(1)}, u32[]{:S(2)}, u32[]{:S(2)}) %collective-permute-start.6) | collective-permute-done | bytes 262176 | tf_op jit(solution)/shard_map/ppermute | solution.py:74
  142.2 0.2 copy.84
  142.4 1.5 broadcast_in_dim.146
  143.9 3.7 %all-to-all-start.4 = ((bf16[4,2,1,512,256]{4,3,1,2,0:T(8,128)(2,1)}), bf16[4,2,1,512,256]{4,3,1,2,0:T(8,128)(2,1)S(1)}, u32[]{:S(2)}, u32[]{:S(2)}) async-start(bf16[4,2,1,512,256]{4,3,1,2,0:T(8,128)(2,1)} %broadcast_in_dim.146), calls=%async_computation.4 | async-start | bytes 4194304 | tf_op jit(solution)/shard_map/all_to_all | solution.py:83
  147.7 25.7 %all-to-all-done.4 = bf16[4,2,1,512,256]{4,3,1,2,0:T(8,128)(2,1)S(1)} async-done(((bf16[4,2,1,512,256]{4,3,1,2,0:T(8,128)(2,1)}), bf16[4,2,1,512,256]{4,3,1,2,0:T(8,128)(2,1)S(1)}, u32[]{:S(2)}, u32[]{:S(2)}) %all-to-all-start.4) | async-done | bytes 2097184 | tf_op jit(solution)/shard_map/all_to_all | solution.py:83
  173.4 0.5 fusion.5
  174.0 2.5 %slice-done.1 = bf16[2048,1280]{1,0:T(8,128)(2,1)S(1)} async-done(((bf16[2048,1920]{1,0:T(8,128)(2,1)}), bf16[2048,1280]{1,0:T(8,128)(2,1)S(1)}, s32[]{:S(2)}) %slice-start.1) | async-done | bytes 5242904 | tf_op jit(solution)/shard_map/slice | solution.py:199
  176.5 2.9 %fusion.8 = f32[1,512,1280]{2,1,0:T(8,128)S(1)} fusion(bf16[2,4,256,1280]{3,2,1,0:T(8,128)(2,1)S(1)} %bitcast.150, bf16[4,2,1,512,256]{4,3,1,2,0:T(8,128)(2,1)S(1)} %all-to-all-done.4, f32[4,2,256]{2,1,0:T(2,128)S(1)} %copy.85, f32[512]{0:T(512)S(1)} %add_rsqrt_fusion.1), kind=kOutput, calls=%fused_computation.17 | convolution fusion | flops 2688548864 | bytes 9971712 | tf_op jit(solution)/shard_map/xzpse,zxen->psn/dot_general | solution.py:105
  179.4 1.9 convert_bitcast_fusion
  181.5 27.4 %all_to_all.30 = bf16[4,1,512,2,256]{2,4,3,1,0:T(8,128)(2,1)S(1)} all-to-all(bf16[4,1,512,2,256]{2,4,3,1,0:T(8,128)(2,1)S(1)} %copy.87), channel_id=1, replica_groups=mesh['ry'=4,'rc'=2,'zh'=2,'xx'=4,'page'=4] {'xx'}, dimensions={0} | all-to-all | bytes 4194304 | tf_op jit(solution)/shard_map/all_to_all | solution.py:87
  208.9 0.3 convert_reduce_fusion
  209.2 4.3 %collective-permute-start.7 = (bf16[1,512,256]{1,2,0:T(8,128)(2,1)S(1)}, bf16[1,512,256]{1,2,0:T(8,128)(2,1)S(1)}, u32[]{:S(2)}, u32[]{:S(2)}) collective-permute-start(bf16[1,512,256]{1,2,0:T(8,128)(2,1)S(1)} %bitcast_convert_fusion), channel_id=1, source_target_pairs={{0,16},{16,0},{1,17},{17,1},{2,18},{18,2},{3,19},{19,3},{4,20},{20... | collective-permute-start | bytes 786440 | tf_op jit(solution)/shard_map/ppermute | solution.py:74
  213.7 0.8 scatter_fusion.1
  214.5 7.6 %collective-permute-done.7 = bf16[1,512,256]{1,2,0:T(8,128)(2,1)S(1)} collective-permute-done((bf16[1,512,256]{1,2,0:T(8,128)(2,1)S(1)}, bf16[1,512,256]{1,2,0:T(8,128)(2,1)S(1)}, u32[]{:S(2)}, u32[]{:S(2)}) %collective-permute-start.7) | collective-permute-done | bytes 262176 | tf_op jit(solution)/shard_map/ppermute | solution.py:74
  222.2 0.8 copy.89
  (103 shorter events, 1.9 us)
Async XLA Ops:
  7.2 2.9 %copy-start = (f32[2,64,256]{2,1,0:T(8,128)S(1)}, f32[2,64,256]{2,1,0:T(8,128)}, u32[]{:S(2)}) copy-start(f32[2,64,256]{2,1,0:T(8,128)} %param.18) | copy-start | bytes 393220
  7.2 3.8 %copy-start.17 = (f32[128,64]{0,1:T(8,128)S(1)}, f32[128,64]{0,1:T(8,128)}, u32[]{:S(2)}) copy-start(f32[128,64]{0,1:T(8,128)} %param.19) | copy-start | bytes 98308
  7.2 10.5 %copy-start.13 = (bf16[1,512,256]{2,1,0:T(8,128)(2,1)S(1)}, bf16[1,512,256]{2,1,0:T(8,128)(2,1)}, u32[]{:S(2)}) copy-start(bf16[1,512,256]{2,1,0:T(8,128)(2,1)} %param.14) | copy-start | bytes 786436
  7.2 166.8 %all-gather.2.cloned.1.call-start = ((), (), s32[]{:S(2)}) async-start(), calls=%async_computation.6 | async-start | bytes 8110080 | tf_op jit(solution)/shard_map/all_gather | solution.py:196
  11.7 13.8 %all-to-all-start.1 = ((bf16[4,64,384]{2,1,0:T(8,128)(2,1)}), bf16[4,64,384]{2,1,0:T(8,128)(2,1)S(1)}, u32[]{:S(2)}, u32[]{:S(2)}) async-start(bf16[4,64,384]{2,1,0:T(8,128)(2,1)} %broadcast_in_dim.79), calls=%async_computation.1 | async-start | bytes 393216 | tf_op jit(solution)/shard_map/all_to_all | solution.py:115
  17.8 14.9 %collective-permute-start = (bf16[1,512,256]{1,2,0:T(8,128)(2,1)S(1)}, bf16[1,512,256]{1,2,0:T(8,128)(2,1)S(1)}, u32[]{:S(2)}, u32[]{:S(2)}) collective-permute-start(bf16[1,512,256]{1,2,0:T(8,128)(2,1)S(1)} %copy.68), channel_id=1, source_target_pairs={{0,16},{16,0},{1,17},{17,1},{2,18},{18,2},{3,19},{19,3},{4,20},{20... | collective-permute-start | bytes 786440 | tf_op jit(solution)/shard_map/ppermute | solution.py:74
  25.5 13.3 %collective-permute-start.3 = (bf16[256,384]{1,0:T(8,128)(2,1)S(1)}, bf16[256,384]{1,0:T(8,128)(2,1)S(1)}, u32[]{:S(2)}, u32[]{:S(2)}) collective-permute-start(bf16[256,384]{1,0:T(8,128)(2,1)S(1)} %bitcast.161), channel_id=1, source_target_pairs={{0,192},{64,0},{128,64},{192,128},{1,193},{65,1},{129,65},{193,129... | collective-permute-start | bytes 589832 | tf_op jit(solution)/shard_map/ppermute | solution.py:120
  26.0 12.8 %collective-permute-start.2 = (bf16[256,384]{1,0:T(8,128)(2,1)S(1)}, bf16[256,384]{1,0:T(8,128)(2,1)S(1)}, u32[]{:S(2)}, u32[]{:S(2)}) collective-permute-start(bf16[256,384]{1,0:T(8,128)(2,1)S(1)} %bitcast.162), channel_id=1, source_target_pairs={{0,128},{64,192},{128,0},{192,64},{1,129},{65,193},{129,1},{193,65... | collective-permute-start | bytes 589832 | tf_op jit(solution)/shard_map/ppermute | solution.py:120
  28.6 10.3 %collective-permute-start.1 = (bf16[256,384]{1,0:T(8,128)(2,1)S(1)}, bf16[256,384]{1,0:T(8,128)(2,1)S(1)}, u32[]{:S(2)}, u32[]{:S(2)}) collective-permute-start(bf16[256,384]{1,0:T(8,128)(2,1)S(1)} %bitcast.163), channel_id=1, source_target_pairs={{0,64},{64,128},{128,192},{192,0},{1,65},{65,129},{129,193},{193,1... | collective-permute-start | bytes 589832 | tf_op jit(solution)/shard_map/ppermute | solution.py:120
  34.5 29.9 %all-to-all-start = ((bf16[4,2,1,512,256]{4,3,1,2,0:T(8,128)(2,1)}), bf16[4,2,1,512,256]{4,3,1,2,0:T(8,128)(2,1)S(1)}, u32[]{:S(2)}, u32[]{:S(2)}) async-start(bf16[4,2,1,512,256]{4,3,1,2,0:T(8,128)(2,1)} %broadcast_in_dim.77), calls=%async_computation | async-start | bytes 4194304 | tf_op jit(solution)/shard_map/all_to_all | solution.py:83
  38.9 4.0 %copy-start.18 = (f32[2048]{0:T(1024)S(1)}, f32[2048]{0:T(1024)}, u32[]{:S(2)}) copy-start(f32[2048]{0:T(1024)} %param.22) | copy-start | bytes 24580
  42.8 2.7 %collective-permute-start.4 = (bf16[4,256,384]{2,1,0:T(8,128)(2,1)}, bf16[4,256,384]{2,1,0:T(8,128)(2,1)}, u32[]{:S(2)}, u32[]{:S(2)}) collective-permute-start(bf16[4,256,384]{2,1,0:T(8,128)(2,1)} %broadcast_select_fusion), channel_id=1, source_target_pairs={{0,32},{32,0},{1,33},{33,1},{2,34},{34,2},{3,35},{35,3},{4,36},{36... | collective-permute-start | bytes 2359304 | tf_op jit(solution)/shard_map/ppermute | solution.py:125
  64.5 1.2 copy-start.3
  65.7 0.9 copy-start.21
  65.7 1.4 copy-start.22
  65.7 1.5 copy-start.15
  65.7 1.5 copy-start.16
  66.6 1.0 copy-start.14
  67.0 1.2 copy-start.9
  67.1 1.1 copy-start.11
  71.3 3.8 %copy-start.20 = (s32[4,4]{1,0:T(4,128)S(1)}, s32[4,4]{1,0:T(4,128)}, u32[]{:S(2)}) copy-start(s32[4,4]{1,0:T(4,128)} %param.16) | copy-start | bytes 196
  71.3 4.1 %copy-start.10 = (bf16[512,64]{0,1:T(8,128)(2,1)S(1)}, bf16[512,64]{0,1:T(8,128)(2,1)}, u32[]{:S(2)}) copy-start(bf16[512,64]{0,1:T(8,128)(2,1)} %copy-done.9) | copy-start | bytes 196612
  71.3 4.1 %copy-start.12 = (bf16[512,64]{0,1:T(8,128)(2,1)S(1)}, bf16[512,64]{0,1:T(8,128)(2,1)}, u32[]{:S(2)}) copy-start(bf16[512,64]{0,1:T(8,128)(2,1)} %copy-done.11) | copy-start | bytes 196612
  71.3 28.5 %all-to-all-start.3 = ((bf16[4,1,512,2,256]{2,4,3,1,0:T(8,128)(2,1)}), bf16[4,1,512,2,256]{2,4,3,1,0:T(8,128)(2,1)S(1)}, u32[]{:S(2)}, u32[]{:S(2)}) async-start(bf16[4,1,512,2,256]{2,4,3,1,0:T(8,128)(2,1)} %copy.81), calls=%async_computation.3 | async-start | bytes 4194304 | tf_op jit(solution)/shard_map/all_to_all | solution.py:87
  99.8 4.9 %copy-start.7 = (bf16[1,4,128,128]{2,1,3,0:T(4,128)(2,1)S(1)}, bf16[1,4,128,128]{2,1,3,0:T(4,128)(2,1)}, u32[]{:S(2)}) copy-start(bf16[1,4,128,128]{2,1,3,0:T(4,128)(2,1)} %get-tuple-element.34) | copy-start | bytes 393220
  99.8 4.9 %copy-start.8 = (bf16[1,4,128,128]{2,1,3,0:T(4,128)(2,1)S(1)}, bf16[1,4,128,128]{2,1,3,0:T(4,128)(2,1)}, u32[]{:S(2)}) copy-start(bf16[1,4,128,128]{2,1,3,0:T(4,128)(2,1)} %get-tuple-element.35) | copy-start | bytes 393220
  100.2 13.0 %collective-permute-start.5 = (bf16[1,512,256]{1,2,0:T(8,128)(2,1)S(1)}, bf16[1,512,256]{1,2,0:T(8,128)(2,1)S(1)}, u32[]{:S(2)}, u32[]{:S(2)}) collective-permute-start(bf16[1,512,256]{1,2,0:T(8,128)(2,1)S(1)} %bitcast_convert_fusion.1), channel_id=1, source_target_pairs={{0,16},{16,0},{1,17},{17,1},{2,18},{18,2},{3,19},{19,3},{4,20},{20... | collective-permute-start | bytes 786440 | tf_op jit(solution)/shard_map/ppermute | solution.py:74
  106.6 17.7 %all-to-all-start.2 = ((bf16[2,4,128,128]{3,2,0,1:T(8,128)(2,1)}), bf16[2,4,128,128]{3,2,0,1:T(8,128)(2,1)S(1)}, u32[]{:S(2)}, u32[]{:S(2)}) async-start(bf16[2,4,128,128]{3,2,0,1:T(8,128)(2,1)} %copy.77), calls=%async_computation.2 | async-start | bytes 524288 | tf_op jit(solution)/shard_map/all_to_all | solution.py:157
  113.2 30.7 %copy-start.1 = (bf16[1,512,256]{1,2,0:T(8,128)(2,1)}, bf16[1,512,256]{1,2,0:T(8,128)(2,1)S(1)}, u32[]{:S(2)}) copy-start(bf16[1,512,256]{1,2,0:T(8,128)(2,1)S(1)} %fusion.32) | copy-start | bytes 786436
  124.3 17.8 %copy-start.4 = (bf16[2,4,128,128]{3,2,0,1:T(8,128)(2,1)}, bf16[2,4,128,128]{3,2,0,1:T(8,128)(2,1)S(1)}, u32[]{:S(2)}) copy-start(bf16[2,4,128,128]{3,2,0,1:T(8,128)(2,1)S(1)} %all-to-all-done.2) | copy-start | bytes 786436
  124.3 17.8 %collective-permute-start.6 = (bf16[1,512,256]{1,2,0:T(8,128)(2,1)S(1)}, bf16[1,512,256]{1,2,0:T(8,128)(2,1)S(1)}, u32[]{:S(2)}, u32[]{:S(2)}) collective-permute-start(bf16[1,512,256]{1,2,0:T(8,128)(2,1)S(1)} %fusion.32), channel_id=1, source_target_pairs={{0,16},{16,0},{1,17},{17,1},{2,18},{18,2},{3,19},{19,3},{4,20},{20... | collective-permute-start | bytes 786440 | tf_op jit(solution)/shard_map/ppermute | solution.py:74
  143.9 3.8 %copy-start.19 = (f32[2048]{0:T(1024)S(1)}, f32[2048]{0:T(1024)}, u32[]{:S(2)}) copy-start(f32[2048]{0:T(1024)} %param.23) | copy-start | bytes 24580
  143.9 29.5 %all-to-all-start.4 = ((bf16[4,2,1,512,256]{4,3,1,2,0:T(8,128)(2,1)}), bf16[4,2,1,512,256]{4,3,1,2,0:T(8,128)(2,1)S(1)}, u32[]{:S(2)}, u32[]{:S(2)}) async-start(bf16[4,2,1,512,256]{4,3,1,2,0:T(8,128)(2,1)} %broadcast_in_dim.146), calls=%async_computation.4 | async-start | bytes 4194304 | tf_op jit(solution)/shard_map/all_to_all | solution.py:83
  174.0 2.5 %slice-start.1 = ((bf16[2048,1920]{1,0:T(8,128)(2,1)}), bf16[2048,1280]{1,0:T(8,128)(2,1)S(1)}, s32[]{:S(2)}) async-start(bf16[2048,1920]{1,0:T(8,128)(2,1)} %all-gather.2.cloned.1.call-done), calls=%async_computation.8 | async-start | bytes 10485760 | tf_op jit(solution)/shard_map/slice | solution.py:199
  176.5 2.9 %slice-start = ((bf16[2048,1920]{1,0:T(8,128)(2,1)}), bf16[2048,640]{1,0:T(8,128)(2,1)S(1)}, s32[]{:S(2)}) async-start(bf16[2048,1920]{1,0:T(8,128)(2,1)} %all-gather.2.cloned.1.call-done), calls=%async_computation.7 | async-start | bytes 5242880 | tf_op jit(solution)/shard_map/slice | solution.py:200
  208.9 4.9 %copy-start.5 = (bf16[2,4,128,128]{3,2,0,1:T(8,128)(2,1)S(1)}, bf16[2,4,128,128]{3,2,0,1:T(8,128)(2,1)}, u32[]{:S(2)}) copy-start(bf16[2,4,128,128]{3,2,0,1:T(8,128)(2,1)} %copy-done.4) | copy-start | bytes 786436
  208.9 13.3 %copy-start.2 = (bf16[1,512,256]{1,2,0:T(8,128)(2,1)S(1)}, bf16[1,512,256]{1,2,0:T(8,128)(2,1)}, u32[]{:S(2)}) copy-start(bf16[1,512,256]{1,2,0:T(8,128)(2,1)} %copy-done.1) | copy-start | bytes 786436
  209.2 12.9 %collective-permute-start.7 = (bf16[1,512,256]{1,2,0:T(8,128)(2,1)S(1)}, bf16[1,512,256]{1,2,0:T(8,128)(2,1)S(1)}, u32[]{:S(2)}, u32[]{:S(2)}) collective-permute-start(bf16[1,512,256]{1,2,0:T(8,128)(2,1)S(1)} %bitcast_convert_fusion), channel_id=1, source_target_pairs={{0,16},{16,0},{1,17},{17,1},{2,18},{18,2},{3,19},{19,3},{4,20},{20... | collective-permute-start | bytes 786440 | tf_op jit(solution)/shard_map/ppermute | solution.py:74
  214.5 8.6 %copy-start.6 = (bf16[2,4,128,128]{3,2,1,0:T(8,128)(2,1)}, bf16[2,4,128,128]{3,2,1,0:T(8,128)(2,1)S(1)}, u32[]{:S(2)}) copy-start(bf16[2,4,128,128]{3,2,1,0:T(8,128)(2,1)S(1)} %scatter_fusion.1) | copy-start | bytes 786436
Sparse Core Ops, SparseCore 0:
  10.1 104.1 all-gather.1

commit v15 on v13

--- a/solution.py
+++ b/solution.py
@@ -110,12 +110,20 @@
     return jnp.einsum("psk,zxek->xpsze", values, w, preferred_element_type=jnp.float32)
 
 
+def gather_shifts(x, axis_name):
+    count = lax.axis_size(axis_name)
+    index = lax.axis_index(axis_name)
+    shifted = [x] + [
+        lax.ppermute(x, axis_name, [(i, (i + k) % count) for i in range(count)]) for k in range(1, count)
+    ]
+    source_shift = (index - jnp.arange(count, dtype=jnp.int32)) % count
+    return jnp.take(jnp.stack(shifted), source_shift, axis=0)
+
+
 def gather_rows(x):
-    pages = lax.axis_size("page")
-    got = lax.all_to_all(jnp.broadcast_to(x[None], (pages,) + x.shape), "page", 0, 0, tiled=True)
-    got = got.reshape((-1,) + x.shape[1:])
+    got = gather_shifts(x, "page").reshape((-1,) + x.shape[1:])
+    got = gather_shifts(got, "ry")
     chips = lax.axis_size("ry")
-    got = lax.all_to_all(jnp.broadcast_to(got[None], (chips,) + got.shape), "ry", 0, 0, tiled=True)
     core = lax.axis_index("rc")
     other = lax.ppermute(got, "rc", [(0, 1), (1, 0)])
     got = jnp.stack([jnp.where(core == 0, got, other), jnp.where(core == 0, other, got)], axis=1)

time: 235 us -> 231 us (0.983)
  the two profiles are of different devices: /device:TPU:8 before, /device:TPU:56 now
where the time goes in v15:
time: 231 us; the launch traced here: 230 us
  waiting for transfers between devices  112 us (48%)
  starting transfers between devices  35 us (15%)
  blocking collectives  27.8 us (12%)
  local copies, waits for them, and re-layouts  19.2 us (8%)
  between operations  15.4 us (7%)
  other arithmetic  13.4 us (6%)
  matrix products  7.83 us (3%)
    ppermute x4, waiting for transfers between devices, swap_halves(): return lax.ppermute(x, 'zh', [(0, 1), (1, 0)])  43.9 us
    all_to_all x2, waiting for transfers between devices, gather_col(): return lax.all_to_all(copies, 'xx', 0, 0, tiled=True)  40.8 us
    all_to_all x1, blocking collectives, scatter_sum_col(): got = lax.all_to_all(terms, 'xx', 0, 0, tiled=True)  27.8 us
    all_to_all x1, waiting for transfers between devices, scatter_sum_col(): got = lax.all_to_all(terms, 'xx', 0, 0, tiled=True)  24.2 us
    all_to_all x2, starting transfers between devices, gather_col(): return lax.all_to_all(copies, 'xx', 0, 0, tiled=True)  10.5 us
    ppermute x6, starting transfers between devices, gather_shifts(): lax.ppermute(x, axis_name, [(i, (i + k) % count) for i in range(count)])  10.2 us
    ppermute x4, starting transfers between devices, swap_halves(): return lax.ppermute(x, 'zh', [(0, 1), (1, 0)])  6.88 us
  transfers between devices with their start and end apart: 16, of which 9 were waited for; matrix products, arithmetic and copies ran while one was open for 12% of the time, Pallas kernels for 0%

profile of v15, /device:TPU:56, one launch (start us, length us, event | category | flops | bytes accessed | tf_op | source)
XLA Modules:
  0.0 230.4 jit_solution(5843099141630842655)
XLA Ops:
  7.2 1.0 convert_bitcast_fusion.3
  8.2 1.0 convert_bitcast_fusion.2
  9.3 0.7 pad_maximum_fusion.2
  10.3 0.8 convert_element_type.105
  11.1 0.2 collective-permute-start.3
  11.2 3.3 %collective-permute-start.2 = (bf16[64,384]{1,0:T(8,128)(2,1)S(1)}, bf16[64,384]{1,0:T(8,128)(2,1)S(1)}, u32[]{:S(2)}, u32[]{:S(2)}) collective-permute-start(bf16[64,384]{1,0:T(8,128)(2,1)S(1)} %get-tuple-element.33), channel_id=1, source_target_pairs={{0,2},{1,3},{2,0},{3,1},{4,6},{5,7},{6,4},{7,5},{8,10},{9,11},{10,... | collective-permute-start | bytes 147464 | tf_op jit(solution)/shard_map/ppermute | solution.py:117
  14.5 2.8 %collective-permute-start.1 = (bf16[64,384]{1,0:T(8,128)(2,1)S(1)}, bf16[64,384]{1,0:T(8,128)(2,1)S(1)}, u32[]{:S(2)}, u32[]{:S(2)}) collective-permute-start(bf16[64,384]{1,0:T(8,128)(2,1)S(1)} %get-tuple-element.33), channel_id=1, source_target_pairs={{0,1},{1,2},{2,3},{3,0},{4,5},{5,6},{6,7},{7,4},{8,9},{9,10},{10,1... | collective-permute-start | bytes 147464 | tf_op jit(solution)/shard_map/ppermute | solution.py:117
  17.5 4.6 %collective-permute-start = (bf16[1,512,256]{1,2,0:T(8,128)(2,1)S(1)}, bf16[1,512,256]{1,2,0:T(8,128)(2,1)S(1)}, u32[]{:S(2)}, u32[]{:S(2)}) collective-permute-start(bf16[1,512,256]{1,2,0:T(8,128)(2,1)S(1)} %copy.68), channel_id=1, source_target_pairs={{0,16},{16,0},{1,17},{17,1},{2,18},{18,2},{3,19},{19,3},{4,20},{20... | collective-permute-start | bytes 786440 | tf_op jit(solution)/shard_map/ppermute | solution.py:74
  22.4 0.6 gather_fusion
  23.1 0.8 collective-permute-start.6
  23.9 0.9 collective-permute-start.5
  24.8 2.2 collective-permute-start.4
  27.1 10.8 %collective-permute-done = bf16[1,512,256]{1,2,0:T(8,128)(2,1)S(1)} collective-permute-done((bf16[1,512,256]{1,2,0:T(8,128)(2,1)S(1)}, bf16[1,512,256]{1,2,0:T(8,128)(2,1)S(1)}, u32[]{:S(2)}, u32[]{:S(2)}) %collective-permute-start) | collective-permute-done | bytes 262176 | tf_op jit(solution)/shard_map/ppermute | solution.py:74
  38.0 0.2 copy.70
  38.2 1.5 broadcast_in_dim.144
  39.7 4.3 %all-to-all-start = ((bf16[4,2,1,512,256]{4,3,1,2,0:T(8,128)(2,1)}), bf16[4,2,1,512,256]{4,3,1,2,0:T(8,128)(2,1)S(1)}, u32[]{:S(2)}, u32[]{:S(2)}) async-start(bf16[4,2,1,512,256]{4,3,1,2,0:T(8,128)(2,1)} %broadcast_in_dim.144), calls=%async_computation | async-start | bytes 4194304 | tf_op jit(solution)/shard_map/all_to_all | solution.py:83
  44.1 1.0 pad_maximum_fusion.1
  45.1 1.9 gather_fusion.1
  47.0 1.1 broadcast_select_fusion
  48.7 1.0 fusion.41
  49.7 0.8 fusion.26
  50.5 0.2 collective-permute-done.7
  50.7 1.4 select_bitcast_fusion.1
  52.3 1.0 slice.68
  53.4 2.3 copy.74
  55.7 14.7 %all-to-all-done = bf16[4,2,1,512,256]{4,3,1,2,0:T(8,128)(2,1)S(1)} async-done(((bf16[4,2,1,512,256]{4,3,1,2,0:T(8,128)(2,1)}), bf16[4,2,1,512,256]{4,3,1,2,0:T(8,128)(2,1)S(1)}, u32[]{:S(2)}, u32[]{:S(2)}) %all-to-all-start) | async-done | bytes 2097184 | tf_op jit(solution)/shard_map/all_to_all | solution.py:83
  70.4 0.5 fusion.2
  70.8 0.7 copy-done.3
  71.6 0.8 fusion.22
  72.6 0.3 fusion.47
  73.2 0.2 copy-done.14
  73.4 0.7 fusion.20
  74.2 0.7 fusion.25
  74.9 0.7 convert_bitcast_fusion.1
  75.6 1.6 copy.81
  77.2 3.9 %all-to-all-start.2 = ((bf16[4,1,512,2,256]{2,4,3,1,0:T(8,128)(2,1)}), bf16[4,1,512,2,256]{2,4,3,1,0:T(8,128)(2,1)S(1)}, u32[]{:S(2)}, u32[]{:S(2)}) async-start(bf16[4,1,512,2,256]{2,4,3,1,0:T(8,128)(2,1)} %copy.81), calls=%async_computation.2 | async-start | bytes 4194304 | tf_op jit(solution)/shard_map/all_to_all | solution.py:87
  81.2 0.2 convert_reduce_fusion.2
  81.6 0.8 broadcast_select_fusion.2
  82.4 24.2 %all-to-all-done.2 = bf16[4,1,512,2,256]{2,4,3,1,0:T(8,128)(2,1)S(1)} async-done(((bf16[4,1,512,2,256]{2,4,3,1,0:T(8,128)(2,1)}), bf16[4,1,512,2,256]{2,4,3,1,0:T(8,128)(2,1)S(1)}, u32[]{:S(2)}, u32[]{:S(2)}) %all-to-all-start.2) | async-done | bytes 2097184 | tf_op jit(solution)/shard_map/all_to_all | solution.py:87
  106.6 0.3 convert_reduce_fusion.1
  106.9 0.3 collective-permute-start.8
  107.2 0.2 copy-done.7
  107.7 0.2 copy.76
  108.0 0.8 scatter_fusion
  108.7 0.7 copy.77
  109.5 3.4 %all-to-all-start.1 = ((bf16[2,4,128,128]{3,2,0,1:T(8,128)(2,1)}), bf16[2,4,128,128]{3,2,0,1:T(8,128)(2,1)S(1)}, u32[]{:S(2)}, u32[]{:S(2)}) async-start(bf16[2,4,128,128]{3,2,0,1:T(8,128)(2,1)} %copy.77), calls=%async_computation.1 | async-start | bytes 524288 | tf_op jit(solution)/shard_map/all_to_all | solution.py:160
  112.9 6.9 %collective-permute-done.8 = bf16[1,512,256]{1,2,0:T(8,128)(2,1)S(1)} collective-permute-done((bf16[1,512,256]{1,2,0:T(8,128)(2,1)S(1)}, bf16[1,512,256]{1,2,0:T(8,128)(2,1)S(1)}, u32[]{:S(2)}, u32[]{:S(2)}) %collective-permute-start.8) | collective-permute-done | bytes 262176 | tf_op jit(solution)/shard_map/ppermute | solution.py:74
  119.9 2.7 %all-to-all-done.1 = bf16[2,4,128,128]{3,2,0,1:T(8,128)(2,1)S(1)} async-done(((bf16[2,4,128,128]{3,2,0,1:T(8,128)(2,1)}), bf16[2,4,128,128]{3,2,0,1:T(8,128)(2,1)S(1)}, u32[]{:S(2)}, u32[]{:S(2)}) %all-to-all-start.1) | async-done | bytes 262176 | tf_op jit(solution)/shard_map/all_to_all | solution.py:160
  122.6 1.9 collective-permute-start.9
  124.5 11.8 %collective-permute-done.9 = bf16[1,512,256]{1,2,0:T(8,128)(2,1)S(1)} collective-permute-done((bf16[1,512,256]{1,2,0:T(8,128)(2,1)S(1)}, bf16[1,512,256]{1,2,0:T(8,128)(2,1)S(1)}, u32[]{:S(2)}, u32[]{:S(2)}) %collective-permute-start.9) | collective-permute-done | bytes 262176 | tf_op jit(solution)/shard_map/ppermute | solution.py:74
  136.4 0.2 copy.84
  136.7 1.5 broadcast_in_dim.163
  138.2 6.2 %all-to-all-start.3 = ((bf16[4,2,1,512,256]{4,3,1,2,0:T(8,128)(2,1)}), bf16[4,2,1,512,256]{4,3,1,2,0:T(8,128)(2,1)S(1)}, u32[]{:S(2)}, u32[]{:S(2)}) async-start(bf16[4,2,1,512,256]{4,3,1,2,0:T(8,128)(2,1)} %broadcast_in_dim.163), calls=%async_computation.3 | async-start | bytes 4194304 | tf_op jit(solution)/shard_map/all_to_all | solution.py:83
  144.4 26.1 %all-to-all-done.3 = bf16[4,2,1,512,256]{4,3,1,2,0:T(8,128)(2,1)S(1)} async-done(((bf16[4,2,1,512,256]{4,3,1,2,0:T(8,128)(2,1)}), bf16[4,2,1,512,256]{4,3,1,2,0:T(8,128)(2,1)S(1)}, u32[]{:S(2)}, u32[]{:S(2)}) %all-to-all-start.3) | async-done | bytes 2097184 | tf_op jit(solution)/shard_map/all_to_all | solution.py:83
  170.6 0.5 fusion.5
  171.1 2.5 %slice-done.1 = bf16[2048,1280]{1,0:T(8,128)(2,1)S(1)} async-done(((bf16[2048,1920]{1,0:T(8,128)(2,1)}), bf16[2048,1280]{1,0:T(8,128)(2,1)S(1)}, s32[]{:S(2)}) %slice-start.1) | async-done | bytes 5242904 | tf_op jit(solution)/shard_map/slice | solution.py:202
  173.6 2.9 %fusion.8 = f32[1,512,1280]{2,1,0:T(8,128)S(1)} fusion(bf16[2,4,256,1280]{3,2,1,0:T(8,128)(2,1)S(1)} %bitcast.160, bf16[4,2,1,512,256]{4,3,1,2,0:T(8,128)(2,1)S(1)} %all-to-all-done.3, f32[4,2,256]{2,1,0:T(2,128)S(1)} %copy.85, f32[512]{0:T(512)S(1)} %add_rsqrt_fusion.1), kind=kOutput, calls=%fused_computation.18 | convolution fusion | flops 2688548864 | bytes 9971712 | tf_op jit(solution)/shard_map/xzpse,zxen->psn/dot_general | solution.py:105
  176.6 1.9 convert_bitcast_fusion
  178.6 27.8 %all_to_all.25 = bf16[4,1,512,2,256]{2,4,3,1,0:T(8,128)(2,1)S(1)} all-to-all(bf16[4,1,512,2,256]{2,4,3,1,0:T(8,128)(2,1)S(1)} %copy.87), channel_id=1, replica_groups=mesh['ry'=4,'rc'=2,'zh'=2,'xx'=4,'page'=4] {'xx'}, dimensions={0} | all-to-all | bytes 4194304 | tf_op jit(solution)/shard_map/all_to_all | solution.py:87
  206.4 0.3 convert_reduce_fusion
  207.0 0.3 copy-done.5
  207.3 0.8 scatter_fusion.1
  208.1 14.5 %collective-permute-done.10 = bf16[1,512,256]{1,2,0:T(8,128)(2,1)S(1)} collective-permute-done((bf16[1,512,256]{1,2,0:T(8,128)(2,1)S(1)}, bf16[1,512,256]{1,2,0:T(8,128)(2,1)S(1)}, u32[]{:S(2)}, u32[]{:S(2)}) %collective-permute-start.10) | collective-permute-done | bytes 262176 | tf_op jit(solution)/shard_map/ppermute | solution.py:74
  222.7 0.8 copy.89
  (114 shorter events, 3.0 us)
Async XLA Ops:
  7.2 2.9 %copy-start = (f32[2,64,256]{2,1,0:T(8,128)S(1)}, f32[2,64,256]{2,1,0:T(8,128)}, u32[]{:S(2)}) copy-start(f32[2,64,256]{2,1,0:T(8,128)} %param.18) | copy-start | bytes 393220
  7.2 3.9 %copy-start.17 = (f32[128,64]{0,1:T(8,128)S(1)}, f32[128,64]{0,1:T(8,128)}, u32[]{:S(2)}) copy-start(f32[128,64]{0,1:T(8,128)} %param.19) | copy-start | bytes 98308
  7.2 10.1 %copy-start.13 = (bf16[1,512,256]{2,1,0:T(8,128)(2,1)S(1)}, bf16[1,512,256]{2,1,0:T(8,128)(2,1)}, u32[]{:S(2)}) copy-start(bf16[1,512,256]{2,1,0:T(8,128)(2,1)} %param.14) | copy-start | bytes 786436
  7.2 163.9 %all-gather.2.cloned.1.call-start = ((), (), s32[]{:S(2)}) async-start(), calls=%async_computation.5 | async-start | bytes 8110080 | tf_op jit(solution)/shard_map/all_gather | solution.py:199
  11.1 11.2 %collective-permute-start.3 = (bf16[64,384]{1,0:T(8,128)(2,1)S(1)}, bf16[64,384]{1,0:T(8,128)(2,1)S(1)}, u32[]{:S(2)}, u32[]{:S(2)}) collective-permute-start(bf16[64,384]{1,0:T(8,128)(2,1)S(1)} %get-tuple-element.33), channel_id=1, source_target_pairs={{0,3},{1,0},{2,1},{3,2},{4,7},{5,4},{6,5},{7,6},{8,11},{9,8},{10,9... | collective-permute-start | bytes 147464 | tf_op jit(solution)/shard_map/ppermute | solution.py:117
  11.2 11.1 %collective-permute-start.2 = (bf16[64,384]{1,0:T(8,128)(2,1)S(1)}, bf16[64,384]{1,0:T(8,128)(2,1)S(1)}, u32[]{:S(2)}, u32[]{:S(2)}) collective-permute-start(bf16[64,384]{1,0:T(8,128)(2,1)S(1)} %get-tuple-element.33), channel_id=1, source_target_pairs={{0,2},{1,3},{2,0},{3,1},{4,6},{5,7},{6,4},{7,5},{8,10},{9,11},{10,... | collective-permute-start | bytes 147464 | tf_op jit(solution)/shard_map/ppermute | solution.py:117
  14.5 7.8 %collective-permute-start.1 = (bf16[64,384]{1,0:T(8,128)(2,1)S(1)}, bf16[64,384]{1,0:T(8,128)(2,1)S(1)}, u32[]{:S(2)}, u32[]{:S(2)}) collective-permute-start(bf16[64,384]{1,0:T(8,128)(2,1)S(1)} %get-tuple-element.33), channel_id=1, source_target_pairs={{0,1},{1,2},{2,3},{3,0},{4,5},{5,6},{6,7},{7,4},{8,9},{9,10},{10,1... | collective-permute-start | bytes 147464 | tf_op jit(solution)/shard_map/ppermute | solution.py:117
  17.5 20.4 %collective-permute-start = (bf16[1,512,256]{1,2,0:T(8,128)(2,1)S(1)}, bf16[1,512,256]{1,2,0:T(8,128)(2,1)S(1)}, u32[]{:S(2)}, u32[]{:S(2)}) collective-permute-start(bf16[1,512,256]{1,2,0:T(8,128)(2,1)S(1)} %copy.68), channel_id=1, source_target_pairs={{0,16},{16,0},{1,17},{17,1},{2,18},{18,2},{3,19},{19,3},{4,20},{20... | collective-permute-start | bytes 786440 | tf_op jit(solution)/shard_map/ppermute | solution.py:74
  23.1 21.0 %collective-permute-start.6 = (bf16[256,384]{1,0:T(8,128)(2,1)S(1)}, bf16[256,384]{1,0:T(8,128)(2,1)S(1)}, u32[]{:S(2)}, u32[]{:S(2)}) collective-permute-start(bf16[256,384]{1,0:T(8,128)(2,1)S(1)} %bitcast_select_fusion), channel_id=1, source_target_pairs={{0,192},{64,0},{128,64},{192,128},{1,193},{65,1},{129,65},{193,129... | collective-permute-start | bytes 589832 | tf_op jit(solution)/shard_map/ppermute | solution.py:117
  23.9 20.2 %collective-permute-start.5 = (bf16[256,384]{1,0:T(8,128)(2,1)S(1)}, bf16[256,384]{1,0:T(8,128)(2,1)S(1)}, u32[]{:S(2)}, u32[]{:S(2)}) collective-permute-start(bf16[256,384]{1,0:T(8,128)(2,1)S(1)} %bitcast_select_fusion), channel_id=1, source_target_pairs={{0,128},{64,192},{128,0},{192,64},{1,129},{65,193},{129,1},{193,65... | collective-permute-start | bytes 589832 | tf_op jit(solution)/shard_map/ppermute | solution.py:117
  24.8 19.2 %collective-permute-start.4 = (bf16[256,384]{1,0:T(8,128)(2,1)S(1)}, bf16[256,384]{1,0:T(8,128)(2,1)S(1)}, u32[]{:S(2)}, u32[]{:S(2)}) collective-permute-start(bf16[256,384]{1,0:T(8,128)(2,1)S(1)} %bitcast_select_fusion), channel_id=1, source_target_pairs={{0,64},{64,128},{128,192},{192,0},{1,65},{65,129},{129,193},{193,1... | collective-permute-start | bytes 589832 | tf_op jit(solution)/shard_map/ppermute | solution.py:117
  39.7 30.6 %all-to-all-start = ((bf16[4,2,1,512,256]{4,3,1,2,0:T(8,128)(2,1)}), bf16[4,2,1,512,256]{4,3,1,2,0:T(8,128)(2,1)S(1)}, u32[]{:S(2)}, u32[]{:S(2)}) async-start(bf16[4,2,1,512,256]{4,3,1,2,0:T(8,128)(2,1)} %broadcast_in_dim.144), calls=%async_computation | async-start | bytes 4194304 | tf_op jit(solution)/shard_map/all_to_all | solution.py:83
  44.1 4.0 %copy-start.18 = (f32[2048]{0:T(1024)S(1)}, f32[2048]{0:T(1024)}, u32[]{:S(2)}) copy-start(f32[2048]{0:T(1024)} %param.22) | copy-start | bytes 24580
  48.0 2.7 %collective-permute-start.7 = (bf16[4,256,384]{2,1,0:T(8,128)(2,1)}, bf16[4,256,384]{2,1,0:T(8,128)(2,1)}, u32[]{:S(2)}, u32[]{:S(2)}) collective-permute-start(bf16[4,256,384]{2,1,0:T(8,128)(2,1)} %broadcast_select_fusion), channel_id=1, source_target_pairs={{0,32},{32,0},{1,33},{33,1},{2,34},{34,2},{3,35},{35,3},{4,36},{36... | collective-permute-start | bytes 2359304 | tf_op jit(solution)/shard_map/ppermute | solution.py:128
  70.3 1.2 copy-start.3
  71.6 0.9 copy-start.21
  71.6 1.4 copy-start.22
  71.6 1.5 copy-start.15
  71.6 1.5 copy-start.16
  72.4 1.0 copy-start.14
  72.9 1.2 copy-start.9
  73.0 1.1 copy-start.11
  77.2 4.0 %copy-start.20 = (s32[4,4]{1,0:T(4,128)S(1)}, s32[4,4]{1,0:T(4,128)}, u32[]{:S(2)}) copy-start(s32[4,4]{1,0:T(4,128)} %param.16) | copy-start | bytes 196
  77.2 4.2 %copy-start.10 = (bf16[512,64]{0,1:T(8,128)(2,1)S(1)}, bf16[512,64]{0,1:T(8,128)(2,1)}, u32[]{:S(2)}) copy-start(bf16[512,64]{0,1:T(8,128)(2,1)} %copy-done.9) | copy-start | bytes 196612
  77.2 4.3 %copy-start.12 = (bf16[512,64]{0,1:T(8,128)(2,1)S(1)}, bf16[512,64]{0,1:T(8,128)(2,1)}, u32[]{:S(2)}) copy-start(bf16[512,64]{0,1:T(8,128)(2,1)} %copy-done.11) | copy-start | bytes 196612
  77.2 29.4 %all-to-all-start.2 = ((bf16[4,1,512,2,256]{2,4,3,1,0:T(8,128)(2,1)}), bf16[4,1,512,2,256]{2,4,3,1,0:T(8,128)(2,1)S(1)}, u32[]{:S(2)}, u32[]{:S(2)}) async-start(bf16[4,1,512,2,256]{2,4,3,1,0:T(8,128)(2,1)} %copy.81), calls=%async_computation.2 | async-start | bytes 4194304 | tf_op jit(solution)/shard_map/all_to_all | solution.py:87
  106.5 0.9 copy-start.7
  106.6 1.0 copy-start.8
  106.9 12.8 %collective-permute-start.8 = (bf16[1,512,256]{1,2,0:T(8,128)(2,1)S(1)}, bf16[1,512,256]{1,2,0:T(8,128)(2,1)S(1)}, u32[]{:S(2)}, u32[]{:S(2)}) collective-permute-start(bf16[1,512,256]{1,2,0:T(8,128)(2,1)S(1)} %bitcast_convert_fusion.1), channel_id=1, source_target_pairs={{0,16},{16,0},{1,17},{17,1},{2,18},{18,2},{3,19},{19,3},{4,20},{20... | collective-permute-start | bytes 786440 | tf_op jit(solution)/shard_map/ppermute | solution.py:74
  109.5 13.1 %all-to-all-start.1 = ((bf16[2,4,128,128]{3,2,0,1:T(8,128)(2,1)}), bf16[2,4,128,128]{3,2,0,1:T(8,128)(2,1)S(1)}, u32[]{:S(2)}, u32[]{:S(2)}) async-start(bf16[2,4,128,128]{3,2,0,1:T(8,128)(2,1)} %copy.77), calls=%async_computation.1 | async-start | bytes 524288 | tf_op jit(solution)/shard_map/all_to_all | solution.py:160
  119.9 18.3 %copy-start.1 = (bf16[1,512,256]{1,2,0:T(8,128)(2,1)}, bf16[1,512,256]{1,2,0:T(8,128)(2,1)S(1)}, u32[]{:S(2)}) copy-start(bf16[1,512,256]{1,2,0:T(8,128)(2,1)S(1)} %fusion.32) | copy-start | bytes 786436
  122.6 13.8 %copy-start.4 = (bf16[2,4,128,128]{3,2,0,1:T(8,128)(2,1)}, bf16[2,4,128,128]{3,2,0,1:T(8,128)(2,1)S(1)}, u32[]{:S(2)}) copy-start(bf16[2,4,128,128]{3,2,0,1:T(8,128)(2,1)S(1)} %all-to-all-done.1) | copy-start | bytes 786436
  122.6 13.7 %collective-permute-start.9 = (bf16[1,512,256]{1,2,0:T(8,128)(2,1)S(1)}, bf16[1,512,256]{1,2,0:T(8,128)(2,1)S(1)}, u32[]{:S(2)}, u32[]{:S(2)}) collective-permute-start(bf16[1,512,256]{1,2,0:T(8,128)(2,1)S(1)} %fusion.32), channel_id=1, source_target_pairs={{0,16},{16,0},{1,17},{17,1},{2,18},{18,2},{3,19},{19,3},{4,20},{20... | collective-permute-start | bytes 786440 | tf_op jit(solution)/shard_map/ppermute | solution.py:74
  138.2 6.2 %copy-start.19 = (f32[2048]{0:T(1024)S(1)}, f32[2048]{0:T(1024)}, u32[]{:S(2)}) copy-start(f32[2048]{0:T(1024)} %param.23) | copy-start | bytes 24580
  138.2 32.4 %all-to-all-start.3 = ((bf16[4,2,1,512,256]{4,3,1,2,0:T(8,128)(2,1)}), bf16[4,2,1,512,256]{4,3,1,2,0:T(8,128)(2,1)S(1)}, u32[]{:S(2)}, u32[]{:S(2)}) async-start(bf16[4,2,1,512,256]{4,3,1,2,0:T(8,128)(2,1)} %broadcast_in_dim.163), calls=%async_computation.3 | async-start | bytes 4194304 | tf_op jit(solution)/shard_map/all_to_all | solution.py:83
  171.1 2.5 %slice-start.1 = ((bf16[2048,1920]{1,0:T(8,128)(2,1)}), bf16[2048,1280]{1,0:T(8,128)(2,1)S(1)}, s32[]{:S(2)}) async-start(bf16[2048,1920]{1,0:T(8,128)(2,1)} %all-gather.2.cloned.1.call-done), calls=%async_computation.7 | async-start | bytes 10485760 | tf_op jit(solution)/shard_map/slice | solution.py:202
  173.6 2.9 %slice-start = ((bf16[2048,1920]{1,0:T(8,128)(2,1)}), bf16[2048,640]{1,0:T(8,128)(2,1)S(1)}, s32[]{:S(2)}) async-start(bf16[2048,1920]{1,0:T(8,128)(2,1)} %all-gather.2.cloned.1.call-done), calls=%async_computation.6 | async-start | bytes 5242880 | tf_op jit(solution)/shard_map/slice | solution.py:203
  206.4 1.0 copy-start.5
  206.4 16.2 %copy-start.2 = (bf16[1,512,256]{1,2,0:T(8,128)(2,1)S(1)}, bf16[1,512,256]{1,2,0:T(8,128)(2,1)}, u32[]{:S(2)}) copy-start(bf16[1,512,256]{1,2,0:T(8,128)(2,1)} %copy-done.1) | copy-start | bytes 786436
  206.8 15.8 %collective-permute-start.10 = (bf16[1,512,256]{1,2,0:T(8,128)(2,1)S(1)}, bf16[1,512,256]{1,2,0:T(8,128)(2,1)S(1)}, u32[]{:S(2)}, u32[]{:S(2)}) collective-permute-start(bf16[1,512,256]{1,2,0:T(8,128)(2,1)S(1)} %bitcast_convert_fusion), channel_id=1, source_target_pairs={{0,16},{16,0},{1,17},{17,1},{2,18},{18,2},{3,19},{19,3},{4,20},{20... | collective-permute-start | bytes 786440 | tf_op jit(solution)/shard_map/ppermute | solution.py:74
  208.1 15.5 %copy-start.6 = (bf16[2,4,128,128]{3,2,1,0:T(8,128)(2,1)}, bf16[2,4,128,128]{3,2,1,0:T(8,128)(2,1)S(1)}, u32[]{:S(2)}) copy-start(bf16[2,4,128,128]{3,2,1,0:T(8,128)(2,1)S(1)} %scatter_fusion.1) | copy-start | bytes 786436
Sparse Core Ops, SparseCore 0:
  10.1 104.2 all-gather.1

commit v16 on v14

--- a/solution.py
+++ b/solution.py
@@ -229,7 +229,11 @@
     gate_up = project_blocks(ffn_in, gateup_w)
     hidden = (jax.nn.silu(gate_up[..., :unit_count]) * gate_up[..., unit_count:]).astype(jnp.bfloat16)
     ffn_terms = terms_blocks(hidden, down_t, xx_count, zh_count)
-    ffn_sum = scatter_sum_col(ffn_terms.astype(jnp.bfloat16))
+    ffn_terms = ffn_terms.astype(jnp.bfloat16)
+    mid = seq_len // 2
+    ffn_sum = jnp.concatenate(
+        [scatter_sum_col(ffn_terms[:, :, :mid]), scatter_sum_col(ffn_terms[:, :, mid:])], axis=1
+    )
     layer_out = (residual.astype(jnp.float32) + ffn_sum).astype(jnp.bfloat16)
     page_index = lax.axis_index("page")
     page_count = lax.axis_size("page")

time: 231 us -> 234 us (1.013)
  blocking collectives: 27.4 us -> 0 us
  waiting for transfers between devices: 102 us -> 118 us
  starting transfers between devices: 45.8 us -> 57.9 us
    all_to_all x1 -> x0, blocking collectives: 27.4 us -> none  [scatter_sum_col(): got = lax.all_to_all(terms, 'xx', 0, 0, tiled=True)]
    all_to_all x1 -> x3, waiting for transfers between devices: 23.5 us -> 43.5 us  [scatter_sum_col(): got = lax.all_to_all(terms, 'xx', 0, 0, tiled=True)]
    all_to_all x1 -> x3, starting transfers between devices: 3.74 us -> 10.8 us  [scatter_sum_col(): got = lax.all_to_all(terms, 'xx', 0, 0, tiled=True)]
    ppermute x4 -> x5, starting transfers between devices: 16.7 us -> 21.7 us  [swap_halves(): return lax.ppermute(x, 'zh', [(0, 1), (1, 0)])]
    ppermute x4 -> x5, waiting for transfers between devices: 24.5 us -> 20.7 us  [swap_halves(): return lax.ppermute(x, 'zh', [(0, 1), (1, 0)])]
  transfers between devices with their start and end apart: 14 -> 17, of which waited for: 9 -> 11; matrix products, arithmetic and copies ran while one was open for 12% -> 12% of each run, Pallas kernels for 0% -> 0%
where the time goes in v16:
time: 234 us; the launch traced here: 233 us
  waiting for transfers between devices  118 us (50%)
  starting transfers between devices  57.9 us (25%)
  local copies, waits for them, and re-layouts  20.7 us (9%)
  between operations  15.4 us (7%)
  other arithmetic  13.1 us (6%)
  matrix products  7.83 us (3%)
    all_to_all x3, waiting for transfers between devices, scatter_sum_col(): got = lax.all_to_all(terms, 'xx', 0, 0, tiled=True)  43.5 us
    all_to_all x2, waiting for transfers between devices, gather_col(): return lax.all_to_all(copies, 'xx', 0, 0, tiled=True)  39.8 us
    ppermute x5, starting transfers between devices, swap_halves(): return lax.ppermute(x, 'zh', [(0, 1), (1, 0)])  21.7 us
    ppermute x5, waiting for transfers between devices, swap_halves(): return lax.ppermute(x, 'zh', [(0, 1), (1, 0)])  20.7 us
    all_to_all x1, waiting for transfers between devices, send_pages(): lax.all_to_all(outgoing, 'page', split_axis=1, concat_axis=1, tiled=True)  11.1 us
    all_to_all x3, starting transfers between devices, scatter_sum_col(): got = lax.all_to_all(terms, 'xx', 0, 0, tiled=True)  10.8 us
    all_to_all x2, starting transfers between devices, gather_col(): return lax.all_to_all(copies, 'xx', 0, 0, tiled=True)  8.03 us
    all_to_all x1, starting transfers between devices, send_pages(): lax.all_to_all(outgoing, 'page', split_axis=1, concat_axis=1, tiled=True)  6.56 us
  transfers between devices with their start and end apart: 17, of which 11 were waited for; matrix products, arithmetic and copies ran while one was open for 12% of the time, Pallas kernels for 0%

profile of v16, /device:TPU:8, one launch (start us, length us, event | category | flops | bytes accessed | tf_op | source)
XLA Modules:
  0.0 233.1 jit_solution(14213664273260676257)
XLA Ops:
  7.2 1.0 convert_bitcast_fusion.3
  8.2 1.0 convert_bitcast_fusion.2
  9.3 0.7 pad_maximum_fusion.2
  10.3 0.8 convert_element_type.114
  11.1 0.7 broadcast_in_dim.88
  11.8 5.9 %all-to-all-start.1 = ((bf16[4,64,384]{2,1,0:T(8,128)(2,1)}), bf16[4,64,384]{2,1,0:T(8,128)(2,1)S(1)}, u32[]{:S(2)}, u32[]{:S(2)}) async-start(bf16[4,64,384]{2,1,0:T(8,128)(2,1)} %broadcast_in_dim.88), calls=%async_computation.1 | async-start | bytes 393216 | tf_op jit(solution)/shard_map/all_to_all | solution.py:115
  17.8 4.8 %collective-permute-start = (bf16[1,512,256]{1,2,0:T(8,128)(2,1)S(1)}, bf16[1,512,256]{1,2,0:T(8,128)(2,1)S(1)}, u32[]{:S(2)}, u32[]{:S(2)}) collective-permute-start(bf16[1,512,256]{1,2,0:T(8,128)(2,1)S(1)} %copy.70), channel_id=1, source_target_pairs={{0,16},{16,0},{1,17},{17,1},{2,18},{18,2},{3,19},{19,3},{4,20},{20... | collective-permute-start | bytes 786440 | tf_op jit(solution)/shard_map/ppermute | solution.py:74
  22.6 2.9 %all-to-all-done.1 = bf16[4,64,384]{2,1,0:T(8,128)(2,1)S(1)} async-done(((bf16[4,64,384]{2,1,0:T(8,128)(2,1)}), bf16[4,64,384]{2,1,0:T(8,128)(2,1)S(1)}, u32[]{:S(2)}, u32[]{:S(2)}) %all-to-all-start.1) | async-done | bytes 196640 | tf_op jit(solution)/shard_map/all_to_all | solution.py:115
  25.5 0.4 collective-permute-start.3
  26.0 2.6 %collective-permute-start.2 = (bf16[256,384]{1,0:T(8,128)(2,1)S(1)}, bf16[256,384]{1,0:T(8,128)(2,1)S(1)}, u32[]{:S(2)}, u32[]{:S(2)}) collective-permute-start(bf16[256,384]{1,0:T(8,128)(2,1)S(1)} %bitcast.165), channel_id=1, source_target_pairs={{0,128},{64,192},{128,0},{192,64},{1,129},{65,193},{129,1},{193,65... | collective-permute-start | bytes 589832 | tf_op jit(solution)/shard_map/ppermute | solution.py:120
  28.6 1.9 collective-permute-start.1
  30.5 2.2 collective-permute-done
  32.8 0.2 copy.72
  33.0 1.5 broadcast_in_dim.86
  34.5 4.3 %all-to-all-start = ((bf16[4,2,1,512,256]{4,3,1,2,0:T(8,128)(2,1)}), bf16[4,2,1,512,256]{4,3,1,2,0:T(8,128)(2,1)S(1)}, u32[]{:S(2)}, u32[]{:S(2)}) async-start(bf16[4,2,1,512,256]{4,3,1,2,0:T(8,128)(2,1)} %broadcast_in_dim.86), calls=%async_computation | async-start | bytes 4194304 | tf_op jit(solution)/shard_map/all_to_all | solution.py:83
  38.9 1.0 pad_maximum_fusion.1
  39.9 1.9 gather_fusion
  41.7 1.1 broadcast_select_fusion
  43.5 1.0 fusion.40
  44.5 0.8 fusion.26
  45.5 1.4 select_bitcast_fusion.1
  47.0 1.0 slice.85
  48.1 2.3 copy.76
  50.4 14.1 %all-to-all-done = bf16[4,2,1,512,256]{4,3,1,2,0:T(8,128)(2,1)S(1)} async-done(((bf16[4,2,1,512,256]{4,3,1,2,0:T(8,128)(2,1)}), bf16[4,2,1,512,256]{4,3,1,2,0:T(8,128)(2,1)S(1)}, u32[]{:S(2)}, u32[]{:S(2)}) %all-to-all-start) | async-done | bytes 2097184 | tf_op jit(solution)/shard_map/all_to_all | solution.py:83
  64.5 0.5 fusion.2
  65.0 0.7 copy-done.4
  65.7 0.8 fusion.22
  66.7 0.3 fusion.46
  67.3 0.2 copy-done.13
  67.5 0.7 fusion.20
  68.3 0.7 fusion.25
  69.0 0.7 convert_bitcast_fusion.1
  69.7 1.6 copy.83
  71.3 3.7 %all-to-all-start.3 = ((bf16[4,1,512,2,256]{2,4,3,1,0:T(8,128)(2,1)}), bf16[4,1,512,2,256]{2,4,3,1,0:T(8,128)(2,1)S(1)}, u32[]{:S(2)}, u32[]{:S(2)}) async-start(bf16[4,1,512,2,256]{2,4,3,1,0:T(8,128)(2,1)} %copy.83), calls=%async_computation.3 | async-start | bytes 4194304 | tf_op jit(solution)/shard_map/all_to_all | solution.py:87
  75.1 0.2 convert_reduce_fusion.3
  75.5 0.8 broadcast_select_fusion.2
  76.3 23.5 %all-to-all-done.3 = bf16[4,1,512,2,256]{2,4,3,1,0:T(8,128)(2,1)S(1)} async-done(((bf16[4,1,512,2,256]{2,4,3,1,0:T(8,128)(2,1)}), bf16[4,1,512,2,256]{2,4,3,1,0:T(8,128)(2,1)S(1)}, u32[]{:S(2)}, u32[]{:S(2)}) %all-to-all-start.3) | async-done | bytes 2097184 | tf_op jit(solution)/shard_map/all_to_all | solution.py:87
  99.8 0.3 convert_reduce_fusion
  100.2 4.4 %collective-permute-start.5 = (bf16[1,512,256]{1,2,0:T(8,128)(2,1)S(1)}, bf16[1,512,256]{1,2,0:T(8,128)(2,1)S(1)}, u32[]{:S(2)}, u32[]{:S(2)}) collective-permute-start(bf16[1,512,256]{1,2,0:T(8,128)(2,1)S(1)} %bitcast_convert_fusion), channel_id=1, source_target_pairs={{0,16},{16,0},{1,17},{17,1},{2,18},{18,2},{3,19},{19,3},{4,20},{20... | collective-permute-start | bytes 786440 | tf_op jit(solution)/shard_map/ppermute | solution.py:74
  104.8 0.2 copy.78
  105.1 0.8 scatter_fusion
  105.9 0.7 copy.79
  106.6 6.6 %all-to-all-start.2 = ((bf16[2,4,128,128]{3,2,0,1:T(8,128)(2,1)}), bf16[2,4,128,128]{3,2,0,1:T(8,128)(2,1)S(1)}, u32[]{:S(2)}, u32[]{:S(2)}) async-start(bf16[2,4,128,128]{3,2,0,1:T(8,128)(2,1)} %copy.79), calls=%async_computation.2 | async-start | bytes 524288 | tf_op jit(solution)/shard_map/all_to_all | solution.py:157
  113.3 11.1 %all-to-all-done.2 = bf16[2,4,128,128]{3,2,0,1:T(8,128)(2,1)S(1)} async-done(((bf16[2,4,128,128]{3,2,0,1:T(8,128)(2,1)}), bf16[2,4,128,128]{3,2,0,1:T(8,128)(2,1)S(1)}, u32[]{:S(2)}, u32[]{:S(2)}) %all-to-all-start.2) | async-done | bytes 262176 | tf_op jit(solution)/shard_map/all_to_all | solution.py:157
  124.4 3.1 %collective-permute-start.6 = (bf16[1,512,256]{1,2,0:T(8,128)(2,1)S(1)}, bf16[1,512,256]{1,2,0:T(8,128)(2,1)S(1)}, u32[]{:S(2)}, u32[]{:S(2)}) collective-permute-start(bf16[1,512,256]{1,2,0:T(8,128)(2,1)S(1)} %fusion.31), channel_id=1, source_target_pairs={{0,16},{16,0},{1,17},{17,1},{2,18},{18,2},{3,19},{19,3},{4,20},{20... | collective-permute-start | bytes 786440 | tf_op jit(solution)/shard_map/ppermute | solution.py:74
  127.5 14.7 %collective-permute-done.6 = bf16[1,512,256]{1,2,0:T(8,128)(2,1)S(1)} collective-permute-done((bf16[1,512,256]{1,2,0:T(8,128)(2,1)S(1)}, bf16[1,512,256]{1,2,0:T(8,128)(2,1)S(1)}, u32[]{:S(2)}, u32[]{:S(2)}) %collective-permute-start.6) | collective-permute-done | bytes 262176 | tf_op jit(solution)/shard_map/ppermute | solution.py:74
  142.5 1.5 broadcast_in_dim.155
  144.0 3.7 %all-to-all-start.4 = ((bf16[4,2,1,512,256]{4,3,1,2,0:T(8,128)(2,1)}), bf16[4,2,1,512,256]{4,3,1,2,0:T(8,128)(2,1)S(1)}, u32[]{:S(2)}, u32[]{:S(2)}) async-start(bf16[4,2,1,512,256]{4,3,1,2,0:T(8,128)(2,1)} %broadcast_in_dim.155), calls=%async_computation.4 | async-start | bytes 4194304 | tf_op jit(solution)/shard_map/all_to_all | solution.py:83
  147.8 25.7 %all-to-all-done.4 = bf16[4,2,1,512,256]{4,3,1,2,0:T(8,128)(2,1)S(1)} async-done(((bf16[4,2,1,512,256]{4,3,1,2,0:T(8,128)(2,1)}), bf16[4,2,1,512,256]{4,3,1,2,0:T(8,128)(2,1)S(1)}, u32[]{:S(2)}, u32[]{:S(2)}) %all-to-all-start.4) | async-done | bytes 2097184 | tf_op jit(solution)/shard_map/all_to_all | solution.py:83
  173.5 0.5 fusion.5
  174.1 2.5 %slice-done.1 = bf16[2048,1280]{1,0:T(8,128)(2,1)S(1)} async-done(((bf16[2048,1920]{1,0:T(8,128)(2,1)}), bf16[2048,1280]{1,0:T(8,128)(2,1)S(1)}, s32[]{:S(2)}) %slice-start.1) | async-done | bytes 5242904 | tf_op jit(solution)/shard_map/slice | solution.py:199
  176.6 2.9 %fusion.8 = f32[1,512,1280]{2,1,0:T(8,128)S(1)} fusion(bf16[2,4,256,1280]{3,2,1,0:T(8,128)(2,1)S(1)} %bitcast.151, bf16[4,2,1,512,256]{4,3,1,2,0:T(8,128)(2,1)S(1)} %all-to-all-done.4, f32[4,2,256]{2,1,0:T(2,128)S(1)} %copy.87, f32[512]{0:T(512)S(1)} %add_rsqrt_fusion.1), kind=kOutput, calls=%fused_computation.16 | convolution fusion | flops 2688548864 | bytes 9971712 | tf_op jit(solution)/shard_map/xzpse,zxen->psn/dot_general | solution.py:105
  179.5 1.9 convert_bitcast_fusion
  181.6 1.1 copy.91
  182.7 3.5 %all-to-all-start.6 = ((bf16[4,1,256,2,256]{2,4,3,1,0:T(8,128)(2,1)}), bf16[4,1,256,2,256]{2,4,3,1,0:T(8,128)(2,1)S(1)}, u32[]{:S(2)}, u32[]{:S(2)}) async-start(bf16[4,1,256,2,256]{2,4,3,1,0:T(8,128)(2,1)} %copy.91), calls=%async_computation.6 | async-start | bytes 2097152 | tf_op jit(solution)/shard_map/all_to_all | solution.py:87
  186.2 1.0 copy.89
  187.2 12.6 %all-to-all-done.6 = bf16[4,1,256,2,256]{2,4,3,1,0:T(8,128)(2,1)S(1)} async-done(((bf16[4,1,256,2,256]{2,4,3,1,0:T(8,128)(2,1)}), bf16[4,1,256,2,256]{2,4,3,1,0:T(8,128)(2,1)S(1)}, u32[]{:S(2)}, u32[]{:S(2)}) %all-to-all-start.6) | async-done | bytes 1048608 | tf_op jit(solution)/shard_map/all_to_all | solution.py:87
  199.9 3.5 %all-to-all-start.5 = ((bf16[4,1,256,2,256]{2,4,3,1,0:T(8,128)(2,1)}), bf16[4,1,256,2,256]{2,4,3,1,0:T(8,128)(2,1)S(1)}, u32[]{:S(2)}, u32[]{:S(2)}) async-start(bf16[4,1,256,2,256]{2,4,3,1,0:T(8,128)(2,1)} %copy.89), calls=%async_computation.5 | async-start | bytes 2097152 | tf_op jit(solution)/shard_map/all_to_all | solution.py:87
  203.6 0.8 scatter_fusion.1
  204.6 4.3 %collective-permute-start.8 = (bf16[1,256,256]{1,2,0:T(8,128)(2,1)S(1)}, bf16[1,256,256]{1,2,0:T(8,128)(2,1)S(1)}, u32[]{:S(2)}, u32[]{:S(2)}) collective-permute-start(bf16[1,256,256]{1,2,0:T(8,128)(2,1)S(1)} %bitcast_convert_fusion.1), channel_id=1, source_target_pairs={{0,16},{16,0},{1,17},{17,1},{2,18},{18,2},{3,19},{19,3},{4,20},{20... | collective-permute-start | bytes 393224 | tf_op jit(solution)/shard_map/ppermute | solution.py:74
  208.8 7.4 %all-to-all-done.5 = bf16[4,1,256,2,256]{2,4,3,1,0:T(8,128)(2,1)S(1)} async-done(((bf16[4,1,256,2,256]{2,4,3,1,0:T(8,128)(2,1)}), bf16[4,1,256,2,256]{2,4,3,1,0:T(8,128)(2,1)S(1)}, u32[]{:S(2)}, u32[]{:S(2)}) %all-to-all-start.5) | async-done | bytes 1048608 | tf_op jit(solution)/shard_map/all_to_all | solution.py:87
  216.4 5.1 %collective-permute-start.7 = (bf16[1,256,256]{1,2,0:T(8,128)(2,1)S(1)}, bf16[1,256,256]{1,2,0:T(8,128)(2,1)S(1)}, u32[]{:S(2)}, u32[]{:S(2)}) collective-permute-start(bf16[1,256,256]{1,2,0:T(8,128)(2,1)S(1)} %bitcast_convert_fusion.2), channel_id=1, source_target_pairs={{0,16},{16,0},{1,17},{17,1},{2,18},{18,2},{3,19},{19,3},{4,20},{20... | collective-permute-start | bytes 393224 | tf_op jit(solution)/shard_map/ppermute | solution.py:74
  221.6 3.8 %collective-permute-done.7 = bf16[1,256,256]{1,2,0:T(8,128)(2,1)S(1)} collective-permute-done((bf16[1,256,256]{1,2,0:T(8,128)(2,1)S(1)}, bf16[1,256,256]{1,2,0:T(8,128)(2,1)S(1)}, u32[]{:S(2)}, u32[]{:S(2)}) %collective-permute-start.7) | collective-permute-done | bytes 131104 | tf_op jit(solution)/shard_map/ppermute | solution.py:74
  225.5 0.8 copy.93
  (112 shorter events, 3.1 us)
Async XLA Ops:
  7.2 2.9 %copy-start = (f32[2,64,256]{2,1,0:T(8,128)S(1)}, f32[2,64,256]{2,1,0:T(8,128)}, u32[]{:S(2)}) copy-start(f32[2,64,256]{2,1,0:T(8,128)} %param.20) | copy-start | bytes 393220
  7.2 3.9 %copy-start.16 = (f32[128,64]{0,1:T(8,128)S(1)}, f32[128,64]{0,1:T(8,128)}, u32[]{:S(2)}) copy-start(f32[128,64]{0,1:T(8,128)} %param.21) | copy-start | bytes 98308
  7.2 10.5 %copy-start.12 = (bf16[1,512,256]{2,1,0:T(8,128)(2,1)S(1)}, bf16[1,512,256]{2,1,0:T(8,128)(2,1)}, u32[]{:S(2)}) copy-start(bf16[1,512,256]{2,1,0:T(8,128)(2,1)} %param.16) | copy-start | bytes 786436
  7.2 166.9 %all-gather.2.cloned.1.call-start = ((), (), s32[]{:S(2)}) async-start(), calls=%async_computation.7 | async-start | bytes 8110080 | tf_op jit(solution)/shard_map/all_gather | solution.py:196
  11.8 13.8 %all-to-all-start.1 = ((bf16[4,64,384]{2,1,0:T(8,128)(2,1)}), bf16[4,64,384]{2,1,0:T(8,128)(2,1)S(1)}, u32[]{:S(2)}, u32[]{:S(2)}) async-start(bf16[4,64,384]{2,1,0:T(8,128)(2,1)} %broadcast_in_dim.88), calls=%async_computation.1 | async-start | bytes 393216 | tf_op jit(solution)/shard_map/all_to_all | solution.py:115
  17.8 14.9 %collective-permute-start = (bf16[1,512,256]{1,2,0:T(8,128)(2,1)S(1)}, bf16[1,512,256]{1,2,0:T(8,128)(2,1)S(1)}, u32[]{:S(2)}, u32[]{:S(2)}) collective-permute-start(bf16[1,512,256]{1,2,0:T(8,128)(2,1)S(1)} %copy.70), channel_id=1, source_target_pairs={{0,16},{16,0},{1,17},{17,1},{2,18},{18,2},{3,19},{19,3},{4,20},{20... | collective-permute-start | bytes 786440 | tf_op jit(solution)/shard_map/ppermute | solution.py:74
  25.5 13.3 %collective-permute-start.3 = (bf16[256,384]{1,0:T(8,128)(2,1)S(1)}, bf16[256,384]{1,0:T(8,128)(2,1)S(1)}, u32[]{:S(2)}, u32[]{:S(2)}) collective-permute-start(bf16[256,384]{1,0:T(8,128)(2,1)S(1)} %bitcast.164), channel_id=1, source_target_pairs={{0,192},{64,0},{128,64},{192,128},{1,193},{65,1},{129,65},{193,129... | collective-permute-start | bytes 589832 | tf_op jit(solution)/shard_map/ppermute | solution.py:120
  26.0 12.8 %collective-permute-start.2 = (bf16[256,384]{1,0:T(8,128)(2,1)S(1)}, bf16[256,384]{1,0:T(8,128)(2,1)S(1)}, u32[]{:S(2)}, u32[]{:S(2)}) collective-permute-start(bf16[256,384]{1,0:T(8,128)(2,1)S(1)} %bitcast.165), channel_id=1, source_target_pairs={{0,128},{64,192},{128,0},{192,64},{1,129},{65,193},{129,1},{193,65... | collective-permute-start | bytes 589832 | tf_op jit(solution)/shard_map/ppermute | solution.py:120
  28.6 10.3 %collective-permute-start.1 = (bf16[256,384]{1,0:T(8,128)(2,1)S(1)}, bf16[256,384]{1,0:T(8,128)(2,1)S(1)}, u32[]{:S(2)}, u32[]{:S(2)}) collective-permute-start(bf16[256,384]{1,0:T(8,128)(2,1)S(1)} %bitcast.166), channel_id=1, source_target_pairs={{0,64},{64,128},{128,192},{192,0},{1,65},{65,129},{129,193},{193,1... | collective-permute-start | bytes 589832 | tf_op jit(solution)/shard_map/ppermute | solution.py:120
  34.5 29.9 %all-to-all-start = ((bf16[4,2,1,512,256]{4,3,1,2,0:T(8,128)(2,1)}), bf16[4,2,1,512,256]{4,3,1,2,0:T(8,128)(2,1)S(1)}, u32[]{:S(2)}, u32[]{:S(2)}) async-start(bf16[4,2,1,512,256]{4,3,1,2,0:T(8,128)(2,1)} %broadcast_in_dim.86), calls=%async_computation | async-start | bytes 4194304 | tf_op jit(solution)/shard_map/all_to_all | solution.py:83
  38.9 3.9 %copy-start.17 = (f32[2048]{0:T(1024)S(1)}, f32[2048]{0:T(1024)}, u32[]{:S(2)}) copy-start(f32[2048]{0:T(1024)} %param.24) | copy-start | bytes 24580
  42.8 2.7 %collective-permute-start.4 = (bf16[4,256,384]{2,1,0:T(8,128)(2,1)}, bf16[4,256,384]{2,1,0:T(8,128)(2,1)}, u32[]{:S(2)}, u32[]{:S(2)}) collective-permute-start(bf16[4,256,384]{2,1,0:T(8,128)(2,1)} %broadcast_select_fusion), channel_id=1, source_target_pairs={{0,32},{32,0},{1,33},{33,1},{2,34},{34,2},{3,35},{35,3},{4,36},{36... | collective-permute-start | bytes 2359304 | tf_op jit(solution)/shard_map/ppermute | solution.py:125
  64.5 1.2 copy-start.4
  65.7 0.9 copy-start.20
  65.7 1.4 copy-start.21
  65.7 1.5 copy-start.14
  65.7 1.5 copy-start.15
  66.6 1.0 copy-start.13
  67.1 1.1 copy-start.10
  71.3 3.8 %copy-start.19 = (s32[4,4]{1,0:T(4,128)S(1)}, s32[4,4]{1,0:T(4,128)}, u32[]{:S(2)}) copy-start(s32[4,4]{1,0:T(4,128)} %param.18) | copy-start | bytes 196
  71.3 4.1 %copy-start.11 = (bf16[512,64]{0,1:T(8,128)(2,1)S(1)}, bf16[512,64]{0,1:T(8,128)(2,1)}, u32[]{:S(2)}) copy-start(bf16[512,64]{0,1:T(8,128)(2,1)} %copy-done.10) | copy-start | bytes 196612
  71.3 28.5 %all-to-all-start.3 = ((bf16[4,1,512,2,256]{2,4,3,1,0:T(8,128)(2,1)}), bf16[4,1,512,2,256]{2,4,3,1,0:T(8,128)(2,1)S(1)}, u32[]{:S(2)}, u32[]{:S(2)}) async-start(bf16[4,1,512,2,256]{2,4,3,1,0:T(8,128)(2,1)} %copy.83), calls=%async_computation.3 | async-start | bytes 4194304 | tf_op jit(solution)/shard_map/all_to_all | solution.py:87
  76.3 28.3 %copy-start.8 = (bf16[1,4,128,128]{2,1,3,0:T(4,128)(2,1)S(1)}, bf16[1,4,128,128]{2,1,3,0:T(4,128)(2,1)}, u32[]{:S(2)}) copy-start(bf16[1,4,128,128]{2,1,3,0:T(4,128)(2,1)} %get-tuple-element.48) | copy-start | bytes 393220
  99.8 4.8 %copy-start.9 = (bf16[1,4,128,128]{2,1,3,0:T(4,128)(2,1)S(1)}, bf16[1,4,128,128]{2,1,3,0:T(4,128)(2,1)}, u32[]{:S(2)}) copy-start(bf16[1,4,128,128]{2,1,3,0:T(4,128)(2,1)} %get-tuple-element.49) | copy-start | bytes 393220
  100.2 13.0 %collective-permute-start.5 = (bf16[1,512,256]{1,2,0:T(8,128)(2,1)S(1)}, bf16[1,512,256]{1,2,0:T(8,128)(2,1)S(1)}, u32[]{:S(2)}, u32[]{:S(2)}) collective-permute-start(bf16[1,512,256]{1,2,0:T(8,128)(2,1)S(1)} %bitcast_convert_fusion), channel_id=1, source_target_pairs={{0,16},{16,0},{1,17},{17,1},{2,18},{18,2},{3,19},{19,3},{4,20},{20... | collective-permute-start | bytes 786440 | tf_op jit(solution)/shard_map/ppermute | solution.py:74
  106.6 17.8 %all-to-all-start.2 = ((bf16[2,4,128,128]{3,2,0,1:T(8,128)(2,1)}), bf16[2,4,128,128]{3,2,0,1:T(8,128)(2,1)S(1)}, u32[]{:S(2)}, u32[]{:S(2)}) async-start(bf16[2,4,128,128]{3,2,0,1:T(8,128)(2,1)} %copy.79), calls=%async_computation.2 | async-start | bytes 524288 | tf_op jit(solution)/shard_map/all_to_all | solution.py:157
  113.3 30.8 %copy-start.2 = (bf16[1,512,256]{1,2,0:T(8,128)(2,1)}, bf16[1,512,256]{1,2,0:T(8,128)(2,1)S(1)}, u32[]{:S(2)}) copy-start(bf16[1,512,256]{1,2,0:T(8,128)(2,1)S(1)} %fusion.31) | copy-start | bytes 786436
  124.4 17.9 %copy-start.5 = (bf16[2,4,128,128]{3,2,0,1:T(8,128)(2,1)}, bf16[2,4,128,128]{3,2,0,1:T(8,128)(2,1)S(1)}, u32[]{:S(2)}) copy-start(bf16[2,4,128,128]{3,2,0,1:T(8,128)(2,1)S(1)} %all-to-all-done.2) | copy-start | bytes 786436
  124.4 17.8 %collective-permute-start.6 = (bf16[1,512,256]{1,2,0:T(8,128)(2,1)S(1)}, bf16[1,512,256]{1,2,0:T(8,128)(2,1)S(1)}, u32[]{:S(2)}, u32[]{:S(2)}) collective-permute-start(bf16[1,512,256]{1,2,0:T(8,128)(2,1)S(1)} %fusion.31), channel_id=1, source_target_pairs={{0,16},{16,0},{1,17},{17,1},{2,18},{18,2},{3,19},{19,3},{4,20},{20... | collective-permute-start | bytes 786440 | tf_op jit(solution)/shard_map/ppermute | solution.py:74
  144.0 3.8 %copy-start.18 = (f32[2048]{0:T(1024)S(1)}, f32[2048]{0:T(1024)}, u32[]{:S(2)}) copy-start(f32[2048]{0:T(1024)} %param.25) | copy-start | bytes 24580
  144.0 29.5 %all-to-all-start.4 = ((bf16[4,2,1,512,256]{4,3,1,2,0:T(8,128)(2,1)}), bf16[4,2,1,512,256]{4,3,1,2,0:T(8,128)(2,1)S(1)}, u32[]{:S(2)}, u32[]{:S(2)}) async-start(bf16[4,2,1,512,256]{4,3,1,2,0:T(8,128)(2,1)} %broadcast_in_dim.155), calls=%async_computation.4 | async-start | bytes 4194304 | tf_op jit(solution)/shard_map/all_to_all | solution.py:83
  174.1 2.5 %slice-start.1 = ((bf16[2048,1920]{1,0:T(8,128)(2,1)}), bf16[2048,1280]{1,0:T(8,128)(2,1)S(1)}, s32[]{:S(2)}) async-start(bf16[2048,1920]{1,0:T(8,128)(2,1)} %all-gather.2.cloned.1.call-done), calls=%async_computation.9 | async-start | bytes 10485760 | tf_op jit(solution)/shard_map/slice | solution.py:199
  176.6 2.9 %slice-start = ((bf16[2048,1920]{1,0:T(8,128)(2,1)}), bf16[2048,640]{1,0:T(8,128)(2,1)S(1)}, s32[]{:S(2)}) async-start(bf16[2048,1920]{1,0:T(8,128)(2,1)} %all-gather.2.cloned.1.call-done), calls=%async_computation.8 | async-start | bytes 5242880 | tf_op jit(solution)/shard_map/slice | solution.py:200
  182.7 17.2 %all-to-all-start.6 = ((bf16[4,1,256,2,256]{2,4,3,1,0:T(8,128)(2,1)}), bf16[4,1,256,2,256]{2,4,3,1,0:T(8,128)(2,1)S(1)}, u32[]{:S(2)}, u32[]{:S(2)}) async-start(bf16[4,1,256,2,256]{2,4,3,1,0:T(8,128)(2,1)} %copy.91), calls=%async_computation.6 | async-start | bytes 2097152 | tf_op jit(solution)/shard_map/all_to_all | solution.py:87
  186.2 17.4 %copy-start.6 = (bf16[2,4,128,128]{3,2,0,1:T(8,128)(2,1)S(1)}, bf16[2,4,128,128]{3,2,0,1:T(8,128)(2,1)}, u32[]{:S(2)}) copy-start(bf16[2,4,128,128]{3,2,0,1:T(8,128)(2,1)} %copy-done.5) | copy-start | bytes 786436
  199.9 16.3 %all-to-all-start.5 = ((bf16[4,1,256,2,256]{2,4,3,1,0:T(8,128)(2,1)}), bf16[4,1,256,2,256]{2,4,3,1,0:T(8,128)(2,1)S(1)}, u32[]{:S(2)}, u32[]{:S(2)}) async-start(bf16[4,1,256,2,256]{2,4,3,1,0:T(8,128)(2,1)} %copy.89), calls=%async_computation.5 | async-start | bytes 2097152 | tf_op jit(solution)/shard_map/all_to_all | solution.py:87
  204.4 17.2 %copy-start.7 = (bf16[2,4,128,128]{3,2,1,0:T(8,128)(2,1)}, bf16[2,4,128,128]{3,2,1,0:T(8,128)(2,1)S(1)}, u32[]{:S(2)}) copy-start(bf16[2,4,128,128]{3,2,1,0:T(8,128)(2,1)S(1)} %scatter_fusion.1) | copy-start | bytes 786436
  204.5 20.9 %copy-start.3 = (bf16[1,512,256]{1,2,0:T(8,128)(2,1)S(1)}, bf16[1,512,256]{1,2,0:T(8,128)(2,1)}, u32[]{:S(2)}) copy-start(bf16[1,512,256]{1,2,0:T(8,128)(2,1)} %copy-done.2) | copy-start | bytes 786436
  204.5 21.8 %copy-start.1 = (f32[2,64,256]{2,1,0:T(8,128)S(1)}, f32[2,64,256]{2,1,0:T(8,128)}, u32[]{:S(2)}) copy-start(f32[2,64,256]{2,1,0:T(8,128)} %param.20) | copy-start | bytes 393220
  204.6 16.9 %collective-permute-start.8 = (bf16[1,256,256]{1,2,0:T(8,128)(2,1)S(1)}, bf16[1,256,256]{1,2,0:T(8,128)(2,1)S(1)}, u32[]{:S(2)}, u32[]{:S(2)}) collective-permute-start(bf16[1,256,256]{1,2,0:T(8,128)(2,1)S(1)} %bitcast_convert_fusion.1), channel_id=1, source_target_pairs={{0,16},{16,0},{1,17},{17,1},{2,18},{18,2},{3,19},{19,3},{4,20},{20... | collective-permute-start | bytes 393224 | tf_op jit(solution)/shard_map/ppermute | solution.py:74
  216.4 9.0 %collective-permute-start.7 = (bf16[1,256,256]{1,2,0:T(8,128)(2,1)S(1)}, bf16[1,256,256]{1,2,0:T(8,128)(2,1)S(1)}, u32[]{:S(2)}, u32[]{:S(2)}) collective-permute-start(bf16[1,256,256]{1,2,0:T(8,128)(2,1)S(1)} %bitcast_convert_fusion.2), channel_id=1, source_target_pairs={{0,16},{16,0},{1,17},{17,1},{2,18},{18,2},{3,19},{19,3},{4,20},{20... | collective-permute-start | bytes 393224 | tf_op jit(solution)/shard_map/ppermute | solution.py:74
Sparse Core Ops, SparseCore 0:
  10.1 104.2 all-gather.1
